TPU v7x, 256 devices: a whole 4x4x8 slice. The times are simulated.
256 devices in a mesh: win: 8 (over y, core), chan: 32 (over x, z).
Axes of the slice: x: 4, y: 4, z: 8, core: 2. Of those that a mesh axis runs over, the one named last changes fastest.
Arguments:
- traces: float32 [8, 15000, 4096], P('win', None, 'chan'), may hold values from -200 to 200
- pair_blocks: int32 [192, 2], P('chan'), may hold values from -1 to 31, as said below
Outputs:
- stacks: float32 [192, 512, 128], P('chan', 'win')
Inputs may be any that keep to these rules, and one draw needn't show every extreme that they name: `pair_blocks`: owner o holds rows o * 6 to (o + 1) * 6 - 1. Each row is a block pair (i, i + d) with 1 <= d <= 3, or (-1, -1) for an empty slot; every block pair with an offset in that range stands in exactly one row; some owner has all 6 of its slots filled.
All inputs are finite; a program needn't handle non-finite values.
Results may differ from a plain program's by a relative error of at most 0.003.
Values may be sent and summed in bfloat16 or wider, within the bound.
No kernel may reach another device: no remote copies, remote signals or barrier semaphores. Data moves between devices by JAX's collectives and lax.ppermute only.
A program may use at most 64 MiB of HBM per device.

v0:
```python
import math

import jax
import jax.numpy as jnp
from jax import lax
from jax.sharding import PartitionSpec as P

L = 15000
NB = 512
F_LO = 64
HALF = 32
LAGS = 512


two_pi = 2.0 * math.pi


def band_tables():
    width = NB + 2 * HALF
    rows = lax.broadcasted_iota(jnp.int32, (NB, width), 0)
    cols = lax.broadcasted_iota(jnp.int32, (NB, width), 1)
    smoother = jnp.where(
        (cols >= rows) & (cols <= rows + 2 * HALF), 1.0 / (2 * HALF + 1), 0.0
    ).astype(jnp.float32)
    taper = jnp.sin(
        math.pi * (lax.broadcasted_iota(jnp.int32, (NB,), 0).astype(jnp.float32) + 0.5) / NB
    )
    bins = F_LO + lax.broadcasted_iota(jnp.int32, (LAGS, NB), 1)
    lagged = lax.broadcasted_iota(jnp.int32, (LAGS, NB), 0) - LAGS // 2
    angle = (bins * lagged % L).astype(jnp.float32) * (two_pi / L)
    table = jnp.stack([jnp.cos(angle), -jnp.sin(angle)], axis=1).astype(jnp.bfloat16)
    return (smoother, taper, table)


def whiten_local(traces, smoother, taper):
    width = NB + 2 * HALF
    windows, total, channels = traces.shape
    block = math.gcd(total, 3000)

    def add_block(index, acc):
        start = index * block
        piece = lax.dynamic_slice_in_dim(traces, start, block, 1)
        bins = F_LO - HALF + lax.broadcasted_iota(jnp.int32, (width, block), 0)
        times = start + lax.broadcasted_iota(jnp.int32, (width, block), 1)
        angle = (bins * times % total).astype(jnp.float32) * (two_pi / total)
        basis = jnp.concatenate([jnp.cos(angle), -jnp.sin(angle)], axis=0)
        return acc + jnp.einsum(
            "qn,wnc->wqc",
            basis,
            piece,
            precision=lax.Precision.HIGHEST,
            preferred_element_type=jnp.float32,
        )

    spec = lax.fori_loop(
        0, total // block, add_block, jnp.zeros((windows, 2 * width, channels), jnp.float32)
    )
    real = spec[:, :width]
    imag = spec[:, width:]
    power = real * real + imag * imag
    level = jnp.einsum("bm,wmc->wbc", smoother, power, precision=lax.Precision.HIGHEST) + 1e-06
    factor = taper[None, :, None] * lax.rsqrt(level)
    white = jnp.stack(
        [real[:, HALF : HALF + NB] * factor, imag[:, HALF : HALF + NB] * factor], axis=1
    )
    return white.astype(jnp.bfloat16)


def cross_spectra(left, right):
    left_re = left[..., 0, :, :].astype(jnp.float32)
    left_im = left[..., 1, :, :].astype(jnp.float32)
    right_re = right[..., 0, :, :].astype(jnp.float32)
    right_im = right[..., 1, :, :].astype(jnp.float32)
    real = left_re * right_re + left_im * right_im
    imag = left_im * right_re - left_re * right_im
    return jnp.stack([real, imag], axis=-3).astype(jnp.bfloat16)


def correlate(cross, table, factor):
    return jnp.einsum("tqb,swqbk->stk", table, cross, preferred_element_type=jnp.float32) * factor


def body(traces, pair_blocks):
    smoother, taper, table = band_tables()
    white = whiten_local(traces, smoother, taper)
    windows_all = traces.shape[0] * lax.axis_size("win")
    factor = 1.0 / math.sqrt(NB * windows_all)
    filled = (pair_blocks[:, 0] >= 0)[:, None, None]
    every = lax.all_gather(white[None], "chan", axis=0, tiled=True)
    left_index = jnp.maximum(pair_blocks[:, 0], 0)
    right_index = jnp.maximum(pair_blocks[:, 1], 0)
    cross = cross_spectra(jnp.take(every, left_index, axis=0), jnp.take(every, right_index, axis=0))
    local = correlate(cross, table, factor)
    local = jnp.where(filled, local, 0.0)
    return lax.psum_scatter(local, "win", scatter_dimension=1, tiled=True)


def solution(mesh):
    in_specs = (P("win", None, "chan"), P("chan", None))
    out_specs = P("chan", "win", None)
    return jax.shard_map(body, mesh=mesh, in_specs=in_specs, out_specs=out_specs, check_vma=False)
```

profile of v0, /device:TPU:6, one launch (start us, length us, event | category | flops | bytes accessed | tf_op | source)
XLA Modules:
  0.0 422.1 jit_solution(8498667945533063919)
XLA Ops:
  6.6 253.2 %while.16 = (s32[]{:T(128)}, f32[1,1152,128]{1,2,0:T(8,128)S(1)}, f32[1,15000,128]{2,1,0:T(8,128)}, s32[]{:T(128)}, s32[]{:T(128)}, /*index=5*/s32[]{:T(128)}, s32[]{:T(128)}) while((s32[]{:T(128)}, f32[1,1152,128]{1,2,0:T(8,128)S(1)}, f32[1,15000,128]{2,1,0:T(8,128)}, s32[]{:T(128)}, s32[]{:T(128)}, /*index=5*/s32[]{:T(128)}, ...), condition=%wide.region_1.2_spmd.clone, body=%wide.region_0.1_spmd.clone.sunk | while | flops 5329450496 | bytes 30724180 | solution.py:55
  6.6 30.7 %fusion.84 = (f32[576,3000]{1,0:T(8,128)}, f32[576,3000]{1,0:T(8,128)}) fusion(s32[3000]{0:T(1024)S(1)} %iota_add_fusion.6, s32[576]{0:T(1024)S(1)} %iota_add_fusion.7), kind=kLoop, calls=%fused_computation.13.clone.1 | loop fusion | flops 17280000 | bytes 13838304 | tf_op jit(solution)/shard_map/while/body/eval_jaxpr/cos | solution.py:46
  37.4 19.8 %fusion.85 = f32[1,1152,128]{1,2,0:T(8,128)S(1)} fusion(f32[576,3000]{1,0:T(8,128)} %get-tuple-element.151, f32[576,3000]{1,0:T(8,128)} %get-tuple-element.152, f32[1,15000,128]{2,1,0:T(8,128)} %get-tuple-element.169, s32[]{:T(128)S(6)} %select_n.131, f32[1,1152,128]{1,2,0:T(8,128)S(1)} %get-tuple-element.161, pred[]{:T(512)S(6)} %compare.3), kind=kOutput, calls=%fused_computation.16.clone.1 | convolution fusion | flops 5312166912 | bytes 16871428 | tf_op jit(solution)/shard_map/while/body/eval_jaxpr/qn,wnc->wqc/dot_general | solution.py:47
  57.2 30.7 %fusion.84 = (f32[576,3000]{1,0:T(8,128)}, f32[576,3000]{1,0:T(8,128)}) fusion(s32[3000]{0:T(1024)S(1)} %iota_add_fusion.6, s32[576]{0:T(1024)S(1)} %iota_add_fusion.7), kind=kLoop, calls=%fused_computation.13.clone.1 | loop fusion | flops 17280000 | bytes 13838304 | tf_op jit(solution)/shard_map/while/body/eval_jaxpr/cos | solution.py:46
  88.0 19.8 %fusion.85 = f32[1,1152,128]{1,2,0:T(8,128)S(1)} fusion(f32[576,3000]{1,0:T(8,128)} %get-tuple-element.151, f32[576,3000]{1,0:T(8,128)} %get-tuple-element.152, f32[1,15000,128]{2,1,0:T(8,128)} %get-tuple-element.169, s32[]{:T(128)S(6)} %select_n.131, f32[1,1152,128]{1,2,0:T(8,128)S(1)} %get-tuple-element.161, pred[]{:T(512)S(6)} %compare.3), kind=kOutput, calls=%fused_computation.16.clone.1 | convolution fusion | flops 5312166912 | bytes 16871428 | tf_op jit(solution)/shard_map/while/body/eval_jaxpr/qn,wnc->wqc/dot_general | solution.py:47
  107.8 30.7 %fusion.84 = (f32[576,3000]{1,0:T(8,128)}, f32[576,3000]{1,0:T(8,128)}) fusion(s32[3000]{0:T(1024)S(1)} %iota_add_fusion.6, s32[576]{0:T(1024)S(1)} %iota_add_fusion.7), kind=kLoop, calls=%fused_computation.13.clone.1 | loop fusion | flops 17280000 | bytes 13838304 | tf_op jit(solution)/shard_map/while/body/eval_jaxpr/cos | solution.py:46
  138.6 19.8 %fusion.85 = f32[1,1152,128]{1,2,0:T(8,128)S(1)} fusion(f32[576,3000]{1,0:T(8,128)} %get-tuple-element.151, f32[576,3000]{1,0:T(8,128)} %get-tuple-element.152, f32[1,15000,128]{2,1,0:T(8,128)} %get-tuple-element.169, s32[]{:T(128)S(6)} %select_n.131, f32[1,1152,128]{1,2,0:T(8,128)S(1)} %get-tuple-element.161, pred[]{:T(512)S(6)} %compare.3), kind=kOutput, calls=%fused_computation.16.clone.1 | convolution fusion | flops 5312166912 | bytes 16871428 | tf_op jit(solution)/shard_map/while/body/eval_jaxpr/qn,wnc->wqc/dot_general | solution.py:47
  158.4 30.7 %fusion.84 = (f32[576,3000]{1,0:T(8,128)}, f32[576,3000]{1,0:T(8,128)}) fusion(s32[3000]{0:T(1024)S(1)} %iota_add_fusion.6, s32[576]{0:T(1024)S(1)} %iota_add_fusion.7), kind=kLoop, calls=%fused_computation.13.clone.1 | loop fusion | flops 17280000 | bytes 13838304 | tf_op jit(solution)/shard_map/while/body/eval_jaxpr/cos | solution.py:46
  189.2 19.8 %fusion.85 = f32[1,1152,128]{1,2,0:T(8,128)S(1)} fusion(f32[576,3000]{1,0:T(8,128)} %get-tuple-element.151, f32[576,3000]{1,0:T(8,128)} %get-tuple-element.152, f32[1,15000,128]{2,1,0:T(8,128)} %get-tuple-element.169, s32[]{:T(128)S(6)} %select_n.131, f32[1,1152,128]{1,2,0:T(8,128)S(1)} %get-tuple-element.161, pred[]{:T(512)S(6)} %compare.3), kind=kOutput, calls=%fused_computation.16.clone.1 | convolution fusion | flops 5312166912 | bytes 16871428 | tf_op jit(solution)/shard_map/while/body/eval_jaxpr/qn,wnc->wqc/dot_general | solution.py:47
  209.0 30.7 %fusion.84 = (f32[576,3000]{1,0:T(8,128)}, f32[576,3000]{1,0:T(8,128)}) fusion(s32[3000]{0:T(1024)S(1)} %iota_add_fusion.6, s32[576]{0:T(1024)S(1)} %iota_add_fusion.7), kind=kLoop, calls=%fused_computation.13.clone.1 | loop fusion | flops 17280000 | bytes 13838304 | tf_op jit(solution)/shard_map/while/body/eval_jaxpr/cos | solution.py:46
  239.8 19.8 %fusion.85 = f32[1,1152,128]{1,2,0:T(8,128)S(1)} fusion(f32[576,3000]{1,0:T(8,128)} %get-tuple-element.151, f32[576,3000]{1,0:T(8,128)} %get-tuple-element.152, f32[1,15000,128]{2,1,0:T(8,128)} %get-tuple-element.169, s32[]{:T(128)S(6)} %select_n.131, f32[1,1152,128]{1,2,0:T(8,128)S(1)} %get-tuple-element.161, pred[]{:T(512)S(6)} %compare.3), kind=kOutput, calls=%fused_computation.16.clone.1 | convolution fusion | flops 5312166912 | bytes 16871428 | tf_op jit(solution)/shard_map/while/body/eval_jaxpr/qn,wnc->wqc/dot_general | solution.py:47
  259.8 0.0 copy-start.2
  259.8 1.4 fusion.69
  261.3 0.8 copy.21
  262.1 0.0 all-gather.2.cloned.1.call-update
  262.1 0.0 reduce-scatter.2.cloned.1.call-start
  262.3 5.7 %cosine_convert_fusion = (bf16[512,1,512]{2,0,1:T(8,128)(2,1)}, bf16[512,1,512]{2,0,1:T(8,128)(2,1)}) fusion(s32[512]{0:T(512)S(1)} %iota_add_fusion.2, s32[512]{0:T(512)S(1)} %iota_add_fusion.3), kind=kLoop, calls=%fused_computation.57 | loop fusion | flops 3145728 | bytes 1052672 | tf_op jit(solution)/shard_map/convert
  268.0 93.6 %all-gather.2.cloned.1.call-done = bf16[32,1,2,512,128]{4,3,2,1,0:T(8,128)(2,1)} async-done(((bf16[1,1,2,512,128]{4,3,2,1,0:T(8,128)(2,1)}), bf16[32,1,2,512,128]{4,3,2,1,0:T(8,128)(2,1)}) %all-gather.2.cloned.1.call-update) | async-done | bytes 8388624 | tf_op jit(solution)/shard_map/all_gather | solution.py:89
  361.6 4.2 %gather_fusion.1 = bf16[6,2,512,128]{3,2,1,0:T(8,128)(2,1)S(1)} fusion(bf16[32,2,512,128]{3,2,1,0:T(8,128)(2,1)} %bitcast.65, s32[1024]{0:T(1024)S(1)} %pad_clamp_fusion), kind=kCustom, calls=%fused_computation.1.clone | custom fusion | bytes 3145752 | tf_op jit(solution)/shard_map/jit(_take)/gather | solution.py:92
  365.9 0.7 copy.23
  366.6 4.2 %gather_fusion = bf16[6,2,512,128]{3,2,1,0:T(8,128)(2,1)S(1)} fusion(bf16[32,2,512,128]{3,2,1,0:T(8,128)(2,1)} %bitcast.66, s32[1024]{0:T(1024)S(1)} %pad_clamp_fusion.1), kind=kCustom, calls=%fused_computation.clone | custom fusion | bytes 3145752 | tf_op jit(solution)/shard_map/jit(_take)/gather | solution.py:92
  370.8 1.6 copy.22
  372.4 1.7 bitcast_select_fusion
  374.2 0.0 copy-start
  374.2 0.6 fusion.59
  374.8 0.4 copy-done
  375.2 0.2 copy-done.1
  375.4 1.0 fusion.29
  376.4 1.8 copy.24
  378.2 0.0 reduce-scatter.2.cloned.1.call-update
  378.2 35.3 %reduce-scatter.2.cloned.1.call-done = f32[6,64,128]{2,0,1:T(8,128)} async-done(((f32[6,512,128]{2,0,1:T(8,128)}), f32[6,64,128]{2,0,1:T(8,128)}) %reduce-scatter.2.cloned.1.call-update) | async-done | bytes 196624 | tf_op jit(solution)/shard_map/reduce_scatter | solution.py:95
  413.6 1.7 copy.25
  (22 shorter events, 0.2 us)
Async XLA Ops:
  6.5 355.1 %all-gather.2.cloned.1.call-start = ((), (), s32[]{:S(2)}) async-start(), calls=%async_computation.1 | async-start | bytes 8650752 | tf_op jit(solution)/shard_map/all_gather | solution.py:89
  259.8 2.4 copy-start.2
  262.1 151.4 %reduce-scatter.2.cloned.1.call-start = ((), (), s32[]{:S(2)}) async-start(), calls=%async_computation.2 | async-start | bytes 2359296 | tf_op jit(solution)/shard_map/reduce_scatter | solution.py:95
  374.2 1.0 copy-start
  374.2 1.2 copy-start.1
Sparse Core Ops, SparseCore 0:
  262.2 99.3 all-gather.1
  378.4 35.1 reduce-scatter.1
where the time goes:
time: 422 us
  other arithmetic  162 us (38%)
  waiting for transfers between devices  129 us (31%)
  matrix products  101 us (24%)
  local copies, waits for them, and re-layouts  15.7 us (4%)
  between operations  13.5 us (3%)
    cos x5, other arithmetic, add_block(): basis = jnp.concatenate([jnp.cos(angle), -jnp.sin(angle)], axis=0)  154 us
    dot_general x5, matrix products, add_block(): jnp.einsum('qn,wnc->wqc', basis, piece, precision=lax.Precision.HIGHEST,...  99.1 us
    all_gather x1, waiting for transfers between devices, body(): every = lax.all_gather(white[None], 'chan', axis=0, tiled=True)  93.6 us
    reduce_scatter x1, waiting for transfers between devices, body(): return lax.psum_scatter(local, 'win', scatter_dimension=1, tiled=True)  35.3 us
  transfers between devices with their start and end apart: 2, of which 2 were waited for; matrix products, arithmetic and copies ran while one was open for 1% of the time, Pallas kernels for 0%

commit v1 on v0

v1 whole, which is shorter than its diff:
```python
import math

import jax
import jax.numpy as jnp
from jax import lax
from jax.sharding import PartitionSpec as P

L = 15000
NB = 512
F_LO = 64
HALF = 32
LAGS = 512
REACH = 3

two_pi = 2.0 * math.pi


def band_tables():
    width = NB + 2 * HALF
    rows = lax.broadcasted_iota(jnp.int32, (NB, width), 0)
    cols = lax.broadcasted_iota(jnp.int32, (NB, width), 1)
    smoother = jnp.where(
        (cols >= rows) & (cols <= rows + 2 * HALF), 1.0 / (2 * HALF + 1), 0.0
    ).astype(jnp.float32)
    taper = jnp.sin(
        math.pi * (lax.broadcasted_iota(jnp.int32, (NB,), 0).astype(jnp.float32) + 0.5) / NB
    )
    bins = F_LO + lax.broadcasted_iota(jnp.int32, (LAGS, NB), 1)
    lagged = lax.broadcasted_iota(jnp.int32, (LAGS, NB), 0) - LAGS // 2
    angle = (bins * lagged % L).astype(jnp.float32) * (two_pi / L)
    table = jnp.stack([jnp.cos(angle), -jnp.sin(angle)], axis=1).astype(jnp.bfloat16)
    return (smoother, taper, table)


def band_dft(x, f0, nbins, outer=125, prec=lax.Precision.HIGH):
    total, channels = x.shape
    inner = total // outer
    half = outer // 2 + 1
    xb = x.reshape(outer, inner, channels)
    r = lax.broadcasted_iota(jnp.int32, (half, outer), 0)
    b = lax.broadcasted_iota(jnp.int32, (half, outer), 1)
    ang1 = ((r * b) % outer).astype(jnp.float32) * (two_pi / outer)
    basis1 = jnp.concatenate([jnp.cos(ang1), -jnp.sin(ang1)], axis=0)
    z = jnp.einsum("rb,bac->rac", basis1, xb, precision=prec, preferred_element_type=jnp.float32)
    zr, zi = z[:half], z[half:]
    r2 = lax.broadcasted_iota(jnp.int32, (half, inner), 0)
    a2 = lax.broadcasted_iota(jnp.int32, (half, inner), 1)
    ang2 = ((r2 * a2) % total).astype(jnp.float32) * (two_pi / total)
    dc = jnp.cos(ang2)[:, :, None]
    ds = jnp.sin(ang2)[:, :, None]
    wr = dc * zr + ds * zi
    wi = dc * zi - ds * zr
    nj = (f0 + nbins + outer - 1) // outer + 1
    j3 = lax.broadcasted_iota(jnp.int32, (nj, inner), 0)
    a3 = lax.broadcasted_iota(jnp.int32, (nj, inner), 1)
    ang3 = ((j3 * a3) % inner).astype(jnp.float32) * (two_pi / inner)
    basis2 = jnp.concatenate([jnp.cos(ang3), jnp.sin(ang3)], axis=0)
    u = jnp.einsum(
        "ja,srac->sjrc", basis2, jnp.stack([wr, wi]), precision=prec,
        preferred_element_type=jnp.float32,
    )
    u1, u4 = u[0, :nj], u[0, nj:]
    u3, u2 = u[1, :nj], u[1, nj:]
    dre, dim = u1 + u2, u3 - u4
    cre, cim = u1 - u2, -u3 - u4
    res_re, res_im = [], []
    f = f0
    end = f0 + nbins
    while f < end:
        j, rr = divmod(f, outer)
        if rr < half:
            stop = min(half, rr + (end - f))
            res_re.append(dre[j, rr:stop])
            res_im.append(dim[j, rr:stop])
            f += stop - rr
        else:
            s0 = outer * (j + 1) - f
            s_end = max(0, s0 - (end - f))
            res_re.append(jnp.flip(cre[j + 1, s_end + 1 : s0 + 1], axis=0))
            res_im.append(jnp.flip(cim[j + 1, s_end + 1 : s0 + 1], axis=0))
            f += s0 - s_end
    return jnp.concatenate(res_re, 0), jnp.concatenate(res_im, 0)


def whiten_local(trace, smoother, taper):
    width = NB + 2 * HALF
    real, imag = band_dft(trace, F_LO - HALF, width)
    power = real * real + imag * imag
    level = jnp.dot(smoother, power, precision=lax.Precision.HIGHEST) + 1e-06
    factor = taper[:, None] * lax.rsqrt(level)
    white = jnp.stack([real[HALF : HALF + NB] * factor, imag[HALF : HALF + NB] * factor])
    return white.astype(jnp.bfloat16)


def cross_spectra(left, right):
    left_re = left[..., 0, :, :].astype(jnp.float32)
    left_im = left[..., 1, :, :].astype(jnp.float32)
    right_re = right[..., 0, :, :].astype(jnp.float32)
    right_im = right[..., 1, :, :].astype(jnp.float32)
    real = left_re * right_re + left_im * right_im
    imag = left_im * right_re - left_re * right_im
    return jnp.stack([real, imag], axis=-3).astype(jnp.bfloat16)


def body(traces, pair_blocks):
    smoother, taper, table = band_tables()
    white = whiten_local(traces[0], smoother, taper)
    blocks = lax.axis_size("chan")
    windows_all = traces.shape[0] * lax.axis_size("win")
    factor = 1.0 / math.sqrt(NB * windows_all)
    partners = []
    for d in range(1, REACH + 1):
        perm = [(i + d, i) for i in range(blocks - d)]
        partners.append(lax.ppermute(white, "chan", perm))
    right = jnp.stack(partners)
    cross = cross_spectra(white[None], right)
    corr = jnp.einsum("tqb,dqbk->tdk", table, cross, preferred_element_type=jnp.float32) * factor
    corr = lax.psum_scatter(corr, "win", scatter_dimension=0, tiled=True)
    every = lax.all_gather(corr, "chan", axis=0)
    left_block = pair_blocks[:, 0]
    offset = pair_blocks[:, 1] - pair_blocks[:, 0]
    filled = left_block >= 0
    block_index = jnp.where(filled, left_block, 0)
    offset_index = jnp.where(filled, offset - 1, 0)
    picked = every[block_index, :, offset_index, :]
    return jnp.where(filled[:, None, None], picked, 0.0)


def solution(mesh):
    in_specs = (P("win", None, "chan"), P("chan", None))
    out_specs = P("chan", "win", None)
    return jax.shard_map(body, mesh=mesh, in_specs=in_specs, out_specs=out_specs, check_vma=False)
```

time: 422 us -> 205 us (0.49)
  other arithmetic: 162 us -> 11.3 us
  matrix products: 101 us -> 17 us
  starting transfers between devices: 0.04 us -> 13.8 us
  waiting for transfers between devices: 129 us -> 139 us
  local copies, waits for them, and re-layouts: 15.7 us -> 8.53 us
    cos x5 -> x0, other arithmetic: 154 us -> none  [add_block(): basis = jnp.concatenate([jnp.cos(angle), -jnp.sin(angle)], axis=0)]
    dot_general x7 -> x4, matrix products: 101 us -> 17 us  [the longest x1 7.84 us: band_dft(): jnp.einsum('rb,bac->rac', basis1, xb, precision=prec, preferred_element_t...]
    ppermute x0 -> x3, waiting for transfers between devices: none -> 23 us  [body(): partners.append(lax.ppermute(white, 'chan', perm))]
    ppermute x0 -> x3, starting transfers between devices: none -> 13.8 us  [body(): partners.append(lax.ppermute(white, 'chan', perm))]
    all_gather x1, waiting for transfers between devices: 93.6 us -> 80.4 us  [body(): every = lax.all_gather(corr, 'chan', axis=0)]
    gather x4 -> x1, local copies, waits for them, and re-layouts: 10.8 us -> 0.58 us  [body(): picked = every[block_index, :, offset_index, :]]
    concatenate x0 -> x4, local copies, waits for them, and re-layouts: none -> 5.27 us  [band_dft(): return (jnp.concatenate(res_re, 0), jnp.concatenate(res_im, 0))]
    another operation x3 -> x6, other arithmetic: 6.39 us -> 9.83 us
  transfers between devices with their start and end apart: 2 -> 5, of which waited for: 2 -> 5; matrix products, arithmetic and copies ran while one was open for 1% -> 2% of each run, Pallas kernels for 0% -> 0%
where the time goes in v1:
time: 205 us; the launch traced here: 204 us
  waiting for transfers between devices  139 us (68%)
  matrix products  17 us (8%)
  starting transfers between devices  13.8 us (7%)
  between operations  13.8 us (7%)
  other arithmetic  11.3 us (6%)
  local copies, waits for them, and re-layouts  8.53 us (4%)
    all_gather x1, waiting for transfers between devices, body(): every = lax.all_gather(corr, 'chan', axis=0)  80.4 us
    reduce_scatter x1, waiting for transfers between devices, body(): corr = lax.psum_scatter(corr, 'win', scatter_dimension=0, tiled=True)  35.9 us
    ppermute x3, waiting for transfers between devices, body(): partners.append(lax.ppermute(white, 'chan', perm))  23 us
    ppermute x3, starting transfers between devices, body(): partners.append(lax.ppermute(white, 'chan', perm))  13.8 us
    dot_general x1, matrix products, band_dft(): jnp.einsum('rb,bac->rac', basis1, xb, precision=prec, preferred_element_t...  7.84 us
    dot_general x1, matrix products, band_dft(): jnp.einsum('ja,srac->sjrc', basis2, jnp.stack([wr, wi]), precision=prec,...  6.09 us
    concatenate x4, local copies, waits for them, and re-layouts, band_dft(): return (jnp.concatenate(res_re, 0), jnp.concatenate(res_im, 0))  5.27 us
    another operation x2, other arithmetic  5.2 us
  transfers between devices with their start and end apart: 5, of which 5 were waited for; matrix products, arithmetic and copies ran while one was open for 2% of the time, Pallas kernels for 0%

profile of v1, /device:TPU:6, one launch (start us, length us, event | category | flops | bytes accessed | tf_op | source)
XLA Modules:
  0.0 203.6 jit_solution(3976673133231069044)
XLA Ops:
  6.5 0.2 sine_negate_fusion
  6.7 0.3 fusion.50
  7.0 0.1 fusion.65
  7.0 7.8 %fusion = f32[126,120,128]{2,0,1:T(8,128)S(1)} fusion(f32[125,120,128]{2,1,0:T(8,128)} %bitcast.98, f32[63,125]{1,0:T(8,128)S(1)} %get-tuple-element.39, f32[63,125]{1,0:T(8,128)S(1)} %get-tuple-element.40), kind=kOutput, calls=%fused_computation.2 | convolution fusion | flops 1451535744 | bytes 15484440 | tf_op jit(solution)/shard_map/rb,bac->rac/dot_general | solution.py:44
  14.9 3.0 %add_bitcast_fusion = (f32[1,63,120,128]{3,1,2,0:T(8,128)S(1)}, f32[1,63,120,128]{3,1,2,0:T(8,128)S(1)}) fusion(f32[126,120,128]{2,0,1:T(8,128)S(1)} %fusion, f32[63,120]{0,1:T(8,128)S(1)} %get-tuple-element.41, f32[63,120]{0,1:T(8,128)S(1)} %get-tuple-element.42), kind=kLoop, calls=%fused_computation.7 | loop fusion | flops 5806080 | bytes 15543360 | tf_op jit(solution)/shard_map/stack | solution.py:59
  17.9 1.5 pad_maximum_fusion
  19.4 6.1 %fusion.4 = f32[2,12,63,128]{3,1,2,0:T(8,128)S(1)} fusion(f32[2,63,120,128]{3,1,2,0:T(8,128)S(1)} %pad_maximum_fusion, f32[6,120]{1,0:T(8,128)S(1)} %get-tuple-element.43, f32[6,120]{1,0:T(8,128)S(1)} %get-tuple-element.44), kind=kOutput, calls=%fused_computation.11 | convolution fusion | flops 139347360 | bytes 8521344 | tf_op jit(solution)/shard_map/ja,srac->sjrc/dot_general | solution.py:58
  25.6 0.1 subtract_bitcast_fusion.1
  25.7 0.1 fusion.83
  25.9 0.1 fusion.82
  26.2 1.2 concatenate.31
  27.4 1.5 concatenate.32
  29.1 1.2 concatenate.34
  30.3 1.5 concatenate.33
  31.7 1.4 fusion.77
  33.2 8.0 %collective-permute-start = (bf16[2,512,128]{2,1,0:T(8,128)(2,1)S(1)}, bf16[2,512,128]{2,1,0:T(8,128)(2,1)S(1)}, u32[]{:S(2)}, u32[]{:S(2)}) collective-permute-start(bf16[2,512,128]{2,1,0:T(8,128)(2,1)S(1)} %pad_maximum_fusion.2), channel_id=1, source_target_pairs={{1,0},{2,1},{3,2},{4,3},{5,4},{6,5},{7,6},{8,7},{9,8},{10,9},{11,1... | collective-permute-start | bytes 786440 | tf_op jit(solution)/shard_map/ppermute | solution.py:114
  41.3 3.4 %collective-permute-start.1 = (bf16[2,512,128]{2,1,0:T(8,128)(2,1)S(1)}, bf16[2,512,128]{2,1,0:T(8,128)(2,1)S(1)}, u32[]{:S(2)}, u32[]{:S(2)}) collective-permute-start(bf16[2,512,128]{2,1,0:T(8,128)(2,1)S(1)} %pad_maximum_fusion.2), channel_id=1, source_target_pairs={{2,0},{3,1},{4,2},{5,3},{6,4},{7,5},{8,6},{9,7},{10,8},{11,9},{12,... | collective-permute-start | bytes 786440 | tf_op jit(solution)/shard_map/ppermute | solution.py:114
  44.6 2.4 %collective-permute-start.2 = (bf16[2,512,128]{2,1,0:T(8,128)(2,1)S(1)}, bf16[2,512,128]{2,1,0:T(8,128)(2,1)S(1)}, u32[]{:S(2)}, u32[]{:S(2)}) collective-permute-start(bf16[2,512,128]{2,1,0:T(8,128)(2,1)S(1)} %pad_maximum_fusion.2), channel_id=1, source_target_pairs={{3,0},{4,1},{5,2},{6,3},{7,4},{8,5},{9,6},{10,7},{11,8},{12,9},{13... | collective-permute-start | bytes 786440 | tf_op jit(solution)/shard_map/ppermute | solution.py:114
  47.0 4.9 %cosine_convert_fusion = (bf16[512,1,512]{2,0,1:T(8,128)(2,1)S(1)}, bf16[512,1,512]{2,0,1:T(8,128)(2,1)S(1)}) fusion(s32[512]{0:T(512)S(1)} %get-tuple-element.45, s32[512]{0:T(512)S(1)} %get-tuple-element.46), kind=kLoop, calls=%fused_computation.26 | loop fusion | flops 3145728 | bytes 1052672 | tf_op jit(solution)/shard_map/convert.12
  51.9 0.9 collective-permute-done
  52.9 9.4 %collective-permute-done.1 = bf16[2,512,128]{2,1,0:T(8,128)(2,1)S(1)} collective-permute-done((bf16[2,512,128]{2,1,0:T(8,128)(2,1)S(1)}, bf16[2,512,128]{2,1,0:T(8,128)(2,1)S(1)}, u32[]{:S(2)}, u32[]{:S(2)}) %collective-permute-start.1) | collective-permute-done | bytes 262176 | tf_op jit(solution)/shard_map/ppermute | solution.py:114
  62.2 12.7 %collective-permute-done.2 = bf16[2,512,128]{2,1,0:T(8,128)(2,1)S(1)} collective-permute-done((bf16[2,512,128]{2,1,0:T(8,128)(2,1)S(1)}, bf16[2,512,128]{2,1,0:T(8,128)(2,1)S(1)}, u32[]{:S(2)}, u32[]{:S(2)}) %collective-permute-start.2) | collective-permute-done | bytes 262176 | tf_op jit(solution)/shard_map/ppermute | solution.py:114
  74.9 0.1 pad_maximum_fusion.1
  75.0 0.3 fusion.29
  75.3 1.6 fusion.11
  76.9 0.0 reduce-scatter.2.cloned.1.call-update
  76.9 0.0 all-gather.3.cloned.1.call-start
  76.9 35.9 %reduce-scatter.2.cloned.1.call-done = f32[64,3,128]{2,0,1:T(8,128)} async-done(((f32[512,3,128]{2,0,1:T(8,128)}), f32[64,3,128]{2,0,1:T(8,128)}) %reduce-scatter.2.cloned.1.call-update) | async-done | bytes 98320 | tf_op jit(solution)/shard_map/reduce_scatter | solution.py:118
  112.9 80.4 %all-gather.3.cloned.1.call-done = f32[2048,3,128]{2,0,1:T(8,128)} async-done(((f32[64,3,128]{2,0,1:T(8,128)}), f32[2048,3,128]{2,0,1:T(8,128)}) %all-gather.3.cloned.1.call-update) | async-done | bytes 3145744 | tf_op jit(solution)/shard_map/all_gather | solution.py:119
  193.3 2.1 %copy.19 = f32[32,64,3,128]{3,1,2,0:T(8,128)S(1)} copy(f32[32,64,3,128]{3,1,0,2:T(8,128)} %bitcast.99) | data formatting | bytes 6291456 | tf_op jit(solution)/shard_map/all_gather | solution.py:119
  195.4 0.6 gather_fusion
  196.0 0.8 broadcast_select_fusion
  (37 shorter events, 0.5 us)
Async XLA Ops:
  6.5 106.3 %reduce-scatter.2.cloned.1.call-start = ((), (), s32[]{:S(2)}) async-start(), calls=%async_computation.1 | async-start | bytes 884736 | tf_op jit(solution)/shard_map/reduce_scatter | solution.py:118
  33.2 19.6 %collective-permute-start = (bf16[2,512,128]{2,1,0:T(8,128)(2,1)S(1)}, bf16[2,512,128]{2,1,0:T(8,128)(2,1)S(1)}, u32[]{:S(2)}, u32[]{:S(2)}) collective-permute-start(bf16[2,512,128]{2,1,0:T(8,128)(2,1)S(1)} %pad_maximum_fusion.2), channel_id=1, source_target_pairs={{1,0},{2,1},{3,2},{4,3},{5,4},{6,5},{7,6},{8,7},{9,8},{10,9},{11,1... | collective-permute-start | bytes 786440 | tf_op jit(solution)/shard_map/ppermute | solution.py:114
  41.3 20.9 %collective-permute-start.1 = (bf16[2,512,128]{2,1,0:T(8,128)(2,1)S(1)}, bf16[2,512,128]{2,1,0:T(8,128)(2,1)S(1)}, u32[]{:S(2)}, u32[]{:S(2)}) collective-permute-start(bf16[2,512,128]{2,1,0:T(8,128)(2,1)S(1)} %pad_maximum_fusion.2), channel_id=1, source_target_pairs={{2,0},{3,1},{4,2},{5,3},{6,4},{7,5},{8,6},{9,7},{10,8},{11,9},{12,... | collective-permute-start | bytes 786440 | tf_op jit(solution)/shard_map/ppermute | solution.py:114
  44.6 30.3 %collective-permute-start.2 = (bf16[2,512,128]{2,1,0:T(8,128)(2,1)S(1)}, bf16[2,512,128]{2,1,0:T(8,128)(2,1)S(1)}, u32[]{:S(2)}, u32[]{:S(2)}) collective-permute-start(bf16[2,512,128]{2,1,0:T(8,128)(2,1)S(1)} %pad_maximum_fusion.2), channel_id=1, source_target_pairs={{3,0},{4,1},{5,2},{6,3},{7,4},{8,5},{9,6},{10,7},{11,8},{12,9},{13... | collective-permute-start | bytes 786440 | tf_op jit(solution)/shard_map/ppermute | solution.py:114
  75.0 37.9 %copy-start = (s32[6,2]{0,1:T(2,128)S(1)}, s32[6,2]{0,1:T(2,128)}, u32[]{:S(2)}) copy-start(s32[6,2]{0,1:T(2,128)} %param.3) | copy-start | bytes 148
  76.9 116.4 %all-gather.3.cloned.1.call-start = ((), (), s32[]{:S(2)}) async-start(), calls=%async_computation.2 | async-start | bytes 3244032 | tf_op jit(solution)/shard_map/all_gather | solution.py:119
Sparse Core Ops, SparseCore 0:
  77.0 35.7 reduce-scatter.1
  115.7 77.4 all-gather.2

commit v2 on v1

--- a/solution.py
+++ b/solution.py
@@ -105,28 +105,46 @@
 def body(traces, pair_blocks):
     smoother, taper, table = band_tables()
     white = whiten_local(traces[0], smoother, taper)
-    blocks = lax.axis_size("chan")
-    windows_all = traces.shape[0] * lax.axis_size("win")
+    nx = lax.axis_size("cx")
+    nz = lax.axis_size("cz")
+    blocks = nx * nz
+    nwin = lax.axis_size("win")
+    windows_all = traces.shape[0] * nwin
     factor = 1.0 / math.sqrt(NB * windows_all)
-    partners = []
-    for d in range(1, REACH + 1):
-        perm = [(i + d, i) for i in range(blocks - d)]
-        partners.append(lax.ppermute(white, "chan", perm))
-    right = jnp.stack(partners)
-    cross = cross_spectra(white[None], right)
+    received = {}
+    for shift in (-1, 1, 2):
+        perm = [(k + shift, k) for k in range(blocks) if 0 <= k + shift < blocks]
+        received[shift] = lax.ppermute(white, ("cx", "cz"), perm)
+    left = jnp.stack([white, received[-1], received[-1]])
+    right = jnp.stack([received[1], received[1], received[2]])
+    cross = cross_spectra(left, right)
     corr = jnp.einsum("tqb,dqbk->tdk", table, cross, preferred_element_type=jnp.float32) * factor
-    corr = lax.psum_scatter(corr, "win", scatter_dimension=0, tiled=True)
-    every = lax.all_gather(corr, "chan", axis=0)
-    left_block = pair_blocks[:, 0]
-    offset = pair_blocks[:, 1] - pair_blocks[:, 0]
-    filled = left_block >= 0
-    block_index = jnp.where(filled, left_block, 0)
-    offset_index = jnp.where(filled, offset - 1, 0)
-    picked = every[block_index, :, offset_index, :]
-    return jnp.where(filled[:, None, None], picked, 0.0)
+    lags = corr.shape[0] // nwin
+    corr = corr.reshape((nwin, lags) + corr.shape[1:])
+    corr = lax.all_to_all(corr, "win", 0, 0).sum(axis=0)
+    ring = lax.all_to_all(jnp.broadcast_to(corr[None], (nz,) + corr.shape), "cz", 0, 0)
+    owners = lax.all_gather(pair_blocks, "cx", axis=0)
+    lb = owners[..., 0]
+    offset = owners[..., 1] - lb
+    filled = lb >= 0
+    holder = jnp.where(filled, lb + (offset > 1).astype(jnp.int32), 0)
+    mine = filled & (holder // nz == lax.axis_index("cx"))
+    zi = jnp.where(mine, holder % nz, 0)
+    di = jnp.where(mine, offset - 1, 0)
+    picked = ring[zi, :, di, :]
+    picked = jnp.where(mine[..., None, None], picked, 0.0)
+    got = lax.all_to_all(picked, "cx", 0, 0).sum(axis=0)
+    return jnp.where(filled_local(pair_blocks)[:, None, None], got, 0.0)
+
+
+def filled_local(pair_blocks):
+    return pair_blocks[:, 0] >= 0
 
 
 def solution(mesh):
-    in_specs = (P("win", None, "chan"), P("chan", None))
-    out_specs = P("chan", "win", None)
-    return jax.shard_map(body, mesh=mesh, in_specs=in_specs, out_specs=out_specs, check_vma=False)
+    nx = 4
+    devices = mesh.devices.reshape(mesh.devices.shape[0], nx, -1)
+    grid = jax.sharding.Mesh(devices, ("win", "cx", "cz"))
+    in_specs = (P("win", None, ("cx", "cz")), P(("cx", "cz"), None))
+    out_specs = P(("cx", "cz"), "win", None)
+    return jax.shard_map(body, mesh=grid, in_specs=in_specs, out_specs=out_specs, check_vma=False)

time: 205 us -> 120 us (0.59)
  waiting for transfers between devices: 139 us -> 30.7 us
  blocking collectives: 0 us -> 25.3 us
  between operations: 13.8 us -> 0.4 us
  starting transfers between devices: 13.8 us -> 25.6 us
    all_gather x1 -> x0, waiting for transfers between devices: 80.4 us -> none  [body(): every = lax.all_gather(corr, 'chan', axis=0)]
    reduce_scatter x1 -> x0, waiting for transfers between devices: 35.9 us -> none  [body(): corr = lax.psum_scatter(corr, 'win', scatter_dimension=0, tiled=True)]
    all_to_all x0 -> x2, waiting for transfers between devices: none -> 25.2 us  [the longest x1 14.8 us: body(): lax.all_to_all(jnp.broadcast_to(corr[None], (nz,) + corr.shape), 'cz', 0, 0)]
    all_to_all x0 -> x1, blocking collectives: none -> 17.5 us  [body(): corr = lax.all_to_all(corr, 'win', 0, 0).sum(axis=0)]
    ppermute x3, waiting for transfers between devices: 23 us -> 5.53 us  [body(): received[shift] = lax.ppermute(white, ('cx', 'cz'), perm)]
    all_to_all x0 -> x2, starting transfers between devices: none -> 11.3 us  [the longest x1 5.99 us: body(): got = lax.all_to_all(picked, 'cx', 0, 0).sum(axis=0)]
    all_gather x0 -> x1, blocking collectives: none -> 7.81 us  [body(): owners = lax.all_gather(pair_blocks, 'cx', axis=0)]
    all_gather x1 -> x0, local copies, waits for them, and re-layouts: 2.11 us -> none  [body(): every = lax.all_gather(corr, 'chan', axis=0)]
  transfers between devices with their start and end apart: 5 -> 5, of which waited for: 5 -> 4; matrix products, arithmetic and copies ran while one was open for 2% -> 4% of each run, Pallas kernels for 0% -> 0%
where the time goes in v2:
time: 120 us; the launch traced here: 118 us
  waiting for transfers between devices  30.7 us (26%)
  starting transfers between devices  25.6 us (21%)
  blocking collectives  25.3 us (21%)
  matrix products  16.1 us (13%)
  other arithmetic  12.5 us (10%)
  local copies, waits for them, and re-layouts  7.66 us (6%)
    all_to_all x1, blocking collectives, body(): corr = lax.all_to_all(corr, 'win', 0, 0).sum(axis=0)  17.5 us
    all_to_all x1, waiting for transfers between devices, body(): lax.all_to_all(jnp.broadcast_to(corr[None], (nz,) + corr.shape), 'cz', 0, 0)  14.8 us
    ppermute x3, starting transfers between devices, body(): received[shift] = lax.ppermute(white, ('cx', 'cz'), perm)  14.3 us
    all_to_all x1, waiting for transfers between devices, body(): got = lax.all_to_all(picked, 'cx', 0, 0).sum(axis=0)  10.4 us
    dot_general x1, matrix products, band_dft(): jnp.einsum('rb,bac->rac', basis1, xb, precision=prec, preferred_element_t...  7.85 us
    all_gather x1, blocking collectives, body(): owners = lax.all_gather(pair_blocks, 'cx', axis=0)  7.81 us
    dot_general x1, matrix products, band_dft(): jnp.einsum('ja,srac->sjrc', basis2, jnp.stack([wr, wi]), precision=prec,...  6.09 us
    all_to_all x1, starting transfers between devices, body(): got = lax.all_to_all(picked, 'cx', 0, 0).sum(axis=0)  5.99 us
  transfers between devices with their start and end apart: 5, of which 4 were waited for; matrix products, arithmetic and copies ran while one was open for 4% of the time, Pallas kernels for 0%

profile of v2, /device:TPU:6, one launch (start us, length us, event | category | flops | bytes accessed | tf_op | source)
XLA Modules:
  0.0 118.3 jit_solution(11686605116656730473)
XLA Ops:
  0.0 0.2 sine_negate_fusion
  0.2 0.3 fusion.50
  0.5 7.9 %fusion = f32[126,120,128]{2,0,1:T(8,128)S(1)} fusion(f32[125,120,128]{2,1,0:T(8,128)} %bitcast.102, f32[63,125]{1,0:T(8,128)S(1)} %get-tuple-element.38, f32[63,125]{1,0:T(8,128)S(1)} %get-tuple-element.39), kind=kOutput, calls=%fused_computation.2 | convolution fusion | flops 1451535744 | bytes 15484440 | tf_op jit(solution)/shard_map/rb,bac->rac/dot_general | solution.py:44
  8.4 3.0 %add_bitcast_fusion = (f32[1,63,120,128]{3,1,2,0:T(8,128)S(1)}, f32[1,63,120,128]{3,1,2,0:T(8,128)S(1)}) fusion(f32[126,120,128]{2,0,1:T(8,128)S(1)} %fusion, f32[63,120]{0,1:T(8,128)S(1)} %get-tuple-element.40, f32[63,120]{0,1:T(8,128)S(1)} %get-tuple-element.41), kind=kLoop, calls=%fused_computation.7 | loop fusion | flops 5806080 | bytes 15543360 | tf_op jit(solution)/shard_map/stack | solution.py:59
  11.4 1.5 %pad_maximum_fusion = f32[2,63,120,128]{3,1,2,0:T(8,128)S(1)} fusion(f32[1,63,120,128]{3,1,2,0:T(8,128)S(1)} %get-tuple-element.6, f32[1,63,120,128]{3,1,2,0:T(8,128)S(1)} %get-tuple-element.5), kind=kLoop, calls=%fused_computation.1 | loop fusion | flops 1935360 | bytes 15482880 | tf_op jit(solution)/shard_map/stack | solution.py:59
  12.9 6.1 %fusion.4 = f32[2,12,63,128]{3,1,2,0:T(8,128)S(1)} fusion(f32[2,63,120,128]{3,1,2,0:T(8,128)S(1)} %pad_maximum_fusion, f32[6,120]{1,0:T(8,128)S(1)} %get-tuple-element.42, f32[6,120]{1,0:T(8,128)S(1)} %get-tuple-element.43), kind=kOutput, calls=%fused_computation.11 | convolution fusion | flops 139347360 | bytes 8521344 | tf_op jit(solution)/shard_map/ja,srac->sjrc/dot_general | solution.py:58
  19.2 0.1 fusion.87
  19.3 0.1 fusion.86
  19.7 1.2 concatenate.31
  20.8 1.5 %concatenate.32 = f32[576,128]{1,0:T(8,128)S(1)} concatenate(f32[31,128]{1,0:T(8,128)S(1)} %slice_bitcast_fusion.11, f32[62,128]{1,0:T(8,128)S(1)} %rev.32, f32[63,128]{1,0:T(8,128)S(1)} %get-tuple-element.28, f32[62,128]{1,0:T(8,128)S(1)} %rev.33, f32[63,128]{1,0:T(8,128)S(1)} %get-tuple-element.27, f32[62,128]{1,0:T(8,128)S(1)} %rev.34, f32[63,128]{1,0:T(8,128)S(1)} %get-tuple-element.26, ...), dimensions={0} | concatenate | bytes 589824 | tf_op jit(solution)/shard_map/concatenate | solution.py:82
  22.6 1.2 concatenate.34
  23.7 1.5 %concatenate.33 = f32[576,128]{1,0:T(8,128)S(1)} concatenate(f32[31,128]{1,0:T(8,128)S(1)} %bitcast.126, f32[62,128]{1,0:T(8,128)S(1)} %rev.37, f32[63,128]{1,0:T(8,128)S(1)} %bitcast.115, f32[62,128]{1,0:T(8,128)S(1)} %rev.38, f32[63,128]{1,0:T(8,128)S(1)} %bitcast.113, f32[62,128]{1,0:T(8,128)S(1)} %rev.39, f32[63,128]{1,0:T(8,128)S(1)} %bitcast.111, f32[62,128]{1,0:T(8,128)S(1)} %rev.40, ...), dimensions={0} | concatenate | bytes 589824 | tf_op jit(solution)/shard_map/concatenate | solution.py:82
  25.2 1.4 %fusion.42 = (bf16[512,128]{1,0:T(8,128)(2,1)S(1)}, bf16[512,128]{1,0:T(8,128)(2,1)S(1)}) fusion(f32[545,128]{1,0:T(8,128)S(1)} %concatenate.31, f32[545,128]{1,0:T(8,128)S(1)} %concatenate.34, f32[576,128]{1,0:T(8,128)S(1)} %concatenate.33, f32[576,128]{1,0:T(8,128)S(1)} %concatenate.32, s32[512]{0:T(512)S(1)} %get-tuple-element.45, ...), kind=kOutput, calls=%fused_computation.54 | convolution fusion | flops 454778880 | bytes 1380352 | tf_op jit(solution)/shard_map/dot_general | solution.py:89
  26.7 8.0 %collective-permute-start.1 = (bf16[2,512,128]{2,1,0:T(8,128)(2,1)S(1)}, bf16[2,512,128]{2,1,0:T(8,128)(2,1)S(1)}, u32[]{:S(2)}, u32[]{:S(2)}) collective-permute-start(bf16[2,512,128]{2,1,0:T(8,128)(2,1)S(1)} %pad_maximum_fusion.3), channel_id=1, source_target_pairs={{1,0},{2,1},{3,2},{4,3},{5,4},{6,5},{7,6},{8,7},{9,8},{10,9},{11,1... | collective-permute-start | bytes 786440 | tf_op jit(solution)/shard_map/ppermute | solution.py:117
  34.7 3.3 %collective-permute-start.2 = (bf16[2,512,128]{2,1,0:T(8,128)(2,1)S(1)}, bf16[2,512,128]{2,1,0:T(8,128)(2,1)S(1)}, u32[]{:S(2)}, u32[]{:S(2)}) collective-permute-start(bf16[2,512,128]{2,1,0:T(8,128)(2,1)S(1)} %pad_maximum_fusion.3), channel_id=1, source_target_pairs={{2,0},{3,1},{4,2},{5,3},{6,4},{7,5},{8,6},{9,7},{10,8},{11,9},{12,... | collective-permute-start | bytes 786440 | tf_op jit(solution)/shard_map/ppermute | solution.py:117
  38.1 2.9 %collective-permute-start = (bf16[2,512,128]{2,1,0:T(8,128)(2,1)S(1)}, bf16[2,512,128]{2,1,0:T(8,128)(2,1)S(1)}, u32[]{:S(2)}, u32[]{:S(2)}) collective-permute-start(bf16[2,512,128]{2,1,0:T(8,128)(2,1)S(1)} %pad_maximum_fusion.3), channel_id=1, source_target_pairs={{0,1},{1,2},{2,3},{3,4},{4,5},{5,6},{6,7},{7,8},{8,9},{9,10},{10,1... | collective-permute-start | bytes 786440 | tf_op jit(solution)/shard_map/ppermute | solution.py:117
  41.0 4.9 %cosine_convert_fusion = (bf16[512,1,512]{2,0,1:T(8,128)(2,1)S(1)}, bf16[512,1,512]{2,0,1:T(8,128)(2,1)S(1)}) fusion(s32[512]{0:T(512)S(1)} %get-tuple-element.44, s32[512]{0:T(512)S(1)} %get-tuple-element.45), kind=kLoop, calls=%fused_computation.26 | loop fusion | flops 3145728 | bytes 1052672 | tf_op jit(solution)/shard_map/convert.10
  46.0 0.9 collective-permute-done.1
  46.9 4.6 %collective-permute-done.2 = bf16[2,512,128]{2,1,0:T(8,128)(2,1)S(1)} collective-permute-done((bf16[2,512,128]{2,1,0:T(8,128)(2,1)S(1)}, bf16[2,512,128]{2,1,0:T(8,128)(2,1)S(1)}, u32[]{:S(2)}, u32[]{:S(2)}) %collective-permute-start.2) | collective-permute-done | bytes 262176 | tf_op jit(solution)/shard_map/ppermute | solution.py:117
  51.6 0.1 pad_maximum_fusion.1
  51.7 0.3 fusion.29
  52.0 0.7 fusion.11
  52.8 17.5 %all_to_all.15 = f32[8,64,3,128]{3,1,2,0:T(8,128)S(1)} all-to-all(f32[8,64,3,128]{3,1,2,0:T(8,128)S(1)} %copy.27), channel_id=1, replica_groups=mesh['win'=8,'cx'=4,'cz'=8] {'win'}, dimensions={0} | all-to-all | bytes 1572864 | tf_op jit(solution)/shard_map/all_to_all | solution.py:124
  70.3 1.0 broadcast_in_dim.53
  71.3 5.3 %all-to-all-start.1 = ((f32[8,64,3,128]{3,1,2,0:T(8,128)}), f32[8,64,3,128]{3,1,2,0:T(8,128)S(1)}, u32[]{:S(2)}, u32[]{:S(2)}) async-start(f32[8,64,3,128]{3,1,2,0:T(8,128)} %broadcast_in_dim.53), calls=%async_computation.1 | async-start | bytes 1572864 | tf_op jit(solution)/shard_map/all_to_all | solution.py:125
  76.6 7.8 %all-gather.1 = s32[4,6,2]{1,2,0:T(2,128)S(1)} all-gather(s32[1,6,2]{1,2,0:T(2,128)S(1)} %bitcast.129), channel_id=2, replica_groups=mesh['win'=8,'cx'=4,'cz'=8] {'cx'}, dimensions={0}, use_global_device_ids=true | all-gather | bytes 240 | tf_op jit(solution)/shard_map/all_gather | solution.py:126
  84.6 14.8 %all-to-all-done.1 = f32[8,64,3,128]{3,1,2,0:T(8,128)S(1)} async-done(((f32[8,64,3,128]{3,1,2,0:T(8,128)}), f32[8,64,3,128]{3,1,2,0:T(8,128)S(1)}, u32[]{:S(2)}, u32[]{:S(2)}) %all-to-all-start.1) | async-done | bytes 786464 | tf_op jit(solution)/shard_map/all_to_all | solution.py:125
  99.4 0.7 gather_fusion
  100.1 1.0 broadcast_select_fusion
  101.1 6.0 %all-to-all-start.2 = ((f32[4,6,64,128]{3,2,1,0:T(8,128)}), f32[4,6,64,128]{3,2,1,0:T(8,128)S(1)}, u32[]{:S(2)}, u32[]{:S(2)}) async-start(f32[4,6,64,128]{3,2,1,0:T(8,128)} %broadcast_select_fusion), calls=%async_computation.2 | async-start | bytes 1572864 | tf_op jit(solution)/shard_map/all_to_all | solution.py:136
  107.1 10.4 %all-to-all-done.2 = f32[4,6,64,128]{3,2,1,0:T(8,128)S(1)} async-done(((f32[4,6,64,128]{3,2,1,0:T(8,128)}), f32[4,6,64,128]{3,2,1,0:T(8,128)S(1)}, u32[]{:S(2)}, u32[]{:S(2)}) %all-to-all-start.2) | async-done | bytes 786464 | tf_op jit(solution)/shard_map/all_to_all | solution.py:136
  117.5 0.8 broadcast_select_fusion.1
  (44 shorter events, 1.0 us)
Async XLA Ops:
  26.7 20.2 %collective-permute-start.1 = (bf16[2,512,128]{2,1,0:T(8,128)(2,1)S(1)}, bf16[2,512,128]{2,1,0:T(8,128)(2,1)S(1)}, u32[]{:S(2)}, u32[]{:S(2)}) collective-permute-start(bf16[2,512,128]{2,1,0:T(8,128)(2,1)S(1)} %pad_maximum_fusion.3), channel_id=1, source_target_pairs={{1,0},{2,1},{3,2},{4,3},{5,4},{6,5},{7,6},{8,7},{9,8},{10,9},{11,1... | collective-permute-start | bytes 786440 | tf_op jit(solution)/shard_map/ppermute | solution.py:117
  34.7 16.8 %collective-permute-start.2 = (bf16[2,512,128]{2,1,0:T(8,128)(2,1)S(1)}, bf16[2,512,128]{2,1,0:T(8,128)(2,1)S(1)}, u32[]{:S(2)}, u32[]{:S(2)}) collective-permute-start(bf16[2,512,128]{2,1,0:T(8,128)(2,1)S(1)} %pad_maximum_fusion.3), channel_id=1, source_target_pairs={{2,0},{3,1},{4,2},{5,3},{6,4},{7,5},{8,6},{9,7},{10,8},{11,9},{12,... | collective-permute-start | bytes 786440 | tf_op jit(solution)/shard_map/ppermute | solution.py:117
  38.1 13.5 %collective-permute-start = (bf16[2,512,128]{2,1,0:T(8,128)(2,1)S(1)}, bf16[2,512,128]{2,1,0:T(8,128)(2,1)S(1)}, u32[]{:S(2)}, u32[]{:S(2)}) collective-permute-start(bf16[2,512,128]{2,1,0:T(8,128)(2,1)S(1)} %pad_maximum_fusion.3), channel_id=1, source_target_pairs={{0,1},{1,2},{2,3},{3,4},{4,5},{5,6},{6,7},{7,8},{8,9},{9,10},{10,1... | collective-permute-start | bytes 786440 | tf_op jit(solution)/shard_map/ppermute | solution.py:117
  52.7 23.9 %copy-start = (s32[6,2]{0,1:T(2,128)S(1)}, s32[6,2]{0,1:T(2,128)}, u32[]{:S(2)}) copy-start(s32[6,2]{0,1:T(2,128)} %param.3) | copy-start | bytes 148
  71.3 28.0 %all-to-all-start.1 = ((f32[8,64,3,128]{3,1,2,0:T(8,128)}), f32[8,64,3,128]{3,1,2,0:T(8,128)S(1)}, u32[]{:S(2)}, u32[]{:S(2)}) async-start(f32[8,64,3,128]{3,1,2,0:T(8,128)} %broadcast_in_dim.53), calls=%async_computation.1 | async-start | bytes 1572864 | tf_op jit(solution)/shard_map/all_to_all | solution.py:125
  101.1 16.4 %all-to-all-start.2 = ((f32[4,6,64,128]{3,2,1,0:T(8,128)}), f32[4,6,64,128]{3,2,1,0:T(8,128)S(1)}, u32[]{:S(2)}, u32[]{:S(2)}) async-start(f32[4,6,64,128]{3,2,1,0:T(8,128)} %broadcast_select_fusion), calls=%async_computation.2 | async-start | bytes 1572864 | tf_op jit(solution)/shard_map/all_to_all | solution.py:136

commit v3 on v2

--- a/solution.py
+++ b/solution.py
@@ -1,6 +1,8 @@
 import math
 
 import jax
+import ml_dtypes
+import numpy as np
 import jax.numpy as jnp
 from jax import lax
 from jax.sharding import PartitionSpec as P
@@ -15,6 +17,15 @@
 two_pi = 2.0 * math.pi
 
 
+def lag_table():
+    bins = F_LO + np.arange(NB, dtype=np.int64)[None, :]
+    lagged = np.arange(LAGS, dtype=np.int64)[:, None] - LAGS // 2
+    angle = ((bins * lagged) % L).astype(np.float32) * np.float32(two_pi / L)
+    angle = angle.astype(np.float64)
+    table = np.stack([np.cos(angle), -np.sin(angle)], axis=1).astype(np.float32)
+    return table.astype(ml_dtypes.bfloat16)
+
+
 def band_tables():
     width = NB + 2 * HALF
     rows = lax.broadcasted_iota(jnp.int32, (NB, width), 0)
@@ -25,10 +36,7 @@
     taper = jnp.sin(
         math.pi * (lax.broadcasted_iota(jnp.int32, (NB,), 0).astype(jnp.float32) + 0.5) / NB
     )
-    bins = F_LO + lax.broadcasted_iota(jnp.int32, (LAGS, NB), 1)
-    lagged = lax.broadcasted_iota(jnp.int32, (LAGS, NB), 0) - LAGS // 2
-    angle = (bins * lagged % L).astype(jnp.float32) * (two_pi / L)
-    table = jnp.stack([jnp.cos(angle), -jnp.sin(angle)], axis=1).astype(jnp.bfloat16)
+    table = jnp.asarray(lag_table())
     return (smoother, taper, table)
 
 
@@ -112,23 +120,28 @@
     windows_all = traces.shape[0] * nwin
     factor = 1.0 / math.sqrt(NB * windows_all)
     received = {}
-    for shift in (-1, 1, 2):
+    for shift in (-1, 2):
         perm = [(k + shift, k) for k in range(blocks) if 0 <= k + shift < blocks]
         received[shift] = lax.ppermute(white, ("cx", "cz"), perm)
-    left = jnp.stack([white, received[-1], received[-1]])
-    right = jnp.stack([received[1], received[1], received[2]])
+    left = jnp.stack([received[-1], white, received[-1]])
+    right = jnp.stack([white, received[2], received[2]])
     cross = cross_spectra(left, right)
     corr = jnp.einsum("tqb,dqbk->tdk", table, cross, preferred_element_type=jnp.float32) * factor
     lags = corr.shape[0] // nwin
     corr = corr.reshape((nwin, lags) + corr.shape[1:])
     corr = lax.all_to_all(corr, "win", 0, 0).sum(axis=0)
     ring = lax.all_to_all(jnp.broadcast_to(corr[None], (nz,) + corr.shape), "cz", 0, 0)
-    owners = lax.all_gather(pair_blocks, "cx", axis=0)
+    me_x = lax.axis_index("cx")
+    shifted = [pair_blocks]
+    for step in range(1, nx):
+        shifted.append(lax.ppermute(pair_blocks, "cx", [(k, (k + step) % nx) for k in range(nx)]))
+    shifted = jnp.stack(shifted)
+    owners = shifted[(me_x - jnp.arange(nx)) % nx]
     lb = owners[..., 0]
     offset = owners[..., 1] - lb
     filled = lb >= 0
-    holder = jnp.where(filled, lb + (offset > 1).astype(jnp.int32), 0)
-    mine = filled & (holder // nz == lax.axis_index("cx"))
+    holder = jnp.where(filled, lb + (offset != 2).astype(jnp.int32), 0)
+    mine = filled & (holder // nz == me_x)
     zi = jnp.where(mine, holder % nz, 0)
     di = jnp.where(mine, offset - 1, 0)
     picked = ring[zi, :, di, :]

time: 120 us -> 118 us (0.983)
  waiting for transfers between devices: 30.7 us -> 39.1 us
  blocking collectives: 25.3 us -> 17.5 us
  other arithmetic: 12.5 us -> 7.64 us
  starting transfers between devices: 25.6 us -> 26.9 us
    all_gather x1 -> x0, blocking collectives: 7.81 us -> none  [body(): owners = lax.all_gather(pair_blocks, 'cx', axis=0)]
    ppermute x3 -> x2, waiting for transfers between devices: 5.53 us -> 10.7 us  [body(): received[shift] = lax.ppermute(white, ('cx', 'cz'), perm)]
    another operation x4 -> x3, other arithmetic: 5.41 us -> 0.49 us
    ppermute x0 -> x3, waiting for transfers between devices: none -> 4.74 us  [body(): lax.ppermute(pair_blocks, 'cx', [(k, (k + step) % nx) for k in range(nx)])]
    ppermute x0 -> x3, starting transfers between devices: none -> 3.98 us  [body(): lax.ppermute(pair_blocks, 'cx', [(k, (k + step) % nx) for k in range(nx)])]
    ppermute x3 -> x2, starting transfers between devices: 14.3 us -> 11.6 us  [body(): received[shift] = lax.ppermute(white, ('cx', 'cz'), perm)]
    all_to_all x1, waiting for transfers between devices: 14.8 us -> 13.2 us  [body(): lax.all_to_all(jnp.broadcast_to(corr[None], (nz,) + corr.shape), 'cz', 0, 0)]
  transfers between devices with their start and end apart: 5 -> 7, of which waited for: 4 -> 6; matrix products, arithmetic and copies ran while one was open for 4% -> 1% of each run, Pallas kernels for 0% -> 0%
where the time goes in v3:
time: 118 us; the launch traced here: 116 us
  waiting for transfers between devices  39.1 us (33%)
  starting transfers between devices  26.9 us (23%)
  blocking collectives  17.5 us (15%)
  matrix products  16 us (14%)
  local copies, waits for them, and re-layouts  8.5 us (7%)
  other arithmetic  7.64 us (6%)
    all_to_all x1, blocking collectives, body(): corr = lax.all_to_all(corr, 'win', 0, 0).sum(axis=0)  17.5 us
    all_to_all x1, waiting for transfers between devices, body(): lax.all_to_all(jnp.broadcast_to(corr[None], (nz,) + corr.shape), 'cz', 0, 0)  13.2 us
    ppermute x2, starting transfers between devices, body(): received[shift] = lax.ppermute(white, ('cx', 'cz'), perm)  11.6 us
    ppermute x2, waiting for transfers between devices, body(): received[shift] = lax.ppermute(white, ('cx', 'cz'), perm)  10.7 us
    all_to_all x1, waiting for transfers between devices, body(): got = lax.all_to_all(picked, 'cx', 0, 0).sum(axis=0)  10.4 us
    dot_general x1, matrix products, band_dft(): jnp.einsum('rb,bac->rac', basis1, xb, precision=prec, preferred_element_t...  7.85 us
    dot_general x1, matrix products, band_dft(): jnp.einsum('ja,srac->sjrc', basis2, jnp.stack([wr, wi]), precision=prec,...  6.09 us
    all_to_all x1, starting transfers between devices, body(): got = lax.all_to_all(picked, 'cx', 0, 0).sum(axis=0)  5.77 us
  transfers between devices with their start and end apart: 7, of which 6 were waited for; matrix products, arithmetic and copies ran while one was open for 1% of the time, Pallas kernels for 0%

profile of v3, /device:TPU:6, one launch (start us, length us, event | category | flops | bytes accessed | tf_op | source)
XLA Modules:
  0.0 116.0 jit_solution(8334112415411755437)
XLA Ops:
  0.2 0.3 fusion.44
  0.5 7.9 %fusion = f32[126,120,128]{2,0,1:T(8,128)S(1)} fusion(f32[125,120,128]{2,1,0:T(8,128)} %bitcast.109, f32[63,125]{1,0:T(8,128)S(1)} %get-tuple-element.38, f32[63,125]{1,0:T(8,128)S(1)} %get-tuple-element.39), kind=kOutput, calls=%fused_computation.3 | convolution fusion | flops 1451535744 | bytes 15484440 | tf_op jit(solution)/shard_map/rb,bac->rac/dot_general | solution.py:52
  8.4 3.0 %add_bitcast_fusion = (f32[1,63,120,128]{3,1,2,0:T(8,128)S(1)}, f32[1,63,120,128]{3,1,2,0:T(8,128)S(1)}) fusion(f32[126,120,128]{2,0,1:T(8,128)S(1)} %fusion, f32[63,120]{0,1:T(8,128)S(1)} %get-tuple-element.40, f32[63,120]{0,1:T(8,128)S(1)} %get-tuple-element.41), kind=kLoop, calls=%fused_computation.8 | loop fusion | flops 5806080 | bytes 15543360 | tf_op jit(solution)/shard_map/stack | solution.py:67
  11.4 1.5 %pad_maximum_fusion = f32[2,63,120,128]{3,1,2,0:T(8,128)S(1)} fusion(f32[1,63,120,128]{3,1,2,0:T(8,128)S(1)} %get-tuple-element.6, f32[1,63,120,128]{3,1,2,0:T(8,128)S(1)} %get-tuple-element.5), kind=kLoop, calls=%fused_computation.2 | loop fusion | flops 1935360 | bytes 15482880 | tf_op jit(solution)/shard_map/stack | solution.py:67
  12.9 6.1 %fusion.4 = f32[2,12,63,128]{3,1,2,0:T(8,128)S(1)} fusion(f32[2,63,120,128]{3,1,2,0:T(8,128)S(1)} %pad_maximum_fusion, f32[6,120]{1,0:T(8,128)S(1)} %get-tuple-element.42, f32[6,120]{1,0:T(8,128)S(1)} %get-tuple-element.43), kind=kOutput, calls=%fused_computation.11 | convolution fusion | flops 139347360 | bytes 8521344 | tf_op jit(solution)/shard_map/ja,srac->sjrc/dot_general | solution.py:66
  19.7 1.2 %concatenate.31 = f32[545,128]{1,0:T(8,128)S(1)} concatenate(f32[62,128]{1,0:T(8,128)S(1)} %rev.32, f32[63,128]{1,0:T(8,128)S(1)} %get-tuple-element.30, f32[62,128]{1,0:T(8,128)S(1)} %rev.33, f32[63,128]{1,0:T(8,128)S(1)} %get-tuple-element.29, f32[62,128]{1,0:T(8,128)S(1)} %rev.34, f32[63,128]{1,0:T(8,128)S(1)} %get-tuple-element.28, f32[62,128]{1,0:T(8,128)S(1)} %rev.35, ...), dimensions={0} | concatenate | bytes 558080 | tf_op jit(solution)/shard_map/concatenate | solution.py:90
  20.8 1.5 %concatenate.32 = f32[576,128]{1,0:T(8,128)S(1)} concatenate(f32[31,128]{1,0:T(8,128)S(1)} %slice_bitcast_fusion.11, f32[62,128]{1,0:T(8,128)S(1)} %rev.32, f32[63,128]{1,0:T(8,128)S(1)} %get-tuple-element.30, f32[62,128]{1,0:T(8,128)S(1)} %rev.33, f32[63,128]{1,0:T(8,128)S(1)} %get-tuple-element.29, f32[62,128]{1,0:T(8,128)S(1)} %rev.34, f32[63,128]{1,0:T(8,128)S(1)} %get-tuple-element.28, ...), dimensions={0} | concatenate | bytes 589824 | tf_op jit(solution)/shard_map/concatenate | solution.py:90
  22.6 1.2 %concatenate.34 = f32[545,128]{1,0:T(8,128)S(1)} concatenate(f32[62,128]{1,0:T(8,128)S(1)} %rev.37, f32[63,128]{1,0:T(8,128)S(1)} %bitcast.119, f32[62,128]{1,0:T(8,128)S(1)} %rev.38, f32[63,128]{1,0:T(8,128)S(1)} %bitcast.117, f32[62,128]{1,0:T(8,128)S(1)} %rev.39, f32[63,128]{1,0:T(8,128)S(1)} %bitcast.123, f32[62,128]{1,0:T(8,128)S(1)} %rev.40, f32[63,128]{1,0:T(8,128)S(1)} %bitcast.121, ...), dimensions={0} | concatenate | bytes 558080 | tf_op jit(solution)/shard_map/concatenate | solution.py:90
  23.7 1.5 %concatenate.33 = f32[576,128]{1,0:T(8,128)S(1)} concatenate(f32[31,128]{1,0:T(8,128)S(1)} %bitcast.132, f32[62,128]{1,0:T(8,128)S(1)} %rev.37, f32[63,128]{1,0:T(8,128)S(1)} %bitcast.120, f32[62,128]{1,0:T(8,128)S(1)} %rev.38, f32[63,128]{1,0:T(8,128)S(1)} %bitcast.118, f32[62,128]{1,0:T(8,128)S(1)} %rev.39, f32[63,128]{1,0:T(8,128)S(1)} %bitcast.124, f32[62,128]{1,0:T(8,128)S(1)} %rev.40, ...), dimensions={0} | concatenate | bytes 589824 | tf_op jit(solution)/shard_map/concatenate | solution.py:90
  25.2 1.4 %fusion.36 = (bf16[512,128]{1,0:T(8,128)(2,1)S(1)}, bf16[512,128]{1,0:T(8,128)(2,1)S(1)}) fusion(f32[545,128]{1,0:T(8,128)S(1)} %concatenate.31, f32[545,128]{1,0:T(8,128)S(1)} %concatenate.34, f32[576,128]{1,0:T(8,128)S(1)} %concatenate.33, f32[576,128]{1,0:T(8,128)S(1)} %concatenate.32, s32[512]{0:T(512)S(1)} %iota_add_fusion, f32[512]{0:T(512)S(1)} %multiply_sine_fusion), kind=kOutput, calls=%fused_computation.44 | convolution fusion | flops 454778880 | bytes 1380352 | tf_op jit(solution)/shard_map/dot_general | solution.py:97
  26.7 3.8 %collective-permute-start.3 = (bf16[2,512,128]{2,1,0:T(8,128)(2,1)S(1)}, bf16[2,512,128]{2,1,0:T(8,128)(2,1)S(1)}, u32[]{:S(2)}, u32[]{:S(2)}) collective-permute-start(bf16[2,512,128]{2,1,0:T(8,128)(2,1)S(1)} %pad_maximum_fusion.3), channel_id=1, source_target_pairs={{0,1},{1,2},{2,3},{3,4},{4,5},{5,6},{6,7},{7,8},{8,9},{9,10},{10,1... | collective-permute-start | bytes 786440 | tf_op jit(solution)/shard_map/ppermute | solution.py:125
  30.5 7.8 %collective-permute-start.4 = (bf16[2,512,128]{2,1,0:T(8,128)(2,1)S(1)}, bf16[2,512,128]{2,1,0:T(8,128)(2,1)S(1)}, u32[]{:S(2)}, u32[]{:S(2)}) collective-permute-start(bf16[2,512,128]{2,1,0:T(8,128)(2,1)S(1)} %pad_maximum_fusion.3), channel_id=1, source_target_pairs={{2,0},{3,1},{4,2},{5,3},{6,4},{7,5},{8,6},{9,7},{10,8},{11,9},{12,... | collective-permute-start | bytes 786440 | tf_op jit(solution)/shard_map/ppermute | solution.py:125
  38.3 2.7 %collective-permute-done.3 = bf16[2,512,128]{2,1,0:T(8,128)(2,1)S(1)} collective-permute-done((bf16[2,512,128]{2,1,0:T(8,128)(2,1)S(1)}, bf16[2,512,128]{2,1,0:T(8,128)(2,1)S(1)}, u32[]{:S(2)}, u32[]{:S(2)}) %collective-permute-start.3) | collective-permute-done | bytes 262176 | tf_op jit(solution)/shard_map/ppermute | solution.py:125
  41.0 8.0 %collective-permute-done.4 = bf16[2,512,128]{2,1,0:T(8,128)(2,1)S(1)} collective-permute-done((bf16[2,512,128]{2,1,0:T(8,128)(2,1)S(1)}, bf16[2,512,128]{2,1,0:T(8,128)(2,1)S(1)}, u32[]{:S(2)}, u32[]{:S(2)}) %collective-permute-start.4) | collective-permute-done | bytes 262176 | tf_op jit(solution)/shard_map/ppermute | solution.py:125
  49.0 0.2 pad_maximum_fusion.1
  49.2 0.3 fusion.23
  49.5 0.6 fusion.12
  50.2 0.3 copy.32
  50.5 17.5 %all_to_all.15 = f32[8,64,3,128]{3,1,2,0:T(8,128)S(1)} all-to-all(f32[8,64,3,128]{3,1,2,0:T(8,128)S(1)} %copy.33), channel_id=1, replica_groups=mesh['win'=8,'cx'=4,'cz'=8] {'win'}, dimensions={0} | all-to-all | bytes 1572864 | tf_op jit(solution)/shard_map/all_to_all | solution.py:132
  68.1 1.0 broadcast_in_dim.54
  69.1 5.5 %all-to-all-start.1 = ((f32[8,64,3,128]{3,1,2,0:T(8,128)}), f32[8,64,3,128]{3,1,2,0:T(8,128)S(1)}, u32[]{:S(2)}, u32[]{:S(2)}) async-start(f32[8,64,3,128]{3,1,2,0:T(8,128)} %broadcast_in_dim.54), calls=%async_computation.1 | async-start | bytes 1572864 | tf_op jit(solution)/shard_map/all_to_all | solution.py:133
  74.6 1.6 %collective-permute-start = (s32[6,2]{0,1:T(2,128)S(1)}, s32[6,2]{0,1:T(2,128)S(1)}, u32[]{:S(2)}, u32[]{:S(2)}) collective-permute-start(s32[6,2]{0,1:T(2,128)S(1)} %copy-done), channel_id=1, source_target_pairs={{0,8},{8,16},{16,24},{24,0},{1,9},{9,17},{17,25},{25,1},{2,10},{10... | collective-permute-start | bytes 152 | tf_op jit(solution)/shard_map/ppermute | solution.py:137
  76.1 2.4 %collective-permute-start.1 = (s32[6,2]{0,1:T(2,128)S(1)}, s32[6,2]{0,1:T(2,128)S(1)}, u32[]{:S(2)}, u32[]{:S(2)}) collective-permute-start(s32[6,2]{0,1:T(2,128)S(1)} %copy-done), channel_id=1, source_target_pairs={{0,16},{8,24},{16,0},{24,8},{1,17},{9,25},{17,1},{25,9},{2,18},{10... | collective-permute-start | bytes 152 | tf_op jit(solution)/shard_map/ppermute | solution.py:137
  78.6 2.6 %collective-permute-done.1 = s32[6,2]{0,1:T(2,128)S(1)} collective-permute-done((s32[6,2]{0,1:T(2,128)S(1)}, s32[6,2]{0,1:T(2,128)S(1)}, u32[]{:S(2)}, u32[]{:S(2)}) %collective-permute-start.1) | collective-permute-done | bytes 80 | tf_op jit(solution)/shard_map/ppermute | solution.py:137
  81.2 2.1 %collective-permute-done.2 = s32[6,2]{0,1:T(2,128)S(1)} collective-permute-done((s32[6,2]{0,1:T(2,128)S(1)}, s32[6,2]{0,1:T(2,128)S(1)}, u32[]{:S(2)}, u32[]{:S(2)}) %collective-permute-start.2) | collective-permute-done | bytes 80 | tf_op jit(solution)/shard_map/ppermute | solution.py:137
  83.3 0.6 gather_fusion
  84.0 13.2 %all-to-all-done.1 = f32[8,64,3,128]{3,1,2,0:T(8,128)S(1)} async-done(((f32[8,64,3,128]{3,1,2,0:T(8,128)}), f32[8,64,3,128]{3,1,2,0:T(8,128)S(1)}, u32[]{:S(2)}, u32[]{:S(2)}) %all-to-all-start.1) | async-done | bytes 786464 | tf_op jit(solution)/shard_map/all_to_all | solution.py:133
  97.3 0.7 gather_fusion.1
  98.0 1.0 broadcast_select_fusion
  99.0 5.8 %all-to-all-start.2 = ((f32[4,6,64,128]{3,2,1,0:T(8,128)}), f32[4,6,64,128]{3,2,1,0:T(8,128)S(1)}, u32[]{:S(2)}, u32[]{:S(2)}) async-start(f32[4,6,64,128]{3,2,1,0:T(8,128)} %broadcast_select_fusion), calls=%async_computation.2 | async-start | bytes 1572864 | tf_op jit(solution)/shard_map/all_to_all | solution.py:149
  104.8 10.4 %all-to-all-done.2 = f32[4,6,64,128]{3,2,1,0:T(8,128)S(1)} async-done(((f32[4,6,64,128]{3,2,1,0:T(8,128)}), f32[4,6,64,128]{3,2,1,0:T(8,128)S(1)}, u32[]{:S(2)}, u32[]{:S(2)}) %all-to-all-start.2) | async-done | bytes 786464 | tf_op jit(solution)/shard_map/all_to_all | solution.py:149
  115.2 0.8 broadcast_select_fusion.1
  (52 shorter events, 1.3 us)
Async XLA Ops:
  25.2 24.3 %copy-start.1 = (bf16[512,2,512,1]{2,0,1,3:T(8,128)(2,1)S(1)}, bf16[512,2,512,1]{2,0,1,3:T(8,128)(2,1)}, u32[]{:S(2)}) copy-start(bf16[512,2,512,1]{2,0,1,3:T(8,128)(2,1)} %constant.131) | copy-start | bytes 3145732
  26.7 14.3 %collective-permute-start.3 = (bf16[2,512,128]{2,1,0:T(8,128)(2,1)S(1)}, bf16[2,512,128]{2,1,0:T(8,128)(2,1)S(1)}, u32[]{:S(2)}, u32[]{:S(2)}) collective-permute-start(bf16[2,512,128]{2,1,0:T(8,128)(2,1)S(1)} %pad_maximum_fusion.3), channel_id=1, source_target_pairs={{0,1},{1,2},{2,3},{3,4},{4,5},{5,6},{6,7},{7,8},{8,9},{9,10},{10,1... | collective-permute-start | bytes 786440 | tf_op jit(solution)/shard_map/ppermute | solution.py:125
  30.5 18.5 %collective-permute-start.4 = (bf16[2,512,128]{2,1,0:T(8,128)(2,1)S(1)}, bf16[2,512,128]{2,1,0:T(8,128)(2,1)S(1)}, u32[]{:S(2)}, u32[]{:S(2)}) collective-permute-start(bf16[2,512,128]{2,1,0:T(8,128)(2,1)S(1)} %pad_maximum_fusion.3), channel_id=1, source_target_pairs={{2,0},{3,1},{4,2},{5,3},{6,4},{7,5},{8,6},{9,7},{10,8},{11,9},{12,... | collective-permute-start | bytes 786440 | tf_op jit(solution)/shard_map/ppermute | solution.py:125
  50.2 24.4 %copy-start = (s32[6,2]{0,1:T(2,128)S(1)}, s32[6,2]{0,1:T(2,128)}, u32[]{:S(2)}) copy-start(s32[6,2]{0,1:T(2,128)} %param.4) | copy-start | bytes 148
  69.1 28.2 %all-to-all-start.1 = ((f32[8,64,3,128]{3,1,2,0:T(8,128)}), f32[8,64,3,128]{3,1,2,0:T(8,128)S(1)}, u32[]{:S(2)}, u32[]{:S(2)}) async-start(f32[8,64,3,128]{3,1,2,0:T(8,128)} %broadcast_in_dim.54), calls=%async_computation.1 | async-start | bytes 1572864 | tf_op jit(solution)/shard_map/all_to_all | solution.py:133
  74.6 4.0 %collective-permute-start = (s32[6,2]{0,1:T(2,128)S(1)}, s32[6,2]{0,1:T(2,128)S(1)}, u32[]{:S(2)}, u32[]{:S(2)}) collective-permute-start(s32[6,2]{0,1:T(2,128)S(1)} %copy-done), channel_id=1, source_target_pairs={{0,8},{8,16},{16,24},{24,0},{1,9},{9,17},{17,25},{25,1},{2,10},{10... | collective-permute-start | bytes 152 | tf_op jit(solution)/shard_map/ppermute | solution.py:137
  76.1 5.1 %collective-permute-start.1 = (s32[6,2]{0,1:T(2,128)S(1)}, s32[6,2]{0,1:T(2,128)S(1)}, u32[]{:S(2)}, u32[]{:S(2)}) collective-permute-start(s32[6,2]{0,1:T(2,128)S(1)} %copy-done), channel_id=1, source_target_pairs={{0,16},{8,24},{16,0},{24,8},{1,17},{9,25},{17,1},{25,9},{2,18},{10... | collective-permute-start | bytes 152 | tf_op jit(solution)/shard_map/ppermute | solution.py:137
  78.5 4.8 %collective-permute-start.2 = (s32[6,2]{0,1:T(2,128)S(1)}, s32[6,2]{0,1:T(2,128)S(1)}, u32[]{:S(2)}, u32[]{:S(2)}) collective-permute-start(s32[6,2]{0,1:T(2,128)S(1)} %copy-done), channel_id=1, source_target_pairs={{0,24},{8,0},{16,8},{24,16},{1,25},{9,1},{17,9},{25,17},{2,26},{10... | collective-permute-start | bytes 152 | tf_op jit(solution)/shard_map/ppermute | solution.py:137
  99.0 16.2 %all-to-all-start.2 = ((f32[4,6,64,128]{3,2,1,0:T(8,128)}), f32[4,6,64,128]{3,2,1,0:T(8,128)S(1)}, u32[]{:S(2)}, u32[]{:S(2)}) async-start(f32[4,6,64,128]{3,2,1,0:T(8,128)} %broadcast_select_fusion), calls=%async_computation.2 | async-start | bytes 1572864 | tf_op jit(solution)/shard_map/all_to_all | solution.py:149

commit v4 on v3

--- a/solution.py
+++ b/solution.py
@@ -1,8 +1,6 @@
 import math
 
 import jax
-import ml_dtypes
-import numpy as np
 import jax.numpy as jnp
 from jax import lax
 from jax.sharding import PartitionSpec as P
@@ -17,15 +15,6 @@
 two_pi = 2.0 * math.pi
 
 
-def lag_table():
-    bins = F_LO + np.arange(NB, dtype=np.int64)[None, :]
-    lagged = np.arange(LAGS, dtype=np.int64)[:, None] - LAGS // 2
-    angle = ((bins * lagged) % L).astype(np.float32) * np.float32(two_pi / L)
-    angle = angle.astype(np.float64)
-    table = np.stack([np.cos(angle), -np.sin(angle)], axis=1).astype(np.float32)
-    return table.astype(ml_dtypes.bfloat16)
-
-
 def band_tables():
     width = NB + 2 * HALF
     rows = lax.broadcasted_iota(jnp.int32, (NB, width), 0)
@@ -36,7 +25,10 @@
     taper = jnp.sin(
         math.pi * (lax.broadcasted_iota(jnp.int32, (NB,), 0).astype(jnp.float32) + 0.5) / NB
     )
-    table = jnp.asarray(lag_table())
+    bins = F_LO + lax.broadcasted_iota(jnp.int32, (LAGS, NB), 1)
+    lagged = lax.broadcasted_iota(jnp.int32, (LAGS, NB), 0) - LAGS // 2
+    angle = (bins * lagged % L).astype(jnp.float32) * (two_pi / L)
+    table = jnp.stack([jnp.cos(angle), -jnp.sin(angle)], axis=1).astype(jnp.bfloat16)
     return (smoother, taper, table)
 
 
@@ -130,7 +122,15 @@
     lags = corr.shape[0] // nwin
     corr = corr.reshape((nwin, lags) + corr.shape[1:])
     corr = lax.all_to_all(corr, "win", 0, 0).sum(axis=0)
-    ring = lax.all_to_all(jnp.broadcast_to(corr[None], (nz,) + corr.shape), "cz", 0, 0)
+    forward, backward = corr, corr
+    gathered = {0: corr}
+    for step in range(1, nz // 2 + 1):
+        forward = lax.ppermute(forward, "cz", [(k, (k + 1) % nz) for k in range(nz)])
+        gathered[-step % nz] = forward
+        if step < nz - nz // 2:
+            backward = lax.ppermute(backward, "cz", [(k, (k - 1) % nz) for k in range(nz)])
+            gathered[step % nz] = backward
+    ring = jnp.stack([gathered[j] for j in range(nz)])
     me_x = lax.axis_index("cx")
     shifted = [pair_blocks]
     for step in range(1, nx):
@@ -142,11 +142,14 @@
     filled = lb >= 0
     holder = jnp.where(filled, lb + (offset != 2).astype(jnp.int32), 0)
     mine = filled & (holder // nz == me_x)
-    zi = jnp.where(mine, holder % nz, 0)
+    zi = jnp.where(mine, (holder - lax.axis_index("cz")) % nz, 0)
     di = jnp.where(mine, offset - 1, 0)
     picked = ring[zi, :, di, :]
     picked = jnp.where(mine[..., None, None], picked, 0.0)
-    got = lax.all_to_all(picked, "cx", 0, 0).sum(axis=0)
+    got = lax.dynamic_index_in_dim(picked, me_x, 0, keepdims=False)
+    for step in range(1, nx):
+        chunk = lax.dynamic_index_in_dim(picked, (me_x + step) % nx, 0, keepdims=False)
+        got = got + lax.ppermute(chunk, "cx", [(k, (k + step) % nx) for k in range(nx)])
     return jnp.where(filled_local(pair_blocks)[:, None, None], got, 0.0)
 
 

time: 118 us -> 107 us (0.907); the launches traced: 116 us -> 106 us
  blocking collectives: 17.5 us -> 0 us
  starting transfers between devices: 26.9 us -> 30.7 us
  other arithmetic: 7.64 us -> 11.4 us
    ppermute x0 -> x10, waiting for transfers between devices: none -> 23.8 us  [the longest x4 11.8 us: body(): lax.ppermute(forward, 'cz', [(k, (k + 1) % nz) for k in range(nz)])]
    all_to_all x1 -> x0, blocking collectives: 17.5 us -> none  [body(): corr = lax.all_to_all(corr, 'win', 0, 0).sum(axis=0)]
    ppermute x0 -> x10, starting transfers between devices: none -> 11.9 us  [the longest x3 5.44 us: body(): lax.ppermute(chunk, 'cx', [(k, (k + step) % nx) for k in range(nx)])]
    all_to_all x2 -> x1, waiting for transfers between devices: 23.6 us -> 12.3 us  [body(): corr = lax.all_to_all(corr, 'win', 0, 0).sum(axis=0)]
    ppermute x2, waiting for transfers between devices: 10.7 us -> 3.28 us  [body(): received[shift] = lax.ppermute(white, ('cx', 'cz'), perm)]
    all_to_all x2 -> x1, starting transfers between devices: 11.3 us -> 4.47 us  [body(): corr = lax.all_to_all(corr, 'win', 0, 0).sum(axis=0)]
    ppermute x3, waiting for transfers between devices: 4.74 us -> 0.01 us  [body(): lax.ppermute(pair_blocks, 'cx', [(k, (k + step) % nx) for k in range(nx)])]
    another operation x1 -> x2, other arithmetic: 0.31 us -> 5.01 us
  transfers between devices with their start and end apart: 7 -> 16, of which waited for: 6 -> 11; matrix products, arithmetic and copies ran while one was open for 1% -> 7% of each run, Pallas kernels for 0% -> 0%
where the time goes in v4:
time: 107 us; the launch traced here: 106 us
  waiting for transfers between devices  39.4 us (37%)
  starting transfers between devices  30.7 us (29%)
  matrix products  16.1 us (15%)
  other arithmetic  11.4 us (11%)
  local copies, waits for them, and re-layouts  8.28 us (8%)
    all_to_all x1, waiting for transfers between devices, body(): corr = lax.all_to_all(corr, 'win', 0, 0).sum(axis=0)  12.3 us
    ppermute x4, waiting for transfers between devices, body(): lax.ppermute(forward, 'cz', [(k, (k + 1) % nz) for k in range(nz)])  11.8 us
    ppermute x2, starting transfers between devices, body(): received[shift] = lax.ppermute(white, ('cx', 'cz'), perm)  11.4 us
    dot_general x1, matrix products, band_dft(): jnp.einsum('rb,bac->rac', basis1, xb, precision=prec, preferred_element_t...  7.85 us
    ppermute x3, waiting for transfers between devices, body(): lax.ppermute(chunk, 'cx', [(k, (k + step) % nx) for k in range(nx)])  6.87 us
    dot_general x1, matrix products, band_dft(): jnp.einsum('ja,srac->sjrc', basis2, jnp.stack([wr, wi]), precision=prec,...  6.09 us
    ppermute x3, starting transfers between devices, body(): lax.ppermute(chunk, 'cx', [(k, (k + step) % nx) for k in range(nx)])  5.44 us
    concatenate x4, local copies, waits for them, and re-layouts, band_dft(): return (jnp.concatenate(res_re, 0), jnp.concatenate(res_im, 0))  5.27 us
  transfers between devices with their start and end apart: 16, of which 11 were waited for; matrix products, arithmetic and copies ran while one was open for 7% of the time, Pallas kernels for 0%

profile of v4, /device:TPU:6, one launch (start us, length us, event | category | flops | bytes accessed | tf_op | source)
XLA Modules:
  0.0 106.4 jit_solution(9119239107473308092)
XLA Ops:
  0.5 7.9 %fusion = f32[126,120,128]{2,0,1:T(8,128)S(1)} fusion(f32[125,120,128]{2,1,0:T(8,128)} %bitcast.136, f32[63,125]{1,0:T(8,128)S(1)} %get-tuple-element.43, f32[63,125]{1,0:T(8,128)S(1)} %get-tuple-element.44), kind=kOutput, calls=%fused_computation.3 | convolution fusion | flops 1451535744 | bytes 15484440 | tf_op jit(solution)/shard_map/rb,bac->rac/dot_general | solution.py:44
  8.4 3.0 %add_bitcast_fusion = (f32[1,63,120,128]{3,1,2,0:T(8,128)S(1)}, f32[1,63,120,128]{3,1,2,0:T(8,128)S(1)}) fusion(f32[126,120,128]{2,0,1:T(8,128)S(1)} %fusion, f32[63,120]{0,1:T(8,128)S(1)} %get-tuple-element.45, f32[63,120]{0,1:T(8,128)S(1)} %get-tuple-element.46), kind=kLoop, calls=%fused_computation.8 | loop fusion | flops 5806080 | bytes 15543360 | tf_op jit(solution)/shard_map/stack | solution.py:59
  11.4 1.5 %pad_maximum_fusion = f32[2,63,120,128]{3,1,2,0:T(8,128)S(1)} fusion(f32[1,63,120,128]{3,1,2,0:T(8,128)S(1)} %get-tuple-element.6, f32[1,63,120,128]{3,1,2,0:T(8,128)S(1)} %get-tuple-element.5), kind=kLoop, calls=%fused_computation.2 | loop fusion | flops 1935360 | bytes 15482880 | tf_op jit(solution)/shard_map/stack | solution.py:59
  12.9 6.1 %fusion.4 = f32[2,12,63,128]{3,1,2,0:T(8,128)S(1)} fusion(f32[2,63,120,128]{3,1,2,0:T(8,128)S(1)} %pad_maximum_fusion, f32[6,120]{1,0:T(8,128)S(1)} %get-tuple-element.47, f32[6,120]{1,0:T(8,128)S(1)} %get-tuple-element.48), kind=kOutput, calls=%fused_computation.12 | convolution fusion | flops 139347360 | bytes 8521344 | tf_op jit(solution)/shard_map/ja,srac->sjrc/dot_general | solution.py:58
  19.7 1.2 %concatenate.31 = f32[545,128]{1,0:T(8,128)S(1)} concatenate(f32[62,128]{1,0:T(8,128)S(1)} %rev.32, f32[63,128]{1,0:T(8,128)S(1)} %get-tuple-element.33, f32[62,128]{1,0:T(8,128)S(1)} %rev.33, f32[63,128]{1,0:T(8,128)S(1)} %get-tuple-element.32, f32[62,128]{1,0:T(8,128)S(1)} %rev.34, f32[63,128]{1,0:T(8,128)S(1)} %get-tuple-element.31, f32[62,128]{1,0:T(8,128)S(1)} %rev.35, ...), dimensions={0} | concatenate | bytes 558080 | tf_op jit(solution)/shard_map/concatenate | solution.py:82
  20.9 1.5 %concatenate.32 = f32[576,128]{1,0:T(8,128)S(1)} concatenate(f32[31,128]{1,0:T(8,128)S(1)} %slice_bitcast_fusion.11, f32[62,128]{1,0:T(8,128)S(1)} %rev.32, f32[63,128]{1,0:T(8,128)S(1)} %get-tuple-element.33, f32[62,128]{1,0:T(8,128)S(1)} %rev.33, f32[63,128]{1,0:T(8,128)S(1)} %get-tuple-element.32, f32[62,128]{1,0:T(8,128)S(1)} %rev.34, f32[63,128]{1,0:T(8,128)S(1)} %get-tuple-element.31, ...), dimensions={0} | concatenate | bytes 589824 | tf_op jit(solution)/shard_map/concatenate | solution.py:82
  22.6 1.2 %concatenate.34 = f32[545,128]{1,0:T(8,128)S(1)} concatenate(f32[62,128]{1,0:T(8,128)S(1)} %rev.37, f32[63,128]{1,0:T(8,128)S(1)} %bitcast.148, f32[62,128]{1,0:T(8,128)S(1)} %rev.38, f32[63,128]{1,0:T(8,128)S(1)} %bitcast.146, f32[62,128]{1,0:T(8,128)S(1)} %rev.39, f32[63,128]{1,0:T(8,128)S(1)} %bitcast.144, f32[62,128]{1,0:T(8,128)S(1)} %rev.40, f32[63,128]{1,0:T(8,128)S(1)} %bitcast.150, ...), dimensions={0} | concatenate | bytes 558080 | tf_op jit(solution)/shard_map/concatenate | solution.py:82
  23.7 1.5 %concatenate.33 = f32[576,128]{1,0:T(8,128)S(1)} concatenate(f32[31,128]{1,0:T(8,128)S(1)} %bitcast.159, f32[62,128]{1,0:T(8,128)S(1)} %rev.37, f32[63,128]{1,0:T(8,128)S(1)} %bitcast.149, f32[62,128]{1,0:T(8,128)S(1)} %rev.38, f32[63,128]{1,0:T(8,128)S(1)} %bitcast.147, f32[62,128]{1,0:T(8,128)S(1)} %rev.39, f32[63,128]{1,0:T(8,128)S(1)} %bitcast.145, f32[62,128]{1,0:T(8,128)S(1)} %rev.40, ...), dimensions={0} | concatenate | bytes 589824 | tf_op jit(solution)/shard_map/concatenate | solution.py:82
  25.2 1.4 %fusion.42 = (bf16[512,128]{1,0:T(8,128)(2,1)S(1)}, bf16[512,128]{1,0:T(8,128)(2,1)S(1)}) fusion(f32[545,128]{1,0:T(8,128)S(1)} %concatenate.31, f32[545,128]{1,0:T(8,128)S(1)} %concatenate.34, f32[576,128]{1,0:T(8,128)S(1)} %concatenate.33, f32[576,128]{1,0:T(8,128)S(1)} %concatenate.32, s32[512]{0:T(512)S(1)} %get-tuple-element.50, ...), kind=kOutput, calls=%fused_computation.55 | convolution fusion | flops 454778880 | bytes 1380352 | tf_op jit(solution)/shard_map/dot_general | solution.py:89
  26.7 3.8 %collective-permute-start.3 = (bf16[2,512,128]{2,1,0:T(8,128)(2,1)S(1)}, bf16[2,512,128]{2,1,0:T(8,128)(2,1)S(1)}, u32[]{:S(2)}, u32[]{:S(2)}) collective-permute-start(bf16[2,512,128]{2,1,0:T(8,128)(2,1)S(1)} %pad_maximum_fusion.3), channel_id=1, source_target_pairs={{0,1},{1,2},{2,3},{3,4},{4,5},{5,6},{6,7},{7,8},{8,9},{9,10},{10,1... | collective-permute-start | bytes 786440 | tf_op jit(solution)/shard_map/ppermute | solution.py:117
  30.5 7.6 %collective-permute-start.4 = (bf16[2,512,128]{2,1,0:T(8,128)(2,1)S(1)}, bf16[2,512,128]{2,1,0:T(8,128)(2,1)S(1)}, u32[]{:S(2)}, u32[]{:S(2)}) collective-permute-start(bf16[2,512,128]{2,1,0:T(8,128)(2,1)S(1)} %pad_maximum_fusion.3), channel_id=1, source_target_pairs={{2,0},{3,1},{4,2},{5,3},{6,4},{7,5},{8,6},{9,7},{10,8},{11,9},{12,... | collective-permute-start | bytes 786440 | tf_op jit(solution)/shard_map/ppermute | solution.py:117
  38.4 2.6 %collective-permute-start.1 = (s32[6,2]{0,1:T(2,128)S(1)}, s32[6,2]{0,1:T(2,128)S(1)}, u32[]{:S(2)}, u32[]{:S(2)}) collective-permute-start(s32[6,2]{0,1:T(2,128)S(1)} %copy-done), channel_id=1, source_target_pairs={{0,16},{8,24},{16,0},{24,8},{1,17},{9,25},{17,1},{25,9},{2,18},{10... | collective-permute-start | bytes 152 | tf_op jit(solution)/shard_map/ppermute | solution.py:137
  41.0 4.7 %cosine_convert_fusion = (bf16[512,1,512]{2,0,1:T(8,128)(2,1)S(1)}, bf16[512,1,512]{2,0,1:T(8,128)(2,1)S(1)}) fusion(s32[512]{0:T(512)S(1)} %get-tuple-element.49, s32[512]{0:T(512)S(1)} %get-tuple-element.50), kind=kLoop, calls=%fused_computation.27 | loop fusion | flops 3145728 | bytes 1052672 | tf_op jit(solution)/shard_map/convert.10
  45.7 3.3 %collective-permute-done.4 = bf16[2,512,128]{2,1,0:T(8,128)(2,1)S(1)} collective-permute-done((bf16[2,512,128]{2,1,0:T(8,128)(2,1)S(1)}, bf16[2,512,128]{2,1,0:T(8,128)(2,1)S(1)}, u32[]{:S(2)}, u32[]{:S(2)}) %collective-permute-start.4) | collective-permute-done | bytes 262176 | tf_op jit(solution)/shard_map/ppermute | solution.py:117
  49.5 0.7 fusion.11
  50.2 1.0 copy.27
  51.2 4.5 %all-to-all-start = ((f32[8,64,3,128]{3,1,2,0:T(8,128)}), f32[8,64,3,128]{3,1,2,0:T(8,128)S(1)}, u32[]{:S(2)}, u32[]{:S(2)}) async-start(f32[8,64,3,128]{3,1,2,0:T(8,128)} %copy.27), calls=%async_computation | async-start | bytes 1572864 | tf_op jit(solution)/shard_map/all_to_all | solution.py:124
  56.5 12.3 %all-to-all-done = f32[8,64,3,128]{3,1,2,0:T(8,128)S(1)} async-done(((f32[8,64,3,128]{3,1,2,0:T(8,128)}), f32[8,64,3,128]{3,1,2,0:T(8,128)S(1)}, u32[]{:S(2)}, u32[]{:S(2)}) %all-to-all-start) | async-done | bytes 786464 | tf_op jit(solution)/shard_map/all_to_all | solution.py:124
  69.0 2.0 %collective-permute-start.8 = (f32[64,3,128]{2,0,1:T(8,128)S(1)}, f32[64,3,128]{2,0,1:T(8,128)S(1)}, u32[]{:S(2)}, u32[]{:S(2)}) collective-permute-start(f32[64,3,128]{2,0,1:T(8,128)S(1)} %reduce_sum.9), channel_id=1, source_target_pairs={{0,1},{1,2},{2,3},{3,4},{4,5},{5,6},{6,7},{7,0},{8,9},{9,10},{10,1... | collective-permute-start | bytes 294920 | tf_op jit(solution)/shard_map/ppermute | solution.py:128
  71.0 2.6 %collective-permute-done.5 = f32[64,3,128]{2,0,1:T(8,128)S(1)} collective-permute-done((f32[64,3,128]{2,0,1:T(8,128)S(1)}, f32[64,3,128]{2,0,1:T(8,128)S(1)}, u32[]{:S(2)}, u32[]{:S(2)}) %collective-permute-start.5) | collective-permute-done | bytes 98336 | tf_op jit(solution)/shard_map/ppermute | solution.py:131
  73.6 1.2 %collective-permute-start.6 = (f32[64,3,128]{2,0,1:T(8,128)S(1)}, f32[64,3,128]{2,0,1:T(8,128)S(1)}, u32[]{:S(2)}, u32[]{:S(2)}) collective-permute-start(f32[64,3,128]{2,0,1:T(8,128)S(1)} %collective-permute-done.5), channel_id=1, source_target_pairs={{0,7},{1,0},{2,1},{3,2},{4,3},{5,4},{6,5},{7,6},{8,15},{9,8},{10,9... | collective-permute-start | bytes 294920 | tf_op jit(solution)/shard_map/ppermute | solution.py:131
  74.9 0.7 collective-permute-start.9
  75.6 2.6 %collective-permute-done.6 = f32[64,3,128]{2,0,1:T(8,128)S(1)} collective-permute-done((f32[64,3,128]{2,0,1:T(8,128)S(1)}, f32[64,3,128]{2,0,1:T(8,128)S(1)}, u32[]{:S(2)}, u32[]{:S(2)}) %collective-permute-start.6) | collective-permute-done | bytes 98336 | tf_op jit(solution)/shard_map/ppermute | solution.py:131
  78.2 2.4 %collective-permute-start.7 = (f32[64,3,128]{2,0,1:T(8,128)S(1)}, f32[64,3,128]{2,0,1:T(8,128)S(1)}, u32[]{:S(2)}, u32[]{:S(2)}) collective-permute-start(f32[64,3,128]{2,0,1:T(8,128)S(1)} %collective-permute-done.6), channel_id=1, source_target_pairs={{0,7},{1,0},{2,1},{3,2},{4,3},{5,4},{6,5},{7,6},{8,15},{9,8},{10,9... | collective-permute-start | bytes 294920 | tf_op jit(solution)/shard_map/ppermute | solution.py:131
  80.7 5.8 %collective-permute-done.10 = f32[64,3,128]{2,0,1:T(8,128)S(1)} collective-permute-done((f32[64,3,128]{2,0,1:T(8,128)S(1)}, f32[64,3,128]{2,0,1:T(8,128)S(1)}, u32[]{:S(2)}, u32[]{:S(2)}) %collective-permute-start.10) | collective-permute-done | bytes 98336 | tf_op jit(solution)/shard_map/ppermute | solution.py:128
  86.6 5.8 %collective-permute-done.11 = f32[64,3,128]{2,0,1:T(8,128)S(1)} collective-permute-done((f32[64,3,128]{2,0,1:T(8,128)S(1)}, f32[64,3,128]{2,0,1:T(8,128)S(1)}, u32[]{:S(2)}, u32[]{:S(2)}) %collective-permute-start.11) | collective-permute-done | bytes 98336 | tf_op jit(solution)/shard_map/ppermute | solution.py:128
  93.3 3.0 %collective-permute-start.12 = (f32[6,64,128]{2,1,0:T(8,128)S(1)}, f32[6,64,128]{2,1,0:T(8,128)S(1)}, u32[]{:S(2)}, u32[]{:S(2)}) collective-permute-start(f32[6,64,128]{2,1,0:T(8,128)S(1)} %get-tuple-element.13), channel_id=1, source_target_pairs={{0,8},{8,16},{16,24},{24,0},{1,9},{9,17},{17,25},{25,1},{2,10},{10... | collective-permute-start | bytes 589832 | tf_op jit(solution)/shard_map/ppermute | solution.py:152
  96.3 2.4 %collective-permute-start.13 = (f32[6,64,128]{2,1,0:T(8,128)S(1)}, f32[6,64,128]{2,1,0:T(8,128)S(1)}, u32[]{:S(2)}, u32[]{:S(2)}) collective-permute-start(f32[6,64,128]{2,1,0:T(8,128)S(1)} %get-tuple-element.15), channel_id=1, source_target_pairs={{0,16},{8,24},{16,0},{24,8},{1,17},{9,25},{17,1},{25,9},{2,18},{10... | collective-permute-start | bytes 589832 | tf_op jit(solution)/shard_map/ppermute | solution.py:152
  98.8 1.6 %collective-permute-done.12 = f32[6,64,128]{2,1,0:T(8,128)S(1)} collective-permute-done((f32[6,64,128]{2,1,0:T(8,128)S(1)}, f32[6,64,128]{2,1,0:T(8,128)S(1)}, u32[]{:S(2)}, u32[]{:S(2)}) %collective-permute-start.12) | collective-permute-done | bytes 196640 | tf_op jit(solution)/shard_map/ppermute | solution.py:152
  100.3 3.2 %collective-permute-done.13 = f32[6,64,128]{2,1,0:T(8,128)S(1)} collective-permute-done((f32[6,64,128]{2,1,0:T(8,128)S(1)}, f32[6,64,128]{2,1,0:T(8,128)S(1)}, u32[]{:S(2)}, u32[]{:S(2)}) %collective-permute-start.13) | collective-permute-done | bytes 196640 | tf_op jit(solution)/shard_map/ppermute | solution.py:152
  103.5 2.1 %collective-permute-done.14 = f32[6,64,128]{2,1,0:T(8,128)S(1)} collective-permute-done((f32[6,64,128]{2,1,0:T(8,128)S(1)}, f32[6,64,128]{2,1,0:T(8,128)S(1)}, u32[]{:S(2)}, u32[]{:S(2)}) %collective-permute-start.14) | collective-permute-done | bytes 196640 | tf_op jit(solution)/shard_map/ppermute | solution.py:152
  105.6 0.8 fusion.46
  (74 shorter events, 4.0 us)
Async XLA Ops:
  19.2 18.9 %copy-start = (s32[6,2]{0,1:T(2,128)S(1)}, s32[6,2]{0,1:T(2,128)}, u32[]{:S(2)}) copy-start(s32[6,2]{0,1:T(2,128)} %param.3) | copy-start | bytes 148
  26.7 19.0 %collective-permute-start.3 = (bf16[2,512,128]{2,1,0:T(8,128)(2,1)S(1)}, bf16[2,512,128]{2,1,0:T(8,128)(2,1)S(1)}, u32[]{:S(2)}, u32[]{:S(2)}) collective-permute-start(bf16[2,512,128]{2,1,0:T(8,128)(2,1)S(1)} %pad_maximum_fusion.3), channel_id=1, source_target_pairs={{0,1},{1,2},{2,3},{3,4},{4,5},{5,6},{6,7},{7,8},{8,9},{9,10},{10,1... | collective-permute-start | bytes 786440 | tf_op jit(solution)/shard_map/ppermute | solution.py:117
  30.5 18.5 %collective-permute-start.4 = (bf16[2,512,128]{2,1,0:T(8,128)(2,1)S(1)}, bf16[2,512,128]{2,1,0:T(8,128)(2,1)S(1)}, u32[]{:S(2)}, u32[]{:S(2)}) collective-permute-start(bf16[2,512,128]{2,1,0:T(8,128)(2,1)S(1)} %pad_maximum_fusion.3), channel_id=1, source_target_pairs={{2,0},{3,1},{4,2},{5,3},{6,4},{7,5},{8,6},{9,7},{10,8},{11,9},{12,... | collective-permute-start | bytes 786440 | tf_op jit(solution)/shard_map/ppermute | solution.py:117
  38.1 17.6 %collective-permute-start = (s32[6,2]{0,1:T(2,128)S(1)}, s32[6,2]{0,1:T(2,128)S(1)}, u32[]{:S(2)}, u32[]{:S(2)}) collective-permute-start(s32[6,2]{0,1:T(2,128)S(1)} %copy-done), channel_id=1, source_target_pairs={{0,8},{8,16},{16,24},{24,0},{1,9},{9,17},{17,25},{25,1},{2,10},{10... | collective-permute-start | bytes 152 | tf_op jit(solution)/shard_map/ppermute | solution.py:137
  38.4 17.3 %collective-permute-start.1 = (s32[6,2]{0,1:T(2,128)S(1)}, s32[6,2]{0,1:T(2,128)S(1)}, u32[]{:S(2)}, u32[]{:S(2)}) collective-permute-start(s32[6,2]{0,1:T(2,128)S(1)} %copy-done), channel_id=1, source_target_pairs={{0,16},{8,24},{16,0},{24,8},{1,17},{9,25},{17,1},{25,9},{2,18},{10... | collective-permute-start | bytes 152 | tf_op jit(solution)/shard_map/ppermute | solution.py:137
  41.0 14.8 %collective-permute-start.2 = (s32[6,2]{0,1:T(2,128)S(1)}, s32[6,2]{0,1:T(2,128)S(1)}, u32[]{:S(2)}, u32[]{:S(2)}) collective-permute-start(s32[6,2]{0,1:T(2,128)S(1)} %copy-done), channel_id=1, source_target_pairs={{0,24},{8,0},{16,8},{24,16},{1,25},{9,1},{17,9},{25,17},{2,26},{10... | collective-permute-start | bytes 152 | tf_op jit(solution)/shard_map/ppermute | solution.py:137
  51.2 17.6 %all-to-all-start = ((f32[8,64,3,128]{3,1,2,0:T(8,128)}), f32[8,64,3,128]{3,1,2,0:T(8,128)S(1)}, u32[]{:S(2)}, u32[]{:S(2)}) async-start(f32[8,64,3,128]{3,1,2,0:T(8,128)} %copy.27), calls=%async_computation | async-start | bytes 1572864 | tf_op jit(solution)/shard_map/all_to_all | solution.py:124
  68.9 4.7 %collective-permute-start.5 = (f32[64,3,128]{2,0,1:T(8,128)S(1)}, f32[64,3,128]{2,0,1:T(8,128)S(1)}, u32[]{:S(2)}, u32[]{:S(2)}) collective-permute-start(f32[64,3,128]{2,0,1:T(8,128)S(1)} %reduce_sum.9), channel_id=1, source_target_pairs={{0,7},{1,0},{2,1},{3,2},{4,3},{5,4},{6,5},{7,6},{8,15},{9,8},{10,9... | collective-permute-start | bytes 294920 | tf_op jit(solution)/shard_map/ppermute | solution.py:131
  69.0 5.9 %collective-permute-start.8 = (f32[64,3,128]{2,0,1:T(8,128)S(1)}, f32[64,3,128]{2,0,1:T(8,128)S(1)}, u32[]{:S(2)}, u32[]{:S(2)}) collective-permute-start(f32[64,3,128]{2,0,1:T(8,128)S(1)} %reduce_sum.9), channel_id=1, source_target_pairs={{0,1},{1,2},{2,3},{3,4},{4,5},{5,6},{6,7},{7,0},{8,9},{9,10},{10,1... | collective-permute-start | bytes 294920 | tf_op jit(solution)/shard_map/ppermute | solution.py:128
  73.6 4.6 %collective-permute-start.6 = (f32[64,3,128]{2,0,1:T(8,128)S(1)}, f32[64,3,128]{2,0,1:T(8,128)S(1)}, u32[]{:S(2)}, u32[]{:S(2)}) collective-permute-start(f32[64,3,128]{2,0,1:T(8,128)S(1)} %collective-permute-done.5), channel_id=1, source_target_pairs={{0,7},{1,0},{2,1},{3,2},{4,3},{5,4},{6,5},{7,6},{8,15},{9,8},{10,9... | collective-permute-start | bytes 294920 | tf_op jit(solution)/shard_map/ppermute | solution.py:131
  74.9 5.8 %collective-permute-start.9 = (f32[64,3,128]{2,0,1:T(8,128)S(1)}, f32[64,3,128]{2,0,1:T(8,128)S(1)}, u32[]{:S(2)}, u32[]{:S(2)}) collective-permute-start(f32[64,3,128]{2,0,1:T(8,128)S(1)} %collective-permute-done.8), channel_id=1, source_target_pairs={{0,1},{1,2},{2,3},{3,4},{4,5},{5,6},{6,7},{7,0},{8,9},{9,10},{10,1... | collective-permute-start | bytes 294920 | tf_op jit(solution)/shard_map/ppermute | solution.py:128
  78.2 8.3 %collective-permute-start.7 = (f32[64,3,128]{2,0,1:T(8,128)S(1)}, f32[64,3,128]{2,0,1:T(8,128)S(1)}, u32[]{:S(2)}, u32[]{:S(2)}) collective-permute-start(f32[64,3,128]{2,0,1:T(8,128)S(1)} %collective-permute-done.6), channel_id=1, source_target_pairs={{0,7},{1,0},{2,1},{3,2},{4,3},{5,4},{6,5},{7,6},{8,15},{9,8},{10,9... | collective-permute-start | bytes 294920 | tf_op jit(solution)/shard_map/ppermute | solution.py:131
  80.7 5.8 %collective-permute-start.10 = (f32[64,3,128]{2,0,1:T(8,128)S(1)}, f32[64,3,128]{2,0,1:T(8,128)S(1)}, u32[]{:S(2)}, u32[]{:S(2)}) collective-permute-start(f32[64,3,128]{2,0,1:T(8,128)S(1)} %collective-permute-done.9), channel_id=1, source_target_pairs={{0,1},{1,2},{2,3},{3,4},{4,5},{5,6},{6,7},{7,0},{8,9},{9,10},{10,1... | collective-permute-start | bytes 294920 | tf_op jit(solution)/shard_map/ppermute | solution.py:128
  86.5 5.8 %collective-permute-start.11 = (f32[64,3,128]{2,0,1:T(8,128)S(1)}, f32[64,3,128]{2,0,1:T(8,128)S(1)}, u32[]{:S(2)}, u32[]{:S(2)}) collective-permute-start(f32[64,3,128]{2,0,1:T(8,128)S(1)} %collective-permute-done.10), channel_id=1, source_target_pairs={{0,1},{1,2},{2,3},{3,4},{4,5},{5,6},{6,7},{7,0},{8,9},{9,10},{10,1... | collective-permute-start | bytes 294920 | tf_op jit(solution)/shard_map/ppermute | solution.py:128
  93.3 7.0 %collective-permute-start.12 = (f32[6,64,128]{2,1,0:T(8,128)S(1)}, f32[6,64,128]{2,1,0:T(8,128)S(1)}, u32[]{:S(2)}, u32[]{:S(2)}) collective-permute-start(f32[6,64,128]{2,1,0:T(8,128)S(1)} %get-tuple-element.13), channel_id=1, source_target_pairs={{0,8},{8,16},{16,24},{24,0},{1,9},{9,17},{17,25},{25,1},{2,10},{10... | collective-permute-start | bytes 589832 | tf_op jit(solution)/shard_map/ppermute | solution.py:152
  96.3 7.2 %collective-permute-start.13 = (f32[6,64,128]{2,1,0:T(8,128)S(1)}, f32[6,64,128]{2,1,0:T(8,128)S(1)}, u32[]{:S(2)}, u32[]{:S(2)}) collective-permute-start(f32[6,64,128]{2,1,0:T(8,128)S(1)} %get-tuple-element.15), channel_id=1, source_target_pairs={{0,16},{8,24},{16,0},{24,8},{1,17},{9,25},{17,1},{25,9},{2,18},{10... | collective-permute-start | bytes 589832 | tf_op jit(solution)/shard_map/ppermute | solution.py:152
  98.7 6.9 %collective-permute-start.14 = (f32[6,64,128]{2,1,0:T(8,128)S(1)}, f32[6,64,128]{2,1,0:T(8,128)S(1)}, u32[]{:S(2)}, u32[]{:S(2)}) collective-permute-start(f32[6,64,128]{2,1,0:T(8,128)S(1)} %get-tuple-element.14), channel_id=1, source_target_pairs={{0,24},{8,0},{16,8},{24,16},{1,25},{9,1},{17,9},{25,17},{2,26},{10... | collective-permute-start | bytes 589832 | tf_op jit(solution)/shard_map/ppermute | solution.py:152

commit v5 on v4

--- a/solution.py
+++ b/solution.py
@@ -122,14 +122,16 @@
     lags = corr.shape[0] // nwin
     corr = corr.reshape((nwin, lags) + corr.shape[1:])
     corr = lax.all_to_all(corr, "win", 0, 0).sum(axis=0)
-    forward, backward = corr, corr
+    def shift_z(value, step):
+        return lax.ppermute(value, "cz", [(k, (k - step) % nz) for k in range(nz)])
+
     gathered = {0: corr}
-    for step in range(1, nz // 2 + 1):
-        forward = lax.ppermute(forward, "cz", [(k, (k + 1) % nz) for k in range(nz)])
-        gathered[-step % nz] = forward
-        if step < nz - nz // 2:
-            backward = lax.ppermute(backward, "cz", [(k, (k - 1) % nz) for k in range(nz)])
-            gathered[step % nz] = backward
+    for step in (1, -1, 2, -2):
+        gathered[step % nz] = shift_z(corr, step)
+    ahead = shift_z(jnp.stack([gathered[1], gathered[2]]), 2)
+    behind = shift_z(gathered[nz - 1], -2)
+    gathered[3], gathered[4] = ahead[0], ahead[1]
+    gathered[nz - 3] = behind
     ring = jnp.stack([gathered[j] for j in range(nz)])
     me_x = lax.axis_index("cx")
     shifted = [pair_blocks]

time: 107 us -> 105 us (0.981)
  waiting for transfers between devices: 39.4 us -> 36.4 us
  starting transfers between devices: 30.7 us -> 32.2 us
    ppermute x7 -> x6, waiting for transfers between devices: 16.9 us -> 10.9 us  [shift_z(): return lax.ppermute(value, 'cz', [(k, (k - step) % nz) for k in range(nz)])]
    ppermute x7 -> x6, starting transfers between devices: 6.47 us -> 10.1 us  [shift_z(): return lax.ppermute(value, 'cz', [(k, (k - step) % nz) for k in range(nz)])]
    ppermute x3, waiting for transfers between devices: 6.87 us -> 9.84 us  [body(): lax.ppermute(chunk, 'cx', [(k, (k + step) % nx) for k in range(nx)])]
    ppermute x3, starting transfers between devices: 5.44 us -> 3.26 us  [body(): lax.ppermute(chunk, 'cx', [(k, (k + step) % nx) for k in range(nx)])]
    another operation x2 -> x3, other arithmetic: 5.01 us -> 5.02 us
  transfers between devices with their start and end apart: 16 -> 15, of which waited for: 11 -> 8; matrix products, arithmetic and copies ran while one was open for 7% -> 7% of each run, Pallas kernels for 0% -> 0%
where the time goes in v5:
time: 105 us
  waiting for transfers between devices  36.4 us (35%)
  starting transfers between devices  32.2 us (31%)
  matrix products  16.1 us (15%)
  other arithmetic  11.4 us (11%)
  local copies, waits for them, and re-layouts  8.27 us (8%)
    all_to_all x1, waiting for transfers between devices, body(): corr = lax.all_to_all(corr, 'win', 0, 0).sum(axis=0)  12.3 us
    ppermute x2, starting transfers between devices, body(): received[shift] = lax.ppermute(white, ('cx', 'cz'), perm)  11.4 us
    ppermute x6, waiting for transfers between devices, shift_z(): return lax.ppermute(value, 'cz', [(k, (k - step) % nz) for k in range(nz)])  10.9 us
    ppermute x6, starting transfers between devices, shift_z(): return lax.ppermute(value, 'cz', [(k, (k - step) % nz) for k in range(nz)])  10.1 us
    ppermute x3, waiting for transfers between devices, body(): lax.ppermute(chunk, 'cx', [(k, (k + step) % nx) for k in range(nx)])  9.84 us
    dot_general x1, matrix products, band_dft(): jnp.einsum('rb,bac->rac', basis1, xb, precision=prec, preferred_element_t...  7.85 us
    dot_general x1, matrix products, band_dft(): jnp.einsum('ja,srac->sjrc', basis2, jnp.stack([wr, wi]), precision=prec,...  6.09 us
    concatenate x4, local copies, waits for them, and re-layouts, band_dft(): return (jnp.concatenate(res_re, 0), jnp.concatenate(res_im, 0))  5.27 us
  transfers between devices with their start and end apart: 15, of which 8 were waited for; matrix products, arithmetic and copies ran while one was open for 7% of the time, Pallas kernels for 0%

profile of v5, /device:TPU:6, one launch (start us, length us, event | category | flops | bytes accessed | tf_op | source)
XLA Modules:
  0.0 104.8 jit_solution(3303158939905415297)
XLA Ops:
  0.5 7.9 %fusion = f32[126,120,128]{2,0,1:T(8,128)S(1)} fusion(f32[125,120,128]{2,1,0:T(8,128)} %bitcast.132, f32[63,125]{1,0:T(8,128)S(1)} %get-tuple-element.43, f32[63,125]{1,0:T(8,128)S(1)} %get-tuple-element.44), kind=kOutput, calls=%fused_computation.3 | convolution fusion | flops 1451535744 | bytes 15484440 | tf_op jit(solution)/shard_map/rb,bac->rac/dot_general | solution.py:44
  8.4 3.0 %add_bitcast_fusion = (f32[1,63,120,128]{3,1,2,0:T(8,128)S(1)}, f32[1,63,120,128]{3,1,2,0:T(8,128)S(1)}) fusion(f32[126,120,128]{2,0,1:T(8,128)S(1)} %fusion, f32[63,120]{0,1:T(8,128)S(1)} %get-tuple-element.45, f32[63,120]{0,1:T(8,128)S(1)} %get-tuple-element.46), kind=kLoop, calls=%fused_computation.8 | loop fusion | flops 5806080 | bytes 15543360 | tf_op jit(solution)/shard_map/stack | solution.py:59
  11.4 1.5 %pad_maximum_fusion = f32[2,63,120,128]{3,1,2,0:T(8,128)S(1)} fusion(f32[1,63,120,128]{3,1,2,0:T(8,128)S(1)} %get-tuple-element.6, f32[1,63,120,128]{3,1,2,0:T(8,128)S(1)} %get-tuple-element.5), kind=kLoop, calls=%fused_computation.2 | loop fusion | flops 1935360 | bytes 15482880 | tf_op jit(solution)/shard_map/stack | solution.py:59
  12.9 6.1 %fusion.4 = f32[2,12,63,128]{3,1,2,0:T(8,128)S(1)} fusion(f32[2,63,120,128]{3,1,2,0:T(8,128)S(1)} %pad_maximum_fusion, f32[6,120]{1,0:T(8,128)S(1)} %get-tuple-element.47, f32[6,120]{1,0:T(8,128)S(1)} %get-tuple-element.48), kind=kOutput, calls=%fused_computation.12 | convolution fusion | flops 139347360 | bytes 8521344 | tf_op jit(solution)/shard_map/ja,srac->sjrc/dot_general | solution.py:58
  19.7 1.2 %concatenate.31 = f32[545,128]{1,0:T(8,128)S(1)} concatenate(f32[62,128]{1,0:T(8,128)S(1)} %rev.32, f32[63,128]{1,0:T(8,128)S(1)} %get-tuple-element.33, f32[62,128]{1,0:T(8,128)S(1)} %rev.33, f32[63,128]{1,0:T(8,128)S(1)} %get-tuple-element.32, f32[62,128]{1,0:T(8,128)S(1)} %rev.34, f32[63,128]{1,0:T(8,128)S(1)} %get-tuple-element.31, f32[62,128]{1,0:T(8,128)S(1)} %rev.35, ...), dimensions={0} | concatenate | bytes 558080 | tf_op jit(solution)/shard_map/concatenate | solution.py:82
  20.9 1.5 %concatenate.32 = f32[576,128]{1,0:T(8,128)S(1)} concatenate(f32[31,128]{1,0:T(8,128)S(1)} %slice_bitcast_fusion.11, f32[62,128]{1,0:T(8,128)S(1)} %rev.32, f32[63,128]{1,0:T(8,128)S(1)} %get-tuple-element.33, f32[62,128]{1,0:T(8,128)S(1)} %rev.33, f32[63,128]{1,0:T(8,128)S(1)} %get-tuple-element.32, f32[62,128]{1,0:T(8,128)S(1)} %rev.34, f32[63,128]{1,0:T(8,128)S(1)} %get-tuple-element.31, ...), dimensions={0} | concatenate | bytes 589824 | tf_op jit(solution)/shard_map/concatenate | solution.py:82
  22.6 1.2 %concatenate.34 = f32[545,128]{1,0:T(8,128)S(1)} concatenate(f32[62,128]{1,0:T(8,128)S(1)} %rev.37, f32[63,128]{1,0:T(8,128)S(1)} %bitcast.146, f32[62,128]{1,0:T(8,128)S(1)} %rev.38, f32[63,128]{1,0:T(8,128)S(1)} %bitcast.144, f32[62,128]{1,0:T(8,128)S(1)} %rev.39, f32[63,128]{1,0:T(8,128)S(1)} %bitcast.142, f32[62,128]{1,0:T(8,128)S(1)} %rev.40, f32[63,128]{1,0:T(8,128)S(1)} %bitcast.148, ...), dimensions={0} | concatenate | bytes 558080 | tf_op jit(solution)/shard_map/concatenate | solution.py:82
  23.7 1.5 %concatenate.33 = f32[576,128]{1,0:T(8,128)S(1)} concatenate(f32[31,128]{1,0:T(8,128)S(1)} %bitcast.157, f32[62,128]{1,0:T(8,128)S(1)} %rev.37, f32[63,128]{1,0:T(8,128)S(1)} %bitcast.147, f32[62,128]{1,0:T(8,128)S(1)} %rev.38, f32[63,128]{1,0:T(8,128)S(1)} %bitcast.145, f32[62,128]{1,0:T(8,128)S(1)} %rev.39, f32[63,128]{1,0:T(8,128)S(1)} %bitcast.143, f32[62,128]{1,0:T(8,128)S(1)} %rev.40, ...), dimensions={0} | concatenate | bytes 589824 | tf_op jit(solution)/shard_map/concatenate | solution.py:82
  25.2 1.4 %fusion.42 = (bf16[512,128]{1,0:T(8,128)(2,1)S(1)}, bf16[512,128]{1,0:T(8,128)(2,1)S(1)}) fusion(f32[545,128]{1,0:T(8,128)S(1)} %concatenate.31, f32[545,128]{1,0:T(8,128)S(1)} %concatenate.34, f32[576,128]{1,0:T(8,128)S(1)} %concatenate.33, f32[576,128]{1,0:T(8,128)S(1)} %concatenate.32, s32[512]{0:T(512)S(1)} %get-tuple-element.50, ...), kind=kOutput, calls=%fused_computation.55 | convolution fusion | flops 454778880 | bytes 1380352 | tf_op jit(solution)/shard_map/dot_general | solution.py:89
  26.7 3.8 %collective-permute-start.3 = (bf16[2,512,128]{2,1,0:T(8,128)(2,1)S(1)}, bf16[2,512,128]{2,1,0:T(8,128)(2,1)S(1)}, u32[]{:S(2)}, u32[]{:S(2)}) collective-permute-start(bf16[2,512,128]{2,1,0:T(8,128)(2,1)S(1)} %pad_maximum_fusion.3), channel_id=1, source_target_pairs={{0,1},{1,2},{2,3},{3,4},{4,5},{5,6},{6,7},{7,8},{8,9},{9,10},{10,1... | collective-permute-start | bytes 786440 | tf_op jit(solution)/shard_map/ppermute | solution.py:117
  30.5 7.6 %collective-permute-start.4 = (bf16[2,512,128]{2,1,0:T(8,128)(2,1)S(1)}, bf16[2,512,128]{2,1,0:T(8,128)(2,1)S(1)}, u32[]{:S(2)}, u32[]{:S(2)}) collective-permute-start(bf16[2,512,128]{2,1,0:T(8,128)(2,1)S(1)} %pad_maximum_fusion.3), channel_id=1, source_target_pairs={{2,0},{3,1},{4,2},{5,3},{6,4},{7,5},{8,6},{9,7},{10,8},{11,9},{12,... | collective-permute-start | bytes 786440 | tf_op jit(solution)/shard_map/ppermute | solution.py:117
  38.4 2.6 %collective-permute-start.1 = (s32[6,2]{0,1:T(2,128)S(1)}, s32[6,2]{0,1:T(2,128)S(1)}, u32[]{:S(2)}, u32[]{:S(2)}) collective-permute-start(s32[6,2]{0,1:T(2,128)S(1)} %copy-done), channel_id=1, source_target_pairs={{0,16},{8,24},{16,0},{24,8},{1,17},{9,25},{17,1},{25,9},{2,18},{10... | collective-permute-start | bytes 152 | tf_op jit(solution)/shard_map/ppermute | solution.py:139
  41.0 4.7 %cosine_convert_fusion = (bf16[512,1,512]{2,0,1:T(8,128)(2,1)S(1)}, bf16[512,1,512]{2,0,1:T(8,128)(2,1)S(1)}) fusion(s32[512]{0:T(512)S(1)} %get-tuple-element.49, s32[512]{0:T(512)S(1)} %get-tuple-element.50), kind=kLoop, calls=%fused_computation.27 | loop fusion | flops 3145728 | bytes 1052672 | tf_op jit(solution)/shard_map/convert.10
  45.7 3.3 %collective-permute-done.4 = bf16[2,512,128]{2,1,0:T(8,128)(2,1)S(1)} collective-permute-done((bf16[2,512,128]{2,1,0:T(8,128)(2,1)S(1)}, bf16[2,512,128]{2,1,0:T(8,128)(2,1)S(1)}, u32[]{:S(2)}, u32[]{:S(2)}) %collective-permute-start.4) | collective-permute-done | bytes 262176 | tf_op jit(solution)/shard_map/ppermute | solution.py:117
  49.5 0.7 fusion.11
  50.2 1.0 copy.27
  51.2 4.5 %all-to-all-start = ((f32[8,64,3,128]{3,1,2,0:T(8,128)}), f32[8,64,3,128]{3,1,2,0:T(8,128)S(1)}, u32[]{:S(2)}, u32[]{:S(2)}) async-start(f32[8,64,3,128]{3,1,2,0:T(8,128)} %copy.27), calls=%async_computation | async-start | bytes 1572864 | tf_op jit(solution)/shard_map/all_to_all | solution.py:124
  56.5 12.3 %all-to-all-done = f32[8,64,3,128]{3,1,2,0:T(8,128)S(1)} async-done(((f32[8,64,3,128]{3,1,2,0:T(8,128)}), f32[8,64,3,128]{3,1,2,0:T(8,128)S(1)}, u32[]{:S(2)}, u32[]{:S(2)}) %all-to-all-start) | async-done | bytes 786464 | tf_op jit(solution)/shard_map/all_to_all | solution.py:124
  69.0 2.9 %collective-permute-start.6 = (f32[64,3,128]{2,0,1:T(8,128)S(1)}, f32[64,3,128]{2,0,1:T(8,128)S(1)}, u32[]{:S(2)}, u32[]{:S(2)}) collective-permute-start(f32[64,3,128]{2,0,1:T(8,128)S(1)} %reduce_sum.9), channel_id=1, source_target_pairs={{0,6},{1,7},{2,0},{3,1},{4,2},{5,3},{6,4},{7,5},{8,14},{9,15},{10,... | collective-permute-start | bytes 294920 | tf_op jit(solution)/shard_map/ppermute | solution.py:126
  72.2 1.8 %collective-permute-start.10 = (f32[64,3,128]{2,0,1:T(8,128)S(1)}, f32[64,3,128]{2,0,1:T(8,128)S(1)}, u32[]{:S(2)}, u32[]{:S(2)}) collective-permute-start(f32[64,3,128]{2,0,1:T(8,128)S(1)} %reduce_sum.9), channel_id=1, source_target_pairs={{0,2},{1,3},{2,4},{3,5},{4,6},{5,7},{6,0},{7,1},{8,10},{9,11},{10,... | collective-permute-start | bytes 294920 | tf_op jit(solution)/shard_map/ppermute | solution.py:126
  74.0 1.5 %collective-permute-done.5 = f32[64,3,128]{2,0,1:T(8,128)S(1)} collective-permute-done((f32[64,3,128]{2,0,1:T(8,128)S(1)}, f32[64,3,128]{2,0,1:T(8,128)S(1)}, u32[]{:S(2)}, u32[]{:S(2)}) %collective-permute-start.5) | collective-permute-done | bytes 98336 | tf_op jit(solution)/shard_map/ppermute | solution.py:126
  75.5 2.6 %collective-permute-done.6 = f32[64,3,128]{2,0,1:T(8,128)S(1)} collective-permute-done((f32[64,3,128]{2,0,1:T(8,128)S(1)}, f32[64,3,128]{2,0,1:T(8,128)S(1)}, u32[]{:S(2)}, u32[]{:S(2)}) %collective-permute-start.6) | collective-permute-done | bytes 98336 | tf_op jit(solution)/shard_map/ppermute | solution.py:126
  78.2 1.3 %collective-permute-start.7 = (f32[2,64,3,128]{3,1,2,0:T(8,128)S(1)}, f32[2,64,3,128]{3,1,2,0:T(8,128)S(1)}, u32[]{:S(2)}, u32[]{:S(2)}) collective-permute-start(f32[2,64,3,128]{3,1,2,0:T(8,128)S(1)} %pad_maximum_fusion.4), channel_id=1, source_target_pairs={{0,6},{1,7},{2,0},{3,1},{4,2},{5,3},{6,4},{7,5},{8,14},{9,15},{10,... | collective-permute-start | bytes 589832 | tf_op jit(solution)/shard_map/ppermute | solution.py:126
  79.4 3.8 %collective-permute-start.9 = (f32[64,3,128]{2,0,1:T(8,128)S(1)}, f32[64,3,128]{2,0,1:T(8,128)S(1)}, u32[]{:S(2)}, u32[]{:S(2)}) collective-permute-start(f32[64,3,128]{2,0,1:T(8,128)S(1)} %collective-permute-done.8), channel_id=1, source_target_pairs={{0,2},{1,3},{2,4},{3,5},{4,6},{5,7},{6,0},{7,1},{8,10},{9,11},{10,... | collective-permute-start | bytes 294920 | tf_op jit(solution)/shard_map/ppermute | solution.py:126
  83.3 6.7 %collective-permute-done.7 = f32[2,64,3,128]{3,1,2,0:T(8,128)S(1)} collective-permute-done((f32[2,64,3,128]{3,1,2,0:T(8,128)S(1)}, f32[2,64,3,128]{3,1,2,0:T(8,128)S(1)}, u32[]{:S(2)}, u32[]{:S(2)}) %collective-permute-start.7) | collective-permute-done | bytes 196640 | tf_op jit(solution)/shard_map/ppermute | solution.py:126
  90.1 0.7 gather_fusion.1
  91.0 1.0 collective-permute-start.11
  91.9 2.3 %collective-permute-start.12 = (f32[6,64,128]{2,1,0:T(8,128)S(1)}, f32[6,64,128]{2,1,0:T(8,128)S(1)}, u32[]{:S(2)}, u32[]{:S(2)}) collective-permute-start(f32[6,64,128]{2,1,0:T(8,128)S(1)} %get-tuple-element.15), channel_id=1, source_target_pairs={{0,16},{8,24},{16,0},{24,8},{1,17},{9,25},{17,1},{25,9},{2,18},{10... | collective-permute-start | bytes 589832 | tf_op jit(solution)/shard_map/ppermute | solution.py:154
  94.2 4.6 %collective-permute-done.11 = f32[6,64,128]{2,1,0:T(8,128)S(1)} collective-permute-done((f32[6,64,128]{2,1,0:T(8,128)S(1)}, f32[6,64,128]{2,1,0:T(8,128)S(1)}, u32[]{:S(2)}, u32[]{:S(2)}) %collective-permute-start.11) | collective-permute-done | bytes 196640 | tf_op jit(solution)/shard_map/ppermute | solution.py:154
  98.8 2.4 %collective-permute-done.12 = f32[6,64,128]{2,1,0:T(8,128)S(1)} collective-permute-done((f32[6,64,128]{2,1,0:T(8,128)S(1)}, f32[6,64,128]{2,1,0:T(8,128)S(1)}, u32[]{:S(2)}, u32[]{:S(2)}) %collective-permute-start.12) | collective-permute-done | bytes 196640 | tf_op jit(solution)/shard_map/ppermute | solution.py:154
  101.3 2.8 %collective-permute-done.13 = f32[6,64,128]{2,1,0:T(8,128)S(1)} collective-permute-done((f32[6,64,128]{2,1,0:T(8,128)S(1)}, f32[6,64,128]{2,1,0:T(8,128)S(1)}, u32[]{:S(2)}, u32[]{:S(2)}) %collective-permute-start.13) | collective-permute-done | bytes 196640 | tf_op jit(solution)/shard_map/ppermute | solution.py:154
  104.1 0.8 fusion.46
  (72 shorter events, 3.5 us)
Async XLA Ops:
  19.2 18.9 %copy-start = (s32[6,2]{0,1:T(2,128)S(1)}, s32[6,2]{0,1:T(2,128)}, u32[]{:S(2)}) copy-start(s32[6,2]{0,1:T(2,128)} %param.3) | copy-start | bytes 148
  26.7 19.0 %collective-permute-start.3 = (bf16[2,512,128]{2,1,0:T(8,128)(2,1)S(1)}, bf16[2,512,128]{2,1,0:T(8,128)(2,1)S(1)}, u32[]{:S(2)}, u32[]{:S(2)}) collective-permute-start(bf16[2,512,128]{2,1,0:T(8,128)(2,1)S(1)} %pad_maximum_fusion.3), channel_id=1, source_target_pairs={{0,1},{1,2},{2,3},{3,4},{4,5},{5,6},{6,7},{7,8},{8,9},{9,10},{10,1... | collective-permute-start | bytes 786440 | tf_op jit(solution)/shard_map/ppermute | solution.py:117
  30.5 18.5 %collective-permute-start.4 = (bf16[2,512,128]{2,1,0:T(8,128)(2,1)S(1)}, bf16[2,512,128]{2,1,0:T(8,128)(2,1)S(1)}, u32[]{:S(2)}, u32[]{:S(2)}) collective-permute-start(bf16[2,512,128]{2,1,0:T(8,128)(2,1)S(1)} %pad_maximum_fusion.3), channel_id=1, source_target_pairs={{2,0},{3,1},{4,2},{5,3},{6,4},{7,5},{8,6},{9,7},{10,8},{11,9},{12,... | collective-permute-start | bytes 786440 | tf_op jit(solution)/shard_map/ppermute | solution.py:117
  38.1 17.6 %collective-permute-start = (s32[6,2]{0,1:T(2,128)S(1)}, s32[6,2]{0,1:T(2,128)S(1)}, u32[]{:S(2)}, u32[]{:S(2)}) collective-permute-start(s32[6,2]{0,1:T(2,128)S(1)} %copy-done), channel_id=1, source_target_pairs={{0,8},{8,16},{16,24},{24,0},{1,9},{9,17},{17,25},{25,1},{2,10},{10... | collective-permute-start | bytes 152 | tf_op jit(solution)/shard_map/ppermute | solution.py:139
  38.4 17.3 %collective-permute-start.1 = (s32[6,2]{0,1:T(2,128)S(1)}, s32[6,2]{0,1:T(2,128)S(1)}, u32[]{:S(2)}, u32[]{:S(2)}) collective-permute-start(s32[6,2]{0,1:T(2,128)S(1)} %copy-done), channel_id=1, source_target_pairs={{0,16},{8,24},{16,0},{24,8},{1,17},{9,25},{17,1},{25,9},{2,18},{10... | collective-permute-start | bytes 152 | tf_op jit(solution)/shard_map/ppermute | solution.py:139
  41.0 14.8 %collective-permute-start.2 = (s32[6,2]{0,1:T(2,128)S(1)}, s32[6,2]{0,1:T(2,128)S(1)}, u32[]{:S(2)}, u32[]{:S(2)}) collective-permute-start(s32[6,2]{0,1:T(2,128)S(1)} %copy-done), channel_id=1, source_target_pairs={{0,24},{8,0},{16,8},{24,16},{1,25},{9,1},{17,9},{25,17},{2,26},{10... | collective-permute-start | bytes 152 | tf_op jit(solution)/shard_map/ppermute | solution.py:139
  51.2 17.6 %all-to-all-start = ((f32[8,64,3,128]{3,1,2,0:T(8,128)}), f32[8,64,3,128]{3,1,2,0:T(8,128)S(1)}, u32[]{:S(2)}, u32[]{:S(2)}) async-start(f32[8,64,3,128]{3,1,2,0:T(8,128)} %copy.27), calls=%async_computation | async-start | bytes 1572864 | tf_op jit(solution)/shard_map/all_to_all | solution.py:124
  68.9 6.6 %collective-permute-start.5 = (f32[64,3,128]{2,0,1:T(8,128)S(1)}, f32[64,3,128]{2,0,1:T(8,128)S(1)}, u32[]{:S(2)}, u32[]{:S(2)}) collective-permute-start(f32[64,3,128]{2,0,1:T(8,128)S(1)} %reduce_sum.9), channel_id=1, source_target_pairs={{0,7},{1,0},{2,1},{3,2},{4,3},{5,4},{6,5},{7,6},{8,15},{9,8},{10,9... | collective-permute-start | bytes 294920 | tf_op jit(solution)/shard_map/ppermute | solution.py:126
  69.0 9.2 %collective-permute-start.6 = (f32[64,3,128]{2,0,1:T(8,128)S(1)}, f32[64,3,128]{2,0,1:T(8,128)S(1)}, u32[]{:S(2)}, u32[]{:S(2)}) collective-permute-start(f32[64,3,128]{2,0,1:T(8,128)S(1)} %reduce_sum.9), channel_id=1, source_target_pairs={{0,6},{1,7},{2,0},{3,1},{4,2},{5,3},{6,4},{7,5},{8,14},{9,15},{10,... | collective-permute-start | bytes 294920 | tf_op jit(solution)/shard_map/ppermute | solution.py:126
  71.9 7.6 %collective-permute-start.8 = (f32[64,3,128]{2,0,1:T(8,128)S(1)}, f32[64,3,128]{2,0,1:T(8,128)S(1)}, u32[]{:S(2)}, u32[]{:S(2)}) collective-permute-start(f32[64,3,128]{2,0,1:T(8,128)S(1)} %reduce_sum.9), channel_id=1, source_target_pairs={{0,1},{1,2},{2,3},{3,4},{4,5},{5,6},{6,7},{7,0},{8,9},{9,10},{10,1... | collective-permute-start | bytes 294920 | tf_op jit(solution)/shard_map/ppermute | solution.py:126
  72.2 17.8 %collective-permute-start.10 = (f32[64,3,128]{2,0,1:T(8,128)S(1)}, f32[64,3,128]{2,0,1:T(8,128)S(1)}, u32[]{:S(2)}, u32[]{:S(2)}) collective-permute-start(f32[64,3,128]{2,0,1:T(8,128)S(1)} %reduce_sum.9), channel_id=1, source_target_pairs={{0,2},{1,3},{2,4},{3,5},{4,6},{5,7},{6,0},{7,1},{8,10},{9,11},{10,... | collective-permute-start | bytes 294920 | tf_op jit(solution)/shard_map/ppermute | solution.py:126
  78.2 11.8 %collective-permute-start.7 = (f32[2,64,3,128]{3,1,2,0:T(8,128)S(1)}, f32[2,64,3,128]{3,1,2,0:T(8,128)S(1)}, u32[]{:S(2)}, u32[]{:S(2)}) collective-permute-start(f32[2,64,3,128]{3,1,2,0:T(8,128)S(1)} %pad_maximum_fusion.4), channel_id=1, source_target_pairs={{0,6},{1,7},{2,0},{3,1},{4,2},{5,3},{6,4},{7,5},{8,14},{9,15},{10,... | collective-permute-start | bytes 589832 | tf_op jit(solution)/shard_map/ppermute | solution.py:126
  79.4 10.6 %collective-permute-start.9 = (f32[64,3,128]{2,0,1:T(8,128)S(1)}, f32[64,3,128]{2,0,1:T(8,128)S(1)}, u32[]{:S(2)}, u32[]{:S(2)}) collective-permute-start(f32[64,3,128]{2,0,1:T(8,128)S(1)} %collective-permute-done.8), channel_id=1, source_target_pairs={{0,2},{1,3},{2,4},{3,5},{4,6},{5,7},{6,0},{7,1},{8,10},{9,11},{10,... | collective-permute-start | bytes 294920 | tf_op jit(solution)/shard_map/ppermute | solution.py:126
  91.0 7.8 %collective-permute-start.11 = (f32[6,64,128]{2,1,0:T(8,128)S(1)}, f32[6,64,128]{2,1,0:T(8,128)S(1)}, u32[]{:S(2)}, u32[]{:S(2)}) collective-permute-start(f32[6,64,128]{2,1,0:T(8,128)S(1)} %get-tuple-element.13), channel_id=1, source_target_pairs={{0,8},{8,16},{16,24},{24,0},{1,9},{9,17},{17,25},{25,1},{2,10},{10... | collective-permute-start | bytes 589832 | tf_op jit(solution)/shard_map/ppermute | solution.py:154
  91.9 9.3 %collective-permute-start.12 = (f32[6,64,128]{2,1,0:T(8,128)S(1)}, f32[6,64,128]{2,1,0:T(8,128)S(1)}, u32[]{:S(2)}, u32[]{:S(2)}) collective-permute-start(f32[6,64,128]{2,1,0:T(8,128)S(1)} %get-tuple-element.15), channel_id=1, source_target_pairs={{0,16},{8,24},{16,0},{24,8},{1,17},{9,25},{17,1},{25,9},{2,18},{10... | collective-permute-start | bytes 589832 | tf_op jit(solution)/shard_map/ppermute | solution.py:154
  94.2 9.8 %collective-permute-start.13 = (f32[6,64,128]{2,1,0:T(8,128)S(1)}, f32[6,64,128]{2,1,0:T(8,128)S(1)}, u32[]{:S(2)}, u32[]{:S(2)}) collective-permute-start(f32[6,64,128]{2,1,0:T(8,128)S(1)} %get-tuple-element.14), channel_id=1, source_target_pairs={{0,24},{8,0},{16,8},{24,16},{1,25},{9,1},{17,9},{25,17},{2,26},{10... | collective-permute-start | bytes 589832 | tf_op jit(solution)/shard_map/ppermute | solution.py:154

commit v6 on v5

--- a/solution.py
+++ b/solution.py
@@ -32,7 +32,7 @@
     return (smoother, taper, table)
 
 
-def band_dft(x, f0, nbins, outer=125, prec=lax.Precision.HIGH):
+def band_dft(x, f0, nbins, tie, outer=125, prec=lax.Precision.HIGH):
     total, channels = x.shape
     inner = total // outer
     half = outer // 2 + 1
@@ -42,6 +42,7 @@
     ang1 = ((r * b) % outer).astype(jnp.float32) * (two_pi / outer)
     basis1 = jnp.concatenate([jnp.cos(ang1), -jnp.sin(ang1)], axis=0)
     z = jnp.einsum("rb,bac->rac", basis1, xb, precision=prec, preferred_element_type=jnp.float32)
+    z, tie = lax.optimization_barrier((z, tie))
     zr, zi = z[:half], z[half:]
     r2 = lax.broadcasted_iota(jnp.int32, (half, inner), 0)
     a2 = lax.broadcasted_iota(jnp.int32, (half, inner), 1)
@@ -79,17 +80,17 @@
             res_re.append(jnp.flip(cre[j + 1, s_end + 1 : s0 + 1], axis=0))
             res_im.append(jnp.flip(cim[j + 1, s_end + 1 : s0 + 1], axis=0))
             f += s0 - s_end
-    return jnp.concatenate(res_re, 0), jnp.concatenate(res_im, 0)
+    return jnp.concatenate(res_re, 0), jnp.concatenate(res_im, 0), tie
 
 
-def whiten_local(trace, smoother, taper):
+def whiten_local(trace, smoother, taper, tie):
     width = NB + 2 * HALF
-    real, imag = band_dft(trace, F_LO - HALF, width)
+    real, imag, tie = band_dft(trace, F_LO - HALF, width, tie)
     power = real * real + imag * imag
     level = jnp.dot(smoother, power, precision=lax.Precision.HIGHEST) + 1e-06
     factor = taper[:, None] * lax.rsqrt(level)
     white = jnp.stack([real[HALF : HALF + NB] * factor, imag[HALF : HALF + NB] * factor])
-    return white.astype(jnp.bfloat16)
+    return white.astype(jnp.bfloat16), tie
 
 
 def cross_spectra(left, right):
@@ -104,8 +105,12 @@
 
 def body(traces, pair_blocks):
     smoother, taper, table = band_tables()
-    white = whiten_local(traces[0], smoother, taper)
     nx = lax.axis_size("cx")
+    me_x = lax.axis_index("cx")
+    shifted = [pair_blocks]
+    for step in range(1, nx):
+        shifted.append(lax.ppermute(pair_blocks, "cx", [(k, (k + step) % nx) for k in range(nx)]))
+    white, shifted = whiten_local(traces[0], smoother, taper, jnp.stack(shifted))
     nz = lax.axis_size("cz")
     blocks = nx * nz
     nwin = lax.axis_size("win")
@@ -133,11 +138,6 @@
     gathered[3], gathered[4] = ahead[0], ahead[1]
     gathered[nz - 3] = behind
     ring = jnp.stack([gathered[j] for j in range(nz)])
-    me_x = lax.axis_index("cx")
-    shifted = [pair_blocks]
-    for step in range(1, nx):
-        shifted.append(lax.ppermute(pair_blocks, "cx", [(k, (k + step) % nx) for k in range(nx)]))
-    shifted = jnp.stack(shifted)
     owners = shifted[(me_x - jnp.arange(nx)) % nx]
     lb = owners[..., 0]
     offset = owners[..., 1] - lb

time: 105 us -> 110 us (1.048)
  waiting for transfers between devices: 36.4 us -> 39.1 us
  starting transfers between devices: 32.2 us -> 34 us
    ppermute x2, waiting for transfers between devices: 3.28 us -> 5.11 us  [body(): received[shift] = lax.ppermute(white, ('cx', 'cz'), perm)]
    ppermute x3, starting transfers between devices: 3.26 us -> 4.76 us  [body(): lax.ppermute(chunk, 'cx', [(k, (k + step) % nx) for k in range(nx)])]
  transfers between devices with their start and end apart: 15 -> 15, of which waited for: 8 -> 8; matrix products, arithmetic and copies ran while one was open for 7% -> 13% of each run, Pallas kernels for 0% -> 0%
where the time goes in v6:
time: 110 us
  waiting for transfers between devices  39.1 us (36%)
  starting transfers between devices  34 us (31%)
  matrix products  16.1 us (15%)
  other arithmetic  11.6 us (11%)
  local copies, waits for them, and re-layouts  8.27 us (8%)
    all_to_all x1, waiting for transfers between devices, body(): corr = lax.all_to_all(corr, 'win', 0, 0).sum(axis=0)  12.4 us
    ppermute x2, starting transfers between devices, body(): received[shift] = lax.ppermute(white, ('cx', 'cz'), perm)  11.5 us
    ppermute x6, waiting for transfers between devices, shift_z(): return lax.ppermute(value, 'cz', [(k, (k - step) % nz) for k in range(nz)])  10.9 us
    ppermute x3, waiting for transfers between devices, body(): lax.ppermute(chunk, 'cx', [(k, (k + step) % nx) for k in range(nx)])  10.6 us
    ppermute x6, starting transfers between devices, shift_z(): return lax.ppermute(value, 'cz', [(k, (k - step) % nz) for k in range(nz)])  10.2 us
    dot_general x1, matrix products, band_dft(): jnp.einsum('rb,bac->rac', basis1, xb, precision=prec, preferred_element_t...  7.84 us
    dot_general x1, matrix products, band_dft(): jnp.einsum('ja,srac->sjrc', basis2, jnp.stack([wr, wi]), precision=prec,...  6.09 us
    concatenate x4, local copies, waits for them, and re-layouts, band_dft(): return (jnp.concatenate(res_re, 0), jnp.concatenate(res_im, 0), tie)  5.27 us
  transfers between devices with their start and end apart: 15, of which 8 were waited for; matrix products, arithmetic and copies ran while one was open for 13% of the time, Pallas kernels for 0%

profile of v6, /device:TPU:6, one launch (start us, length us, event | category | flops | bytes accessed | tf_op | source)
XLA Modules:
  0.0 109.6 jit_solution(7796226048654767542)
XLA Ops:
  0.0 2.2 %collective-permute-start = (s32[6,2]{0,1:T(2,128)}, s32[6,2]{0,1:T(2,128)S(1)}, u32[]{:S(2)}, u32[]{:S(2)}) collective-permute-start(s32[6,2]{0,1:T(2,128)} %param.3), channel_id=1, source_target_pairs={{0,8},{8,16},{16,24},{24,0},{1,9},{9,17},{17,25},{25,1},{2,10},{10... | collective-permute-start | bytes 152 | tf_op jit(solution)/shard_map/ppermute | solution.py:112
  3.6 7.8 %fusion = f32[126,120,128]{2,0,1:T(8,128)S(1)} fusion(f32[125,120,128]{2,1,0:T(8,128)} %bitcast.132, f32[63,125]{1,0:T(8,128)S(1)} %get-tuple-element.47, f32[63,125]{1,0:T(8,128)S(1)} %get-tuple-element.48), kind=kOutput, calls=%fused_computation.3 | convolution fusion | flops 1451535744 | bytes 15484440 | tf_op jit(solution)/shard_map/rb,bac->rac/dot_general | solution.py:44
  11.5 3.0 %add_bitcast_fusion = (f32[1,63,120,128]{3,1,2,0:T(8,128)S(1)}, f32[1,63,120,128]{3,1,2,0:T(8,128)S(1)}) fusion(f32[126,120,128]{2,0,1:T(8,128)S(1)} %fusion, f32[63,120]{0,1:T(8,128)S(1)} %get-tuple-element.49, f32[63,120]{0,1:T(8,128)S(1)} %get-tuple-element.50), kind=kLoop, calls=%fused_computation.8 | loop fusion | flops 5806080 | bytes 15543360 | tf_op jit(solution)/shard_map/stack | solution.py:60
  14.5 1.5 %pad_maximum_fusion = f32[2,63,120,128]{3,1,2,0:T(8,128)S(1)} fusion(f32[1,63,120,128]{3,1,2,0:T(8,128)S(1)} %get-tuple-element.10, f32[1,63,120,128]{3,1,2,0:T(8,128)S(1)} %get-tuple-element.9), kind=kLoop, calls=%fused_computation.2 | loop fusion | flops 1935360 | bytes 15482880 | tf_op jit(solution)/shard_map/stack | solution.py:60
  16.1 6.1 %fusion.4 = f32[2,12,63,128]{3,1,2,0:T(8,128)S(1)} fusion(f32[2,63,120,128]{3,1,2,0:T(8,128)S(1)} %pad_maximum_fusion, f32[6,120]{1,0:T(8,128)S(1)} %get-tuple-element.51, f32[6,120]{1,0:T(8,128)S(1)} %get-tuple-element.52), kind=kOutput, calls=%fused_computation.12 | convolution fusion | flops 139347360 | bytes 8521344 | tf_op jit(solution)/shard_map/ja,srac->sjrc/dot_general | solution.py:59
  22.8 1.2 %concatenate.31 = f32[545,128]{1,0:T(8,128)S(1)} concatenate(f32[62,128]{1,0:T(8,128)S(1)} %rev.32, f32[63,128]{1,0:T(8,128)S(1)} %get-tuple-element.37, f32[62,128]{1,0:T(8,128)S(1)} %rev.33, f32[63,128]{1,0:T(8,128)S(1)} %get-tuple-element.36, f32[62,128]{1,0:T(8,128)S(1)} %rev.34, f32[63,128]{1,0:T(8,128)S(1)} %get-tuple-element.35, f32[62,128]{1,0:T(8,128)S(1)} %rev.35, ...), dimensions={0} | concatenate | bytes 558080 | tf_op jit(solution)/shard_map/concatenate | solution.py:83
  24.0 1.5 %concatenate.32 = f32[576,128]{1,0:T(8,128)S(1)} concatenate(f32[31,128]{1,0:T(8,128)S(1)} %slice_bitcast_fusion.11, f32[62,128]{1,0:T(8,128)S(1)} %rev.32, f32[63,128]{1,0:T(8,128)S(1)} %get-tuple-element.37, f32[62,128]{1,0:T(8,128)S(1)} %rev.33, f32[63,128]{1,0:T(8,128)S(1)} %get-tuple-element.36, f32[62,128]{1,0:T(8,128)S(1)} %rev.34, f32[63,128]{1,0:T(8,128)S(1)} %get-tuple-element.35, ...), dimensions={0} | concatenate | bytes 589824 | tf_op jit(solution)/shard_map/concatenate | solution.py:83
  25.7 1.2 %concatenate.34 = f32[545,128]{1,0:T(8,128)S(1)} concatenate(f32[62,128]{1,0:T(8,128)S(1)} %rev.37, f32[63,128]{1,0:T(8,128)S(1)} %bitcast.146, f32[62,128]{1,0:T(8,128)S(1)} %rev.38, f32[63,128]{1,0:T(8,128)S(1)} %bitcast.144, f32[62,128]{1,0:T(8,128)S(1)} %rev.39, f32[63,128]{1,0:T(8,128)S(1)} %bitcast.142, f32[62,128]{1,0:T(8,128)S(1)} %rev.40, f32[63,128]{1,0:T(8,128)S(1)} %bitcast.148, ...), dimensions={0} | concatenate | bytes 558080 | tf_op jit(solution)/shard_map/concatenate | solution.py:83
  26.9 1.5 %concatenate.33 = f32[576,128]{1,0:T(8,128)S(1)} concatenate(f32[31,128]{1,0:T(8,128)S(1)} %bitcast.157, f32[62,128]{1,0:T(8,128)S(1)} %rev.37, f32[63,128]{1,0:T(8,128)S(1)} %bitcast.147, f32[62,128]{1,0:T(8,128)S(1)} %rev.38, f32[63,128]{1,0:T(8,128)S(1)} %bitcast.145, f32[62,128]{1,0:T(8,128)S(1)} %rev.39, f32[63,128]{1,0:T(8,128)S(1)} %bitcast.143, f32[62,128]{1,0:T(8,128)S(1)} %rev.40, ...), dimensions={0} | concatenate | bytes 589824 | tf_op jit(solution)/shard_map/concatenate | solution.py:83
  28.3 1.4 %fusion.42 = (bf16[512,128]{1,0:T(8,128)(2,1)S(1)}, bf16[512,128]{1,0:T(8,128)(2,1)S(1)}) fusion(f32[545,128]{1,0:T(8,128)S(1)} %concatenate.31, f32[545,128]{1,0:T(8,128)S(1)} %concatenate.34, f32[576,128]{1,0:T(8,128)S(1)} %concatenate.33, f32[576,128]{1,0:T(8,128)S(1)} %concatenate.32, s32[512]{0:T(512)S(1)} %get-tuple-element.54, ...), kind=kOutput, calls=%fused_computation.55 | convolution fusion | flops 454778880 | bytes 1380352 | tf_op jit(solution)/shard_map/dot_general | solution.py:90
  29.8 3.7 %collective-permute-start.3 = (bf16[2,512,128]{2,1,0:T(8,128)(2,1)S(1)}, bf16[2,512,128]{2,1,0:T(8,128)(2,1)S(1)}, u32[]{:S(2)}, u32[]{:S(2)}) collective-permute-start(bf16[2,512,128]{2,1,0:T(8,128)(2,1)S(1)} %pad_maximum_fusion.3), channel_id=1, source_target_pairs={{0,1},{1,2},{2,3},{3,4},{4,5},{5,6},{6,7},{7,8},{8,9},{9,10},{10,1... | collective-permute-start | bytes 786440 | tf_op jit(solution)/shard_map/ppermute | solution.py:122
  33.5 7.8 %collective-permute-start.4 = (bf16[2,512,128]{2,1,0:T(8,128)(2,1)S(1)}, bf16[2,512,128]{2,1,0:T(8,128)(2,1)S(1)}, u32[]{:S(2)}, u32[]{:S(2)}) collective-permute-start(bf16[2,512,128]{2,1,0:T(8,128)(2,1)S(1)} %pad_maximum_fusion.3), channel_id=1, source_target_pairs={{2,0},{3,1},{4,2},{5,3},{6,4},{7,5},{8,6},{9,7},{10,8},{11,9},{12,... | collective-permute-start | bytes 786440 | tf_op jit(solution)/shard_map/ppermute | solution.py:122
  41.3 4.9 %cosine_convert_fusion = (bf16[512,1,512]{2,0,1:T(8,128)(2,1)S(1)}, bf16[512,1,512]{2,0,1:T(8,128)(2,1)S(1)}) fusion(s32[512]{0:T(512)S(1)} %get-tuple-element.53, s32[512]{0:T(512)S(1)} %get-tuple-element.54), kind=kLoop, calls=%fused_computation.27 | loop fusion | flops 3145728 | bytes 1052672 | tf_op jit(solution)/shard_map/convert.10
  46.3 5.1 %collective-permute-done.4 = bf16[2,512,128]{2,1,0:T(8,128)(2,1)S(1)} collective-permute-done((bf16[2,512,128]{2,1,0:T(8,128)(2,1)S(1)}, bf16[2,512,128]{2,1,0:T(8,128)(2,1)S(1)}, u32[]{:S(2)}, u32[]{:S(2)}) %collective-permute-start.4) | collective-permute-done | bytes 262176 | tf_op jit(solution)/shard_map/ppermute | solution.py:122
  51.9 0.7 fusion.11
  52.6 1.0 copy.27
  53.6 4.4 %all-to-all-start = ((f32[8,64,3,128]{3,1,2,0:T(8,128)}), f32[8,64,3,128]{3,1,2,0:T(8,128)S(1)}, u32[]{:S(2)}, u32[]{:S(2)}) async-start(f32[8,64,3,128]{3,1,2,0:T(8,128)} %copy.27), calls=%async_computation | async-start | bytes 1572864 | tf_op jit(solution)/shard_map/all_to_all | solution.py:129
  58.8 12.4 %all-to-all-done = f32[8,64,3,128]{3,1,2,0:T(8,128)S(1)} async-done(((f32[8,64,3,128]{3,1,2,0:T(8,128)}), f32[8,64,3,128]{3,1,2,0:T(8,128)S(1)}, u32[]{:S(2)}, u32[]{:S(2)}) %all-to-all-start) | async-done | bytes 786464 | tf_op jit(solution)/shard_map/all_to_all | solution.py:129
  71.3 3.0 %collective-permute-start.6 = (f32[64,3,128]{2,0,1:T(8,128)S(1)}, f32[64,3,128]{2,0,1:T(8,128)S(1)}, u32[]{:S(2)}, u32[]{:S(2)}) collective-permute-start(f32[64,3,128]{2,0,1:T(8,128)S(1)} %reduce_sum.9), channel_id=1, source_target_pairs={{0,6},{1,7},{2,0},{3,1},{4,2},{5,3},{6,4},{7,5},{8,14},{9,15},{10,... | collective-permute-start | bytes 294920 | tf_op jit(solution)/shard_map/ppermute | solution.py:131
  74.6 1.7 %collective-permute-start.10 = (f32[64,3,128]{2,0,1:T(8,128)S(1)}, f32[64,3,128]{2,0,1:T(8,128)S(1)}, u32[]{:S(2)}, u32[]{:S(2)}) collective-permute-start(f32[64,3,128]{2,0,1:T(8,128)S(1)} %reduce_sum.9), channel_id=1, source_target_pairs={{0,2},{1,3},{2,4},{3,5},{4,6},{5,7},{6,0},{7,1},{8,10},{9,11},{10,... | collective-permute-start | bytes 294920 | tf_op jit(solution)/shard_map/ppermute | solution.py:131
  76.4 1.6 %collective-permute-done.5 = f32[64,3,128]{2,0,1:T(8,128)S(1)} collective-permute-done((f32[64,3,128]{2,0,1:T(8,128)S(1)}, f32[64,3,128]{2,0,1:T(8,128)S(1)}, u32[]{:S(2)}, u32[]{:S(2)}) %collective-permute-start.5) | collective-permute-done | bytes 98336 | tf_op jit(solution)/shard_map/ppermute | solution.py:131
  77.9 2.6 %collective-permute-done.6 = f32[64,3,128]{2,0,1:T(8,128)S(1)} collective-permute-done((f32[64,3,128]{2,0,1:T(8,128)S(1)}, f32[64,3,128]{2,0,1:T(8,128)S(1)}, u32[]{:S(2)}, u32[]{:S(2)}) %collective-permute-start.6) | collective-permute-done | bytes 98336 | tf_op jit(solution)/shard_map/ppermute | solution.py:131
  80.5 1.3 %collective-permute-start.7 = (f32[2,64,3,128]{3,1,2,0:T(8,128)S(1)}, f32[2,64,3,128]{3,1,2,0:T(8,128)S(1)}, u32[]{:S(2)}, u32[]{:S(2)}) collective-permute-start(f32[2,64,3,128]{3,1,2,0:T(8,128)S(1)} %pad_maximum_fusion.4), channel_id=1, source_target_pairs={{0,6},{1,7},{2,0},{3,1},{4,2},{5,3},{6,4},{7,5},{8,14},{9,15},{10,... | collective-permute-start | bytes 589832 | tf_op jit(solution)/shard_map/ppermute | solution.py:131
  81.8 3.8 %collective-permute-start.9 = (f32[64,3,128]{2,0,1:T(8,128)S(1)}, f32[64,3,128]{2,0,1:T(8,128)S(1)}, u32[]{:S(2)}, u32[]{:S(2)}) collective-permute-start(f32[64,3,128]{2,0,1:T(8,128)S(1)} %collective-permute-done.8), channel_id=1, source_target_pairs={{0,2},{1,3},{2,4},{3,5},{4,6},{5,7},{6,0},{7,1},{8,10},{9,11},{10,... | collective-permute-start | bytes 294920 | tf_op jit(solution)/shard_map/ppermute | solution.py:131
  85.7 6.7 %collective-permute-done.7 = f32[2,64,3,128]{3,1,2,0:T(8,128)S(1)} collective-permute-done((f32[2,64,3,128]{3,1,2,0:T(8,128)S(1)}, f32[2,64,3,128]{3,1,2,0:T(8,128)S(1)}, u32[]{:S(2)}, u32[]{:S(2)}) %collective-permute-start.7) | collective-permute-done | bytes 196640 | tf_op jit(solution)/shard_map/ppermute | solution.py:131
  92.5 0.7 gather_fusion.1
  93.4 3.2 %collective-permute-start.11 = (f32[6,64,128]{2,1,0:T(8,128)S(1)}, f32[6,64,128]{2,1,0:T(8,128)S(1)}, u32[]{:S(2)}, u32[]{:S(2)}) collective-permute-start(f32[6,64,128]{2,1,0:T(8,128)S(1)} %get-tuple-element.17), channel_id=1, source_target_pairs={{0,8},{8,16},{16,24},{24,0},{1,9},{9,17},{17,25},{25,1},{2,10},{10... | collective-permute-start | bytes 589832 | tf_op jit(solution)/shard_map/ppermute | solution.py:154
  96.8 1.3 %collective-permute-start.13 = (f32[6,64,128]{2,1,0:T(8,128)S(1)}, f32[6,64,128]{2,1,0:T(8,128)S(1)}, u32[]{:S(2)}, u32[]{:S(2)}) collective-permute-start(f32[6,64,128]{2,1,0:T(8,128)S(1)} %get-tuple-element.18), channel_id=1, source_target_pairs={{0,24},{8,0},{16,8},{24,16},{1,25},{9,1},{17,9},{25,17},{2,26},{10... | collective-permute-start | bytes 589832 | tf_op jit(solution)/shard_map/ppermute | solution.py:154
  98.2 7.0 %collective-permute-done.11 = f32[6,64,128]{2,1,0:T(8,128)S(1)} collective-permute-done((f32[6,64,128]{2,1,0:T(8,128)S(1)}, f32[6,64,128]{2,1,0:T(8,128)S(1)}, u32[]{:S(2)}, u32[]{:S(2)}) %collective-permute-start.11) | collective-permute-done | bytes 196640 | tf_op jit(solution)/shard_map/ppermute | solution.py:154
  105.1 0.8 collective-permute-done.12
  105.9 2.9 %collective-permute-done.13 = f32[6,64,128]{2,1,0:T(8,128)S(1)} collective-permute-done((f32[6,64,128]{2,1,0:T(8,128)S(1)}, f32[6,64,128]{2,1,0:T(8,128)S(1)}, u32[]{:S(2)}, u32[]{:S(2)}) %collective-permute-start.13) | collective-permute-done | bytes 196640 | tf_op jit(solution)/shard_map/ppermute | solution.py:154
  108.8 0.8 fusion.46
  (72 shorter events, 4.3 us)
Async XLA Ops:
  0.0 11.5 %collective-permute-start = (s32[6,2]{0,1:T(2,128)}, s32[6,2]{0,1:T(2,128)S(1)}, u32[]{:S(2)}, u32[]{:S(2)}) collective-permute-start(s32[6,2]{0,1:T(2,128)} %param.3), channel_id=1, source_target_pairs={{0,8},{8,16},{16,24},{24,0},{1,9},{9,17},{17,25},{25,1},{2,10},{10... | collective-permute-start | bytes 152 | tf_op jit(solution)/shard_map/ppermute | solution.py:112
  2.2 9.3 %collective-permute-start.1 = (s32[6,2]{0,1:T(2,128)}, s32[6,2]{0,1:T(2,128)S(1)}, u32[]{:S(2)}, u32[]{:S(2)}) collective-permute-start(s32[6,2]{0,1:T(2,128)} %param.3), channel_id=1, source_target_pairs={{0,16},{8,24},{16,0},{24,8},{1,17},{9,25},{17,1},{25,9},{2,18},{10... | collective-permute-start | bytes 152 | tf_op jit(solution)/shard_map/ppermute | solution.py:112
  2.9 8.6 %collective-permute-start.2 = (s32[6,2]{0,1:T(2,128)}, s32[6,2]{0,1:T(2,128)S(1)}, u32[]{:S(2)}, u32[]{:S(2)}) collective-permute-start(s32[6,2]{0,1:T(2,128)} %param.3), channel_id=1, source_target_pairs={{0,24},{8,0},{16,8},{24,16},{1,25},{9,1},{17,9},{25,17},{2,26},{10... | collective-permute-start | bytes 152 | tf_op jit(solution)/shard_map/ppermute | solution.py:112
  3.6 7.9 %copy-start = (s32[6,2]{0,1:T(2,128)S(1)}, s32[6,2]{0,1:T(2,128)}, u32[]{:S(2)}) copy-start(s32[6,2]{0,1:T(2,128)} %param.3) | copy-start | bytes 148
  29.8 16.4 %collective-permute-start.3 = (bf16[2,512,128]{2,1,0:T(8,128)(2,1)S(1)}, bf16[2,512,128]{2,1,0:T(8,128)(2,1)S(1)}, u32[]{:S(2)}, u32[]{:S(2)}) collective-permute-start(bf16[2,512,128]{2,1,0:T(8,128)(2,1)S(1)} %pad_maximum_fusion.3), channel_id=1, source_target_pairs={{0,1},{1,2},{2,3},{3,4},{4,5},{5,6},{6,7},{7,8},{8,9},{9,10},{10,1... | collective-permute-start | bytes 786440 | tf_op jit(solution)/shard_map/ppermute | solution.py:122
  33.5 17.9 %collective-permute-start.4 = (bf16[2,512,128]{2,1,0:T(8,128)(2,1)S(1)}, bf16[2,512,128]{2,1,0:T(8,128)(2,1)S(1)}, u32[]{:S(2)}, u32[]{:S(2)}) collective-permute-start(bf16[2,512,128]{2,1,0:T(8,128)(2,1)S(1)} %pad_maximum_fusion.3), channel_id=1, source_target_pairs={{2,0},{3,1},{4,2},{5,3},{6,4},{7,5},{8,6},{9,7},{10,8},{11,9},{12,... | collective-permute-start | bytes 786440 | tf_op jit(solution)/shard_map/ppermute | solution.py:122
  53.6 17.6 %all-to-all-start = ((f32[8,64,3,128]{3,1,2,0:T(8,128)}), f32[8,64,3,128]{3,1,2,0:T(8,128)S(1)}, u32[]{:S(2)}, u32[]{:S(2)}) async-start(f32[8,64,3,128]{3,1,2,0:T(8,128)} %copy.27), calls=%async_computation | async-start | bytes 1572864 | tf_op jit(solution)/shard_map/all_to_all | solution.py:129
  71.2 6.7 %collective-permute-start.5 = (f32[64,3,128]{2,0,1:T(8,128)S(1)}, f32[64,3,128]{2,0,1:T(8,128)S(1)}, u32[]{:S(2)}, u32[]{:S(2)}) collective-permute-start(f32[64,3,128]{2,0,1:T(8,128)S(1)} %reduce_sum.9), channel_id=1, source_target_pairs={{0,7},{1,0},{2,1},{3,2},{4,3},{5,4},{6,5},{7,6},{8,15},{9,8},{10,9... | collective-permute-start | bytes 294920 | tf_op jit(solution)/shard_map/ppermute | solution.py:131
  71.3 9.2 %collective-permute-start.6 = (f32[64,3,128]{2,0,1:T(8,128)S(1)}, f32[64,3,128]{2,0,1:T(8,128)S(1)}, u32[]{:S(2)}, u32[]{:S(2)}) collective-permute-start(f32[64,3,128]{2,0,1:T(8,128)S(1)} %reduce_sum.9), channel_id=1, source_target_pairs={{0,6},{1,7},{2,0},{3,1},{4,2},{5,3},{6,4},{7,5},{8,14},{9,15},{10,... | collective-permute-start | bytes 294920 | tf_op jit(solution)/shard_map/ppermute | solution.py:131
  74.3 7.5 %collective-permute-start.8 = (f32[64,3,128]{2,0,1:T(8,128)S(1)}, f32[64,3,128]{2,0,1:T(8,128)S(1)}, u32[]{:S(2)}, u32[]{:S(2)}) collective-permute-start(f32[64,3,128]{2,0,1:T(8,128)S(1)} %reduce_sum.9), channel_id=1, source_target_pairs={{0,1},{1,2},{2,3},{3,4},{4,5},{5,6},{6,7},{7,0},{8,9},{9,10},{10,1... | collective-permute-start | bytes 294920 | tf_op jit(solution)/shard_map/ppermute | solution.py:131
  74.6 17.8 %collective-permute-start.10 = (f32[64,3,128]{2,0,1:T(8,128)S(1)}, f32[64,3,128]{2,0,1:T(8,128)S(1)}, u32[]{:S(2)}, u32[]{:S(2)}) collective-permute-start(f32[64,3,128]{2,0,1:T(8,128)S(1)} %reduce_sum.9), channel_id=1, source_target_pairs={{0,2},{1,3},{2,4},{3,5},{4,6},{5,7},{6,0},{7,1},{8,10},{9,11},{10,... | collective-permute-start | bytes 294920 | tf_op jit(solution)/shard_map/ppermute | solution.py:131
  80.5 11.9 %collective-permute-start.7 = (f32[2,64,3,128]{3,1,2,0:T(8,128)S(1)}, f32[2,64,3,128]{3,1,2,0:T(8,128)S(1)}, u32[]{:S(2)}, u32[]{:S(2)}) collective-permute-start(f32[2,64,3,128]{3,1,2,0:T(8,128)S(1)} %pad_maximum_fusion.4), channel_id=1, source_target_pairs={{0,6},{1,7},{2,0},{3,1},{4,2},{5,3},{6,4},{7,5},{8,14},{9,15},{10,... | collective-permute-start | bytes 589832 | tf_op jit(solution)/shard_map/ppermute | solution.py:131
  81.8 10.6 %collective-permute-start.9 = (f32[64,3,128]{2,0,1:T(8,128)S(1)}, f32[64,3,128]{2,0,1:T(8,128)S(1)}, u32[]{:S(2)}, u32[]{:S(2)}) collective-permute-start(f32[64,3,128]{2,0,1:T(8,128)S(1)} %collective-permute-done.8), channel_id=1, source_target_pairs={{0,2},{1,3},{2,4},{3,5},{4,6},{5,7},{6,0},{7,1},{8,10},{9,11},{10,... | collective-permute-start | bytes 294920 | tf_op jit(solution)/shard_map/ppermute | solution.py:131
  93.4 11.7 %collective-permute-start.11 = (f32[6,64,128]{2,1,0:T(8,128)S(1)}, f32[6,64,128]{2,1,0:T(8,128)S(1)}, u32[]{:S(2)}, u32[]{:S(2)}) collective-permute-start(f32[6,64,128]{2,1,0:T(8,128)S(1)} %get-tuple-element.17), channel_id=1, source_target_pairs={{0,8},{8,16},{16,24},{24,0},{1,9},{9,17},{17,25},{25,1},{2,10},{10... | collective-permute-start | bytes 589832 | tf_op jit(solution)/shard_map/ppermute | solution.py:154
  96.6 9.3 %collective-permute-start.12 = (f32[6,64,128]{2,1,0:T(8,128)S(1)}, f32[6,64,128]{2,1,0:T(8,128)S(1)}, u32[]{:S(2)}, u32[]{:S(2)}) collective-permute-start(f32[6,64,128]{2,1,0:T(8,128)S(1)} %get-tuple-element.19), channel_id=1, source_target_pairs={{0,16},{8,24},{16,0},{24,8},{1,17},{9,25},{17,1},{25,9},{2,18},{10... | collective-permute-start | bytes 589832 | tf_op jit(solution)/shard_map/ppermute | solution.py:154
  96.8 12.0 %collective-permute-start.13 = (f32[6,64,128]{2,1,0:T(8,128)S(1)}, f32[6,64,128]{2,1,0:T(8,128)S(1)}, u32[]{:S(2)}, u32[]{:S(2)}) collective-permute-start(f32[6,64,128]{2,1,0:T(8,128)S(1)} %get-tuple-element.18), channel_id=1, source_target_pairs={{0,24},{8,0},{16,8},{24,16},{1,25},{9,1},{17,9},{25,17},{2,26},{10... | collective-permute-start | bytes 589832 | tf_op jit(solution)/shard_map/ppermute | solution.py:154

commit v7 on v5

--- a/solution.py
+++ b/solution.py
@@ -63,23 +63,16 @@
     u3, u2 = u[1, :nj], u[1, nj:]
     dre, dim = u1 + u2, u3 - u4
     cre, cim = u1 - u2, -u3 - u4
-    res_re, res_im = [], []
-    f = f0
-    end = f0 + nbins
-    while f < end:
-        j, rr = divmod(f, outer)
-        if rr < half:
-            stop = min(half, rr + (end - f))
-            res_re.append(dre[j, rr:stop])
-            res_im.append(dim[j, rr:stop])
-            f += stop - rr
-        else:
-            s0 = outer * (j + 1) - f
-            s_end = max(0, s0 - (end - f))
-            res_re.append(jnp.flip(cre[j + 1, s_end + 1 : s0 + 1], axis=0))
-            res_im.append(jnp.flip(cim[j + 1, s_end + 1 : s0 + 1], axis=0))
-            f += s0 - s_end
-    return jnp.concatenate(res_re, 0), jnp.concatenate(res_im, 0)
+    f = f0 + lax.broadcasted_iota(jnp.int32, (nbins, nj, half), 0)
+    jj = lax.broadcasted_iota(jnp.int32, (nbins, nj, half), 1)
+    rr = lax.broadcasted_iota(jnp.int32, (nbins, nj, half), 2)
+    direct = (f == outer * jj + rr)
+    conj = (f == outer * jj - rr) & (rr > 0) & (f % outer >= half)
+    pick = jnp.concatenate([direct, conj], axis=1).astype(jnp.float32).reshape(nbins, 2 * nj * half)
+    parts_re = jnp.concatenate([dre, cre], axis=0).reshape(2 * nj * half, channels)
+    parts_im = jnp.concatenate([dim, cim], axis=0).reshape(2 * nj * half, channels)
+    hi = lax.Precision.HIGHEST
+    return jnp.dot(pick, parts_re, precision=hi), jnp.dot(pick, parts_im, precision=hi)
 
 
 def whiten_local(trace, smoother, taper):

time: 105 us -> 104 us (level)
  local copies, waits for them, and re-layouts: 8.27 us -> 2.43 us
  matrix products: 16.1 us -> 19.8 us
    concatenate x4 -> x0, local copies, waits for them, and re-layouts: 5.27 us -> none  [band_dft(): return (jnp.concatenate(res_re, 0), jnp.concatenate(res_im, 0))]
    dot_general x0 -> x2, matrix products: none -> 3.51 us  [the longest x1 1.76 us: band_dft(): jnp.dot(pick, parts_re, precision=hi)]
where the time goes in v7:
time: 104 us; the launch traced here: 103 us
  waiting for transfers between devices  36.6 us (35%)
  starting transfers between devices  31.9 us (31%)
  matrix products  19.8 us (19%)
  other arithmetic  12 us (12%)
  local copies, waits for them, and re-layouts  2.43 us (2%)
    all_to_all x1, waiting for transfers between devices, body(): corr = lax.all_to_all(corr, 'win', 0, 0).sum(axis=0)  12.3 us
    ppermute x2, starting transfers between devices, body(): received[shift] = lax.ppermute(white, ('cx', 'cz'), perm)  11.4 us
    ppermute x6, waiting for transfers between devices, shift_z(): return lax.ppermute(value, 'cz', [(k, (k - step) % nz) for k in range(nz)])  10.9 us
    ppermute x6, starting transfers between devices, shift_z(): return lax.ppermute(value, 'cz', [(k, (k - step) % nz) for k in range(nz)])  10.2 us
    ppermute x3, waiting for transfers between devices, body(): lax.ppermute(chunk, 'cx', [(k, (k + step) % nx) for k in range(nx)])  9.88 us
    dot_general x1, matrix products, band_dft(): jnp.einsum('rb,bac->rac', basis1, xb, precision=prec, preferred_element_t...  7.83 us
    dot_general x1, matrix products, band_dft(): jnp.einsum('ja,srac->sjrc', basis2, jnp.stack([wr, wi]), precision=prec,...  6.09 us
    another operation x2, other arithmetic  5.01 us
  transfers between devices with their start and end apart: 15, of which 8 were waited for; matrix products, arithmetic and copies ran while one was open for 7% of the time, Pallas kernels for 0%

profile of v7, /device:TPU:6, one launch (start us, length us, event | category | flops | bytes accessed | tf_op | source)
XLA Modules:
  0.0 103.2 jit_solution(14371709573873297337)
XLA Ops:
  0.6 7.8 %fusion = f32[126,120,128]{2,0,1:T(8,128)S(1)} fusion(f32[125,120,128]{2,1,0:T(8,128)} %bitcast.87, f32[63,125]{1,0:T(8,128)S(1)} %get-tuple-element.31, f32[63,125]{1,0:T(8,128)S(1)} %get-tuple-element.32), kind=kOutput, calls=%fused_computation.3 | convolution fusion | flops 1451535744 | bytes 15484440 | tf_op jit(solution)/shard_map/rb,bac->rac/dot_general | solution.py:44
  8.4 3.0 %add_bitcast_fusion = (f32[1,63,120,128]{3,1,2,0:T(8,128)S(1)}, f32[1,63,120,128]{3,1,2,0:T(8,128)S(1)}) fusion(f32[126,120,128]{2,0,1:T(8,128)S(1)} %fusion, f32[63,120]{0,1:T(8,128)S(1)} %get-tuple-element.33, f32[63,120]{0,1:T(8,128)S(1)} %get-tuple-element.34), kind=kLoop, calls=%fused_computation.8 | loop fusion | flops 5806080 | bytes 15543360 | tf_op jit(solution)/shard_map/stack | solution.py:59
  11.4 1.5 %pad_maximum_fusion = f32[2,63,120,128]{3,1,2,0:T(8,128)S(1)} fusion(f32[1,63,120,128]{3,1,2,0:T(8,128)S(1)} %get-tuple-element.6, f32[1,63,120,128]{3,1,2,0:T(8,128)S(1)} %get-tuple-element.5), kind=kLoop, calls=%fused_computation.2 | loop fusion | flops 1935360 | bytes 15482880 | tf_op jit(solution)/shard_map/stack | solution.py:59
  12.9 6.1 %fusion.4 = f32[2,12,63,128]{3,1,2,0:T(8,128)S(1)} fusion(f32[2,63,120,128]{3,1,2,0:T(8,128)S(1)} %pad_maximum_fusion, f32[6,120]{1,0:T(8,128)S(1)} %get-tuple-element.35, f32[6,120]{1,0:T(8,128)S(1)} %get-tuple-element.36), kind=kOutput, calls=%fused_computation.13 | convolution fusion | flops 139347360 | bytes 8521344 | tf_op jit(solution)/shard_map/ja,srac->sjrc/dot_general | solution.py:58
  19.4 0.4 add_compare_fusion
  19.8 1.8 %convolution_bitcast_fusion.1 = f32[576,128]{1,0:T(8,128)S(1)} fusion(pred[576,6,63]{0,2,1:T(8,128)(4,1)S(1)} %get-tuple-element.21, pred[576,6,63]{0,2,1:T(8,128)(4,1)S(1)} %get-tuple-element.20, f32[12,63,128]{2,0,1:T(8,128)S(1)} %pad_maximum_fusion.4), kind=kOutput, calls=%fused_computation.19 | convolution fusion | flops 669295872 | bytes 1117440 | tf_op jit(solution)/shard_map/dot_general | solution.py:75
  21.6 1.8 %convolution_bitcast_fusion.2 = f32[576,128]{1,0:T(8,128)S(1)} fusion(pred[576,6,63]{0,2,1:T(8,128)(4,1)S(1)} %get-tuple-element.21, pred[576,6,63]{0,2,1:T(8,128)(4,1)S(1)} %get-tuple-element.20, f32[12,63,128]{2,0,1:T(8,128)S(1)} %pad_maximum_fusion.3), kind=kOutput, calls=%fused_computation.20 | convolution fusion | flops 669295872 | bytes 1117440 | tf_op jit(solution)/shard_map/dot_general | solution.py:75
  23.3 1.7 %fusion.46 = (bf16[512,128]{1,0:T(8,128)(2,1)S(1)}, bf16[512,128]{1,0:T(8,128)(2,1)S(1)}) fusion(f32[576,128]{1,0:T(8,128)S(1)} %convolution_bitcast_fusion.2, f32[576,128]{1,0:T(8,128)S(1)} %convolution_bitcast_fusion.1, s32[512]{0:T(512)S(1)} %get-tuple-element.28, f32[512]{0:T(512)S(1)} %multiply_sine_fusion), kind=kOutput, calls=%fused_computation.67 | convolution fusion | flops 454778880 | bytes 1380352 | tf_op jit(solution)/shard_map/dot_general | solution.py:82
  25.0 3.8 %collective-permute-start.3 = (bf16[2,512,128]{2,1,0:T(8,128)(2,1)S(1)}, bf16[2,512,128]{2,1,0:T(8,128)(2,1)S(1)}, u32[]{:S(2)}, u32[]{:S(2)}) collective-permute-start(bf16[2,512,128]{2,1,0:T(8,128)(2,1)S(1)} %pad_maximum_fusion.5), channel_id=1, source_target_pairs={{0,1},{1,2},{2,3},{3,4},{4,5},{5,6},{6,7},{7,8},{8,9},{9,10},{10,1... | collective-permute-start | bytes 786440 | tf_op jit(solution)/shard_map/ppermute | solution.py:110
  28.9 7.6 %collective-permute-start.4 = (bf16[2,512,128]{2,1,0:T(8,128)(2,1)S(1)}, bf16[2,512,128]{2,1,0:T(8,128)(2,1)S(1)}, u32[]{:S(2)}, u32[]{:S(2)}) collective-permute-start(bf16[2,512,128]{2,1,0:T(8,128)(2,1)S(1)} %pad_maximum_fusion.5), channel_id=1, source_target_pairs={{2,0},{3,1},{4,2},{5,3},{6,4},{7,5},{8,6},{9,7},{10,8},{11,9},{12,... | collective-permute-start | bytes 786440 | tf_op jit(solution)/shard_map/ppermute | solution.py:110
  36.5 2.6 %collective-permute-start.1 = (s32[6,2]{0,1:T(2,128)S(1)}, s32[6,2]{0,1:T(2,128)S(1)}, u32[]{:S(2)}, u32[]{:S(2)}) collective-permute-start(s32[6,2]{0,1:T(2,128)S(1)} %copy-done), channel_id=1, source_target_pairs={{0,16},{8,24},{16,0},{24,8},{1,17},{9,25},{17,1},{25,9},{2,18},{10... | collective-permute-start | bytes 152 | tf_op jit(solution)/shard_map/ppermute | solution.py:132
  39.2 4.7 %cosine_convert_fusion = (bf16[512,1,512]{2,0,1:T(8,128)(2,1)S(1)}, bf16[512,1,512]{2,0,1:T(8,128)(2,1)S(1)}) fusion(s32[512]{0:T(512)S(1)} %get-tuple-element.27, s32[512]{0:T(512)S(1)} %get-tuple-element.28), kind=kLoop, calls=%fused_computation.30 | loop fusion | flops 3145728 | bytes 1052672 | tf_op jit(solution)/shard_map/convert.10
  43.9 3.5 %collective-permute-done.4 = bf16[2,512,128]{2,1,0:T(8,128)(2,1)S(1)} collective-permute-done((bf16[2,512,128]{2,1,0:T(8,128)(2,1)S(1)}, bf16[2,512,128]{2,1,0:T(8,128)(2,1)S(1)}, u32[]{:S(2)}, u32[]{:S(2)}) %collective-permute-start.4) | collective-permute-done | bytes 262176 | tf_op jit(solution)/shard_map/ppermute | solution.py:110
  47.8 0.7 fusion.11
  48.6 1.0 copy.15
  49.5 4.4 %all-to-all-start = ((f32[8,64,3,128]{3,1,2,0:T(8,128)}), f32[8,64,3,128]{3,1,2,0:T(8,128)S(1)}, u32[]{:S(2)}, u32[]{:S(2)}) async-start(f32[8,64,3,128]{3,1,2,0:T(8,128)} %copy.15), calls=%async_computation | async-start | bytes 1572864 | tf_op jit(solution)/shard_map/all_to_all | solution.py:117
  54.1 0.6 gather_fusion
  54.8 12.3 %all-to-all-done = f32[8,64,3,128]{3,1,2,0:T(8,128)S(1)} async-done(((f32[8,64,3,128]{3,1,2,0:T(8,128)}), f32[8,64,3,128]{3,1,2,0:T(8,128)S(1)}, u32[]{:S(2)}, u32[]{:S(2)}) %all-to-all-start) | async-done | bytes 786464 | tf_op jit(solution)/shard_map/all_to_all | solution.py:117
  67.3 2.9 %collective-permute-start.6 = (f32[64,3,128]{2,0,1:T(8,128)S(1)}, f32[64,3,128]{2,0,1:T(8,128)S(1)}, u32[]{:S(2)}, u32[]{:S(2)}) collective-permute-start(f32[64,3,128]{2,0,1:T(8,128)S(1)} %reduce_sum.9), channel_id=1, source_target_pairs={{0,6},{1,7},{2,0},{3,1},{4,2},{5,3},{6,4},{7,5},{8,14},{9,15},{10,... | collective-permute-start | bytes 294920 | tf_op jit(solution)/shard_map/ppermute | solution.py:119
  70.6 1.7 %collective-permute-start.10 = (f32[64,3,128]{2,0,1:T(8,128)S(1)}, f32[64,3,128]{2,0,1:T(8,128)S(1)}, u32[]{:S(2)}, u32[]{:S(2)}) collective-permute-start(f32[64,3,128]{2,0,1:T(8,128)S(1)} %reduce_sum.9), channel_id=1, source_target_pairs={{0,2},{1,3},{2,4},{3,5},{4,6},{5,7},{6,0},{7,1},{8,10},{9,11},{10,... | collective-permute-start | bytes 294920 | tf_op jit(solution)/shard_map/ppermute | solution.py:119
  72.3 1.6 %collective-permute-done.5 = f32[64,3,128]{2,0,1:T(8,128)S(1)} collective-permute-done((f32[64,3,128]{2,0,1:T(8,128)S(1)}, f32[64,3,128]{2,0,1:T(8,128)S(1)}, u32[]{:S(2)}, u32[]{:S(2)}) %collective-permute-start.5) | collective-permute-done | bytes 98336 | tf_op jit(solution)/shard_map/ppermute | solution.py:119
  73.9 2.6 %collective-permute-done.6 = f32[64,3,128]{2,0,1:T(8,128)S(1)} collective-permute-done((f32[64,3,128]{2,0,1:T(8,128)S(1)}, f32[64,3,128]{2,0,1:T(8,128)S(1)}, u32[]{:S(2)}, u32[]{:S(2)}) %collective-permute-start.6) | collective-permute-done | bytes 98336 | tf_op jit(solution)/shard_map/ppermute | solution.py:119
  76.5 1.3 %collective-permute-start.7 = (f32[2,64,3,128]{3,1,2,0:T(8,128)S(1)}, f32[2,64,3,128]{3,1,2,0:T(8,128)S(1)}, u32[]{:S(2)}, u32[]{:S(2)}) collective-permute-start(f32[2,64,3,128]{3,1,2,0:T(8,128)S(1)} %pad_maximum_fusion.6), channel_id=1, source_target_pairs={{0,6},{1,7},{2,0},{3,1},{4,2},{5,3},{6,4},{7,5},{8,14},{9,15},{10,... | collective-permute-start | bytes 589832 | tf_op jit(solution)/shard_map/ppermute | solution.py:119
  77.8 3.9 %collective-permute-start.9 = (f32[64,3,128]{2,0,1:T(8,128)S(1)}, f32[64,3,128]{2,0,1:T(8,128)S(1)}, u32[]{:S(2)}, u32[]{:S(2)}) collective-permute-start(f32[64,3,128]{2,0,1:T(8,128)S(1)} %collective-permute-done.8), channel_id=1, source_target_pairs={{0,2},{1,3},{2,4},{3,5},{4,6},{5,7},{6,0},{7,1},{8,10},{9,11},{10,... | collective-permute-start | bytes 294920 | tf_op jit(solution)/shard_map/ppermute | solution.py:119
  81.6 6.7 %collective-permute-done.7 = f32[2,64,3,128]{3,1,2,0:T(8,128)S(1)} collective-permute-done((f32[2,64,3,128]{3,1,2,0:T(8,128)S(1)}, f32[2,64,3,128]{3,1,2,0:T(8,128)S(1)}, u32[]{:S(2)}, u32[]{:S(2)}) %collective-permute-start.7) | collective-permute-done | bytes 196640 | tf_op jit(solution)/shard_map/ppermute | solution.py:119
  88.5 0.7 gather_fusion.1
  89.3 0.9 collective-permute-start.11
  90.2 2.3 %collective-permute-start.12 = (f32[6,64,128]{2,1,0:T(8,128)S(1)}, f32[6,64,128]{2,1,0:T(8,128)S(1)}, u32[]{:S(2)}, u32[]{:S(2)}) collective-permute-start(f32[6,64,128]{2,1,0:T(8,128)S(1)} %get-tuple-element.15), channel_id=1, source_target_pairs={{0,16},{8,24},{16,0},{24,8},{1,17},{9,25},{17,1},{25,9},{2,18},{10... | collective-permute-start | bytes 589832 | tf_op jit(solution)/shard_map/ppermute | solution.py:147
  92.5 4.6 %collective-permute-done.11 = f32[6,64,128]{2,1,0:T(8,128)S(1)} collective-permute-done((f32[6,64,128]{2,1,0:T(8,128)S(1)}, f32[6,64,128]{2,1,0:T(8,128)S(1)}, u32[]{:S(2)}, u32[]{:S(2)}) %collective-permute-start.11) | collective-permute-done | bytes 196640 | tf_op jit(solution)/shard_map/ppermute | solution.py:147
  97.2 2.4 %collective-permute-done.12 = f32[6,64,128]{2,1,0:T(8,128)S(1)} collective-permute-done((f32[6,64,128]{2,1,0:T(8,128)S(1)}, f32[6,64,128]{2,1,0:T(8,128)S(1)}, u32[]{:S(2)}, u32[]{:S(2)}) %collective-permute-start.12) | collective-permute-done | bytes 196640 | tf_op jit(solution)/shard_map/ppermute | solution.py:147
  99.6 2.9 %collective-permute-done.13 = f32[6,64,128]{2,1,0:T(8,128)S(1)} collective-permute-done((f32[6,64,128]{2,1,0:T(8,128)S(1)}, f32[6,64,128]{2,1,0:T(8,128)S(1)}, u32[]{:S(2)}, u32[]{:S(2)}) %collective-permute-start.13) | collective-permute-done | bytes 196640 | tf_op jit(solution)/shard_map/ppermute | solution.py:147
  102.4 0.8 fusion.50
  (49 shorter events, 2.3 us)
Async XLA Ops:
  19.4 17.1 %copy-start = (s32[6,2]{0,1:T(2,128)S(1)}, s32[6,2]{0,1:T(2,128)}, u32[]{:S(2)}) copy-start(s32[6,2]{0,1:T(2,128)} %param.3) | copy-start | bytes 148
  25.0 18.8 %collective-permute-start.3 = (bf16[2,512,128]{2,1,0:T(8,128)(2,1)S(1)}, bf16[2,512,128]{2,1,0:T(8,128)(2,1)S(1)}, u32[]{:S(2)}, u32[]{:S(2)}) collective-permute-start(bf16[2,512,128]{2,1,0:T(8,128)(2,1)S(1)} %pad_maximum_fusion.5), channel_id=1, source_target_pairs={{0,1},{1,2},{2,3},{3,4},{4,5},{5,6},{6,7},{7,8},{8,9},{9,10},{10,1... | collective-permute-start | bytes 786440 | tf_op jit(solution)/shard_map/ppermute | solution.py:110
  28.9 18.5 %collective-permute-start.4 = (bf16[2,512,128]{2,1,0:T(8,128)(2,1)S(1)}, bf16[2,512,128]{2,1,0:T(8,128)(2,1)S(1)}, u32[]{:S(2)}, u32[]{:S(2)}) collective-permute-start(bf16[2,512,128]{2,1,0:T(8,128)(2,1)S(1)} %pad_maximum_fusion.5), channel_id=1, source_target_pairs={{2,0},{3,1},{4,2},{5,3},{6,4},{7,5},{8,6},{9,7},{10,8},{11,9},{12,... | collective-permute-start | bytes 786440 | tf_op jit(solution)/shard_map/ppermute | solution.py:110
  36.4 17.6 %collective-permute-start = (s32[6,2]{0,1:T(2,128)S(1)}, s32[6,2]{0,1:T(2,128)S(1)}, u32[]{:S(2)}, u32[]{:S(2)}) collective-permute-start(s32[6,2]{0,1:T(2,128)S(1)} %copy-done), channel_id=1, source_target_pairs={{0,8},{8,16},{16,24},{24,0},{1,9},{9,17},{17,25},{25,1},{2,10},{10... | collective-permute-start | bytes 152 | tf_op jit(solution)/shard_map/ppermute | solution.py:132
  36.5 17.5 %collective-permute-start.1 = (s32[6,2]{0,1:T(2,128)S(1)}, s32[6,2]{0,1:T(2,128)S(1)}, u32[]{:S(2)}, u32[]{:S(2)}) collective-permute-start(s32[6,2]{0,1:T(2,128)S(1)} %copy-done), channel_id=1, source_target_pairs={{0,16},{8,24},{16,0},{24,8},{1,17},{9,25},{17,1},{25,9},{2,18},{10... | collective-permute-start | bytes 152 | tf_op jit(solution)/shard_map/ppermute | solution.py:132
  39.1 14.9 %collective-permute-start.2 = (s32[6,2]{0,1:T(2,128)S(1)}, s32[6,2]{0,1:T(2,128)S(1)}, u32[]{:S(2)}, u32[]{:S(2)}) collective-permute-start(s32[6,2]{0,1:T(2,128)S(1)} %copy-done), channel_id=1, source_target_pairs={{0,24},{8,0},{16,8},{24,16},{1,25},{9,1},{17,9},{25,17},{2,26},{10... | collective-permute-start | bytes 152 | tf_op jit(solution)/shard_map/ppermute | solution.py:132
  49.5 17.6 %all-to-all-start = ((f32[8,64,3,128]{3,1,2,0:T(8,128)}), f32[8,64,3,128]{3,1,2,0:T(8,128)S(1)}, u32[]{:S(2)}, u32[]{:S(2)}) async-start(f32[8,64,3,128]{3,1,2,0:T(8,128)} %copy.15), calls=%async_computation | async-start | bytes 1572864 | tf_op jit(solution)/shard_map/all_to_all | solution.py:117
  67.2 6.7 %collective-permute-start.5 = (f32[64,3,128]{2,0,1:T(8,128)S(1)}, f32[64,3,128]{2,0,1:T(8,128)S(1)}, u32[]{:S(2)}, u32[]{:S(2)}) collective-permute-start(f32[64,3,128]{2,0,1:T(8,128)S(1)} %reduce_sum.9), channel_id=1, source_target_pairs={{0,7},{1,0},{2,1},{3,2},{4,3},{5,4},{6,5},{7,6},{8,15},{9,8},{10,9... | collective-permute-start | bytes 294920 | tf_op jit(solution)/shard_map/ppermute | solution.py:119
  67.3 9.2 %collective-permute-start.6 = (f32[64,3,128]{2,0,1:T(8,128)S(1)}, f32[64,3,128]{2,0,1:T(8,128)S(1)}, u32[]{:S(2)}, u32[]{:S(2)}) collective-permute-start(f32[64,3,128]{2,0,1:T(8,128)S(1)} %reduce_sum.9), channel_id=1, source_target_pairs={{0,6},{1,7},{2,0},{3,1},{4,2},{5,3},{6,4},{7,5},{8,14},{9,15},{10,... | collective-permute-start | bytes 294920 | tf_op jit(solution)/shard_map/ppermute | solution.py:119
  70.2 7.5 %collective-permute-start.8 = (f32[64,3,128]{2,0,1:T(8,128)S(1)}, f32[64,3,128]{2,0,1:T(8,128)S(1)}, u32[]{:S(2)}, u32[]{:S(2)}) collective-permute-start(f32[64,3,128]{2,0,1:T(8,128)S(1)} %reduce_sum.9), channel_id=1, source_target_pairs={{0,1},{1,2},{2,3},{3,4},{4,5},{5,6},{6,7},{7,0},{8,9},{9,10},{10,1... | collective-permute-start | bytes 294920 | tf_op jit(solution)/shard_map/ppermute | solution.py:119
  70.6 17.9 %collective-permute-start.10 = (f32[64,3,128]{2,0,1:T(8,128)S(1)}, f32[64,3,128]{2,0,1:T(8,128)S(1)}, u32[]{:S(2)}, u32[]{:S(2)}) collective-permute-start(f32[64,3,128]{2,0,1:T(8,128)S(1)} %reduce_sum.9), channel_id=1, source_target_pairs={{0,2},{1,3},{2,4},{3,5},{4,6},{5,7},{6,0},{7,1},{8,10},{9,11},{10,... | collective-permute-start | bytes 294920 | tf_op jit(solution)/shard_map/ppermute | solution.py:119
  76.5 11.9 %collective-permute-start.7 = (f32[2,64,3,128]{3,1,2,0:T(8,128)S(1)}, f32[2,64,3,128]{3,1,2,0:T(8,128)S(1)}, u32[]{:S(2)}, u32[]{:S(2)}) collective-permute-start(f32[2,64,3,128]{3,1,2,0:T(8,128)S(1)} %pad_maximum_fusion.6), channel_id=1, source_target_pairs={{0,6},{1,7},{2,0},{3,1},{4,2},{5,3},{6,4},{7,5},{8,14},{9,15},{10,... | collective-permute-start | bytes 589832 | tf_op jit(solution)/shard_map/ppermute | solution.py:119
  77.8 10.6 %collective-permute-start.9 = (f32[64,3,128]{2,0,1:T(8,128)S(1)}, f32[64,3,128]{2,0,1:T(8,128)S(1)}, u32[]{:S(2)}, u32[]{:S(2)}) collective-permute-start(f32[64,3,128]{2,0,1:T(8,128)S(1)} %collective-permute-done.8), channel_id=1, source_target_pairs={{0,2},{1,3},{2,4},{3,5},{4,6},{5,7},{6,0},{7,1},{8,10},{9,11},{10,... | collective-permute-start | bytes 294920 | tf_op jit(solution)/shard_map/ppermute | solution.py:119
  89.3 7.8 %collective-permute-start.11 = (f32[6,64,128]{2,1,0:T(8,128)S(1)}, f32[6,64,128]{2,1,0:T(8,128)S(1)}, u32[]{:S(2)}, u32[]{:S(2)}) collective-permute-start(f32[6,64,128]{2,1,0:T(8,128)S(1)} %get-tuple-element.13), channel_id=1, source_target_pairs={{0,8},{8,16},{16,24},{24,0},{1,9},{9,17},{17,25},{25,1},{2,10},{10... | collective-permute-start | bytes 589832 | tf_op jit(solution)/shard_map/ppermute | solution.py:147
  90.2 9.3 %collective-permute-start.12 = (f32[6,64,128]{2,1,0:T(8,128)S(1)}, f32[6,64,128]{2,1,0:T(8,128)S(1)}, u32[]{:S(2)}, u32[]{:S(2)}) collective-permute-start(f32[6,64,128]{2,1,0:T(8,128)S(1)} %get-tuple-element.15), channel_id=1, source_target_pairs={{0,16},{8,24},{16,0},{24,8},{1,17},{9,25},{17,1},{25,9},{2,18},{10... | collective-permute-start | bytes 589832 | tf_op jit(solution)/shard_map/ppermute | solution.py:147
  92.5 9.9 %collective-permute-start.13 = (f32[6,64,128]{2,1,0:T(8,128)S(1)}, f32[6,64,128]{2,1,0:T(8,128)S(1)}, u32[]{:S(2)}, u32[]{:S(2)}) collective-permute-start(f32[6,64,128]{2,1,0:T(8,128)S(1)} %get-tuple-element.14), channel_id=1, source_target_pairs={{0,24},{8,0},{16,8},{24,16},{1,25},{9,1},{17,9},{25,17},{2,26},{10... | collective-permute-start | bytes 589832 | tf_op jit(solution)/shard_map/ppermute | solution.py:147

commit v8 on v7

--- a/solution.py
+++ b/solution.py
@@ -108,13 +108,16 @@
     for shift in (-1, 2):
         perm = [(k + shift, k) for k in range(blocks) if 0 <= k + shift < blocks]
         received[shift] = lax.ppermute(white, ("cx", "cz"), perm)
-    left = jnp.stack([received[-1], white, received[-1]])
-    right = jnp.stack([white, received[2], received[2]])
-    cross = cross_spectra(left, right)
-    corr = jnp.einsum("tqb,dqbk->tdk", table, cross, preferred_element_type=jnp.float32) * factor
-    lags = corr.shape[0] // nwin
-    corr = corr.reshape((nwin, lags) + corr.shape[1:])
-    corr = lax.all_to_all(corr, "win", 0, 0).sum(axis=0)
+    first = cross_spectra(received[-1][None], white[None])
+    rest = cross_spectra(jnp.stack([white, received[-1]]), jnp.stack([received[2], received[2]]))
+    lags = LAGS // nwin
+
+    def window_sum(cross):
+        corr = jnp.einsum("tqb,dqbk->tdk", table, cross, preferred_element_type=jnp.float32) * factor
+        corr = corr.reshape((nwin, lags) + corr.shape[1:])
+        return lax.all_to_all(corr, "win", 0, 0).sum(axis=0)
+
+    corr = jnp.concatenate([window_sum(first), window_sum(rest)], axis=1)
     def shift_z(value, step):
         return lax.ppermute(value, "cz", [(k, (k - step) % nz) for k in range(nz)])
 

time: 104 us -> 107 us (1.029)
  starting transfers between devices: 31.9 us -> 35.5 us
    all_to_all x1 -> x2, starting transfers between devices: 4.45 us -> 7.94 us  [window_sum(): return lax.all_to_all(corr, 'win', 0, 0).sum(axis=0)]
    ppermute x2, waiting for transfers between devices: 3.49 us -> 0.01 us  [body(): received[shift] = lax.ppermute(white, ('cx', 'cz'), perm)]
    all_to_all x1 -> x2, waiting for transfers between devices: 12.3 us -> 15.4 us  [window_sum(): return lax.all_to_all(corr, 'win', 0, 0).sum(axis=0)]
    ppermute x3, starting transfers between devices: 3.18 us -> 4.94 us  [body(): lax.ppermute(chunk, 'cx', [(k, (k + step) % nx) for k in range(nx)])]
    ppermute x6, starting transfers between devices: 10.2 us -> 8.5 us  [shift_z(): return lax.ppermute(value, 'cz', [(k, (k - step) % nz) for k in range(nz)])]
    another operation x3 -> x4, other arithmetic: 5.18 us -> 5.07 us
  transfers between devices with their start and end apart: 15 -> 16, of which waited for: 8 -> 9; matrix products, arithmetic and copies ran while one was open for 7% -> 8% of each run, Pallas kernels for 0% -> 0%
where the time goes in v8:
time: 107 us; the launch traced here: 106 us
  waiting for transfers between devices  35.6 us (33%)
  starting transfers between devices  35.5 us (33%)
  matrix products  20.7 us (19%)
  other arithmetic  11.9 us (11%)
  local copies, waits for them, and re-layouts  2.31 us (2%)
    all_to_all x2, waiting for transfers between devices, window_sum(): return lax.all_to_all(corr, 'win', 0, 0).sum(axis=0)  15.4 us
    ppermute x2, starting transfers between devices, body(): received[shift] = lax.ppermute(white, ('cx', 'cz'), perm)  11.4 us
    ppermute x3, waiting for transfers between devices, body(): lax.ppermute(chunk, 'cx', [(k, (k + step) % nx) for k in range(nx)])  10.1 us
    ppermute x6, waiting for transfers between devices, shift_z(): return lax.ppermute(value, 'cz', [(k, (k - step) % nz) for k in range(nz)])  10.1 us
    ppermute x6, starting transfers between devices, shift_z(): return lax.ppermute(value, 'cz', [(k, (k - step) % nz) for k in range(nz)])  8.5 us
    all_to_all x2, starting transfers between devices, window_sum(): return lax.all_to_all(corr, 'win', 0, 0).sum(axis=0)  7.94 us
    dot_general x1, matrix products, band_dft(): jnp.einsum('rb,bac->rac', basis1, xb, precision=prec, preferred_element_t...  7.83 us
    dot_general x1, matrix products, band_dft(): jnp.einsum('ja,srac->sjrc', basis2, jnp.stack([wr, wi]), precision=prec,...  6.09 us
  transfers between devices with their start and end apart: 16, of which 9 were waited for; matrix products, arithmetic and copies ran while one was open for 8% of the time, Pallas kernels for 0%

profile of v8, /device:TPU:6, one launch (start us, length us, event | category | flops | bytes accessed | tf_op | source)
XLA Modules:
  0.0 106.5 jit_solution(4910152821372806100)
XLA Ops:
  0.6 7.8 %fusion = f32[126,120,128]{2,0,1:T(8,128)S(1)} fusion(f32[125,120,128]{2,1,0:T(8,128)} %bitcast.103, f32[63,125]{1,0:T(8,128)S(1)} %get-tuple-element.31, f32[63,125]{1,0:T(8,128)S(1)} %get-tuple-element.32), kind=kOutput, calls=%fused_computation.3 | convolution fusion | flops 1451535744 | bytes 15484440 | tf_op jit(solution)/shard_map/rb,bac->rac/dot_general | solution.py:44
  8.4 3.0 %add_bitcast_fusion = (f32[1,63,120,128]{3,1,2,0:T(8,128)S(1)}, f32[1,63,120,128]{3,1,2,0:T(8,128)S(1)}) fusion(f32[126,120,128]{2,0,1:T(8,128)S(1)} %fusion, f32[63,120]{0,1:T(8,128)S(1)} %get-tuple-element.33, f32[63,120]{0,1:T(8,128)S(1)} %get-tuple-element.34), kind=kLoop, calls=%fused_computation.8 | loop fusion | flops 5806080 | bytes 15543360 | tf_op jit(solution)/shard_map/stack | solution.py:59
  11.4 1.5 %pad_maximum_fusion = f32[2,63,120,128]{3,1,2,0:T(8,128)S(1)} fusion(f32[1,63,120,128]{3,1,2,0:T(8,128)S(1)} %get-tuple-element.6, f32[1,63,120,128]{3,1,2,0:T(8,128)S(1)} %get-tuple-element.5), kind=kLoop, calls=%fused_computation.2 | loop fusion | flops 1935360 | bytes 15482880 | tf_op jit(solution)/shard_map/stack | solution.py:59
  12.9 6.1 %fusion.4 = f32[2,12,63,128]{3,1,2,0:T(8,128)S(1)} fusion(f32[2,63,120,128]{3,1,2,0:T(8,128)S(1)} %pad_maximum_fusion, f32[6,120]{1,0:T(8,128)S(1)} %get-tuple-element.35, f32[6,120]{1,0:T(8,128)S(1)} %get-tuple-element.36), kind=kOutput, calls=%fused_computation.13 | convolution fusion | flops 139347360 | bytes 8521344 | tf_op jit(solution)/shard_map/ja,srac->sjrc/dot_general | solution.py:58
  19.8 1.8 %convolution_bitcast_fusion.1 = f32[576,128]{1,0:T(8,128)S(1)} fusion(pred[576,6,63]{0,2,1:T(8,128)(4,1)S(1)} %get-tuple-element.21, pred[576,6,63]{0,2,1:T(8,128)(4,1)S(1)} %get-tuple-element.20, f32[12,63,128]{2,0,1:T(8,128)S(1)} %pad_maximum_fusion.6), kind=kOutput, calls=%fused_computation.19 | convolution fusion | flops 669295872 | bytes 1117440 | tf_op jit(solution)/shard_map/dot_general | solution.py:75
  21.6 1.8 %convolution_bitcast_fusion.2 = f32[576,128]{1,0:T(8,128)S(1)} fusion(pred[576,6,63]{0,2,1:T(8,128)(4,1)S(1)} %get-tuple-element.21, pred[576,6,63]{0,2,1:T(8,128)(4,1)S(1)} %get-tuple-element.20, f32[12,63,128]{2,0,1:T(8,128)S(1)} %pad_maximum_fusion.5), kind=kOutput, calls=%fused_computation.20 | convolution fusion | flops 669295872 | bytes 1117440 | tf_op jit(solution)/shard_map/dot_general | solution.py:75
  23.3 1.7 %fusion.51 = (bf16[512,128]{1,0:T(8,128)(2,1)S(1)}, bf16[512,128]{1,0:T(8,128)(2,1)S(1)}) fusion(f32[576,128]{1,0:T(8,128)S(1)} %convolution_bitcast_fusion.2, f32[576,128]{1,0:T(8,128)S(1)} %convolution_bitcast_fusion.1, s32[512]{0:T(512)S(1)} %get-tuple-element.28, f32[512]{0:T(512)S(1)} %multiply_sine_fusion), kind=kOutput, calls=%fused_computation.79 | convolution fusion | flops 454778880 | bytes 1380352 | tf_op jit(solution)/shard_map/dot_general | solution.py:82
  25.0 3.8 %collective-permute-start.3 = (bf16[2,512,128]{2,1,0:T(8,128)(2,1)S(1)}, bf16[2,512,128]{2,1,0:T(8,128)(2,1)S(1)}, u32[]{:S(2)}, u32[]{:S(2)}) collective-permute-start(bf16[2,512,128]{2,1,0:T(8,128)(2,1)S(1)} %pad_maximum_fusion.8), channel_id=1, source_target_pairs={{0,1},{1,2},{2,3},{3,4},{4,5},{5,6},{6,7},{7,8},{8,9},{9,10},{10,1... | collective-permute-start | bytes 786440 | tf_op jit(solution)/shard_map/ppermute | solution.py:110
  28.9 7.6 %collective-permute-start.4 = (bf16[2,512,128]{2,1,0:T(8,128)(2,1)S(1)}, bf16[2,512,128]{2,1,0:T(8,128)(2,1)S(1)}, u32[]{:S(2)}, u32[]{:S(2)}) collective-permute-start(bf16[2,512,128]{2,1,0:T(8,128)(2,1)S(1)} %pad_maximum_fusion.8), channel_id=1, source_target_pairs={{2,0},{3,1},{4,2},{5,3},{6,4},{7,5},{8,6},{9,7},{10,8},{11,9},{12,... | collective-permute-start | bytes 786440 | tf_op jit(solution)/shard_map/ppermute | solution.py:110
  36.6 2.6 %collective-permute-start.1 = (s32[6,2]{0,1:T(2,128)S(1)}, s32[6,2]{0,1:T(2,128)S(1)}, u32[]{:S(2)}, u32[]{:S(2)}) collective-permute-start(s32[6,2]{0,1:T(2,128)S(1)} %copy-done), channel_id=1, source_target_pairs={{0,16},{8,24},{16,0},{24,8},{1,17},{9,25},{17,1},{25,9},{2,18},{10... | collective-permute-start | bytes 152 | tf_op jit(solution)/shard_map/ppermute | solution.py:135
  39.2 4.7 %cosine_convert_fusion = (bf16[512,1,512]{2,0,1:T(8,128)(2,1)S(1)}, bf16[512,1,512]{2,0,1:T(8,128)(2,1)S(1)}) fusion(s32[512]{0:T(512)S(1)} %get-tuple-element.27, s32[512]{0:T(512)S(1)} %get-tuple-element.28), kind=kLoop, calls=%fused_computation.31 | loop fusion | flops 3145728 | bytes 1052672 | tf_op jit(solution)/shard_map/convert.14
  44.1 1.1 %fusion.12 = f32[512,128]{1,0:T(8,128)} fusion(bf16[512,1,512]{2,0,1:T(8,128)(2,1)S(1)} %get-tuple-element.26, bf16[512,1,512]{2,0,1:T(8,128)(2,1)S(1)} %get-tuple-element.25, bf16[1,512,128]{2,1,0:T(8,128)(2,1)S(1)} %get-tuple-element.17, bf16[1,512,128]{2,1,0:T(8,128)(2,1)S(1)} %get-tuple-element.16), kind=kOutput, calls=%fused_computation.22 | convolution fusion | flops 134938624 | bytes 1572864 | tf_op jit(solution)/shard_map/tqb,dqbk->tdk/dot_general | solution.py:116
  45.2 4.4 %all-to-all-start = ((f32[8,64,1,128]{3,1,2,0:T(8,128)}), f32[8,64,1,128]{3,1,2,0:T(8,128)S(1)}, u32[]{:S(2)}, u32[]{:S(2)}) async-start(f32[8,64,1,128]{3,1,2,0:T(8,128)} %bitcast.30), calls=%async_computation | async-start | bytes 524288 | tf_op jit(solution)/shard_map/all_to_all | solution.py:118
  50.4 0.9 copy.17
  51.2 6.0 %all-to-all-done = f32[8,64,1,128]{3,1,2,0:T(8,128)S(1)} async-done(((f32[8,64,1,128]{3,1,2,0:T(8,128)}), f32[8,64,1,128]{3,1,2,0:T(8,128)S(1)}, u32[]{:S(2)}, u32[]{:S(2)}) %all-to-all-start) | async-done | bytes 262176 | tf_op jit(solution)/shard_map/all_to_all | solution.py:118
  57.2 3.5 %all-to-all-start.1 = ((f32[8,64,2,128]{3,1,2,0:T(8,128)}), f32[8,64,2,128]{3,1,2,0:T(8,128)S(1)}, u32[]{:S(2)}, u32[]{:S(2)}) async-start(f32[8,64,2,128]{3,1,2,0:T(8,128)} %copy.17), calls=%async_computation.1 | async-start | bytes 1048576 | tf_op jit(solution)/shard_map/all_to_all | solution.py:118
  60.7 0.6 gather_fusion
  61.5 9.5 %all-to-all-done.1 = f32[8,64,2,128]{3,1,2,0:T(8,128)S(1)} async-done(((f32[8,64,2,128]{3,1,2,0:T(8,128)}), f32[8,64,2,128]{3,1,2,0:T(8,128)S(1)}, u32[]{:S(2)}, u32[]{:S(2)}) %all-to-all-start.1) | async-done | bytes 524320 | tf_op jit(solution)/shard_map/all_to_all | solution.py:118
  71.0 1.1 %collective-permute-start.5 = (f32[64,3,128]{2,0,1:T(8,128)S(1)}, f32[64,3,128]{2,0,1:T(8,128)S(1)}, u32[]{:S(2)}, u32[]{:S(2)}) collective-permute-start(f32[64,3,128]{2,0,1:T(8,128)S(1)} %pad_maximum_fusion.10), channel_id=1, source_target_pairs={{0,7},{1,0},{2,1},{3,2},{4,3},{5,4},{6,5},{7,6},{8,15},{9,8},{10,9... | collective-permute-start | bytes 294920 | tf_op jit(solution)/shard_map/ppermute | solution.py:122
  72.1 2.7 %collective-permute-start.6 = (f32[64,3,128]{2,0,1:T(8,128)S(1)}, f32[64,3,128]{2,0,1:T(8,128)S(1)}, u32[]{:S(2)}, u32[]{:S(2)}) collective-permute-start(f32[64,3,128]{2,0,1:T(8,128)S(1)} %pad_maximum_fusion.10), channel_id=1, source_target_pairs={{0,6},{1,7},{2,0},{3,1},{4,2},{5,3},{6,4},{7,5},{8,14},{9,15},{10,... | collective-permute-start | bytes 294920 | tf_op jit(solution)/shard_map/ppermute | solution.py:122
  74.8 1.2 %collective-permute-start.10 = (f32[64,3,128]{2,0,1:T(8,128)S(1)}, f32[64,3,128]{2,0,1:T(8,128)S(1)}, u32[]{:S(2)}, u32[]{:S(2)}) collective-permute-start(f32[64,3,128]{2,0,1:T(8,128)S(1)} %pad_maximum_fusion.10), channel_id=1, source_target_pairs={{0,2},{1,3},{2,4},{3,5},{4,6},{5,7},{6,0},{7,1},{8,10},{9,11},{10,... | collective-permute-start | bytes 294920 | tf_op jit(solution)/shard_map/ppermute | solution.py:122
  76.1 1.5 %collective-permute-done.5 = f32[64,3,128]{2,0,1:T(8,128)S(1)} collective-permute-done((f32[64,3,128]{2,0,1:T(8,128)S(1)}, f32[64,3,128]{2,0,1:T(8,128)S(1)}, u32[]{:S(2)}, u32[]{:S(2)}) %collective-permute-start.5) | collective-permute-done | bytes 98336 | tf_op jit(solution)/shard_map/ppermute | solution.py:122
  77.6 1.8 %collective-permute-done.6 = f32[64,3,128]{2,0,1:T(8,128)S(1)} collective-permute-done((f32[64,3,128]{2,0,1:T(8,128)S(1)}, f32[64,3,128]{2,0,1:T(8,128)S(1)}, u32[]{:S(2)}, u32[]{:S(2)}) %collective-permute-start.6) | collective-permute-done | bytes 98336 | tf_op jit(solution)/shard_map/ppermute | solution.py:122
  79.4 3.4 %collective-permute-start.7 = (f32[2,64,3,128]{3,1,2,0:T(8,128)S(1)}, f32[2,64,3,128]{3,1,2,0:T(8,128)S(1)}, u32[]{:S(2)}, u32[]{:S(2)}) collective-permute-start(f32[2,64,3,128]{3,1,2,0:T(8,128)S(1)} %pad_maximum_fusion.9), channel_id=1, source_target_pairs={{0,6},{1,7},{2,0},{3,1},{4,2},{5,3},{6,4},{7,5},{8,14},{9,15},{10,... | collective-permute-start | bytes 589832 | tf_op jit(solution)/shard_map/ppermute | solution.py:122
  82.9 6.7 %collective-permute-done.7 = f32[2,64,3,128]{3,1,2,0:T(8,128)S(1)} collective-permute-done((f32[2,64,3,128]{3,1,2,0:T(8,128)S(1)}, f32[2,64,3,128]{3,1,2,0:T(8,128)S(1)}, u32[]{:S(2)}, u32[]{:S(2)}) %collective-permute-start.7) | collective-permute-done | bytes 196640 | tf_op jit(solution)/shard_map/ppermute | solution.py:122
  89.8 0.7 gather_fusion.1
  90.6 3.3 %collective-permute-start.11 = (f32[6,64,128]{2,1,0:T(8,128)S(1)}, f32[6,64,128]{2,1,0:T(8,128)S(1)}, u32[]{:S(2)}, u32[]{:S(2)}) collective-permute-start(f32[6,64,128]{2,1,0:T(8,128)S(1)} %get-tuple-element.11), channel_id=1, source_target_pairs={{0,8},{8,16},{16,24},{24,0},{1,9},{9,17},{17,25},{25,1},{2,10},{10... | collective-permute-start | bytes 589832 | tf_op jit(solution)/shard_map/ppermute | solution.py:150
  94.3 1.3 %collective-permute-start.13 = (f32[6,64,128]{2,1,0:T(8,128)S(1)}, f32[6,64,128]{2,1,0:T(8,128)S(1)}, u32[]{:S(2)}, u32[]{:S(2)}) collective-permute-start(f32[6,64,128]{2,1,0:T(8,128)S(1)} %get-tuple-element.12), channel_id=1, source_target_pairs={{0,24},{8,0},{16,8},{24,16},{1,25},{9,1},{17,9},{25,17},{2,26},{10... | collective-permute-start | bytes 589832 | tf_op jit(solution)/shard_map/ppermute | solution.py:150
  95.6 6.7 %collective-permute-done.11 = f32[6,64,128]{2,1,0:T(8,128)S(1)} collective-permute-done((f32[6,64,128]{2,1,0:T(8,128)S(1)}, f32[6,64,128]{2,1,0:T(8,128)S(1)}, u32[]{:S(2)}, u32[]{:S(2)}) %collective-permute-start.11) | collective-permute-done | bytes 196640 | tf_op jit(solution)/shard_map/ppermute | solution.py:150
  102.3 1.0 collective-permute-done.12
  103.3 2.4 %collective-permute-done.13 = f32[6,64,128]{2,1,0:T(8,128)S(1)} collective-permute-done((f32[6,64,128]{2,1,0:T(8,128)S(1)}, f32[6,64,128]{2,1,0:T(8,128)S(1)}, u32[]{:S(2)}, u32[]{:S(2)}) %collective-permute-start.13) | collective-permute-done | bytes 196640 | tf_op jit(solution)/shard_map/ppermute | solution.py:150
  105.7 0.8 fusion.58
  (55 shorter events, 3.2 us)
Async XLA Ops:
  19.4 17.1 %copy-start = (s32[6,2]{0,1:T(2,128)S(1)}, s32[6,2]{0,1:T(2,128)}, u32[]{:S(2)}) copy-start(s32[6,2]{0,1:T(2,128)} %param.3) | copy-start | bytes 148
  25.0 18.9 %collective-permute-start.3 = (bf16[2,512,128]{2,1,0:T(8,128)(2,1)S(1)}, bf16[2,512,128]{2,1,0:T(8,128)(2,1)S(1)}, u32[]{:S(2)}, u32[]{:S(2)}) collective-permute-start(bf16[2,512,128]{2,1,0:T(8,128)(2,1)S(1)} %pad_maximum_fusion.8), channel_id=1, source_target_pairs={{0,1},{1,2},{2,3},{3,4},{4,5},{5,6},{6,7},{7,8},{8,9},{9,10},{10,1... | collective-permute-start | bytes 786440 | tf_op jit(solution)/shard_map/ppermute | solution.py:110
  28.9 20.9 %collective-permute-start.4 = (bf16[2,512,128]{2,1,0:T(8,128)(2,1)S(1)}, bf16[2,512,128]{2,1,0:T(8,128)(2,1)S(1)}, u32[]{:S(2)}, u32[]{:S(2)}) collective-permute-start(bf16[2,512,128]{2,1,0:T(8,128)(2,1)S(1)} %pad_maximum_fusion.8), channel_id=1, source_target_pairs={{2,0},{3,1},{4,2},{5,3},{6,4},{7,5},{8,6},{9,7},{10,8},{11,9},{12,... | collective-permute-start | bytes 786440 | tf_op jit(solution)/shard_map/ppermute | solution.py:110
  36.5 24.2 %collective-permute-start = (s32[6,2]{0,1:T(2,128)S(1)}, s32[6,2]{0,1:T(2,128)S(1)}, u32[]{:S(2)}, u32[]{:S(2)}) collective-permute-start(s32[6,2]{0,1:T(2,128)S(1)} %copy-done), channel_id=1, source_target_pairs={{0,8},{8,16},{16,24},{24,0},{1,9},{9,17},{17,25},{25,1},{2,10},{10... | collective-permute-start | bytes 152 | tf_op jit(solution)/shard_map/ppermute | solution.py:135
  36.6 24.2 %collective-permute-start.1 = (s32[6,2]{0,1:T(2,128)S(1)}, s32[6,2]{0,1:T(2,128)S(1)}, u32[]{:S(2)}, u32[]{:S(2)}) collective-permute-start(s32[6,2]{0,1:T(2,128)S(1)} %copy-done), channel_id=1, source_target_pairs={{0,16},{8,24},{16,0},{24,8},{1,17},{9,25},{17,1},{25,9},{2,18},{10... | collective-permute-start | bytes 152 | tf_op jit(solution)/shard_map/ppermute | solution.py:135
  39.2 21.6 %collective-permute-start.2 = (s32[6,2]{0,1:T(2,128)S(1)}, s32[6,2]{0,1:T(2,128)S(1)}, u32[]{:S(2)}, u32[]{:S(2)}) collective-permute-start(s32[6,2]{0,1:T(2,128)S(1)} %copy-done), channel_id=1, source_target_pairs={{0,24},{8,0},{16,8},{24,16},{1,25},{9,1},{17,9},{25,17},{2,26},{10... | collective-permute-start | bytes 152 | tf_op jit(solution)/shard_map/ppermute | solution.py:135
  45.2 12.0 %all-to-all-start = ((f32[8,64,1,128]{3,1,2,0:T(8,128)}), f32[8,64,1,128]{3,1,2,0:T(8,128)S(1)}, u32[]{:S(2)}, u32[]{:S(2)}) async-start(f32[8,64,1,128]{3,1,2,0:T(8,128)} %bitcast.30), calls=%async_computation | async-start | bytes 524288 | tf_op jit(solution)/shard_map/all_to_all | solution.py:118
  57.2 13.8 %all-to-all-start.1 = ((f32[8,64,2,128]{3,1,2,0:T(8,128)}), f32[8,64,2,128]{3,1,2,0:T(8,128)S(1)}, u32[]{:S(2)}, u32[]{:S(2)}) async-start(f32[8,64,2,128]{3,1,2,0:T(8,128)} %copy.17), calls=%async_computation.1 | async-start | bytes 1048576 | tf_op jit(solution)/shard_map/all_to_all | solution.py:118
  71.0 6.6 %collective-permute-start.5 = (f32[64,3,128]{2,0,1:T(8,128)S(1)}, f32[64,3,128]{2,0,1:T(8,128)S(1)}, u32[]{:S(2)}, u32[]{:S(2)}) collective-permute-start(f32[64,3,128]{2,0,1:T(8,128)S(1)} %pad_maximum_fusion.10), channel_id=1, source_target_pairs={{0,7},{1,0},{2,1},{3,2},{4,3},{5,4},{6,5},{7,6},{8,15},{9,8},{10,9... | collective-permute-start | bytes 294920 | tf_op jit(solution)/shard_map/ppermute | solution.py:122
  72.1 7.2 %collective-permute-start.6 = (f32[64,3,128]{2,0,1:T(8,128)S(1)}, f32[64,3,128]{2,0,1:T(8,128)S(1)}, u32[]{:S(2)}, u32[]{:S(2)}) collective-permute-start(f32[64,3,128]{2,0,1:T(8,128)S(1)} %pad_maximum_fusion.10), channel_id=1, source_target_pairs={{0,6},{1,7},{2,0},{3,1},{4,2},{5,3},{6,4},{7,5},{8,14},{9,15},{10,... | collective-permute-start | bytes 294920 | tf_op jit(solution)/shard_map/ppermute | solution.py:122
  74.8 8.0 %collective-permute-start.8 = (f32[64,3,128]{2,0,1:T(8,128)S(1)}, f32[64,3,128]{2,0,1:T(8,128)S(1)}, u32[]{:S(2)}, u32[]{:S(2)}) collective-permute-start(f32[64,3,128]{2,0,1:T(8,128)S(1)} %pad_maximum_fusion.10), channel_id=1, source_target_pairs={{0,1},{1,2},{2,3},{3,4},{4,5},{5,6},{6,7},{7,0},{8,9},{9,10},{10,1... | collective-permute-start | bytes 294920 | tf_op jit(solution)/shard_map/ppermute | solution.py:122
  74.8 14.9 %collective-permute-start.10 = (f32[64,3,128]{2,0,1:T(8,128)S(1)}, f32[64,3,128]{2,0,1:T(8,128)S(1)}, u32[]{:S(2)}, u32[]{:S(2)}) collective-permute-start(f32[64,3,128]{2,0,1:T(8,128)S(1)} %pad_maximum_fusion.10), channel_id=1, source_target_pairs={{0,2},{1,3},{2,4},{3,5},{4,6},{5,7},{6,0},{7,1},{8,10},{9,11},{10,... | collective-permute-start | bytes 294920 | tf_op jit(solution)/shard_map/ppermute | solution.py:122
  79.4 10.2 %collective-permute-start.7 = (f32[2,64,3,128]{3,1,2,0:T(8,128)S(1)}, f32[2,64,3,128]{3,1,2,0:T(8,128)S(1)}, u32[]{:S(2)}, u32[]{:S(2)}) collective-permute-start(f32[2,64,3,128]{3,1,2,0:T(8,128)S(1)} %pad_maximum_fusion.9), channel_id=1, source_target_pairs={{0,6},{1,7},{2,0},{3,1},{4,2},{5,3},{6,4},{7,5},{8,14},{9,15},{10,... | collective-permute-start | bytes 589832 | tf_op jit(solution)/shard_map/ppermute | solution.py:122
  82.8 6.9 %collective-permute-start.9 = (f32[64,3,128]{2,0,1:T(8,128)S(1)}, f32[64,3,128]{2,0,1:T(8,128)S(1)}, u32[]{:S(2)}, u32[]{:S(2)}) collective-permute-start(f32[64,3,128]{2,0,1:T(8,128)S(1)} %collective-permute-done.8), channel_id=1, source_target_pairs={{0,2},{1,3},{2,4},{3,5},{4,6},{5,7},{6,0},{7,1},{8,10},{9,11},{10,... | collective-permute-start | bytes 294920 | tf_op jit(solution)/shard_map/ppermute | solution.py:122
  90.6 11.6 %collective-permute-start.11 = (f32[6,64,128]{2,1,0:T(8,128)S(1)}, f32[6,64,128]{2,1,0:T(8,128)S(1)}, u32[]{:S(2)}, u32[]{:S(2)}) collective-permute-start(f32[6,64,128]{2,1,0:T(8,128)S(1)} %get-tuple-element.11), channel_id=1, source_target_pairs={{0,8},{8,16},{16,24},{24,0},{1,9},{9,17},{17,25},{25,1},{2,10},{10... | collective-permute-start | bytes 589832 | tf_op jit(solution)/shard_map/ppermute | solution.py:150
  94.0 9.3 %collective-permute-start.12 = (f32[6,64,128]{2,1,0:T(8,128)S(1)}, f32[6,64,128]{2,1,0:T(8,128)S(1)}, u32[]{:S(2)}, u32[]{:S(2)}) collective-permute-start(f32[6,64,128]{2,1,0:T(8,128)S(1)} %get-tuple-element.13), channel_id=1, source_target_pairs={{0,16},{8,24},{16,0},{24,8},{1,17},{9,25},{17,1},{25,9},{2,18},{10... | collective-permute-start | bytes 589832 | tf_op jit(solution)/shard_map/ppermute | solution.py:150
  94.3 11.4 %collective-permute-start.13 = (f32[6,64,128]{2,1,0:T(8,128)S(1)}, f32[6,64,128]{2,1,0:T(8,128)S(1)}, u32[]{:S(2)}, u32[]{:S(2)}) collective-permute-start(f32[6,64,128]{2,1,0:T(8,128)S(1)} %get-tuple-element.12), channel_id=1, source_target_pairs={{0,24},{8,0},{16,8},{24,16},{1,25},{9,1},{17,9},{25,17},{2,26},{10... | collective-permute-start | bytes 589832 | tf_op jit(solution)/shard_map/ppermute | solution.py:150

commit v9 on v7

--- a/solution.py
+++ b/solution.py
@@ -104,12 +104,15 @@
     nwin = lax.axis_size("win")
     windows_all = traces.shape[0] * nwin
     factor = 1.0 / math.sqrt(NB * windows_all)
-    received = {}
-    for shift in (-1, 2):
-        perm = [(k + shift, k) for k in range(blocks) if 0 <= k + shift < blocks]
-        received[shift] = lax.ppermute(white, ("cx", "cz"), perm)
-    left = jnp.stack([received[-1], white, received[-1]])
-    right = jnp.stack([white, received[2], received[2]])
+    def shift_chan(value, step):
+        perm = [(k + step, k) for k in range(blocks) if 0 <= k + step < blocks]
+        return lax.ppermute(value, ("cx", "cz"), perm)
+
+    before = shift_chan(white, -1)
+    after = shift_chan(white, 1)
+    further = shift_chan(after, 1)
+    left = jnp.stack([before, before, before])
+    right = jnp.stack([white, after, further])
     cross = cross_spectra(left, right)
     corr = jnp.einsum("tqb,dqbk->tdk", table, cross, preferred_element_type=jnp.float32) * factor
     lags = corr.shape[0] // nwin
@@ -135,7 +138,7 @@
     lb = owners[..., 0]
     offset = owners[..., 1] - lb
     filled = lb >= 0
-    holder = jnp.where(filled, lb + (offset != 2).astype(jnp.int32), 0)
+    holder = jnp.where(filled, lb + 1, 0)
     mine = filled & (holder // nz == me_x)
     zi = jnp.where(mine, (holder - lax.axis_index("cz")) % nz, 0)
     di = jnp.where(mine, offset - 1, 0)

time: 104 us -> 109 us (1.048)
  starting transfers between devices: 31.9 us -> 40.1 us
  waiting for transfers between devices: 36.6 us -> 34.4 us
    ppermute x2 -> x3, starting transfers between devices: 11.4 us -> 16.5 us  [shift_chan(): return lax.ppermute(value, ('cx', 'cz'), perm)]
    ppermute x3, starting transfers between devices: 3.18 us -> 7.38 us  [body(): lax.ppermute(chunk, 'cx', [(k, (k + step) % nx) for k in range(nx)])]
    ppermute x3, waiting for transfers between devices: 9.88 us -> 8.45 us  [body(): lax.ppermute(chunk, 'cx', [(k, (k + step) % nx) for k in range(nx)])]
    ppermute x6, waiting for transfers between devices: 10.9 us -> 9.55 us  [shift_z(): return lax.ppermute(value, 'cz', [(k, (k - step) % nz) for k in range(nz)])]
    ppermute x6, starting transfers between devices: 10.2 us -> 9.07 us  [shift_z(): return lax.ppermute(value, 'cz', [(k, (k - step) % nz) for k in range(nz)])]
    ppermute x2 -> x3, waiting for transfers between devices: 3.49 us -> 4.04 us  [shift_chan(): return lax.ppermute(value, ('cx', 'cz'), perm)]
  transfers between devices with their start and end apart: 15 -> 16, of which waited for: 8 -> 8; matrix products, arithmetic and copies ran while one was open for 7% -> 7% of each run, Pallas kernels for 0% -> 0%
where the time goes in v9:
time: 109 us
  starting transfers between devices  40.1 us (37%)
  waiting for transfers between devices  34.4 us (32%)
  matrix products  19.8 us (18%)
  other arithmetic  11.9 us (11%)
  local copies, waits for them, and re-layouts  2.43 us (2%)
    ppermute x3, starting transfers between devices, shift_chan(): return lax.ppermute(value, ('cx', 'cz'), perm)  16.5 us
    all_to_all x1, waiting for transfers between devices, body(): corr = lax.all_to_all(corr, 'win', 0, 0).sum(axis=0)  12.4 us
    ppermute x6, waiting for transfers between devices, shift_z(): return lax.ppermute(value, 'cz', [(k, (k - step) % nz) for k in range(nz)])  9.55 us
    ppermute x6, starting transfers between devices, shift_z(): return lax.ppermute(value, 'cz', [(k, (k - step) % nz) for k in range(nz)])  9.07 us
    ppermute x3, waiting for transfers between devices, body(): lax.ppermute(chunk, 'cx', [(k, (k + step) % nx) for k in range(nx)])  8.45 us
    dot_general x1, matrix products, band_dft(): jnp.einsum('rb,bac->rac', basis1, xb, precision=prec, preferred_element_t...  7.83 us
    ppermute x3, starting transfers between devices, body(): lax.ppermute(chunk, 'cx', [(k, (k + step) % nx) for k in range(nx)])  7.38 us
    dot_general x1, matrix products, band_dft(): jnp.einsum('ja,srac->sjrc', basis2, jnp.stack([wr, wi]), precision=prec,...  6.09 us
  transfers between devices with their start and end apart: 16, of which 8 were waited for; matrix products, arithmetic and copies ran while one was open for 7% of the time, Pallas kernels for 0%

profile of v9, /device:TPU:6, one launch (start us, length us, event | category | flops | bytes accessed | tf_op | source)
XLA Modules:
  0.0 109.1 jit_solution(2805744585342922828)
XLA Ops:
  0.6 7.8 %fusion = f32[126,120,128]{2,0,1:T(8,128)S(1)} fusion(f32[125,120,128]{2,1,0:T(8,128)} %bitcast.103, f32[63,125]{1,0:T(8,128)S(1)} %get-tuple-element.30, f32[63,125]{1,0:T(8,128)S(1)} %get-tuple-element.31), kind=kOutput, calls=%fused_computation.3 | convolution fusion | flops 1451535744 | bytes 15484440 | tf_op jit(solution)/shard_map/rb,bac->rac/dot_general | solution.py:44
  8.4 3.0 %add_bitcast_fusion = (f32[1,63,120,128]{3,1,2,0:T(8,128)S(1)}, f32[1,63,120,128]{3,1,2,0:T(8,128)S(1)}) fusion(f32[126,120,128]{2,0,1:T(8,128)S(1)} %fusion, f32[63,120]{0,1:T(8,128)S(1)} %get-tuple-element.32, f32[63,120]{0,1:T(8,128)S(1)} %get-tuple-element.33), kind=kLoop, calls=%fused_computation.8 | loop fusion | flops 5806080 | bytes 15543360 | tf_op jit(solution)/shard_map/stack | solution.py:59
  11.4 1.5 %pad_maximum_fusion = f32[2,63,120,128]{3,1,2,0:T(8,128)S(1)} fusion(f32[1,63,120,128]{3,1,2,0:T(8,128)S(1)} %get-tuple-element.6, f32[1,63,120,128]{3,1,2,0:T(8,128)S(1)} %get-tuple-element.5), kind=kLoop, calls=%fused_computation.2 | loop fusion | flops 1935360 | bytes 15482880 | tf_op jit(solution)/shard_map/stack | solution.py:59
  12.9 6.1 %fusion.4 = f32[2,12,63,128]{3,1,2,0:T(8,128)S(1)} fusion(f32[2,63,120,128]{3,1,2,0:T(8,128)S(1)} %pad_maximum_fusion, f32[6,120]{1,0:T(8,128)S(1)} %get-tuple-element.34, f32[6,120]{1,0:T(8,128)S(1)} %get-tuple-element.35), kind=kOutput, calls=%fused_computation.13 | convolution fusion | flops 139347360 | bytes 8521344 | tf_op jit(solution)/shard_map/ja,srac->sjrc/dot_general | solution.py:58
  19.8 1.7 %convolution_bitcast_fusion.1 = f32[576,128]{1,0:T(8,128)S(1)} fusion(pred[576,6,63]{0,2,1:T(8,128)(4,1)S(1)} %get-tuple-element.21, pred[576,6,63]{0,2,1:T(8,128)(4,1)S(1)} %get-tuple-element.20, f32[12,63,128]{2,0,1:T(8,128)S(1)} %pad_maximum_fusion.3), kind=kOutput, calls=%fused_computation.19 | convolution fusion | flops 669295872 | bytes 1117440 | tf_op jit(solution)/shard_map/dot_general | solution.py:75
  21.6 1.8 %convolution_bitcast_fusion.2 = f32[576,128]{1,0:T(8,128)S(1)} fusion(pred[576,6,63]{0,2,1:T(8,128)(4,1)S(1)} %get-tuple-element.21, pred[576,6,63]{0,2,1:T(8,128)(4,1)S(1)} %get-tuple-element.20, f32[12,63,128]{2,0,1:T(8,128)S(1)} %pad_maximum_fusion.2), kind=kOutput, calls=%fused_computation.20 | convolution fusion | flops 669295872 | bytes 1117440 | tf_op jit(solution)/shard_map/dot_general | solution.py:75
  23.3 1.6 %fusion.46 = (bf16[512,128]{1,0:T(8,128)(2,1)S(1)}, bf16[512,128]{1,0:T(8,128)(2,1)S(1)}) fusion(f32[576,128]{1,0:T(8,128)S(1)} %convolution_bitcast_fusion.2, f32[576,128]{1,0:T(8,128)S(1)} %convolution_bitcast_fusion.1, s32[512]{0:T(512)S(1)} %get-tuple-element.27, f32[512]{0:T(512)S(1)} %multiply_sine_fusion), kind=kOutput, calls=%fused_computation.66 | convolution fusion | flops 454778880 | bytes 1380352 | tf_op jit(solution)/shard_map/dot_general | solution.py:82
  25.0 8.0 %collective-permute-start.4 = (bf16[2,512,128]{2,1,0:T(8,128)(2,1)S(1)}, bf16[2,512,128]{2,1,0:T(8,128)(2,1)S(1)}, u32[]{:S(2)}, u32[]{:S(2)}) collective-permute-start(bf16[2,512,128]{2,1,0:T(8,128)(2,1)S(1)} %pad_maximum_fusion.4), channel_id=1, source_target_pairs={{1,0},{2,1},{3,2},{4,3},{5,4},{6,5},{7,6},{8,7},{9,8},{10,9},{11,1... | collective-permute-start | bytes 786440 | tf_op jit(solution)/shard_map/ppermute | solution.py:109
  33.1 1.9 %collective-permute-start.3 = (bf16[2,512,128]{2,1,0:T(8,128)(2,1)S(1)}, bf16[2,512,128]{2,1,0:T(8,128)(2,1)S(1)}, u32[]{:S(2)}, u32[]{:S(2)}) collective-permute-start(bf16[2,512,128]{2,1,0:T(8,128)(2,1)S(1)} %pad_maximum_fusion.4), channel_id=1, source_target_pairs={{0,1},{1,2},{2,3},{3,4},{4,5},{5,6},{6,7},{7,8},{8,9},{9,10},{10,1... | collective-permute-start | bytes 786440 | tf_op jit(solution)/shard_map/ppermute | solution.py:109
  35.1 2.6 %collective-permute-start.1 = (s32[6,2]{0,1:T(2,128)S(1)}, s32[6,2]{0,1:T(2,128)S(1)}, u32[]{:S(2)}, u32[]{:S(2)}) collective-permute-start(s32[6,2]{0,1:T(2,128)S(1)} %copy-done), channel_id=1, source_target_pairs={{0,16},{8,24},{16,0},{24,8},{1,17},{9,25},{17,1},{25,9},{2,18},{10... | collective-permute-start | bytes 152 | tf_op jit(solution)/shard_map/ppermute | solution.py:135
  37.7 4.7 %cosine_convert_fusion = (bf16[512,1,512]{2,0,1:T(8,128)(2,1)S(1)}, bf16[512,1,512]{2,0,1:T(8,128)(2,1)S(1)}) fusion(s32[512]{0:T(512)S(1)} %get-tuple-element.26, s32[512]{0:T(512)S(1)} %get-tuple-element.27), kind=kLoop, calls=%fused_computation.30 | loop fusion | flops 3145728 | bytes 1052672 | tf_op jit(solution)/shard_map/convert.12
  42.4 6.5 %collective-permute-start.5 = (bf16[2,512,128]{2,1,0:T(8,128)(2,1)S(1)}, bf16[2,512,128]{2,1,0:T(8,128)(2,1)S(1)}, u32[]{:S(2)}, u32[]{:S(2)}) collective-permute-start(bf16[2,512,128]{2,1,0:T(8,128)(2,1)S(1)} %collective-permute-done.4), channel_id=1, source_target_pairs={{1,0},{2,1},{3,2},{4,3},{5,4},{6,5},{7,6},{8,7},{9,8},{10,9},{11,1... | collective-permute-start | bytes 786440 | tf_op jit(solution)/shard_map/ppermute | solution.py:109
  49.1 4.0 %collective-permute-done.5 = bf16[2,512,128]{2,1,0:T(8,128)(2,1)S(1)} collective-permute-done((bf16[2,512,128]{2,1,0:T(8,128)(2,1)S(1)}, bf16[2,512,128]{2,1,0:T(8,128)(2,1)S(1)}, u32[]{:S(2)}, u32[]{:S(2)}) %collective-permute-start.5) | collective-permute-done | bytes 262176 | tf_op jit(solution)/shard_map/ppermute | solution.py:109
  53.5 0.7 fusion.11
  54.2 1.0 copy.15
  55.2 4.5 %all-to-all-start = ((f32[8,64,3,128]{3,1,2,0:T(8,128)}), f32[8,64,3,128]{3,1,2,0:T(8,128)S(1)}, u32[]{:S(2)}, u32[]{:S(2)}) async-start(f32[8,64,3,128]{3,1,2,0:T(8,128)} %copy.15), calls=%async_computation | async-start | bytes 1572864 | tf_op jit(solution)/shard_map/all_to_all | solution.py:120
  59.7 0.6 gather_fusion
  60.4 12.4 %all-to-all-done = f32[8,64,3,128]{3,1,2,0:T(8,128)S(1)} async-done(((f32[8,64,3,128]{3,1,2,0:T(8,128)}), f32[8,64,3,128]{3,1,2,0:T(8,128)S(1)}, u32[]{:S(2)}, u32[]{:S(2)}) %all-to-all-start) | async-done | bytes 786464 | tf_op jit(solution)/shard_map/all_to_all | solution.py:120
  72.9 1.6 %collective-permute-start.7 = (f32[64,3,128]{2,0,1:T(8,128)S(1)}, f32[64,3,128]{2,0,1:T(8,128)S(1)}, u32[]{:S(2)}, u32[]{:S(2)}) collective-permute-start(f32[64,3,128]{2,0,1:T(8,128)S(1)} %reduce_sum.9), channel_id=1, source_target_pairs={{0,6},{1,7},{2,0},{3,1},{4,2},{5,3},{6,4},{7,5},{8,14},{9,15},{10,... | collective-permute-start | bytes 294920 | tf_op jit(solution)/shard_map/ppermute | solution.py:122
  74.5 1.9 %collective-permute-start.9 = (f32[64,3,128]{2,0,1:T(8,128)S(1)}, f32[64,3,128]{2,0,1:T(8,128)S(1)}, u32[]{:S(2)}, u32[]{:S(2)}) collective-permute-start(f32[64,3,128]{2,0,1:T(8,128)S(1)} %reduce_sum.9), channel_id=1, source_target_pairs={{0,1},{1,2},{2,3},{3,4},{4,5},{5,6},{6,7},{7,0},{8,9},{9,10},{10,1... | collective-permute-start | bytes 294920 | tf_op jit(solution)/shard_map/ppermute | solution.py:122
  76.4 1.6 %collective-permute-start.11 = (f32[64,3,128]{2,0,1:T(8,128)S(1)}, f32[64,3,128]{2,0,1:T(8,128)S(1)}, u32[]{:S(2)}, u32[]{:S(2)}) collective-permute-start(f32[64,3,128]{2,0,1:T(8,128)S(1)} %reduce_sum.9), channel_id=1, source_target_pairs={{0,2},{1,3},{2,4},{3,5},{4,6},{5,7},{6,0},{7,1},{8,10},{9,11},{10,... | collective-permute-start | bytes 294920 | tf_op jit(solution)/shard_map/ppermute | solution.py:122
  78.0 2.2 %collective-permute-done.6 = f32[64,3,128]{2,0,1:T(8,128)S(1)} collective-permute-done((f32[64,3,128]{2,0,1:T(8,128)S(1)}, f32[64,3,128]{2,0,1:T(8,128)S(1)}, u32[]{:S(2)}, u32[]{:S(2)}) %collective-permute-start.6) | collective-permute-done | bytes 98336 | tf_op jit(solution)/shard_map/ppermute | solution.py:122
  80.5 1.9 %collective-permute-start.8 = (f32[2,64,3,128]{3,1,2,0:T(8,128)S(1)}, f32[2,64,3,128]{3,1,2,0:T(8,128)S(1)}, u32[]{:S(2)}, u32[]{:S(2)}) collective-permute-start(f32[2,64,3,128]{3,1,2,0:T(8,128)S(1)} %pad_maximum_fusion.5), channel_id=1, source_target_pairs={{0,6},{1,7},{2,0},{3,1},{4,2},{5,3},{6,4},{7,5},{8,14},{9,15},{10,... | collective-permute-start | bytes 589832 | tf_op jit(solution)/shard_map/ppermute | solution.py:122
  82.4 2.1 %collective-permute-start.10 = (f32[64,3,128]{2,0,1:T(8,128)S(1)}, f32[64,3,128]{2,0,1:T(8,128)S(1)}, u32[]{:S(2)}, u32[]{:S(2)}) collective-permute-start(f32[64,3,128]{2,0,1:T(8,128)S(1)} %collective-permute-done.9), channel_id=1, source_target_pairs={{0,2},{1,3},{2,4},{3,5},{4,6},{5,7},{6,0},{7,1},{8,10},{9,11},{10,... | collective-permute-start | bytes 294920 | tf_op jit(solution)/shard_map/ppermute | solution.py:122
  84.5 7.0 %collective-permute-done.8 = f32[2,64,3,128]{3,1,2,0:T(8,128)S(1)} collective-permute-done((f32[2,64,3,128]{3,1,2,0:T(8,128)S(1)}, f32[2,64,3,128]{3,1,2,0:T(8,128)S(1)}, u32[]{:S(2)}, u32[]{:S(2)}) %collective-permute-start.8) | collective-permute-done | bytes 196640 | tf_op jit(solution)/shard_map/ppermute | solution.py:122
  91.6 0.7 gather_fusion.1
  92.5 6.4 %collective-permute-start.12 = (f32[6,64,128]{2,1,0:T(8,128)S(1)}, f32[6,64,128]{2,1,0:T(8,128)S(1)}, u32[]{:S(2)}, u32[]{:S(2)}) collective-permute-start(f32[6,64,128]{2,1,0:T(8,128)S(1)} %get-tuple-element.13), channel_id=1, source_target_pairs={{0,8},{8,16},{16,24},{24,0},{1,9},{9,17},{17,25},{25,1},{2,10},{10... | collective-permute-start | bytes 589832 | tf_op jit(solution)/shard_map/ppermute | solution.py:150
  98.9 1.0 collective-permute-start.14
  99.9 5.0 %collective-permute-done.12 = f32[6,64,128]{2,1,0:T(8,128)S(1)} collective-permute-done((f32[6,64,128]{2,1,0:T(8,128)S(1)}, f32[6,64,128]{2,1,0:T(8,128)S(1)}, u32[]{:S(2)}, u32[]{:S(2)}) %collective-permute-start.12) | collective-permute-done | bytes 196640 | tf_op jit(solution)/shard_map/ppermute | solution.py:150
  104.9 1.7 %collective-permute-done.13 = f32[6,64,128]{2,1,0:T(8,128)S(1)} collective-permute-done((f32[6,64,128]{2,1,0:T(8,128)S(1)}, f32[6,64,128]{2,1,0:T(8,128)S(1)}, u32[]{:S(2)}, u32[]{:S(2)}) %collective-permute-start.13) | collective-permute-done | bytes 196640 | tf_op jit(solution)/shard_map/ppermute | solution.py:150
  106.7 1.7 %collective-permute-done.14 = f32[6,64,128]{2,1,0:T(8,128)S(1)} collective-permute-done((f32[6,64,128]{2,1,0:T(8,128)S(1)}, f32[6,64,128]{2,1,0:T(8,128)S(1)}, u32[]{:S(2)}, u32[]{:S(2)}) %collective-permute-start.14) | collective-permute-done | bytes 196640 | tf_op jit(solution)/shard_map/ppermute | solution.py:150
  108.3 0.8 fusion.50
  (53 shorter events, 2.7 us)
Async XLA Ops:
  19.4 15.6 %copy-start = (s32[6,2]{0,1:T(2,128)S(1)}, s32[6,2]{0,1:T(2,128)}, u32[]{:S(2)}) copy-start(s32[6,2]{0,1:T(2,128)} %param.3) | copy-start | bytes 148
  25.0 17.4 %collective-permute-start.4 = (bf16[2,512,128]{2,1,0:T(8,128)(2,1)S(1)}, bf16[2,512,128]{2,1,0:T(8,128)(2,1)S(1)}, u32[]{:S(2)}, u32[]{:S(2)}) collective-permute-start(bf16[2,512,128]{2,1,0:T(8,128)(2,1)S(1)} %pad_maximum_fusion.4), channel_id=1, source_target_pairs={{1,0},{2,1},{3,2},{4,3},{5,4},{6,5},{7,6},{8,7},{9,8},{10,9},{11,1... | collective-permute-start | bytes 786440 | tf_op jit(solution)/shard_map/ppermute | solution.py:109
  33.1 16.0 %collective-permute-start.3 = (bf16[2,512,128]{2,1,0:T(8,128)(2,1)S(1)}, bf16[2,512,128]{2,1,0:T(8,128)(2,1)S(1)}, u32[]{:S(2)}, u32[]{:S(2)}) collective-permute-start(bf16[2,512,128]{2,1,0:T(8,128)(2,1)S(1)} %pad_maximum_fusion.4), channel_id=1, source_target_pairs={{0,1},{1,2},{2,3},{3,4},{4,5},{5,6},{6,7},{7,8},{8,9},{9,10},{10,1... | collective-permute-start | bytes 786440 | tf_op jit(solution)/shard_map/ppermute | solution.py:109
  35.0 24.7 %collective-permute-start = (s32[6,2]{0,1:T(2,128)S(1)}, s32[6,2]{0,1:T(2,128)S(1)}, u32[]{:S(2)}, u32[]{:S(2)}) collective-permute-start(s32[6,2]{0,1:T(2,128)S(1)} %copy-done), channel_id=1, source_target_pairs={{0,8},{8,16},{16,24},{24,0},{1,9},{9,17},{17,25},{25,1},{2,10},{10... | collective-permute-start | bytes 152 | tf_op jit(solution)/shard_map/ppermute | solution.py:135
  35.1 24.6 %collective-permute-start.1 = (s32[6,2]{0,1:T(2,128)S(1)}, s32[6,2]{0,1:T(2,128)S(1)}, u32[]{:S(2)}, u32[]{:S(2)}) collective-permute-start(s32[6,2]{0,1:T(2,128)S(1)} %copy-done), channel_id=1, source_target_pairs={{0,16},{8,24},{16,0},{24,8},{1,17},{9,25},{17,1},{25,9},{2,18},{10... | collective-permute-start | bytes 152 | tf_op jit(solution)/shard_map/ppermute | solution.py:135
  37.7 22.0 %collective-permute-start.2 = (s32[6,2]{0,1:T(2,128)S(1)}, s32[6,2]{0,1:T(2,128)S(1)}, u32[]{:S(2)}, u32[]{:S(2)}) collective-permute-start(s32[6,2]{0,1:T(2,128)S(1)} %copy-done), channel_id=1, source_target_pairs={{0,24},{8,0},{16,8},{24,16},{1,25},{9,1},{17,9},{25,17},{2,26},{10... | collective-permute-start | bytes 152 | tf_op jit(solution)/shard_map/ppermute | solution.py:135
  42.4 10.7 %collective-permute-start.5 = (bf16[2,512,128]{2,1,0:T(8,128)(2,1)S(1)}, bf16[2,512,128]{2,1,0:T(8,128)(2,1)S(1)}, u32[]{:S(2)}, u32[]{:S(2)}) collective-permute-start(bf16[2,512,128]{2,1,0:T(8,128)(2,1)S(1)} %collective-permute-done.4), channel_id=1, source_target_pairs={{1,0},{2,1},{3,2},{4,3},{5,4},{6,5},{7,6},{8,7},{9,8},{10,9},{11,1... | collective-permute-start | bytes 786440 | tf_op jit(solution)/shard_map/ppermute | solution.py:109
  55.2 17.6 %all-to-all-start = ((f32[8,64,3,128]{3,1,2,0:T(8,128)}), f32[8,64,3,128]{3,1,2,0:T(8,128)S(1)}, u32[]{:S(2)}, u32[]{:S(2)}) async-start(f32[8,64,3,128]{3,1,2,0:T(8,128)} %copy.15), calls=%async_computation | async-start | bytes 1572864 | tf_op jit(solution)/shard_map/all_to_all | solution.py:120
  72.9 7.3 %collective-permute-start.6 = (f32[64,3,128]{2,0,1:T(8,128)S(1)}, f32[64,3,128]{2,0,1:T(8,128)S(1)}, u32[]{:S(2)}, u32[]{:S(2)}) collective-permute-start(f32[64,3,128]{2,0,1:T(8,128)S(1)} %reduce_sum.9), channel_id=1, source_target_pairs={{0,7},{1,0},{2,1},{3,2},{4,3},{5,4},{6,5},{7,6},{8,15},{9,8},{10,9... | collective-permute-start | bytes 294920 | tf_op jit(solution)/shard_map/ppermute | solution.py:122
  72.9 7.6 %collective-permute-start.7 = (f32[64,3,128]{2,0,1:T(8,128)S(1)}, f32[64,3,128]{2,0,1:T(8,128)S(1)}, u32[]{:S(2)}, u32[]{:S(2)}) collective-permute-start(f32[64,3,128]{2,0,1:T(8,128)S(1)} %reduce_sum.9), channel_id=1, source_target_pairs={{0,6},{1,7},{2,0},{3,1},{4,2},{5,3},{6,4},{7,5},{8,14},{9,15},{10,... | collective-permute-start | bytes 294920 | tf_op jit(solution)/shard_map/ppermute | solution.py:122
  74.5 7.9 %collective-permute-start.9 = (f32[64,3,128]{2,0,1:T(8,128)S(1)}, f32[64,3,128]{2,0,1:T(8,128)S(1)}, u32[]{:S(2)}, u32[]{:S(2)}) collective-permute-start(f32[64,3,128]{2,0,1:T(8,128)S(1)} %reduce_sum.9), channel_id=1, source_target_pairs={{0,1},{1,2},{2,3},{3,4},{4,5},{5,6},{6,7},{7,0},{8,9},{9,10},{10,1... | collective-permute-start | bytes 294920 | tf_op jit(solution)/shard_map/ppermute | solution.py:122
  76.4 15.2 %collective-permute-start.11 = (f32[64,3,128]{2,0,1:T(8,128)S(1)}, f32[64,3,128]{2,0,1:T(8,128)S(1)}, u32[]{:S(2)}, u32[]{:S(2)}) collective-permute-start(f32[64,3,128]{2,0,1:T(8,128)S(1)} %reduce_sum.9), channel_id=1, source_target_pairs={{0,2},{1,3},{2,4},{3,5},{4,6},{5,7},{6,0},{7,1},{8,10},{9,11},{10,... | collective-permute-start | bytes 294920 | tf_op jit(solution)/shard_map/ppermute | solution.py:122
  80.5 11.0 %collective-permute-start.8 = (f32[2,64,3,128]{3,1,2,0:T(8,128)S(1)}, f32[2,64,3,128]{3,1,2,0:T(8,128)S(1)}, u32[]{:S(2)}, u32[]{:S(2)}) collective-permute-start(f32[2,64,3,128]{3,1,2,0:T(8,128)S(1)} %pad_maximum_fusion.5), channel_id=1, source_target_pairs={{0,6},{1,7},{2,0},{3,1},{4,2},{5,3},{6,4},{7,5},{8,14},{9,15},{10,... | collective-permute-start | bytes 589832 | tf_op jit(solution)/shard_map/ppermute | solution.py:122
  82.4 9.1 %collective-permute-start.10 = (f32[64,3,128]{2,0,1:T(8,128)S(1)}, f32[64,3,128]{2,0,1:T(8,128)S(1)}, u32[]{:S(2)}, u32[]{:S(2)}) collective-permute-start(f32[64,3,128]{2,0,1:T(8,128)S(1)} %collective-permute-done.9), channel_id=1, source_target_pairs={{0,2},{1,3},{2,4},{3,5},{4,6},{5,7},{6,0},{7,1},{8,10},{9,11},{10,... | collective-permute-start | bytes 294920 | tf_op jit(solution)/shard_map/ppermute | solution.py:122
  92.5 12.4 %collective-permute-start.12 = (f32[6,64,128]{2,1,0:T(8,128)S(1)}, f32[6,64,128]{2,1,0:T(8,128)S(1)}, u32[]{:S(2)}, u32[]{:S(2)}) collective-permute-start(f32[6,64,128]{2,1,0:T(8,128)S(1)} %get-tuple-element.13), channel_id=1, source_target_pairs={{0,8},{8,16},{16,24},{24,0},{1,9},{9,17},{17,25},{25,1},{2,10},{10... | collective-permute-start | bytes 589832 | tf_op jit(solution)/shard_map/ppermute | solution.py:150
  98.9 7.7 %collective-permute-start.13 = (f32[6,64,128]{2,1,0:T(8,128)S(1)}, f32[6,64,128]{2,1,0:T(8,128)S(1)}, u32[]{:S(2)}, u32[]{:S(2)}) collective-permute-start(f32[6,64,128]{2,1,0:T(8,128)S(1)} %get-tuple-element.15), channel_id=1, source_target_pairs={{0,16},{8,24},{16,0},{24,8},{1,17},{9,25},{17,1},{25,9},{2,18},{10... | collective-permute-start | bytes 589832 | tf_op jit(solution)/shard_map/ppermute | solution.py:150
  98.9 9.4 %collective-permute-start.14 = (f32[6,64,128]{2,1,0:T(8,128)S(1)}, f32[6,64,128]{2,1,0:T(8,128)S(1)}, u32[]{:S(2)}, u32[]{:S(2)}) collective-permute-start(f32[6,64,128]{2,1,0:T(8,128)S(1)} %get-tuple-element.14), channel_id=1, source_target_pairs={{0,24},{8,0},{16,8},{24,16},{1,25},{9,1},{17,9},{25,17},{2,26},{10... | collective-permute-start | bytes 589832 | tf_op jit(solution)/shard_map/ppermute | solution.py:150

commit v10 on v7

--- a/solution.py
+++ b/solution.py
@@ -114,7 +114,8 @@
     corr = jnp.einsum("tqb,dqbk->tdk", table, cross, preferred_element_type=jnp.float32) * factor
     lags = corr.shape[0] // nwin
     corr = corr.reshape((nwin, lags) + corr.shape[1:])
-    corr = lax.all_to_all(corr, "win", 0, 0).sum(axis=0)
+    corr = lax.all_to_all(corr.astype(jnp.bfloat16), "win", 0, 0)
+    corr = corr.astype(jnp.float32).sum(axis=0)
     def shift_z(value, step):
         return lax.ppermute(value, "cz", [(k, (k - step) % nz) for k in range(nz)])
 

time: 104 us -> 99.4 us (0.956)
  waiting for transfers between devices: 36.6 us -> 32.4 us
    all_to_all x1, waiting for transfers between devices: 12.3 us -> 8.78 us  [body(): corr = lax.all_to_all(corr.astype(jnp.bfloat16), 'win', 0, 0)]
  transfers between devices with their start and end apart: 15 -> 15, of which waited for: 8 -> 8; matrix products, arithmetic and copies ran while one was open for 7% -> 6% of each run, Pallas kernels for 0% -> 0%
where the time goes in v10:
time: 99.4 us; the launch traced here: 98.8 us
  waiting for transfers between devices  32.4 us (33%)
  starting transfers between devices  31.9 us (32%)
  matrix products  19.8 us (20%)
  other arithmetic  12 us (12%)
  local copies, waits for them, and re-layouts  2.24 us (2%)
    ppermute x2, starting transfers between devices, body(): received[shift] = lax.ppermute(white, ('cx', 'cz'), perm)  11.4 us
    ppermute x6, waiting for transfers between devices, shift_z(): return lax.ppermute(value, 'cz', [(k, (k - step) % nz) for k in range(nz)])  10.9 us
    ppermute x6, starting transfers between devices, shift_z(): return lax.ppermute(value, 'cz', [(k, (k - step) % nz) for k in range(nz)])  10.2 us
    ppermute x3, waiting for transfers between devices, body(): lax.ppermute(chunk, 'cx', [(k, (k + step) % nx) for k in range(nx)])  9.88 us
    all_to_all x1, waiting for transfers between devices, body(): corr = lax.all_to_all(corr.astype(jnp.bfloat16), 'win', 0, 0)  8.78 us
    dot_general x1, matrix products, band_dft(): jnp.einsum('rb,bac->rac', basis1, xb, precision=prec, preferred_element_t...  7.83 us
    dot_general x1, matrix products, band_dft(): jnp.einsum('ja,srac->sjrc', basis2, jnp.stack([wr, wi]), precision=prec,...  6.09 us
    another operation x2, other arithmetic  5.01 us
  transfers between devices with their start and end apart: 15, of which 8 were waited for; matrix products, arithmetic and copies ran while one was open for 6% of the time, Pallas kernels for 0%

profile of v10, /device:TPU:6, one launch (start us, length us, event | category | flops | bytes accessed | tf_op | source)
XLA Modules:
  0.0 98.8 jit_solution(8191979698735087609)
XLA Ops:
  0.6 7.8 %fusion = f32[126,120,128]{2,0,1:T(8,128)S(1)} fusion(f32[125,120,128]{2,1,0:T(8,128)} %bitcast.89, f32[63,125]{1,0:T(8,128)S(1)} %get-tuple-element.31, f32[63,125]{1,0:T(8,128)S(1)} %get-tuple-element.32), kind=kOutput, calls=%fused_computation.3 | convolution fusion | flops 1451535744 | bytes 15484440 | tf_op jit(solution)/shard_map/rb,bac->rac/dot_general | solution.py:44
  8.4 3.0 %add_bitcast_fusion = (f32[1,63,120,128]{3,1,2,0:T(8,128)S(1)}, f32[1,63,120,128]{3,1,2,0:T(8,128)S(1)}) fusion(f32[126,120,128]{2,0,1:T(8,128)S(1)} %fusion, f32[63,120]{0,1:T(8,128)S(1)} %get-tuple-element.33, f32[63,120]{0,1:T(8,128)S(1)} %get-tuple-element.34), kind=kLoop, calls=%fused_computation.8 | loop fusion | flops 5806080 | bytes 15543360 | tf_op jit(solution)/shard_map/stack | solution.py:59
  11.4 1.5 %pad_maximum_fusion = f32[2,63,120,128]{3,1,2,0:T(8,128)S(1)} fusion(f32[1,63,120,128]{3,1,2,0:T(8,128)S(1)} %get-tuple-element.6, f32[1,63,120,128]{3,1,2,0:T(8,128)S(1)} %get-tuple-element.5), kind=kLoop, calls=%fused_computation.2 | loop fusion | flops 1935360 | bytes 15482880 | tf_op jit(solution)/shard_map/stack | solution.py:59
  12.9 6.1 %fusion.4 = f32[2,12,63,128]{3,1,2,0:T(8,128)S(1)} fusion(f32[2,63,120,128]{3,1,2,0:T(8,128)S(1)} %pad_maximum_fusion, f32[6,120]{1,0:T(8,128)S(1)} %get-tuple-element.35, f32[6,120]{1,0:T(8,128)S(1)} %get-tuple-element.36), kind=kOutput, calls=%fused_computation.13 | convolution fusion | flops 139347360 | bytes 8521344 | tf_op jit(solution)/shard_map/ja,srac->sjrc/dot_general | solution.py:58
  19.4 0.4 add_compare_fusion
  19.8 1.7 %convolution_bitcast_fusion.1 = f32[576,128]{1,0:T(8,128)S(1)} fusion(pred[576,6,63]{0,2,1:T(8,128)(4,1)S(1)} %get-tuple-element.21, pred[576,6,63]{0,2,1:T(8,128)(4,1)S(1)} %get-tuple-element.20, f32[12,63,128]{2,0,1:T(8,128)S(1)} %pad_maximum_fusion.4), kind=kOutput, calls=%fused_computation.20 | convolution fusion | flops 669295872 | bytes 1117440 | tf_op jit(solution)/shard_map/dot_general | solution.py:75
  21.6 1.8 %convolution_bitcast_fusion.2 = f32[576,128]{1,0:T(8,128)S(1)} fusion(pred[576,6,63]{0,2,1:T(8,128)(4,1)S(1)} %get-tuple-element.21, pred[576,6,63]{0,2,1:T(8,128)(4,1)S(1)} %get-tuple-element.20, f32[12,63,128]{2,0,1:T(8,128)S(1)} %pad_maximum_fusion.3), kind=kOutput, calls=%fused_computation.21 | convolution fusion | flops 669295872 | bytes 1117440 | tf_op jit(solution)/shard_map/dot_general | solution.py:75
  23.3 1.6 %fusion.47 = (bf16[512,128]{1,0:T(8,128)(2,1)S(1)}, bf16[512,128]{1,0:T(8,128)(2,1)S(1)}) fusion(f32[576,128]{1,0:T(8,128)S(1)} %convolution_bitcast_fusion.2, f32[576,128]{1,0:T(8,128)S(1)} %convolution_bitcast_fusion.1, s32[512]{0:T(512)S(1)} %get-tuple-element.28, f32[512]{0:T(512)S(1)} %multiply_sine_fusion), kind=kOutput, calls=%fused_computation.69 | convolution fusion | flops 454778880 | bytes 1380352 | tf_op jit(solution)/shard_map/dot_general | solution.py:82
  25.0 3.8 %collective-permute-start.3 = (bf16[2,512,128]{2,1,0:T(8,128)(2,1)S(1)}, bf16[2,512,128]{2,1,0:T(8,128)(2,1)S(1)}, u32[]{:S(2)}, u32[]{:S(2)}) collective-permute-start(bf16[2,512,128]{2,1,0:T(8,128)(2,1)S(1)} %pad_maximum_fusion.5), channel_id=1, source_target_pairs={{0,1},{1,2},{2,3},{3,4},{4,5},{5,6},{6,7},{7,8},{8,9},{9,10},{10,1... | collective-permute-start | bytes 786440 | tf_op jit(solution)/shard_map/ppermute | solution.py:110
  28.8 7.6 %collective-permute-start.4 = (bf16[2,512,128]{2,1,0:T(8,128)(2,1)S(1)}, bf16[2,512,128]{2,1,0:T(8,128)(2,1)S(1)}, u32[]{:S(2)}, u32[]{:S(2)}) collective-permute-start(bf16[2,512,128]{2,1,0:T(8,128)(2,1)S(1)} %pad_maximum_fusion.5), channel_id=1, source_target_pairs={{2,0},{3,1},{4,2},{5,3},{6,4},{7,5},{8,6},{9,7},{10,8},{11,9},{12,... | collective-permute-start | bytes 786440 | tf_op jit(solution)/shard_map/ppermute | solution.py:110
  36.5 2.6 %collective-permute-start.1 = (s32[6,2]{0,1:T(2,128)S(1)}, s32[6,2]{0,1:T(2,128)S(1)}, u32[]{:S(2)}, u32[]{:S(2)}) collective-permute-start(s32[6,2]{0,1:T(2,128)S(1)} %copy-done), channel_id=1, source_target_pairs={{0,16},{8,24},{16,0},{24,8},{1,17},{9,25},{17,1},{25,9},{2,18},{10... | collective-permute-start | bytes 152 | tf_op jit(solution)/shard_map/ppermute | solution.py:133
  39.1 4.7 %cosine_convert_fusion = (bf16[512,1,512]{2,0,1:T(8,128)(2,1)S(1)}, bf16[512,1,512]{2,0,1:T(8,128)(2,1)S(1)}) fusion(s32[512]{0:T(512)S(1)} %get-tuple-element.27, s32[512]{0:T(512)S(1)} %get-tuple-element.28), kind=kLoop, calls=%fused_computation.31 | loop fusion | flops 3145728 | bytes 1052672 | tf_op jit(solution)/shard_map/convert.10
  44.0 0.6 gather_fusion
  44.5 2.8 %collective-permute-done.4 = bf16[2,512,128]{2,1,0:T(8,128)(2,1)S(1)} collective-permute-done((bf16[2,512,128]{2,1,0:T(8,128)(2,1)S(1)}, bf16[2,512,128]{2,1,0:T(8,128)(2,1)S(1)}, u32[]{:S(2)}, u32[]{:S(2)}) %collective-permute-start.4) | collective-permute-done | bytes 262176 | tf_op jit(solution)/shard_map/ppermute | solution.py:110
  47.8 0.7 fusion.12
  48.6 0.8 copy.15
  49.3 4.4 %all-to-all-start = ((bf16[8,64,3,128]{3,1,2,0:T(8,128)(2,1)}), bf16[8,64,3,128]{3,1,2,0:T(8,128)(2,1)S(1)}, u32[]{:S(2)}, u32[]{:S(2)}) async-start(bf16[8,64,3,128]{3,1,2,0:T(8,128)(2,1)} %copy.15), calls=%async_computation | async-start | bytes 786432 | tf_op jit(solution)/shard_map/all_to_all | solution.py:117
  53.9 8.8 %all-to-all-done = bf16[8,64,3,128]{3,1,2,0:T(8,128)(2,1)S(1)} async-done(((bf16[8,64,3,128]{3,1,2,0:T(8,128)(2,1)}), bf16[8,64,3,128]{3,1,2,0:T(8,128)(2,1)S(1)}, u32[]{:S(2)}, u32[]{:S(2)}) %all-to-all-start) | async-done | bytes 393248 | tf_op jit(solution)/shard_map/all_to_all | solution.py:117
  62.9 2.9 %collective-permute-start.6 = (f32[64,3,128]{2,0,1:T(8,128)S(1)}, f32[64,3,128]{2,0,1:T(8,128)S(1)}, u32[]{:S(2)}, u32[]{:S(2)}) collective-permute-start(f32[64,3,128]{2,0,1:T(8,128)S(1)} %convert_reduce_fusion), channel_id=1, source_target_pairs={{0,6},{1,7},{2,0},{3,1},{4,2},{5,3},{6,4},{7,5},{8,14},{9,15},{10,... | collective-permute-start | bytes 294920 | tf_op jit(solution)/shard_map/ppermute | solution.py:120
  66.2 1.7 %collective-permute-start.10 = (f32[64,3,128]{2,0,1:T(8,128)S(1)}, f32[64,3,128]{2,0,1:T(8,128)S(1)}, u32[]{:S(2)}, u32[]{:S(2)}) collective-permute-start(f32[64,3,128]{2,0,1:T(8,128)S(1)} %convert_reduce_fusion), channel_id=1, source_target_pairs={{0,2},{1,3},{2,4},{3,5},{4,6},{5,7},{6,0},{7,1},{8,10},{9,11},{10,... | collective-permute-start | bytes 294920 | tf_op jit(solution)/shard_map/ppermute | solution.py:120
  67.9 1.6 %collective-permute-done.5 = f32[64,3,128]{2,0,1:T(8,128)S(1)} collective-permute-done((f32[64,3,128]{2,0,1:T(8,128)S(1)}, f32[64,3,128]{2,0,1:T(8,128)S(1)}, u32[]{:S(2)}, u32[]{:S(2)}) %collective-permute-start.5) | collective-permute-done | bytes 98336 | tf_op jit(solution)/shard_map/ppermute | solution.py:120
  69.5 2.5 %collective-permute-done.6 = f32[64,3,128]{2,0,1:T(8,128)S(1)} collective-permute-done((f32[64,3,128]{2,0,1:T(8,128)S(1)}, f32[64,3,128]{2,0,1:T(8,128)S(1)}, u32[]{:S(2)}, u32[]{:S(2)}) %collective-permute-start.6) | collective-permute-done | bytes 98336 | tf_op jit(solution)/shard_map/ppermute | solution.py:120
  72.1 1.3 %collective-permute-start.7 = (f32[2,64,3,128]{3,1,2,0:T(8,128)S(1)}, f32[2,64,3,128]{3,1,2,0:T(8,128)S(1)}, u32[]{:S(2)}, u32[]{:S(2)}) collective-permute-start(f32[2,64,3,128]{3,1,2,0:T(8,128)S(1)} %pad_maximum_fusion.6), channel_id=1, source_target_pairs={{0,6},{1,7},{2,0},{3,1},{4,2},{5,3},{6,4},{7,5},{8,14},{9,15},{10,... | collective-permute-start | bytes 589832 | tf_op jit(solution)/shard_map/ppermute | solution.py:120
  73.4 3.9 %collective-permute-start.9 = (f32[64,3,128]{2,0,1:T(8,128)S(1)}, f32[64,3,128]{2,0,1:T(8,128)S(1)}, u32[]{:S(2)}, u32[]{:S(2)}) collective-permute-start(f32[64,3,128]{2,0,1:T(8,128)S(1)} %collective-permute-done.8), channel_id=1, source_target_pairs={{0,2},{1,3},{2,4},{3,5},{4,6},{5,7},{6,0},{7,1},{8,10},{9,11},{10,... | collective-permute-start | bytes 294920 | tf_op jit(solution)/shard_map/ppermute | solution.py:120
  77.2 6.7 %collective-permute-done.7 = f32[2,64,3,128]{3,1,2,0:T(8,128)S(1)} collective-permute-done((f32[2,64,3,128]{3,1,2,0:T(8,128)S(1)}, f32[2,64,3,128]{3,1,2,0:T(8,128)S(1)}, u32[]{:S(2)}, u32[]{:S(2)}) %collective-permute-start.7) | collective-permute-done | bytes 196640 | tf_op jit(solution)/shard_map/ppermute | solution.py:120
  84.1 0.7 gather_fusion.1
  84.9 0.9 collective-permute-start.11
  85.8 2.3 %collective-permute-start.12 = (f32[6,64,128]{2,1,0:T(8,128)S(1)}, f32[6,64,128]{2,1,0:T(8,128)S(1)}, u32[]{:S(2)}, u32[]{:S(2)}) collective-permute-start(f32[6,64,128]{2,1,0:T(8,128)S(1)} %get-tuple-element.15), channel_id=1, source_target_pairs={{0,16},{8,24},{16,0},{24,8},{1,17},{9,25},{17,1},{25,9},{2,18},{10... | collective-permute-start | bytes 589832 | tf_op jit(solution)/shard_map/ppermute | solution.py:148
  88.1 4.7 %collective-permute-done.11 = f32[6,64,128]{2,1,0:T(8,128)S(1)} collective-permute-done((f32[6,64,128]{2,1,0:T(8,128)S(1)}, f32[6,64,128]{2,1,0:T(8,128)S(1)}, u32[]{:S(2)}, u32[]{:S(2)}) %collective-permute-start.11) | collective-permute-done | bytes 196640 | tf_op jit(solution)/shard_map/ppermute | solution.py:148
  92.8 2.4 %collective-permute-done.12 = f32[6,64,128]{2,1,0:T(8,128)S(1)} collective-permute-done((f32[6,64,128]{2,1,0:T(8,128)S(1)}, f32[6,64,128]{2,1,0:T(8,128)S(1)}, u32[]{:S(2)}, u32[]{:S(2)}) %collective-permute-start.12) | collective-permute-done | bytes 196640 | tf_op jit(solution)/shard_map/ppermute | solution.py:148
  95.1 2.9 %collective-permute-done.13 = f32[6,64,128]{2,1,0:T(8,128)S(1)} collective-permute-done((f32[6,64,128]{2,1,0:T(8,128)S(1)}, f32[6,64,128]{2,1,0:T(8,128)S(1)}, u32[]{:S(2)}, u32[]{:S(2)}) %collective-permute-start.13) | collective-permute-done | bytes 196640 | tf_op jit(solution)/shard_map/ppermute | solution.py:148
  98.0 0.8 fusion.51
  (49 shorter events, 2.3 us)
Async XLA Ops:
  19.4 17.1 %copy-start = (s32[6,2]{0,1:T(2,128)S(1)}, s32[6,2]{0,1:T(2,128)}, u32[]{:S(2)}) copy-start(s32[6,2]{0,1:T(2,128)} %param.3) | copy-start | bytes 148
  25.0 19.5 %collective-permute-start.3 = (bf16[2,512,128]{2,1,0:T(8,128)(2,1)S(1)}, bf16[2,512,128]{2,1,0:T(8,128)(2,1)S(1)}, u32[]{:S(2)}, u32[]{:S(2)}) collective-permute-start(bf16[2,512,128]{2,1,0:T(8,128)(2,1)S(1)} %pad_maximum_fusion.5), channel_id=1, source_target_pairs={{0,1},{1,2},{2,3},{3,4},{4,5},{5,6},{6,7},{7,8},{8,9},{9,10},{10,1... | collective-permute-start | bytes 786440 | tf_op jit(solution)/shard_map/ppermute | solution.py:110
  28.8 18.5 %collective-permute-start.4 = (bf16[2,512,128]{2,1,0:T(8,128)(2,1)S(1)}, bf16[2,512,128]{2,1,0:T(8,128)(2,1)S(1)}, u32[]{:S(2)}, u32[]{:S(2)}) collective-permute-start(bf16[2,512,128]{2,1,0:T(8,128)(2,1)S(1)} %pad_maximum_fusion.5), channel_id=1, source_target_pairs={{2,0},{3,1},{4,2},{5,3},{6,4},{7,5},{8,6},{9,7},{10,8},{11,9},{12,... | collective-permute-start | bytes 786440 | tf_op jit(solution)/shard_map/ppermute | solution.py:110
  36.4 7.5 %collective-permute-start = (s32[6,2]{0,1:T(2,128)S(1)}, s32[6,2]{0,1:T(2,128)S(1)}, u32[]{:S(2)}, u32[]{:S(2)}) collective-permute-start(s32[6,2]{0,1:T(2,128)S(1)} %copy-done), channel_id=1, source_target_pairs={{0,8},{8,16},{16,24},{24,0},{1,9},{9,17},{17,25},{25,1},{2,10},{10... | collective-permute-start | bytes 152 | tf_op jit(solution)/shard_map/ppermute | solution.py:133
  36.5 7.4 %collective-permute-start.1 = (s32[6,2]{0,1:T(2,128)S(1)}, s32[6,2]{0,1:T(2,128)S(1)}, u32[]{:S(2)}, u32[]{:S(2)}) collective-permute-start(s32[6,2]{0,1:T(2,128)S(1)} %copy-done), channel_id=1, source_target_pairs={{0,16},{8,24},{16,0},{24,8},{1,17},{9,25},{17,1},{25,9},{2,18},{10... | collective-permute-start | bytes 152 | tf_op jit(solution)/shard_map/ppermute | solution.py:133
  39.1 4.8 %collective-permute-start.2 = (s32[6,2]{0,1:T(2,128)S(1)}, s32[6,2]{0,1:T(2,128)S(1)}, u32[]{:S(2)}, u32[]{:S(2)}) collective-permute-start(s32[6,2]{0,1:T(2,128)S(1)} %copy-done), channel_id=1, source_target_pairs={{0,24},{8,0},{16,8},{24,16},{1,25},{9,1},{17,9},{25,17},{2,26},{10... | collective-permute-start | bytes 152 | tf_op jit(solution)/shard_map/ppermute | solution.py:133
  49.3 13.4 %all-to-all-start = ((bf16[8,64,3,128]{3,1,2,0:T(8,128)(2,1)}), bf16[8,64,3,128]{3,1,2,0:T(8,128)(2,1)S(1)}, u32[]{:S(2)}, u32[]{:S(2)}) async-start(bf16[8,64,3,128]{3,1,2,0:T(8,128)(2,1)} %copy.15), calls=%async_computation | async-start | bytes 786432 | tf_op jit(solution)/shard_map/all_to_all | solution.py:117
  62.8 6.7 %collective-permute-start.5 = (f32[64,3,128]{2,0,1:T(8,128)S(1)}, f32[64,3,128]{2,0,1:T(8,128)S(1)}, u32[]{:S(2)}, u32[]{:S(2)}) collective-permute-start(f32[64,3,128]{2,0,1:T(8,128)S(1)} %convert_reduce_fusion), channel_id=1, source_target_pairs={{0,7},{1,0},{2,1},{3,2},{4,3},{5,4},{6,5},{7,6},{8,15},{9,8},{10,9... | collective-permute-start | bytes 294920 | tf_op jit(solution)/shard_map/ppermute | solution.py:120
  62.9 9.2 %collective-permute-start.6 = (f32[64,3,128]{2,0,1:T(8,128)S(1)}, f32[64,3,128]{2,0,1:T(8,128)S(1)}, u32[]{:S(2)}, u32[]{:S(2)}) collective-permute-start(f32[64,3,128]{2,0,1:T(8,128)S(1)} %convert_reduce_fusion), channel_id=1, source_target_pairs={{0,6},{1,7},{2,0},{3,1},{4,2},{5,3},{6,4},{7,5},{8,14},{9,15},{10,... | collective-permute-start | bytes 294920 | tf_op jit(solution)/shard_map/ppermute | solution.py:120
  65.8 7.5 %collective-permute-start.8 = (f32[64,3,128]{2,0,1:T(8,128)S(1)}, f32[64,3,128]{2,0,1:T(8,128)S(1)}, u32[]{:S(2)}, u32[]{:S(2)}) collective-permute-start(f32[64,3,128]{2,0,1:T(8,128)S(1)} %convert_reduce_fusion), channel_id=1, source_target_pairs={{0,1},{1,2},{2,3},{3,4},{4,5},{5,6},{6,7},{7,0},{8,9},{9,10},{10,1... | collective-permute-start | bytes 294920 | tf_op jit(solution)/shard_map/ppermute | solution.py:120
  66.2 17.9 %collective-permute-start.10 = (f32[64,3,128]{2,0,1:T(8,128)S(1)}, f32[64,3,128]{2,0,1:T(8,128)S(1)}, u32[]{:S(2)}, u32[]{:S(2)}) collective-permute-start(f32[64,3,128]{2,0,1:T(8,128)S(1)} %convert_reduce_fusion), channel_id=1, source_target_pairs={{0,2},{1,3},{2,4},{3,5},{4,6},{5,7},{6,0},{7,1},{8,10},{9,11},{10,... | collective-permute-start | bytes 294920 | tf_op jit(solution)/shard_map/ppermute | solution.py:120
  72.1 11.9 %collective-permute-start.7 = (f32[2,64,3,128]{3,1,2,0:T(8,128)S(1)}, f32[2,64,3,128]{3,1,2,0:T(8,128)S(1)}, u32[]{:S(2)}, u32[]{:S(2)}) collective-permute-start(f32[2,64,3,128]{3,1,2,0:T(8,128)S(1)} %pad_maximum_fusion.6), channel_id=1, source_target_pairs={{0,6},{1,7},{2,0},{3,1},{4,2},{5,3},{6,4},{7,5},{8,14},{9,15},{10,... | collective-permute-start | bytes 589832 | tf_op jit(solution)/shard_map/ppermute | solution.py:120
  73.4 10.6 %collective-permute-start.9 = (f32[64,3,128]{2,0,1:T(8,128)S(1)}, f32[64,3,128]{2,0,1:T(8,128)S(1)}, u32[]{:S(2)}, u32[]{:S(2)}) collective-permute-start(f32[64,3,128]{2,0,1:T(8,128)S(1)} %collective-permute-done.8), channel_id=1, source_target_pairs={{0,2},{1,3},{2,4},{3,5},{4,6},{5,7},{6,0},{7,1},{8,10},{9,11},{10,... | collective-permute-start | bytes 294920 | tf_op jit(solution)/shard_map/ppermute | solution.py:120
  84.9 7.8 %collective-permute-start.11 = (f32[6,64,128]{2,1,0:T(8,128)S(1)}, f32[6,64,128]{2,1,0:T(8,128)S(1)}, u32[]{:S(2)}, u32[]{:S(2)}) collective-permute-start(f32[6,64,128]{2,1,0:T(8,128)S(1)} %get-tuple-element.13), channel_id=1, source_target_pairs={{0,8},{8,16},{16,24},{24,0},{1,9},{9,17},{17,25},{25,1},{2,10},{10... | collective-permute-start | bytes 589832 | tf_op jit(solution)/shard_map/ppermute | solution.py:148
  85.8 9.3 %collective-permute-start.12 = (f32[6,64,128]{2,1,0:T(8,128)S(1)}, f32[6,64,128]{2,1,0:T(8,128)S(1)}, u32[]{:S(2)}, u32[]{:S(2)}) collective-permute-start(f32[6,64,128]{2,1,0:T(8,128)S(1)} %get-tuple-element.15), channel_id=1, source_target_pairs={{0,16},{8,24},{16,0},{24,8},{1,17},{9,25},{17,1},{25,9},{2,18},{10... | collective-permute-start | bytes 589832 | tf_op jit(solution)/shard_map/ppermute | solution.py:148
  88.1 9.9 %collective-permute-start.13 = (f32[6,64,128]{2,1,0:T(8,128)S(1)}, f32[6,64,128]{2,1,0:T(8,128)S(1)}, u32[]{:S(2)}, u32[]{:S(2)}) collective-permute-start(f32[6,64,128]{2,1,0:T(8,128)S(1)} %get-tuple-element.14), channel_id=1, source_target_pairs={{0,24},{8,0},{16,8},{24,16},{1,25},{9,1},{17,9},{25,17},{2,26},{10... | collective-permute-start | bytes 589832 | tf_op jit(solution)/shard_map/ppermute | solution.py:148

commit v11 on v10

--- a/solution.py
+++ b/solution.py
@@ -37,40 +37,36 @@
     inner = total // outer
     half = outer // 2 + 1
     xb = x.reshape(outer, inner, channels)
-    r = lax.broadcasted_iota(jnp.int32, (half, outer), 0)
-    b = lax.broadcasted_iota(jnp.int32, (half, outer), 1)
+    r = lax.broadcasted_iota(jnp.int32, (half, 2, outer), 0)
+    part = lax.broadcasted_iota(jnp.int32, (half, 2, outer), 1)
+    b = lax.broadcasted_iota(jnp.int32, (half, 2, outer), 2)
     ang1 = ((r * b) % outer).astype(jnp.float32) * (two_pi / outer)
-    basis1 = jnp.concatenate([jnp.cos(ang1), -jnp.sin(ang1)], axis=0)
+    basis1 = jnp.where(part == 0, jnp.cos(ang1), -jnp.sin(ang1)).reshape(2 * half, outer)
     z = jnp.einsum("rb,bac->rac", basis1, xb, precision=prec, preferred_element_type=jnp.float32)
-    zr, zi = z[:half], z[half:]
-    r2 = lax.broadcasted_iota(jnp.int32, (half, inner), 0)
-    a2 = lax.broadcasted_iota(jnp.int32, (half, inner), 1)
-    ang2 = ((r2 * a2) % total).astype(jnp.float32) * (two_pi / total)
-    dc = jnp.cos(ang2)[:, :, None]
-    ds = jnp.sin(ang2)[:, :, None]
-    wr = dc * zr + ds * zi
-    wi = dc * zi - ds * zr
+    z = z.reshape(half, 2, inner, channels)
     nj = (f0 + nbins + outer - 1) // outer + 1
-    j3 = lax.broadcasted_iota(jnp.int32, (nj, inner), 0)
-    a3 = lax.broadcasted_iota(jnp.int32, (nj, inner), 1)
-    ang3 = ((j3 * a3) % inner).astype(jnp.float32) * (two_pi / inner)
-    basis2 = jnp.concatenate([jnp.cos(ang3), jnp.sin(ang3)], axis=0)
-    u = jnp.einsum(
-        "ja,srac->sjrc", basis2, jnp.stack([wr, wi]), precision=prec,
-        preferred_element_type=jnp.float32,
-    )
-    u1, u4 = u[0, :nj], u[0, nj:]
-    u3, u2 = u[1, :nj], u[1, nj:]
-    dre, dim = u1 + u2, u3 - u4
-    cre, cim = u1 - u2, -u3 - u4
-    f = f0 + lax.broadcasted_iota(jnp.int32, (nbins, nj, half), 0)
-    jj = lax.broadcasted_iota(jnp.int32, (nbins, nj, half), 1)
-    rr = lax.broadcasted_iota(jnp.int32, (nbins, nj, half), 2)
-    direct = (f == outer * jj + rr)
-    conj = (f == outer * jj - rr) & (rr > 0) & (f % outer >= half)
-    pick = jnp.concatenate([direct, conj], axis=1).astype(jnp.float32).reshape(nbins, 2 * nj * half)
-    parts_re = jnp.concatenate([dre, cre], axis=0).reshape(2 * nj * half, channels)
-    parts_im = jnp.concatenate([dim, cim], axis=0).reshape(2 * nj * half, channels)
+    shape = (half, 2, nj, inner)
+    r2 = lax.broadcasted_iota(jnp.int32, shape, 0)
+    kind = lax.broadcasted_iota(jnp.int32, shape, 1)
+    j2 = lax.broadcasted_iota(jnp.int32, shape, 2)
+    a2 = lax.broadcasted_iota(jnp.int32, shape, 3)
+    freq = outer * j2 + jnp.where(kind == 0, r2, -r2)
+    ang2 = ((a2 * freq) % total).astype(jnp.float32) * (two_pi / total)
+    c, s = jnp.cos(ang2), jnp.sin(ang2)
+    direct = kind == 0
+    m_re = jnp.stack([c, jnp.where(direct, s, -s)], axis=3)
+    m_im = jnp.stack([-s, jnp.where(direct, c, -c)], axis=3)
+    m = jnp.concatenate([m_re, m_im], axis=1).reshape(half, 4 * nj, 2, inner)
+    u = jnp.einsum("rxpa,rpac->rxc", m, z, precision=prec, preferred_element_type=jnp.float32)
+    f = f0 + lax.broadcasted_iota(jnp.int32, (nbins, half, 2, nj), 0)
+    rr = lax.broadcasted_iota(jnp.int32, (nbins, half, 2, nj), 1)
+    kk = lax.broadcasted_iota(jnp.int32, (nbins, half, 2, nj), 2)
+    jj = lax.broadcasted_iota(jnp.int32, (nbins, half, 2, nj), 3)
+    hit_direct = (kk == 0) & (f == outer * jj + rr)
+    hit_conj = (kk == 1) & (f == outer * jj - rr) & (rr > 0) & (f % outer >= half)
+    pick = (hit_direct | hit_conj).astype(jnp.float32).reshape(nbins, half * 2 * nj)
+    parts_re = u[:, : 2 * nj].reshape(half * 2 * nj, channels)
+    parts_im = u[:, 2 * nj :].reshape(half * 2 * nj, channels)
     hi = lax.Precision.HIGHEST
     return jnp.dot(pick, parts_re, precision=hi), jnp.dot(pick, parts_im, precision=hi)
 

time: 99.4 us -> 98.2 us (0.988)
  other arithmetic: 12 us -> 9.2 us
  local copies, waits for them, and re-layouts: 2.24 us -> 3.43 us
    another operation x4 -> x2, other arithmetic: 9.53 us -> 5.01 us
    dot_general x1, matrix products: 6.09 us -> 8.13 us  [band_dft(): jnp.einsum('rxpa,rpac->rxc', m, z, precision=prec, preferred_element_type...]
    cos x0 -> x1, other arithmetic: none -> 1.73 us  [band_dft(): c, s = (jnp.cos(ang2), jnp.sin(ang2))]
where the time goes in v11:
time: 98.2 us; the launch traced here: 97.6 us
  waiting for transfers between devices  32.3 us (33%)
  starting transfers between devices  32.2 us (33%)
  matrix products  20 us (20%)
  other arithmetic  9.2 us (9%)
  local copies, waits for them, and re-layouts  3.43 us (3%)
    ppermute x2, starting transfers between devices, body(): received[shift] = lax.ppermute(white, ('cx', 'cz'), perm)  11.4 us
    ppermute x6, waiting for transfers between devices, shift_z(): return lax.ppermute(value, 'cz', [(k, (k - step) % nz) for k in range(nz)])  10.9 us
    ppermute x6, starting transfers between devices, shift_z(): return lax.ppermute(value, 'cz', [(k, (k - step) % nz) for k in range(nz)])  10.4 us
    ppermute x3, waiting for transfers between devices, body(): lax.ppermute(chunk, 'cx', [(k, (k + step) % nx) for k in range(nx)])  9.85 us
    all_to_all x1, waiting for transfers between devices, body(): corr = lax.all_to_all(corr.astype(jnp.bfloat16), 'win', 0, 0)  8.78 us
    dot_general x1, matrix products, band_dft(): jnp.einsum('rxpa,rpac->rxc', m, z, precision=prec, preferred_element_type...  8.13 us
    dot_general x1, matrix products, band_dft(): jnp.einsum('rb,bac->rac', basis1, xb, precision=prec, preferred_element_t...  8 us
    another operation x2, other arithmetic  5.01 us
  transfers between devices with their start and end apart: 15, of which 8 were waited for; matrix products, arithmetic and copies ran while one was open for 6% of the time, Pallas kernels for 0%

profile of v11, /device:TPU:6, one launch (start us, length us, event | category | flops | bytes accessed | tf_op | source)
XLA Modules:
  0.0 97.6 jit_solution(3620904313187897602)
XLA Ops:
  0.2 1.7 %fusion.59 = (f32[63,2,6,1,120]{4,0,3,2,1:T(8,128)S(1)}, f32[63,2,6,1,120]{4,0,3,2,1:T(8,128)S(1)}, f32[63,2,6,1,120]{4,0,3,2,1:T(8,128)S(1)}, f32[63,2,6,1,120]{4,0,3,2,1:T(8,128)S(1)}) fusion(s32[63]{0:T(128)S(1)} %iota_negate_fusion, pred[2]{0:T(512)(128)(4,1)S(1)} %iota_compare_fusion.4, s32[6]{0:T(128)S(1)} %iota_multiply_fusion), kind=kLoop, calls=%fused_computation.80 | loop fusion | flops 1360800 | bytes 1451798 | tf_op jit(solution)/shard_map/cos | solution.py:55
  1.9 8.0 %fusion = f32[63,2,120,128]{3,0,2,1:T(8,128)S(1)} fusion(f32[125,120,128]{2,1,0:T(8,128)} %bitcast.72, pred[2]{0:T(512)(128)(4,1)S(1)} %iota_compare_fusion.4), kind=kOutput, calls=%fused_computation.2 | convolution fusion | flops 1451693312 | bytes 15421442 | tf_op jit(solution)/shard_map/rb,bac->rac/dot_general | solution.py:45
  10.1 8.1 %fusion.13 = f32[63,24,128]{2,1,0:T(8,128)S(1)} fusion(f32[63,2,120,128]{3,0,2,1:T(8,128)S(1)} %fusion, f32[63,24,2,120]{3,0,2,1:T(8,128)S(1)} %bitcast.73), kind=kOutput, calls=%fused_computation.20 | convolution fusion | flops 278691840 | bytes 9967104 | tf_op jit(solution)/shard_map/rxpa,rpac->rxc/dot_general | solution.py:60
  19.4 1.0 fusion.6
  20.4 0.9 fusion.101
  21.3 0.9 fusion.100
  22.2 1.4 %fusion.54 = (bf16[512,128]{1,0:T(8,128)(2,1)S(1)}, bf16[512,128]{1,0:T(8,128)(2,1)S(1)}) fusion(f32[576,128]{1,0:T(8,128)S(1)} %fusion.100, f32[576,128]{1,0:T(8,128)S(1)} %fusion.101, s32[512]{0:T(512)S(1)} %get-tuple-element.28, f32[512]{0:T(512)S(1)} %multiply_sine_fusion), kind=kOutput, calls=%fused_computation.68 | convolution fusion | flops 454778880 | bytes 1380352 | tf_op jit(solution)/shard_map/dot_general | solution.py:78
  23.6 3.8 %collective-permute-start.3 = (bf16[2,512,128]{2,1,0:T(8,128)(2,1)S(1)}, bf16[2,512,128]{2,1,0:T(8,128)(2,1)S(1)}, u32[]{:S(2)}, u32[]{:S(2)}) collective-permute-start(bf16[2,512,128]{2,1,0:T(8,128)(2,1)S(1)} %pad_maximum_fusion.2), channel_id=1, source_target_pairs={{0,1},{1,2},{2,3},{3,4},{4,5},{5,6},{6,7},{7,8},{8,9},{9,10},{10,1... | collective-permute-start | bytes 786440 | tf_op jit(solution)/shard_map/ppermute | solution.py:106
  27.5 7.6 %collective-permute-start.4 = (bf16[2,512,128]{2,1,0:T(8,128)(2,1)S(1)}, bf16[2,512,128]{2,1,0:T(8,128)(2,1)S(1)}, u32[]{:S(2)}, u32[]{:S(2)}) collective-permute-start(bf16[2,512,128]{2,1,0:T(8,128)(2,1)S(1)} %pad_maximum_fusion.2), channel_id=1, source_target_pairs={{2,0},{3,1},{4,2},{5,3},{6,4},{7,5},{8,6},{9,7},{10,8},{11,9},{12,... | collective-permute-start | bytes 786440 | tf_op jit(solution)/shard_map/ppermute | solution.py:106
  35.1 2.6 %collective-permute-start.1 = (s32[6,2]{0,1:T(2,128)S(1)}, s32[6,2]{0,1:T(2,128)S(1)}, u32[]{:S(2)}, u32[]{:S(2)}) collective-permute-start(s32[6,2]{0,1:T(2,128)S(1)} %copy-done), channel_id=1, source_target_pairs={{0,16},{8,24},{16,0},{24,8},{1,17},{9,25},{17,1},{25,9},{2,18},{10... | collective-permute-start | bytes 152 | tf_op jit(solution)/shard_map/ppermute | solution.py:129
  37.7 4.7 %cosine_convert_fusion = (bf16[512,1,512]{2,0,1:T(8,128)(2,1)S(1)}, bf16[512,1,512]{2,0,1:T(8,128)(2,1)S(1)}) fusion(s32[512]{0:T(512)S(1)} %get-tuple-element.27, s32[512]{0:T(512)S(1)} %get-tuple-element.28), kind=kLoop, calls=%fused_computation.31 | loop fusion | flops 3145728 | bytes 1052672 | tf_op jit(solution)/shard_map/convert.10
  42.6 0.6 gather_fusion
  43.1 2.8 %collective-permute-done.4 = bf16[2,512,128]{2,1,0:T(8,128)(2,1)S(1)} collective-permute-done((bf16[2,512,128]{2,1,0:T(8,128)(2,1)S(1)}, bf16[2,512,128]{2,1,0:T(8,128)(2,1)S(1)}, u32[]{:S(2)}, u32[]{:S(2)}) %collective-permute-start.4) | collective-permute-done | bytes 262176 | tf_op jit(solution)/shard_map/ppermute | solution.py:106
  46.4 0.7 fusion.18
  47.2 0.8 copy.7
  47.9 4.5 %all-to-all-start = ((bf16[8,64,3,128]{3,1,2,0:T(8,128)(2,1)}), bf16[8,64,3,128]{3,1,2,0:T(8,128)(2,1)S(1)}, u32[]{:S(2)}, u32[]{:S(2)}) async-start(bf16[8,64,3,128]{3,1,2,0:T(8,128)(2,1)} %copy.7), calls=%async_computation | async-start | bytes 786432 | tf_op jit(solution)/shard_map/all_to_all | solution.py:113
  52.6 8.8 %all-to-all-done = bf16[8,64,3,128]{3,1,2,0:T(8,128)(2,1)S(1)} async-done(((bf16[8,64,3,128]{3,1,2,0:T(8,128)(2,1)}), bf16[8,64,3,128]{3,1,2,0:T(8,128)(2,1)S(1)}, u32[]{:S(2)}, u32[]{:S(2)}) %all-to-all-start) | async-done | bytes 393248 | tf_op jit(solution)/shard_map/all_to_all | solution.py:113
  61.7 2.9 %collective-permute-start.6 = (f32[64,3,128]{2,0,1:T(8,128)S(1)}, f32[64,3,128]{2,0,1:T(8,128)S(1)}, u32[]{:S(2)}, u32[]{:S(2)}) collective-permute-start(f32[64,3,128]{2,0,1:T(8,128)S(1)} %convert_reduce_fusion), channel_id=1, source_target_pairs={{0,6},{1,7},{2,0},{3,1},{4,2},{5,3},{6,4},{7,5},{8,14},{9,15},{10,... | collective-permute-start | bytes 294920 | tf_op jit(solution)/shard_map/ppermute | solution.py:116
  64.6 0.4 collective-permute-start.8
  65.0 1.8 %collective-permute-start.10 = (f32[64,3,128]{2,0,1:T(8,128)S(1)}, f32[64,3,128]{2,0,1:T(8,128)S(1)}, u32[]{:S(2)}, u32[]{:S(2)}) collective-permute-start(f32[64,3,128]{2,0,1:T(8,128)S(1)} %convert_reduce_fusion), channel_id=1, source_target_pairs={{0,2},{1,3},{2,4},{3,5},{4,6},{5,7},{6,0},{7,1},{8,10},{9,11},{10,... | collective-permute-start | bytes 294920 | tf_op jit(solution)/shard_map/ppermute | solution.py:116
  66.7 1.6 %collective-permute-done.5 = f32[64,3,128]{2,0,1:T(8,128)S(1)} collective-permute-done((f32[64,3,128]{2,0,1:T(8,128)S(1)}, f32[64,3,128]{2,0,1:T(8,128)S(1)}, u32[]{:S(2)}, u32[]{:S(2)}) %collective-permute-start.5) | collective-permute-done | bytes 98336 | tf_op jit(solution)/shard_map/ppermute | solution.py:116
  68.4 2.5 %collective-permute-done.6 = f32[64,3,128]{2,0,1:T(8,128)S(1)} collective-permute-done((f32[64,3,128]{2,0,1:T(8,128)S(1)}, f32[64,3,128]{2,0,1:T(8,128)S(1)}, u32[]{:S(2)}, u32[]{:S(2)}) %collective-permute-start.6) | collective-permute-done | bytes 98336 | tf_op jit(solution)/shard_map/ppermute | solution.py:116
  70.9 1.3 %collective-permute-start.7 = (f32[2,64,3,128]{3,1,2,0:T(8,128)S(1)}, f32[2,64,3,128]{3,1,2,0:T(8,128)S(1)}, u32[]{:S(2)}, u32[]{:S(2)}) collective-permute-start(f32[2,64,3,128]{3,1,2,0:T(8,128)S(1)} %pad_maximum_fusion.3), channel_id=1, source_target_pairs={{0,6},{1,7},{2,0},{3,1},{4,2},{5,3},{6,4},{7,5},{8,14},{9,15},{10,... | collective-permute-start | bytes 589832 | tf_op jit(solution)/shard_map/ppermute | solution.py:116
  72.2 3.8 %collective-permute-start.9 = (f32[64,3,128]{2,0,1:T(8,128)S(1)}, f32[64,3,128]{2,0,1:T(8,128)S(1)}, u32[]{:S(2)}, u32[]{:S(2)}) collective-permute-start(f32[64,3,128]{2,0,1:T(8,128)S(1)} %collective-permute-done.8), channel_id=1, source_target_pairs={{0,2},{1,3},{2,4},{3,5},{4,6},{5,7},{6,0},{7,1},{8,10},{9,11},{10,... | collective-permute-start | bytes 294920 | tf_op jit(solution)/shard_map/ppermute | solution.py:116
  76.0 6.7 %collective-permute-done.7 = f32[2,64,3,128]{3,1,2,0:T(8,128)S(1)} collective-permute-done((f32[2,64,3,128]{3,1,2,0:T(8,128)S(1)}, f32[2,64,3,128]{3,1,2,0:T(8,128)S(1)}, u32[]{:S(2)}, u32[]{:S(2)}) %collective-permute-start.7) | collective-permute-done | bytes 196640 | tf_op jit(solution)/shard_map/ppermute | solution.py:116
  82.9 0.7 gather_fusion.1
  83.7 0.9 collective-permute-start.11
  84.6 2.3 %collective-permute-start.12 = (f32[6,64,128]{2,1,0:T(8,128)S(1)}, f32[6,64,128]{2,1,0:T(8,128)S(1)}, u32[]{:S(2)}, u32[]{:S(2)}) collective-permute-start(f32[6,64,128]{2,1,0:T(8,128)S(1)} %get-tuple-element.9), channel_id=1, source_target_pairs={{0,16},{8,24},{16,0},{24,8},{1,17},{9,25},{17,1},{25,9},{2,18},{10... | collective-permute-start | bytes 589832 | tf_op jit(solution)/shard_map/ppermute | solution.py:144
  87.0 4.6 %collective-permute-done.11 = f32[6,64,128]{2,1,0:T(8,128)S(1)} collective-permute-done((f32[6,64,128]{2,1,0:T(8,128)S(1)}, f32[6,64,128]{2,1,0:T(8,128)S(1)}, u32[]{:S(2)}, u32[]{:S(2)}) %collective-permute-start.11) | collective-permute-done | bytes 196640 | tf_op jit(solution)/shard_map/ppermute | solution.py:144
  91.6 2.4 %collective-permute-done.12 = f32[6,64,128]{2,1,0:T(8,128)S(1)} collective-permute-done((f32[6,64,128]{2,1,0:T(8,128)S(1)}, f32[6,64,128]{2,1,0:T(8,128)S(1)}, u32[]{:S(2)}, u32[]{:S(2)}) %collective-permute-start.12) | collective-permute-done | bytes 196640 | tf_op jit(solution)/shard_map/ppermute | solution.py:144
  94.0 2.9 %collective-permute-done.13 = f32[6,64,128]{2,1,0:T(8,128)S(1)} collective-permute-done((f32[6,64,128]{2,1,0:T(8,128)S(1)}, f32[6,64,128]{2,1,0:T(8,128)S(1)}, u32[]{:S(2)}, u32[]{:S(2)}) %collective-permute-start.13) | collective-permute-done | bytes 196640 | tf_op jit(solution)/shard_map/ppermute | solution.py:144
  96.8 0.8 fusion.57
  (57 shorter events, 2.9 us)
Async XLA Ops:
  22.2 12.9 %copy-start = (s32[6,2]{0,1:T(2,128)S(1)}, s32[6,2]{0,1:T(2,128)}, u32[]{:S(2)}) copy-start(s32[6,2]{0,1:T(2,128)} %param.3) | copy-start | bytes 148
  23.6 19.5 %collective-permute-start.3 = (bf16[2,512,128]{2,1,0:T(8,128)(2,1)S(1)}, bf16[2,512,128]{2,1,0:T(8,128)(2,1)S(1)}, u32[]{:S(2)}, u32[]{:S(2)}) collective-permute-start(bf16[2,512,128]{2,1,0:T(8,128)(2,1)S(1)} %pad_maximum_fusion.2), channel_id=1, source_target_pairs={{0,1},{1,2},{2,3},{3,4},{4,5},{5,6},{6,7},{7,8},{8,9},{9,10},{10,1... | collective-permute-start | bytes 786440 | tf_op jit(solution)/shard_map/ppermute | solution.py:106
  27.5 18.5 %collective-permute-start.4 = (bf16[2,512,128]{2,1,0:T(8,128)(2,1)S(1)}, bf16[2,512,128]{2,1,0:T(8,128)(2,1)S(1)}, u32[]{:S(2)}, u32[]{:S(2)}) collective-permute-start(bf16[2,512,128]{2,1,0:T(8,128)(2,1)S(1)} %pad_maximum_fusion.2), channel_id=1, source_target_pairs={{2,0},{3,1},{4,2},{5,3},{6,4},{7,5},{8,6},{9,7},{10,8},{11,9},{12,... | collective-permute-start | bytes 786440 | tf_op jit(solution)/shard_map/ppermute | solution.py:106
  35.1 7.5 %collective-permute-start = (s32[6,2]{0,1:T(2,128)S(1)}, s32[6,2]{0,1:T(2,128)S(1)}, u32[]{:S(2)}, u32[]{:S(2)}) collective-permute-start(s32[6,2]{0,1:T(2,128)S(1)} %copy-done), channel_id=1, source_target_pairs={{0,8},{8,16},{16,24},{24,0},{1,9},{9,17},{17,25},{25,1},{2,10},{10... | collective-permute-start | bytes 152 | tf_op jit(solution)/shard_map/ppermute | solution.py:129
  35.1 7.4 %collective-permute-start.1 = (s32[6,2]{0,1:T(2,128)S(1)}, s32[6,2]{0,1:T(2,128)S(1)}, u32[]{:S(2)}, u32[]{:S(2)}) collective-permute-start(s32[6,2]{0,1:T(2,128)S(1)} %copy-done), channel_id=1, source_target_pairs={{0,16},{8,24},{16,0},{24,8},{1,17},{9,25},{17,1},{25,9},{2,18},{10... | collective-permute-start | bytes 152 | tf_op jit(solution)/shard_map/ppermute | solution.py:129
  37.7 4.8 %collective-permute-start.2 = (s32[6,2]{0,1:T(2,128)S(1)}, s32[6,2]{0,1:T(2,128)S(1)}, u32[]{:S(2)}, u32[]{:S(2)}) collective-permute-start(s32[6,2]{0,1:T(2,128)S(1)} %copy-done), channel_id=1, source_target_pairs={{0,24},{8,0},{16,8},{24,16},{1,25},{9,1},{17,9},{25,17},{2,26},{10... | collective-permute-start | bytes 152 | tf_op jit(solution)/shard_map/ppermute | solution.py:129
  47.9 13.4 %all-to-all-start = ((bf16[8,64,3,128]{3,1,2,0:T(8,128)(2,1)}), bf16[8,64,3,128]{3,1,2,0:T(8,128)(2,1)S(1)}, u32[]{:S(2)}, u32[]{:S(2)}) async-start(bf16[8,64,3,128]{3,1,2,0:T(8,128)(2,1)} %copy.7), calls=%async_computation | async-start | bytes 786432 | tf_op jit(solution)/shard_map/all_to_all | solution.py:113
  61.4 7.0 %collective-permute-start.5 = (f32[64,3,128]{2,0,1:T(8,128)S(1)}, f32[64,3,128]{2,0,1:T(8,128)S(1)}, u32[]{:S(2)}, u32[]{:S(2)}) collective-permute-start(f32[64,3,128]{2,0,1:T(8,128)S(1)} %convert_reduce_fusion), channel_id=1, source_target_pairs={{0,7},{1,0},{2,1},{3,2},{4,3},{5,4},{6,5},{7,6},{8,15},{9,8},{10,9... | collective-permute-start | bytes 294920 | tf_op jit(solution)/shard_map/ppermute | solution.py:116
  61.7 9.1 %collective-permute-start.6 = (f32[64,3,128]{2,0,1:T(8,128)S(1)}, f32[64,3,128]{2,0,1:T(8,128)S(1)}, u32[]{:S(2)}, u32[]{:S(2)}) collective-permute-start(f32[64,3,128]{2,0,1:T(8,128)S(1)} %convert_reduce_fusion), channel_id=1, source_target_pairs={{0,6},{1,7},{2,0},{3,1},{4,2},{5,3},{6,4},{7,5},{8,14},{9,15},{10,... | collective-permute-start | bytes 294920 | tf_op jit(solution)/shard_map/ppermute | solution.py:116
  64.6 7.6 %collective-permute-start.8 = (f32[64,3,128]{2,0,1:T(8,128)S(1)}, f32[64,3,128]{2,0,1:T(8,128)S(1)}, u32[]{:S(2)}, u32[]{:S(2)}) collective-permute-start(f32[64,3,128]{2,0,1:T(8,128)S(1)} %convert_reduce_fusion), channel_id=1, source_target_pairs={{0,1},{1,2},{2,3},{3,4},{4,5},{5,6},{6,7},{7,0},{8,9},{9,10},{10,1... | collective-permute-start | bytes 294920 | tf_op jit(solution)/shard_map/ppermute | solution.py:116
  65.0 17.8 %collective-permute-start.10 = (f32[64,3,128]{2,0,1:T(8,128)S(1)}, f32[64,3,128]{2,0,1:T(8,128)S(1)}, u32[]{:S(2)}, u32[]{:S(2)}) collective-permute-start(f32[64,3,128]{2,0,1:T(8,128)S(1)} %convert_reduce_fusion), channel_id=1, source_target_pairs={{0,2},{1,3},{2,4},{3,5},{4,6},{5,7},{6,0},{7,1},{8,10},{9,11},{10,... | collective-permute-start | bytes 294920 | tf_op jit(solution)/shard_map/ppermute | solution.py:116
  70.9 11.9 %collective-permute-start.7 = (f32[2,64,3,128]{3,1,2,0:T(8,128)S(1)}, f32[2,64,3,128]{3,1,2,0:T(8,128)S(1)}, u32[]{:S(2)}, u32[]{:S(2)}) collective-permute-start(f32[2,64,3,128]{3,1,2,0:T(8,128)S(1)} %pad_maximum_fusion.3), channel_id=1, source_target_pairs={{0,6},{1,7},{2,0},{3,1},{4,2},{5,3},{6,4},{7,5},{8,14},{9,15},{10,... | collective-permute-start | bytes 589832 | tf_op jit(solution)/shard_map/ppermute | solution.py:116
  72.2 10.6 %collective-permute-start.9 = (f32[64,3,128]{2,0,1:T(8,128)S(1)}, f32[64,3,128]{2,0,1:T(8,128)S(1)}, u32[]{:S(2)}, u32[]{:S(2)}) collective-permute-start(f32[64,3,128]{2,0,1:T(8,128)S(1)} %collective-permute-done.8), channel_id=1, source_target_pairs={{0,2},{1,3},{2,4},{3,5},{4,6},{5,7},{6,0},{7,1},{8,10},{9,11},{10,... | collective-permute-start | bytes 294920 | tf_op jit(solution)/shard_map/ppermute | solution.py:116
  83.7 7.8 %collective-permute-start.11 = (f32[6,64,128]{2,1,0:T(8,128)S(1)}, f32[6,64,128]{2,1,0:T(8,128)S(1)}, u32[]{:S(2)}, u32[]{:S(2)}) collective-permute-start(f32[6,64,128]{2,1,0:T(8,128)S(1)} %get-tuple-element.7), channel_id=1, source_target_pairs={{0,8},{8,16},{16,24},{24,0},{1,9},{9,17},{17,25},{25,1},{2,10},{10... | collective-permute-start | bytes 589832 | tf_op jit(solution)/shard_map/ppermute | solution.py:144
  84.6 9.3 %collective-permute-start.12 = (f32[6,64,128]{2,1,0:T(8,128)S(1)}, f32[6,64,128]{2,1,0:T(8,128)S(1)}, u32[]{:S(2)}, u32[]{:S(2)}) collective-permute-start(f32[6,64,128]{2,1,0:T(8,128)S(1)} %get-tuple-element.9), channel_id=1, source_target_pairs={{0,16},{8,24},{16,0},{24,8},{1,17},{9,25},{17,1},{25,9},{2,18},{10... | collective-permute-start | bytes 589832 | tf_op jit(solution)/shard_map/ppermute | solution.py:144
  87.0 9.9 %collective-permute-start.13 = (f32[6,64,128]{2,1,0:T(8,128)S(1)}, f32[6,64,128]{2,1,0:T(8,128)S(1)}, u32[]{:S(2)}, u32[]{:S(2)}) collective-permute-start(f32[6,64,128]{2,1,0:T(8,128)S(1)} %get-tuple-element.8), channel_id=1, source_target_pairs={{0,24},{8,0},{16,8},{24,16},{1,25},{9,1},{17,9},{25,17},{2,26},{10... | collective-permute-start | bytes 589832 | tf_op jit(solution)/shard_map/ppermute | solution.py:144

commit v12 on v11

--- a/solution.py
+++ b/solution.py
@@ -44,13 +44,13 @@
     basis1 = jnp.where(part == 0, jnp.cos(ang1), -jnp.sin(ang1)).reshape(2 * half, outer)
     z = jnp.einsum("rb,bac->rac", basis1, xb, precision=prec, preferred_element_type=jnp.float32)
     z = z.reshape(half, 2, inner, channels)
-    nj = (f0 + nbins + outer - 1) // outer + 1
+    nj = (f0 + nbins + outer - 1) // outer
     shape = (half, 2, nj, inner)
     r2 = lax.broadcasted_iota(jnp.int32, shape, 0)
     kind = lax.broadcasted_iota(jnp.int32, shape, 1)
     j2 = lax.broadcasted_iota(jnp.int32, shape, 2)
     a2 = lax.broadcasted_iota(jnp.int32, shape, 3)
-    freq = outer * j2 + jnp.where(kind == 0, r2, -r2)
+    freq = outer * (j2 + kind) + jnp.where(kind == 0, r2, -r2)
     ang2 = ((a2 * freq) % total).astype(jnp.float32) * (two_pi / total)
     c, s = jnp.cos(ang2), jnp.sin(ang2)
     direct = kind == 0
@@ -63,7 +63,7 @@
     kk = lax.broadcasted_iota(jnp.int32, (nbins, half, 2, nj), 2)
     jj = lax.broadcasted_iota(jnp.int32, (nbins, half, 2, nj), 3)
     hit_direct = (kk == 0) & (f == outer * jj + rr)
-    hit_conj = (kk == 1) & (f == outer * jj - rr) & (rr > 0) & (f % outer >= half)
+    hit_conj = (kk == 1) & (f == outer * (jj + 1) - rr) & (rr > 0) & (f % outer >= half)
     pick = (hit_direct | hit_conj).astype(jnp.float32).reshape(nbins, half * 2 * nj)
     parts_re = u[:, : 2 * nj].reshape(half * 2 * nj, channels)
     parts_im = u[:, 2 * nj :].reshape(half * 2 * nj, channels)

time: 98.2 us -> 97.7 us (level)
  no operation moved by 1% of the time
where the time goes in v12:
time: 97.7 us; the launch traced here: 97.1 us
  waiting for transfers between devices  32.3 us (33%)
  starting transfers between devices  32.2 us (33%)
  matrix products  19.5 us (20%)
  other arithmetic  8.86 us (9%)
  local copies, waits for them, and re-layouts  3.74 us (4%)
    ppermute x2, starting transfers between devices, body(): received[shift] = lax.ppermute(white, ('cx', 'cz'), perm)  11.4 us
    ppermute x6, waiting for transfers between devices, shift_z(): return lax.ppermute(value, 'cz', [(k, (k - step) % nz) for k in range(nz)])  10.9 us
    ppermute x6, starting transfers between devices, shift_z(): return lax.ppermute(value, 'cz', [(k, (k - step) % nz) for k in range(nz)])  10.4 us
    ppermute x3, waiting for transfers between devices, body(): lax.ppermute(chunk, 'cx', [(k, (k + step) % nx) for k in range(nx)])  9.84 us
    all_to_all x1, waiting for transfers between devices, body(): corr = lax.all_to_all(corr.astype(jnp.bfloat16), 'win', 0, 0)  8.78 us
    dot_general x1, matrix products, band_dft(): jnp.einsum('rb,bac->rac', basis1, xb, precision=prec, preferred_element_t...  8 us
    dot_general x1, matrix products, band_dft(): jnp.einsum('rxpa,rpac->rxc', m, z, precision=prec, preferred_element_type...  7.93 us
    another operation x2, other arithmetic  5.01 us
  transfers between devices with their start and end apart: 15, of which 8 were waited for; matrix products, arithmetic and copies ran while one was open for 6% of the time, Pallas kernels for 0%

profile of v12, /device:TPU:6, one launch (start us, length us, event | category | flops | bytes accessed | tf_op | source)
XLA Modules:
  0.0 97.1 jit_solution(14591443697060071848)
XLA Ops:
  0.2 1.5 %fusion.59 = (f32[63,2,5,1,120]{4,0,3,2,1:T(8,128)S(1)}, f32[63,2,5,1,120]{4,0,3,2,1:T(8,128)S(1)}, f32[63,2,5,1,120]{4,0,3,2,1:T(8,128)S(1)}, f32[63,2,5,1,120]{4,0,3,2,1:T(8,128)S(1)}) fusion(s32[63]{0:T(128)S(1)} %iota_negate_fusion, pred[2]{0:T(512)(128)(4,1)S(1)} %iota_compare_fusion.4), kind=kLoop, calls=%fused_computation.80 | loop fusion | flops 1285200 | bytes 1209854 | tf_op jit(solution)/shard_map/cos | solution.py:55
  1.6 8.0 %fusion = f32[63,2,120,128]{3,0,2,1:T(8,128)S(1)} fusion(f32[125,120,128]{2,1,0:T(8,128)} %bitcast.72, pred[2]{0:T(512)(128)(4,1)S(1)} %iota_compare_fusion.4), kind=kOutput, calls=%fused_computation.2 | convolution fusion | flops 1451693312 | bytes 15421442 | tf_op jit(solution)/shard_map/rb,bac->rac/dot_general | solution.py:45
  9.8 7.9 %fusion.13 = f32[63,20,128]{2,1,0:T(8,128)S(1)} fusion(f32[63,2,120,128]{3,0,2,1:T(8,128)S(1)} %fusion, f32[63,20,2,120]{3,0,2,1:T(8,128)S(1)} %bitcast.73), kind=kOutput, calls=%fused_computation.20 | convolution fusion | flops 232243200 | bytes 9596160 | tf_op jit(solution)/shard_map/rxpa,rpac->rxc/dot_general | solution.py:60
  19.3 0.8 fusion.7
  20.2 0.7 fusion.102
  20.9 0.7 fusion.101
  21.7 1.4 %fusion.54 = (bf16[512,128]{1,0:T(8,128)(2,1)S(1)}, bf16[512,128]{1,0:T(8,128)(2,1)S(1)}) fusion(f32[576,128]{1,0:T(8,128)S(1)} %fusion.101, f32[576,128]{1,0:T(8,128)S(1)} %fusion.102, s32[512]{0:T(512)S(1)} %get-tuple-element.26, f32[512]{0:T(512)S(1)} %multiply_sine_fusion), kind=kOutput, calls=%fused_computation.68 | convolution fusion | flops 454778880 | bytes 1380352 | tf_op jit(solution)/shard_map/dot_general | solution.py:78
  23.1 3.8 %collective-permute-start.3 = (bf16[2,512,128]{2,1,0:T(8,128)(2,1)S(1)}, bf16[2,512,128]{2,1,0:T(8,128)(2,1)S(1)}, u32[]{:S(2)}, u32[]{:S(2)}) collective-permute-start(bf16[2,512,128]{2,1,0:T(8,128)(2,1)S(1)} %pad_maximum_fusion.2), channel_id=1, source_target_pairs={{0,1},{1,2},{2,3},{3,4},{4,5},{5,6},{6,7},{7,8},{8,9},{9,10},{10,1... | collective-permute-start | bytes 786440 | tf_op jit(solution)/shard_map/ppermute | solution.py:106
  27.0 7.6 %collective-permute-start.4 = (bf16[2,512,128]{2,1,0:T(8,128)(2,1)S(1)}, bf16[2,512,128]{2,1,0:T(8,128)(2,1)S(1)}, u32[]{:S(2)}, u32[]{:S(2)}) collective-permute-start(bf16[2,512,128]{2,1,0:T(8,128)(2,1)S(1)} %pad_maximum_fusion.2), channel_id=1, source_target_pairs={{2,0},{3,1},{4,2},{5,3},{6,4},{7,5},{8,6},{9,7},{10,8},{11,9},{12,... | collective-permute-start | bytes 786440 | tf_op jit(solution)/shard_map/ppermute | solution.py:106
  34.7 2.6 %collective-permute-start.1 = (s32[6,2]{0,1:T(2,128)S(1)}, s32[6,2]{0,1:T(2,128)S(1)}, u32[]{:S(2)}, u32[]{:S(2)}) collective-permute-start(s32[6,2]{0,1:T(2,128)S(1)} %copy-done), channel_id=1, source_target_pairs={{0,16},{8,24},{16,0},{24,8},{1,17},{9,25},{17,1},{25,9},{2,18},{10... | collective-permute-start | bytes 152 | tf_op jit(solution)/shard_map/ppermute | solution.py:129
  37.2 4.7 %cosine_convert_fusion = (bf16[512,1,512]{2,0,1:T(8,128)(2,1)S(1)}, bf16[512,1,512]{2,0,1:T(8,128)(2,1)S(1)}) fusion(s32[512]{0:T(512)S(1)} %get-tuple-element.25, s32[512]{0:T(512)S(1)} %get-tuple-element.26), kind=kLoop, calls=%fused_computation.31 | loop fusion | flops 3145728 | bytes 1052672 | tf_op jit(solution)/shard_map/convert.10
  42.1 0.6 gather_fusion
  42.6 2.8 %collective-permute-done.4 = bf16[2,512,128]{2,1,0:T(8,128)(2,1)S(1)} collective-permute-done((bf16[2,512,128]{2,1,0:T(8,128)(2,1)S(1)}, bf16[2,512,128]{2,1,0:T(8,128)(2,1)S(1)}, u32[]{:S(2)}, u32[]{:S(2)}) %collective-permute-start.4) | collective-permute-done | bytes 262176 | tf_op jit(solution)/shard_map/ppermute | solution.py:106
  45.9 0.7 fusion.18
  46.7 0.8 copy.7
  47.4 4.5 %all-to-all-start = ((bf16[8,64,3,128]{3,1,2,0:T(8,128)(2,1)}), bf16[8,64,3,128]{3,1,2,0:T(8,128)(2,1)S(1)}, u32[]{:S(2)}, u32[]{:S(2)}) async-start(bf16[8,64,3,128]{3,1,2,0:T(8,128)(2,1)} %copy.7), calls=%async_computation | async-start | bytes 786432 | tf_op jit(solution)/shard_map/all_to_all | solution.py:113
  52.1 8.8 %all-to-all-done = bf16[8,64,3,128]{3,1,2,0:T(8,128)(2,1)S(1)} async-done(((bf16[8,64,3,128]{3,1,2,0:T(8,128)(2,1)}), bf16[8,64,3,128]{3,1,2,0:T(8,128)(2,1)S(1)}, u32[]{:S(2)}, u32[]{:S(2)}) %all-to-all-start) | async-done | bytes 393248 | tf_op jit(solution)/shard_map/all_to_all | solution.py:113
  61.2 2.9 %collective-permute-start.6 = (f32[64,3,128]{2,0,1:T(8,128)S(1)}, f32[64,3,128]{2,0,1:T(8,128)S(1)}, u32[]{:S(2)}, u32[]{:S(2)}) collective-permute-start(f32[64,3,128]{2,0,1:T(8,128)S(1)} %convert_reduce_fusion), channel_id=1, source_target_pairs={{0,6},{1,7},{2,0},{3,1},{4,2},{5,3},{6,4},{7,5},{8,14},{9,15},{10,... | collective-permute-start | bytes 294920 | tf_op jit(solution)/shard_map/ppermute | solution.py:116
  64.1 0.4 collective-permute-start.8
  64.5 1.8 %collective-permute-start.10 = (f32[64,3,128]{2,0,1:T(8,128)S(1)}, f32[64,3,128]{2,0,1:T(8,128)S(1)}, u32[]{:S(2)}, u32[]{:S(2)}) collective-permute-start(f32[64,3,128]{2,0,1:T(8,128)S(1)} %convert_reduce_fusion), channel_id=1, source_target_pairs={{0,2},{1,3},{2,4},{3,5},{4,6},{5,7},{6,0},{7,1},{8,10},{9,11},{10,... | collective-permute-start | bytes 294920 | tf_op jit(solution)/shard_map/ppermute | solution.py:116
  66.3 1.7 %collective-permute-done.5 = f32[64,3,128]{2,0,1:T(8,128)S(1)} collective-permute-done((f32[64,3,128]{2,0,1:T(8,128)S(1)}, f32[64,3,128]{2,0,1:T(8,128)S(1)}, u32[]{:S(2)}, u32[]{:S(2)}) %collective-permute-start.5) | collective-permute-done | bytes 98336 | tf_op jit(solution)/shard_map/ppermute | solution.py:116
  67.9 2.4 %collective-permute-done.6 = f32[64,3,128]{2,0,1:T(8,128)S(1)} collective-permute-done((f32[64,3,128]{2,0,1:T(8,128)S(1)}, f32[64,3,128]{2,0,1:T(8,128)S(1)}, u32[]{:S(2)}, u32[]{:S(2)}) %collective-permute-start.6) | collective-permute-done | bytes 98336 | tf_op jit(solution)/shard_map/ppermute | solution.py:116
  70.4 1.3 %collective-permute-start.7 = (f32[2,64,3,128]{3,1,2,0:T(8,128)S(1)}, f32[2,64,3,128]{3,1,2,0:T(8,128)S(1)}, u32[]{:S(2)}, u32[]{:S(2)}) collective-permute-start(f32[2,64,3,128]{3,1,2,0:T(8,128)S(1)} %pad_maximum_fusion.3), channel_id=1, source_target_pairs={{0,6},{1,7},{2,0},{3,1},{4,2},{5,3},{6,4},{7,5},{8,14},{9,15},{10,... | collective-permute-start | bytes 589832 | tf_op jit(solution)/shard_map/ppermute | solution.py:116
  71.7 3.8 %collective-permute-start.9 = (f32[64,3,128]{2,0,1:T(8,128)S(1)}, f32[64,3,128]{2,0,1:T(8,128)S(1)}, u32[]{:S(2)}, u32[]{:S(2)}) collective-permute-start(f32[64,3,128]{2,0,1:T(8,128)S(1)} %collective-permute-done.8), channel_id=1, source_target_pairs={{0,2},{1,3},{2,4},{3,5},{4,6},{5,7},{6,0},{7,1},{8,10},{9,11},{10,... | collective-permute-start | bytes 294920 | tf_op jit(solution)/shard_map/ppermute | solution.py:116
  75.5 6.7 %collective-permute-done.7 = f32[2,64,3,128]{3,1,2,0:T(8,128)S(1)} collective-permute-done((f32[2,64,3,128]{3,1,2,0:T(8,128)S(1)}, f32[2,64,3,128]{3,1,2,0:T(8,128)S(1)}, u32[]{:S(2)}, u32[]{:S(2)}) %collective-permute-start.7) | collective-permute-done | bytes 196640 | tf_op jit(solution)/shard_map/ppermute | solution.py:116
  82.4 0.7 gather_fusion.1
  83.2 0.9 collective-permute-start.11
  84.2 2.3 %collective-permute-start.12 = (f32[6,64,128]{2,1,0:T(8,128)S(1)}, f32[6,64,128]{2,1,0:T(8,128)S(1)}, u32[]{:S(2)}, u32[]{:S(2)}) collective-permute-start(f32[6,64,128]{2,1,0:T(8,128)S(1)} %get-tuple-element.9), channel_id=1, source_target_pairs={{0,16},{8,24},{16,0},{24,8},{1,17},{9,25},{17,1},{25,9},{2,18},{10... | collective-permute-start | bytes 589832 | tf_op jit(solution)/shard_map/ppermute | solution.py:144
  86.5 4.6 %collective-permute-done.11 = f32[6,64,128]{2,1,0:T(8,128)S(1)} collective-permute-done((f32[6,64,128]{2,1,0:T(8,128)S(1)}, f32[6,64,128]{2,1,0:T(8,128)S(1)}, u32[]{:S(2)}, u32[]{:S(2)}) %collective-permute-start.11) | collective-permute-done | bytes 196640 | tf_op jit(solution)/shard_map/ppermute | solution.py:144
  91.1 2.4 %collective-permute-done.12 = f32[6,64,128]{2,1,0:T(8,128)S(1)} collective-permute-done((f32[6,64,128]{2,1,0:T(8,128)S(1)}, f32[6,64,128]{2,1,0:T(8,128)S(1)}, u32[]{:S(2)}, u32[]{:S(2)}) %collective-permute-start.12) | collective-permute-done | bytes 196640 | tf_op jit(solution)/shard_map/ppermute | solution.py:144
  93.5 2.8 %collective-permute-done.13 = f32[6,64,128]{2,1,0:T(8,128)S(1)} collective-permute-done((f32[6,64,128]{2,1,0:T(8,128)S(1)}, f32[6,64,128]{2,1,0:T(8,128)S(1)}, u32[]{:S(2)}, u32[]{:S(2)}) %collective-permute-start.13) | collective-permute-done | bytes 196640 | tf_op jit(solution)/shard_map/ppermute | solution.py:144
  96.3 0.8 fusion.57
  (59 shorter events, 3.2 us)
Async XLA Ops:
  21.7 12.9 %copy-start = (s32[6,2]{0,1:T(2,128)S(1)}, s32[6,2]{0,1:T(2,128)}, u32[]{:S(2)}) copy-start(s32[6,2]{0,1:T(2,128)} %param.3) | copy-start | bytes 148
  23.1 19.5 %collective-permute-start.3 = (bf16[2,512,128]{2,1,0:T(8,128)(2,1)S(1)}, bf16[2,512,128]{2,1,0:T(8,128)(2,1)S(1)}, u32[]{:S(2)}, u32[]{:S(2)}) collective-permute-start(bf16[2,512,128]{2,1,0:T(8,128)(2,1)S(1)} %pad_maximum_fusion.2), channel_id=1, source_target_pairs={{0,1},{1,2},{2,3},{3,4},{4,5},{5,6},{6,7},{7,8},{8,9},{9,10},{10,1... | collective-permute-start | bytes 786440 | tf_op jit(solution)/shard_map/ppermute | solution.py:106
  27.0 18.5 %collective-permute-start.4 = (bf16[2,512,128]{2,1,0:T(8,128)(2,1)S(1)}, bf16[2,512,128]{2,1,0:T(8,128)(2,1)S(1)}, u32[]{:S(2)}, u32[]{:S(2)}) collective-permute-start(bf16[2,512,128]{2,1,0:T(8,128)(2,1)S(1)} %pad_maximum_fusion.2), channel_id=1, source_target_pairs={{2,0},{3,1},{4,2},{5,3},{6,4},{7,5},{8,6},{9,7},{10,8},{11,9},{12,... | collective-permute-start | bytes 786440 | tf_op jit(solution)/shard_map/ppermute | solution.py:106
  34.6 7.5 %collective-permute-start = (s32[6,2]{0,1:T(2,128)S(1)}, s32[6,2]{0,1:T(2,128)S(1)}, u32[]{:S(2)}, u32[]{:S(2)}) collective-permute-start(s32[6,2]{0,1:T(2,128)S(1)} %copy-done), channel_id=1, source_target_pairs={{0,8},{8,16},{16,24},{24,0},{1,9},{9,17},{17,25},{25,1},{2,10},{10... | collective-permute-start | bytes 152 | tf_op jit(solution)/shard_map/ppermute | solution.py:129
  34.7 7.4 %collective-permute-start.1 = (s32[6,2]{0,1:T(2,128)S(1)}, s32[6,2]{0,1:T(2,128)S(1)}, u32[]{:S(2)}, u32[]{:S(2)}) collective-permute-start(s32[6,2]{0,1:T(2,128)S(1)} %copy-done), channel_id=1, source_target_pairs={{0,16},{8,24},{16,0},{24,8},{1,17},{9,25},{17,1},{25,9},{2,18},{10... | collective-permute-start | bytes 152 | tf_op jit(solution)/shard_map/ppermute | solution.py:129
  37.2 4.8 %collective-permute-start.2 = (s32[6,2]{0,1:T(2,128)S(1)}, s32[6,2]{0,1:T(2,128)S(1)}, u32[]{:S(2)}, u32[]{:S(2)}) collective-permute-start(s32[6,2]{0,1:T(2,128)S(1)} %copy-done), channel_id=1, source_target_pairs={{0,24},{8,0},{16,8},{24,16},{1,25},{9,1},{17,9},{25,17},{2,26},{10... | collective-permute-start | bytes 152 | tf_op jit(solution)/shard_map/ppermute | solution.py:129
  47.4 13.4 %all-to-all-start = ((bf16[8,64,3,128]{3,1,2,0:T(8,128)(2,1)}), bf16[8,64,3,128]{3,1,2,0:T(8,128)(2,1)S(1)}, u32[]{:S(2)}, u32[]{:S(2)}) async-start(bf16[8,64,3,128]{3,1,2,0:T(8,128)(2,1)} %copy.7), calls=%async_computation | async-start | bytes 786432 | tf_op jit(solution)/shard_map/all_to_all | solution.py:113
  60.9 7.0 %collective-permute-start.5 = (f32[64,3,128]{2,0,1:T(8,128)S(1)}, f32[64,3,128]{2,0,1:T(8,128)S(1)}, u32[]{:S(2)}, u32[]{:S(2)}) collective-permute-start(f32[64,3,128]{2,0,1:T(8,128)S(1)} %convert_reduce_fusion), channel_id=1, source_target_pairs={{0,7},{1,0},{2,1},{3,2},{4,3},{5,4},{6,5},{7,6},{8,15},{9,8},{10,9... | collective-permute-start | bytes 294920 | tf_op jit(solution)/shard_map/ppermute | solution.py:116
  61.2 9.1 %collective-permute-start.6 = (f32[64,3,128]{2,0,1:T(8,128)S(1)}, f32[64,3,128]{2,0,1:T(8,128)S(1)}, u32[]{:S(2)}, u32[]{:S(2)}) collective-permute-start(f32[64,3,128]{2,0,1:T(8,128)S(1)} %convert_reduce_fusion), channel_id=1, source_target_pairs={{0,6},{1,7},{2,0},{3,1},{4,2},{5,3},{6,4},{7,5},{8,14},{9,15},{10,... | collective-permute-start | bytes 294920 | tf_op jit(solution)/shard_map/ppermute | solution.py:116
  64.1 7.5 %collective-permute-start.8 = (f32[64,3,128]{2,0,1:T(8,128)S(1)}, f32[64,3,128]{2,0,1:T(8,128)S(1)}, u32[]{:S(2)}, u32[]{:S(2)}) collective-permute-start(f32[64,3,128]{2,0,1:T(8,128)S(1)} %convert_reduce_fusion), channel_id=1, source_target_pairs={{0,1},{1,2},{2,3},{3,4},{4,5},{5,6},{6,7},{7,0},{8,9},{9,10},{10,1... | collective-permute-start | bytes 294920 | tf_op jit(solution)/shard_map/ppermute | solution.py:116
  64.5 17.8 %collective-permute-start.10 = (f32[64,3,128]{2,0,1:T(8,128)S(1)}, f32[64,3,128]{2,0,1:T(8,128)S(1)}, u32[]{:S(2)}, u32[]{:S(2)}) collective-permute-start(f32[64,3,128]{2,0,1:T(8,128)S(1)} %convert_reduce_fusion), channel_id=1, source_target_pairs={{0,2},{1,3},{2,4},{3,5},{4,6},{5,7},{6,0},{7,1},{8,10},{9,11},{10,... | collective-permute-start | bytes 294920 | tf_op jit(solution)/shard_map/ppermute | solution.py:116
  70.4 11.9 %collective-permute-start.7 = (f32[2,64,3,128]{3,1,2,0:T(8,128)S(1)}, f32[2,64,3,128]{3,1,2,0:T(8,128)S(1)}, u32[]{:S(2)}, u32[]{:S(2)}) collective-permute-start(f32[2,64,3,128]{3,1,2,0:T(8,128)S(1)} %pad_maximum_fusion.3), channel_id=1, source_target_pairs={{0,6},{1,7},{2,0},{3,1},{4,2},{5,3},{6,4},{7,5},{8,14},{9,15},{10,... | collective-permute-start | bytes 589832 | tf_op jit(solution)/shard_map/ppermute | solution.py:116
  71.7 10.6 %collective-permute-start.9 = (f32[64,3,128]{2,0,1:T(8,128)S(1)}, f32[64,3,128]{2,0,1:T(8,128)S(1)}, u32[]{:S(2)}, u32[]{:S(2)}) collective-permute-start(f32[64,3,128]{2,0,1:T(8,128)S(1)} %collective-permute-done.8), channel_id=1, source_target_pairs={{0,2},{1,3},{2,4},{3,5},{4,6},{5,7},{6,0},{7,1},{8,10},{9,11},{10,... | collective-permute-start | bytes 294920 | tf_op jit(solution)/shard_map/ppermute | solution.py:116
  83.2 7.8 %collective-permute-start.11 = (f32[6,64,128]{2,1,0:T(8,128)S(1)}, f32[6,64,128]{2,1,0:T(8,128)S(1)}, u32[]{:S(2)}, u32[]{:S(2)}) collective-permute-start(f32[6,64,128]{2,1,0:T(8,128)S(1)} %get-tuple-element.7), channel_id=1, source_target_pairs={{0,8},{8,16},{16,24},{24,0},{1,9},{9,17},{17,25},{25,1},{2,10},{10... | collective-permute-start | bytes 589832 | tf_op jit(solution)/shard_map/ppermute | solution.py:144
  84.2 9.3 %collective-permute-start.12 = (f32[6,64,128]{2,1,0:T(8,128)S(1)}, f32[6,64,128]{2,1,0:T(8,128)S(1)}, u32[]{:S(2)}, u32[]{:S(2)}) collective-permute-start(f32[6,64,128]{2,1,0:T(8,128)S(1)} %get-tuple-element.9), channel_id=1, source_target_pairs={{0,16},{8,24},{16,0},{24,8},{1,17},{9,25},{17,1},{25,9},{2,18},{10... | collective-permute-start | bytes 589832 | tf_op jit(solution)/shard_map/ppermute | solution.py:144
  86.5 9.9 %collective-permute-start.13 = (f32[6,64,128]{2,1,0:T(8,128)S(1)}, f32[6,64,128]{2,1,0:T(8,128)S(1)}, u32[]{:S(2)}, u32[]{:S(2)}) collective-permute-start(f32[6,64,128]{2,1,0:T(8,128)S(1)} %get-tuple-element.8), channel_id=1, source_target_pairs={{0,24},{8,0},{16,8},{24,16},{1,25},{9,1},{17,9},{25,17},{2,26},{10... | collective-permute-start | bytes 589832 | tf_op jit(solution)/shard_map/ppermute | solution.py:144

commit v13 on v12

--- a/solution.py
+++ b/solution.py
@@ -65,10 +65,9 @@
     hit_direct = (kk == 0) & (f == outer * jj + rr)
     hit_conj = (kk == 1) & (f == outer * (jj + 1) - rr) & (rr > 0) & (f % outer >= half)
     pick = (hit_direct | hit_conj).astype(jnp.float32).reshape(nbins, half * 2 * nj)
-    parts_re = u[:, : 2 * nj].reshape(half * 2 * nj, channels)
-    parts_im = u[:, 2 * nj :].reshape(half * 2 * nj, channels)
-    hi = lax.Precision.HIGHEST
-    return jnp.dot(pick, parts_re, precision=hi), jnp.dot(pick, parts_im, precision=hi)
+    parts = jnp.concatenate([u[:, : 2 * nj], u[:, 2 * nj :]], axis=-1)
+    both = jnp.dot(pick, parts.reshape(half * 2 * nj, 2 * channels), precision=lax.Precision.HIGHEST)
+    return both[:, :channels], both[:, channels:]
 
 
 def whiten_local(trace, smoother, taper):

time: 97.7 us -> 96.6 us (0.989)
  waiting for transfers between devices: 32.3 us -> 31.1 us
where the time goes in v13:
time: 96.6 us; the launch traced here: 95.7 us
  starting transfers between devices  33 us (34%)
  waiting for transfers between devices  31.1 us (32%)
  matrix products  19.4 us (20%)
  other arithmetic  8.11 us (8%)
  local copies, waits for them, and re-layouts  3.76 us (4%)
    ppermute x2, starting transfers between devices, body(): received[shift] = lax.ppermute(white, ('cx', 'cz'), perm)  11.4 us
    ppermute x6, starting transfers between devices, shift_z(): return lax.ppermute(value, 'cz', [(k, (k - step) % nz) for k in range(nz)])  11.1 us
    ppermute x6, waiting for transfers between devices, shift_z(): return lax.ppermute(value, 'cz', [(k, (k - step) % nz) for k in range(nz)])  10.3 us
    ppermute x3, waiting for transfers between devices, body(): lax.ppermute(chunk, 'cx', [(k, (k + step) % nx) for k in range(nx)])  9.19 us
    all_to_all x1, waiting for transfers between devices, body(): corr = lax.all_to_all(corr.astype(jnp.bfloat16), 'win', 0, 0)  8.78 us
    dot_general x1, matrix products, band_dft(): jnp.einsum('rb,bac->rac', basis1, xb, precision=prec, preferred_element_t...  8 us
    dot_general x1, matrix products, band_dft(): jnp.einsum('rxpa,rpac->rxc', m, z, precision=prec, preferred_element_type...  7.93 us
    another operation x2, other arithmetic  5.01 us
  transfers between devices with their start and end apart: 15, of which 8 were waited for; matrix products, arithmetic and copies ran while one was open for 6% of the time, Pallas kernels for 0%

profile of v13, /device:TPU:6, one launch (start us, length us, event | category | flops | bytes accessed | tf_op | source)
XLA Modules:
  0.0 95.7 jit_solution(3583074349929054387)
XLA Ops:
  0.2 1.5 %fusion.75 = (f32[63,2,5,1,120]{4,0,3,2,1:T(8,128)S(1)}, f32[63,2,5,1,120]{4,0,3,2,1:T(8,128)S(1)}, f32[63,2,5,1,120]{4,0,3,2,1:T(8,128)S(1)}, f32[63,2,5,1,120]{4,0,3,2,1:T(8,128)S(1)}) fusion(s32[63]{0:T(128)S(1)} %iota_negate_fusion, pred[2]{0:T(512)(128)(4,1)S(1)} %iota_compare_fusion.4), kind=kLoop, calls=%fused_computation.97 | loop fusion | flops 1285200 | bytes 1209854 | tf_op jit(solution)/shard_map/cos | solution.py:55
  1.6 8.0 %fusion = f32[63,2,120,128]{3,0,2,1:T(8,128)S(1)} fusion(f32[125,120,128]{2,1,0:T(8,128)} %bitcast.69, pred[2]{0:T(512)(128)(4,1)S(1)} %iota_compare_fusion.4), kind=kOutput, calls=%fused_computation.2 | convolution fusion | flops 1451693312 | bytes 15421442 | tf_op jit(solution)/shard_map/rb,bac->rac/dot_general | solution.py:45
  9.8 7.9 %fusion.20 = f32[63,20,128]{2,1,0:T(8,128)S(1)} fusion(f32[63,2,120,128]{3,0,2,1:T(8,128)S(1)} %fusion, f32[63,20,2,120]{3,0,2,1:T(8,128)S(1)} %bitcast.70), kind=kOutput, calls=%fused_computation.26 | convolution fusion | flops 232243200 | bytes 9596160 | tf_op jit(solution)/shard_map/rxpa,rpac->rxc/dot_general | solution.py:60
  19.2 0.2 iota.229
  19.4 1.3 %fusion.8 = f32[576,256]{1,0:T(8,128)S(1)} fusion(f32[630,256]{1,0:T(8,128)S(1)} %reshape.399, s32[576]{0:T(1024)S(1)} %broadcast_remainder_fusion, s32[576]{0:T(1024)S(1)} %get-tuple-element.28, s32[630]{0:T(1024)S(1)} %sub.65, s32[630]{0:T(1024)S(1)} %add.300, s32[576]{0:T(1024)S(1)} %get-tuple-element.27, pred[576]{0:T(1024)(128)(4,1)S(1)} %compare_and_fusion.1, ...), kind=kOutput, calls=%fused_computation.14 | convolution fusion | flops 1118033280 | bytes 1249362 | tf_op jit(solution)/shard_map/dot_general | solution.py:69
  20.8 1.4 %fusion.70 = (bf16[512,128]{1,0:T(8,128)(2,1)S(1)}, bf16[512,128]{1,0:T(8,128)(2,1)S(1)}) fusion(f32[576,256]{1,0:T(8,128)S(1)} %fusion.8, s32[512]{0:T(512)S(1)} %get-tuple-element.26, f32[512]{0:T(512)S(1)} %multiply_sine_fusion), kind=kOutput, calls=%fused_computation.85 | convolution fusion | flops 454778880 | bytes 1380352 | tf_op jit(solution)/shard_map/dot_general | solution.py:77
  22.2 3.8 %collective-permute-start.3 = (bf16[2,512,128]{2,1,0:T(8,128)(2,1)S(1)}, bf16[2,512,128]{2,1,0:T(8,128)(2,1)S(1)}, u32[]{:S(2)}, u32[]{:S(2)}) collective-permute-start(bf16[2,512,128]{2,1,0:T(8,128)(2,1)S(1)} %pad_maximum_fusion.3), channel_id=1, source_target_pairs={{0,1},{1,2},{2,3},{3,4},{4,5},{5,6},{6,7},{7,8},{8,9},{9,10},{10,1... | collective-permute-start | bytes 786440 | tf_op jit(solution)/shard_map/ppermute | solution.py:105
  26.1 7.6 %collective-permute-start.4 = (bf16[2,512,128]{2,1,0:T(8,128)(2,1)S(1)}, bf16[2,512,128]{2,1,0:T(8,128)(2,1)S(1)}, u32[]{:S(2)}, u32[]{:S(2)}) collective-permute-start(bf16[2,512,128]{2,1,0:T(8,128)(2,1)S(1)} %pad_maximum_fusion.3), channel_id=1, source_target_pairs={{2,0},{3,1},{4,2},{5,3},{6,4},{7,5},{8,6},{9,7},{10,8},{11,9},{12,... | collective-permute-start | bytes 786440 | tf_op jit(solution)/shard_map/ppermute | solution.py:105
  33.7 2.6 %collective-permute-start.1 = (s32[6,2]{0,1:T(2,128)S(1)}, s32[6,2]{0,1:T(2,128)S(1)}, u32[]{:S(2)}, u32[]{:S(2)}) collective-permute-start(s32[6,2]{0,1:T(2,128)S(1)} %copy-done), channel_id=1, source_target_pairs={{0,16},{8,24},{16,0},{24,8},{1,17},{9,25},{17,1},{25,9},{2,18},{10... | collective-permute-start | bytes 152 | tf_op jit(solution)/shard_map/ppermute | solution.py:128
  36.3 4.7 %cosine_convert_fusion = (bf16[512,1,512]{2,0,1:T(8,128)(2,1)S(1)}, bf16[512,1,512]{2,0,1:T(8,128)(2,1)S(1)}) fusion(s32[512]{0:T(512)S(1)} %get-tuple-element.25, s32[512]{0:T(512)S(1)} %get-tuple-element.26), kind=kLoop, calls=%fused_computation.37 | loop fusion | flops 3145728 | bytes 1052672 | tf_op jit(solution)/shard_map/convert.10
  41.2 0.6 gather_fusion
  41.7 2.8 %collective-permute-done.4 = bf16[2,512,128]{2,1,0:T(8,128)(2,1)S(1)} collective-permute-done((bf16[2,512,128]{2,1,0:T(8,128)(2,1)S(1)}, bf16[2,512,128]{2,1,0:T(8,128)(2,1)S(1)}, u32[]{:S(2)}, u32[]{:S(2)}) %collective-permute-start.4) | collective-permute-done | bytes 262176 | tf_op jit(solution)/shard_map/ppermute | solution.py:105
  44.7 0.3 fusion.43
  45.0 0.7 fusion.25
  45.8 0.8 copy.7
  46.5 4.5 %all-to-all-start = ((bf16[8,64,3,128]{3,1,2,0:T(8,128)(2,1)}), bf16[8,64,3,128]{3,1,2,0:T(8,128)(2,1)S(1)}, u32[]{:S(2)}, u32[]{:S(2)}) async-start(bf16[8,64,3,128]{3,1,2,0:T(8,128)(2,1)} %copy.7), calls=%async_computation | async-start | bytes 786432 | tf_op jit(solution)/shard_map/all_to_all | solution.py:112
  51.2 8.8 %all-to-all-done = bf16[8,64,3,128]{3,1,2,0:T(8,128)(2,1)S(1)} async-done(((bf16[8,64,3,128]{3,1,2,0:T(8,128)(2,1)}), bf16[8,64,3,128]{3,1,2,0:T(8,128)(2,1)S(1)}, u32[]{:S(2)}, u32[]{:S(2)}) %all-to-all-start) | async-done | bytes 393248 | tf_op jit(solution)/shard_map/all_to_all | solution.py:112
  60.1 2.9 %collective-permute-start.6 = (f32[64,3,128]{2,0,1:T(8,128)S(1)}, f32[64,3,128]{2,0,1:T(8,128)S(1)}, u32[]{:S(2)}, u32[]{:S(2)}) collective-permute-start(f32[64,3,128]{2,0,1:T(8,128)S(1)} %convert_reduce_fusion), channel_id=1, source_target_pairs={{0,6},{1,7},{2,0},{3,1},{4,2},{5,3},{6,4},{7,5},{8,14},{9,15},{10,... | collective-permute-start | bytes 294920 | tf_op jit(solution)/shard_map/ppermute | solution.py:115
  63.0 0.4 collective-permute-start.8
  63.4 1.9 %collective-permute-start.10 = (f32[64,3,128]{2,0,1:T(8,128)S(1)}, f32[64,3,128]{2,0,1:T(8,128)S(1)}, u32[]{:S(2)}, u32[]{:S(2)}) collective-permute-start(f32[64,3,128]{2,0,1:T(8,128)S(1)} %convert_reduce_fusion), channel_id=1, source_target_pairs={{0,2},{1,3},{2,4},{3,5},{4,6},{5,7},{6,0},{7,1},{8,10},{9,11},{10,... | collective-permute-start | bytes 294920 | tf_op jit(solution)/shard_map/ppermute | solution.py:115
  65.3 1.5 %collective-permute-done.5 = f32[64,3,128]{2,0,1:T(8,128)S(1)} collective-permute-done((f32[64,3,128]{2,0,1:T(8,128)S(1)}, f32[64,3,128]{2,0,1:T(8,128)S(1)}, u32[]{:S(2)}, u32[]{:S(2)}) %collective-permute-start.5) | collective-permute-done | bytes 98336 | tf_op jit(solution)/shard_map/ppermute | solution.py:115
  66.8 1.8 %collective-permute-done.6 = f32[64,3,128]{2,0,1:T(8,128)S(1)} collective-permute-done((f32[64,3,128]{2,0,1:T(8,128)S(1)}, f32[64,3,128]{2,0,1:T(8,128)S(1)}, u32[]{:S(2)}, u32[]{:S(2)}) %collective-permute-start.6) | collective-permute-done | bytes 98336 | tf_op jit(solution)/shard_map/ppermute | solution.py:115
  68.6 2.0 %collective-permute-start.7 = (f32[2,64,3,128]{3,1,2,0:T(8,128)S(1)}, f32[2,64,3,128]{3,1,2,0:T(8,128)S(1)}, u32[]{:S(2)}, u32[]{:S(2)}) collective-permute-start(f32[2,64,3,128]{3,1,2,0:T(8,128)S(1)} %pad_maximum_fusion.4), channel_id=1, source_target_pairs={{0,6},{1,7},{2,0},{3,1},{4,2},{5,3},{6,4},{7,5},{8,14},{9,15},{10,... | collective-permute-start | bytes 589832 | tf_op jit(solution)/shard_map/ppermute | solution.py:115
  70.6 3.8 %collective-permute-start.9 = (f32[64,3,128]{2,0,1:T(8,128)S(1)}, f32[64,3,128]{2,0,1:T(8,128)S(1)}, u32[]{:S(2)}, u32[]{:S(2)}) collective-permute-start(f32[64,3,128]{2,0,1:T(8,128)S(1)} %collective-permute-done.8), channel_id=1, source_target_pairs={{0,2},{1,3},{2,4},{3,5},{4,6},{5,7},{6,0},{7,1},{8,10},{9,11},{10,... | collective-permute-start | bytes 294920 | tf_op jit(solution)/shard_map/ppermute | solution.py:115
  74.4 7.0 %collective-permute-done.7 = f32[2,64,3,128]{3,1,2,0:T(8,128)S(1)} collective-permute-done((f32[2,64,3,128]{3,1,2,0:T(8,128)S(1)}, f32[2,64,3,128]{3,1,2,0:T(8,128)S(1)}, u32[]{:S(2)}, u32[]{:S(2)}) %collective-permute-start.7) | collective-permute-done | bytes 196640 | tf_op jit(solution)/shard_map/ppermute | solution.py:115
  81.5 0.7 gather_fusion.1
  82.4 0.6 collective-permute-start.11
  83.0 2.8 %collective-permute-start.12 = (f32[6,64,128]{2,1,0:T(8,128)S(1)}, f32[6,64,128]{2,1,0:T(8,128)S(1)}, u32[]{:S(2)}, u32[]{:S(2)}) collective-permute-start(f32[6,64,128]{2,1,0:T(8,128)S(1)} %get-tuple-element.11), channel_id=1, source_target_pairs={{0,16},{8,24},{16,0},{24,8},{1,17},{9,25},{17,1},{25,9},{2,18},{10... | collective-permute-start | bytes 589832 | tf_op jit(solution)/shard_map/ppermute | solution.py:143
  85.8 4.5 %collective-permute-done.11 = f32[6,64,128]{2,1,0:T(8,128)S(1)} collective-permute-done((f32[6,64,128]{2,1,0:T(8,128)S(1)}, f32[6,64,128]{2,1,0:T(8,128)S(1)}, u32[]{:S(2)}, u32[]{:S(2)}) %collective-permute-start.11) | collective-permute-done | bytes 196640 | tf_op jit(solution)/shard_map/ppermute | solution.py:143
  90.3 2.1 %collective-permute-done.12 = f32[6,64,128]{2,1,0:T(8,128)S(1)} collective-permute-done((f32[6,64,128]{2,1,0:T(8,128)S(1)}, f32[6,64,128]{2,1,0:T(8,128)S(1)}, u32[]{:S(2)}, u32[]{:S(2)}) %collective-permute-start.12) | collective-permute-done | bytes 196640 | tf_op jit(solution)/shard_map/ppermute | solution.py:143
  92.4 2.6 %collective-permute-done.13 = f32[6,64,128]{2,1,0:T(8,128)S(1)} collective-permute-done((f32[6,64,128]{2,1,0:T(8,128)S(1)}, f32[6,64,128]{2,1,0:T(8,128)S(1)}, u32[]{:S(2)}, u32[]{:S(2)}) %collective-permute-start.13) | collective-permute-done | bytes 196640 | tf_op jit(solution)/shard_map/ppermute | solution.py:143
  95.0 0.8 fusion.73
  (57 shorter events, 2.6 us)
Async XLA Ops:
  20.8 12.9 %copy-start = (s32[6,2]{0,1:T(2,128)S(1)}, s32[6,2]{0,1:T(2,128)}, u32[]{:S(2)}) copy-start(s32[6,2]{0,1:T(2,128)} %param.3) | copy-start | bytes 148
  22.2 19.5 %collective-permute-start.3 = (bf16[2,512,128]{2,1,0:T(8,128)(2,1)S(1)}, bf16[2,512,128]{2,1,0:T(8,128)(2,1)S(1)}, u32[]{:S(2)}, u32[]{:S(2)}) collective-permute-start(bf16[2,512,128]{2,1,0:T(8,128)(2,1)S(1)} %pad_maximum_fusion.3), channel_id=1, source_target_pairs={{0,1},{1,2},{2,3},{3,4},{4,5},{5,6},{6,7},{7,8},{8,9},{9,10},{10,1... | collective-permute-start | bytes 786440 | tf_op jit(solution)/shard_map/ppermute | solution.py:105
  26.1 18.5 %collective-permute-start.4 = (bf16[2,512,128]{2,1,0:T(8,128)(2,1)S(1)}, bf16[2,512,128]{2,1,0:T(8,128)(2,1)S(1)}, u32[]{:S(2)}, u32[]{:S(2)}) collective-permute-start(bf16[2,512,128]{2,1,0:T(8,128)(2,1)S(1)} %pad_maximum_fusion.3), channel_id=1, source_target_pairs={{2,0},{3,1},{4,2},{5,3},{6,4},{7,5},{8,6},{9,7},{10,8},{11,9},{12,... | collective-permute-start | bytes 786440 | tf_op jit(solution)/shard_map/ppermute | solution.py:105
  33.7 7.5 %collective-permute-start = (s32[6,2]{0,1:T(2,128)S(1)}, s32[6,2]{0,1:T(2,128)S(1)}, u32[]{:S(2)}, u32[]{:S(2)}) collective-permute-start(s32[6,2]{0,1:T(2,128)S(1)} %copy-done), channel_id=1, source_target_pairs={{0,8},{8,16},{16,24},{24,0},{1,9},{9,17},{17,25},{25,1},{2,10},{10... | collective-permute-start | bytes 152 | tf_op jit(solution)/shard_map/ppermute | solution.py:128
  33.7 7.4 %collective-permute-start.1 = (s32[6,2]{0,1:T(2,128)S(1)}, s32[6,2]{0,1:T(2,128)S(1)}, u32[]{:S(2)}, u32[]{:S(2)}) collective-permute-start(s32[6,2]{0,1:T(2,128)S(1)} %copy-done), channel_id=1, source_target_pairs={{0,16},{8,24},{16,0},{24,8},{1,17},{9,25},{17,1},{25,9},{2,18},{10... | collective-permute-start | bytes 152 | tf_op jit(solution)/shard_map/ppermute | solution.py:128
  36.3 4.8 %collective-permute-start.2 = (s32[6,2]{0,1:T(2,128)S(1)}, s32[6,2]{0,1:T(2,128)S(1)}, u32[]{:S(2)}, u32[]{:S(2)}) collective-permute-start(s32[6,2]{0,1:T(2,128)S(1)} %copy-done), channel_id=1, source_target_pairs={{0,24},{8,0},{16,8},{24,16},{1,25},{9,1},{17,9},{25,17},{2,26},{10... | collective-permute-start | bytes 152 | tf_op jit(solution)/shard_map/ppermute | solution.py:128
  46.5 13.4 %all-to-all-start = ((bf16[8,64,3,128]{3,1,2,0:T(8,128)(2,1)}), bf16[8,64,3,128]{3,1,2,0:T(8,128)(2,1)S(1)}, u32[]{:S(2)}, u32[]{:S(2)}) async-start(bf16[8,64,3,128]{3,1,2,0:T(8,128)(2,1)} %copy.7), calls=%async_computation | async-start | bytes 786432 | tf_op jit(solution)/shard_map/all_to_all | solution.py:112
  60.0 6.8 %collective-permute-start.5 = (f32[64,3,128]{2,0,1:T(8,128)S(1)}, f32[64,3,128]{2,0,1:T(8,128)S(1)}, u32[]{:S(2)}, u32[]{:S(2)}) collective-permute-start(f32[64,3,128]{2,0,1:T(8,128)S(1)} %convert_reduce_fusion), channel_id=1, source_target_pairs={{0,7},{1,0},{2,1},{3,2},{4,3},{5,4},{6,5},{7,6},{8,15},{9,8},{10,9... | collective-permute-start | bytes 294920 | tf_op jit(solution)/shard_map/ppermute | solution.py:115
  60.1 8.5 %collective-permute-start.6 = (f32[64,3,128]{2,0,1:T(8,128)S(1)}, f32[64,3,128]{2,0,1:T(8,128)S(1)}, u32[]{:S(2)}, u32[]{:S(2)}) collective-permute-start(f32[64,3,128]{2,0,1:T(8,128)S(1)} %convert_reduce_fusion), channel_id=1, source_target_pairs={{0,6},{1,7},{2,0},{3,1},{4,2},{5,3},{6,4},{7,5},{8,14},{9,15},{10,... | collective-permute-start | bytes 294920 | tf_op jit(solution)/shard_map/ppermute | solution.py:115
  63.0 7.5 %collective-permute-start.8 = (f32[64,3,128]{2,0,1:T(8,128)S(1)}, f32[64,3,128]{2,0,1:T(8,128)S(1)}, u32[]{:S(2)}, u32[]{:S(2)}) collective-permute-start(f32[64,3,128]{2,0,1:T(8,128)S(1)} %convert_reduce_fusion), channel_id=1, source_target_pairs={{0,1},{1,2},{2,3},{3,4},{4,5},{5,6},{6,7},{7,0},{8,9},{9,10},{10,1... | collective-permute-start | bytes 294920 | tf_op jit(solution)/shard_map/ppermute | solution.py:115
  63.4 18.1 %collective-permute-start.10 = (f32[64,3,128]{2,0,1:T(8,128)S(1)}, f32[64,3,128]{2,0,1:T(8,128)S(1)}, u32[]{:S(2)}, u32[]{:S(2)}) collective-permute-start(f32[64,3,128]{2,0,1:T(8,128)S(1)} %convert_reduce_fusion), channel_id=1, source_target_pairs={{0,2},{1,3},{2,4},{3,5},{4,6},{5,7},{6,0},{7,1},{8,10},{9,11},{10,... | collective-permute-start | bytes 294920 | tf_op jit(solution)/shard_map/ppermute | solution.py:115
  68.6 12.8 %collective-permute-start.7 = (f32[2,64,3,128]{3,1,2,0:T(8,128)S(1)}, f32[2,64,3,128]{3,1,2,0:T(8,128)S(1)}, u32[]{:S(2)}, u32[]{:S(2)}) collective-permute-start(f32[2,64,3,128]{3,1,2,0:T(8,128)S(1)} %pad_maximum_fusion.4), channel_id=1, source_target_pairs={{0,6},{1,7},{2,0},{3,1},{4,2},{5,3},{6,4},{7,5},{8,14},{9,15},{10,... | collective-permute-start | bytes 589832 | tf_op jit(solution)/shard_map/ppermute | solution.py:115
  70.6 10.9 %collective-permute-start.9 = (f32[64,3,128]{2,0,1:T(8,128)S(1)}, f32[64,3,128]{2,0,1:T(8,128)S(1)}, u32[]{:S(2)}, u32[]{:S(2)}) collective-permute-start(f32[64,3,128]{2,0,1:T(8,128)S(1)} %collective-permute-done.8), channel_id=1, source_target_pairs={{0,2},{1,3},{2,4},{3,5},{4,6},{5,7},{6,0},{7,1},{8,10},{9,11},{10,... | collective-permute-start | bytes 294920 | tf_op jit(solution)/shard_map/ppermute | solution.py:115
  82.4 7.9 %collective-permute-start.11 = (f32[6,64,128]{2,1,0:T(8,128)S(1)}, f32[6,64,128]{2,1,0:T(8,128)S(1)}, u32[]{:S(2)}, u32[]{:S(2)}) collective-permute-start(f32[6,64,128]{2,1,0:T(8,128)S(1)} %get-tuple-element.9), channel_id=1, source_target_pairs={{0,8},{8,16},{16,24},{24,0},{1,9},{9,17},{17,25},{25,1},{2,10},{10... | collective-permute-start | bytes 589832 | tf_op jit(solution)/shard_map/ppermute | solution.py:143
  83.0 9.3 %collective-permute-start.12 = (f32[6,64,128]{2,1,0:T(8,128)S(1)}, f32[6,64,128]{2,1,0:T(8,128)S(1)}, u32[]{:S(2)}, u32[]{:S(2)}) collective-permute-start(f32[6,64,128]{2,1,0:T(8,128)S(1)} %get-tuple-element.11), channel_id=1, source_target_pairs={{0,16},{8,24},{16,0},{24,8},{1,17},{9,25},{17,1},{25,9},{2,18},{10... | collective-permute-start | bytes 589832 | tf_op jit(solution)/shard_map/ppermute | solution.py:143
  85.8 9.2 %collective-permute-start.13 = (f32[6,64,128]{2,1,0:T(8,128)S(1)}, f32[6,64,128]{2,1,0:T(8,128)S(1)}, u32[]{:S(2)}, u32[]{:S(2)}) collective-permute-start(f32[6,64,128]{2,1,0:T(8,128)S(1)} %get-tuple-element.10), channel_id=1, source_target_pairs={{0,24},{8,0},{16,8},{24,16},{1,25},{9,1},{17,9},{25,17},{2,26},{10... | collective-permute-start | bytes 589832 | tf_op jit(solution)/shard_map/ppermute | solution.py:143

commit v14 on v13

--- a/solution.py
+++ b/solution.py
@@ -100,7 +100,7 @@
     windows_all = traces.shape[0] * nwin
     factor = 1.0 / math.sqrt(NB * windows_all)
     received = {}
-    for shift in (-1, 2):
+    for shift in (2, -1):
         perm = [(k + shift, k) for k in range(blocks) if 0 <= k + shift < blocks]
         received[shift] = lax.ppermute(white, ("cx", "cz"), perm)
     left = jnp.stack([received[-1], white, received[-1]])
@@ -115,7 +115,7 @@
         return lax.ppermute(value, "cz", [(k, (k - step) % nz) for k in range(nz)])
 
     gathered = {0: corr}
-    for step in (1, -1, 2, -2):
+    for step in (2, -2, 1, -1):
         gathered[step % nz] = shift_z(corr, step)
     ahead = shift_z(jnp.stack([gathered[1], gathered[2]]), 2)
     behind = shift_z(gathered[nz - 1], -2)
@@ -138,7 +138,7 @@
     picked = ring[zi, :, di, :]
     picked = jnp.where(mine[..., None, None], picked, 0.0)
     got = lax.dynamic_index_in_dim(picked, me_x, 0, keepdims=False)
-    for step in range(1, nx):
+    for step in sorted(range(1, nx), key=lambda t: -min(t, nx - t)):
         chunk = lax.dynamic_index_in_dim(picked, (me_x + step) % nx, 0, keepdims=False)
         got = got + lax.ppermute(chunk, "cx", [(k, (k + step) % nx) for k in range(nx)])
     return jnp.where(filled_local(pair_blocks)[:, None, None], got, 0.0)

time: 96.6 us -> 96.1 us (level)
  no operation moved by 1% of the time
where the time goes in v14:
time: 96.1 us; the launch traced here: 95.7 us
  starting transfers between devices  33.6 us (35%)
  waiting for transfers between devices  30.4 us (32%)
  matrix products  19.4 us (20%)
  other arithmetic  8.11 us (8%)
  local copies, waits for them, and re-layouts  3.76 us (4%)
    ppermute x2, starting transfers between devices, body(): received[shift] = lax.ppermute(white, ('cx', 'cz'), perm)  11.4 us
    ppermute x6, starting transfers between devices, shift_z(): return lax.ppermute(value, 'cz', [(k, (k - step) % nz) for k in range(nz)])  11.1 us
    ppermute x6, waiting for transfers between devices, shift_z(): return lax.ppermute(value, 'cz', [(k, (k - step) % nz) for k in range(nz)])  10.3 us
    all_to_all x1, waiting for transfers between devices, body(): corr = lax.all_to_all(corr.astype(jnp.bfloat16), 'win', 0, 0)  8.78 us
    ppermute x3, waiting for transfers between devices, body(): lax.ppermute(chunk, 'cx', [(k, (k + step) % nx) for k in range(nx)])  8.48 us
    dot_general x1, matrix products, band_dft(): jnp.einsum('rb,bac->rac', basis1, xb, precision=prec, preferred_element_t...  8 us
    dot_general x1, matrix products, band_dft(): jnp.einsum('rxpa,rpac->rxc', m, z, precision=prec, preferred_element_type...  7.93 us
    another operation x2, other arithmetic  5.01 us
  transfers between devices with their start and end apart: 15, of which 8 were waited for; matrix products, arithmetic and copies ran while one was open for 6% of the time, Pallas kernels for 0%

profile of v14, /device:TPU:6, one launch (start us, length us, event | category | flops | bytes accessed | tf_op | source)
XLA Modules:
  0.0 95.7 jit_solution(2976961243290529892)
XLA Ops:
  0.2 1.5 %fusion.75 = (f32[63,2,5,1,120]{4,0,3,2,1:T(8,128)S(1)}, f32[63,2,5,1,120]{4,0,3,2,1:T(8,128)S(1)}, f32[63,2,5,1,120]{4,0,3,2,1:T(8,128)S(1)}, f32[63,2,5,1,120]{4,0,3,2,1:T(8,128)S(1)}) fusion(s32[63]{0:T(128)S(1)} %iota_negate_fusion, pred[2]{0:T(512)(128)(4,1)S(1)} %iota_compare_fusion.4), kind=kLoop, calls=%fused_computation.97 | loop fusion | flops 1285200 | bytes 1209854 | tf_op jit(solution)/shard_map/cos | solution.py:55
  1.6 8.0 %fusion = f32[63,2,120,128]{3,0,2,1:T(8,128)S(1)} fusion(f32[125,120,128]{2,1,0:T(8,128)} %bitcast.69, pred[2]{0:T(512)(128)(4,1)S(1)} %iota_compare_fusion.4), kind=kOutput, calls=%fused_computation.2 | convolution fusion | flops 1451693312 | bytes 15421442 | tf_op jit(solution)/shard_map/rb,bac->rac/dot_general | solution.py:45
  9.8 7.9 %fusion.20 = f32[63,20,128]{2,1,0:T(8,128)S(1)} fusion(f32[63,2,120,128]{3,0,2,1:T(8,128)S(1)} %fusion, f32[63,20,2,120]{3,0,2,1:T(8,128)S(1)} %bitcast.70), kind=kOutput, calls=%fused_computation.26 | convolution fusion | flops 232243200 | bytes 9596160 | tf_op jit(solution)/shard_map/rxpa,rpac->rxc/dot_general | solution.py:60
  19.2 0.2 iota.229
  19.4 1.3 %fusion.8 = f32[576,256]{1,0:T(8,128)S(1)} fusion(f32[630,256]{1,0:T(8,128)S(1)} %reshape.399, s32[576]{0:T(1024)S(1)} %broadcast_remainder_fusion, s32[576]{0:T(1024)S(1)} %get-tuple-element.28, s32[630]{0:T(1024)S(1)} %sub.65, s32[630]{0:T(1024)S(1)} %add.300, s32[576]{0:T(1024)S(1)} %get-tuple-element.27, pred[576]{0:T(1024)(128)(4,1)S(1)} %compare_and_fusion.1, ...), kind=kOutput, calls=%fused_computation.14 | convolution fusion | flops 1118033280 | bytes 1249362 | tf_op jit(solution)/shard_map/dot_general | solution.py:69
  20.8 1.4 %fusion.70 = (bf16[512,128]{1,0:T(8,128)(2,1)S(1)}, bf16[512,128]{1,0:T(8,128)(2,1)S(1)}) fusion(f32[576,256]{1,0:T(8,128)S(1)} %fusion.8, s32[512]{0:T(512)S(1)} %get-tuple-element.26, f32[512]{0:T(512)S(1)} %multiply_sine_fusion), kind=kOutput, calls=%fused_computation.85 | convolution fusion | flops 454778880 | bytes 1380352 | tf_op jit(solution)/shard_map/dot_general | solution.py:77
  22.2 3.8 %collective-permute-start.3 = (bf16[2,512,128]{2,1,0:T(8,128)(2,1)S(1)}, bf16[2,512,128]{2,1,0:T(8,128)(2,1)S(1)}, u32[]{:S(2)}, u32[]{:S(2)}) collective-permute-start(bf16[2,512,128]{2,1,0:T(8,128)(2,1)S(1)} %pad_maximum_fusion.3), channel_id=1, source_target_pairs={{0,1},{1,2},{2,3},{3,4},{4,5},{5,6},{6,7},{7,8},{8,9},{9,10},{10,1... | collective-permute-start | bytes 786440 | tf_op jit(solution)/shard_map/ppermute | solution.py:105
  26.1 7.6 %collective-permute-start.4 = (bf16[2,512,128]{2,1,0:T(8,128)(2,1)S(1)}, bf16[2,512,128]{2,1,0:T(8,128)(2,1)S(1)}, u32[]{:S(2)}, u32[]{:S(2)}) collective-permute-start(bf16[2,512,128]{2,1,0:T(8,128)(2,1)S(1)} %pad_maximum_fusion.3), channel_id=1, source_target_pairs={{2,0},{3,1},{4,2},{5,3},{6,4},{7,5},{8,6},{9,7},{10,8},{11,9},{12,... | collective-permute-start | bytes 786440 | tf_op jit(solution)/shard_map/ppermute | solution.py:105
  33.7 2.6 %collective-permute-start.1 = (s32[6,2]{0,1:T(2,128)S(1)}, s32[6,2]{0,1:T(2,128)S(1)}, u32[]{:S(2)}, u32[]{:S(2)}) collective-permute-start(s32[6,2]{0,1:T(2,128)S(1)} %copy-done), channel_id=1, source_target_pairs={{0,16},{8,24},{16,0},{24,8},{1,17},{9,25},{17,1},{25,9},{2,18},{10... | collective-permute-start | bytes 152 | tf_op jit(solution)/shard_map/ppermute | solution.py:128
  36.3 4.7 %cosine_convert_fusion = (bf16[512,1,512]{2,0,1:T(8,128)(2,1)S(1)}, bf16[512,1,512]{2,0,1:T(8,128)(2,1)S(1)}) fusion(s32[512]{0:T(512)S(1)} %get-tuple-element.25, s32[512]{0:T(512)S(1)} %get-tuple-element.26), kind=kLoop, calls=%fused_computation.37 | loop fusion | flops 3145728 | bytes 1052672 | tf_op jit(solution)/shard_map/convert.10
  41.2 0.6 gather_fusion
  41.7 2.8 %collective-permute-done.4 = bf16[2,512,128]{2,1,0:T(8,128)(2,1)S(1)} collective-permute-done((bf16[2,512,128]{2,1,0:T(8,128)(2,1)S(1)}, bf16[2,512,128]{2,1,0:T(8,128)(2,1)S(1)}, u32[]{:S(2)}, u32[]{:S(2)}) %collective-permute-start.4) | collective-permute-done | bytes 262176 | tf_op jit(solution)/shard_map/ppermute | solution.py:105
  44.7 0.3 fusion.43
  45.0 0.7 fusion.25
  45.8 0.8 copy.7
  46.5 4.5 %all-to-all-start = ((bf16[8,64,3,128]{3,1,2,0:T(8,128)(2,1)}), bf16[8,64,3,128]{3,1,2,0:T(8,128)(2,1)S(1)}, u32[]{:S(2)}, u32[]{:S(2)}) async-start(bf16[8,64,3,128]{3,1,2,0:T(8,128)(2,1)} %copy.7), calls=%async_computation | async-start | bytes 786432 | tf_op jit(solution)/shard_map/all_to_all | solution.py:112
  51.2 8.8 %all-to-all-done = bf16[8,64,3,128]{3,1,2,0:T(8,128)(2,1)S(1)} async-done(((bf16[8,64,3,128]{3,1,2,0:T(8,128)(2,1)}), bf16[8,64,3,128]{3,1,2,0:T(8,128)(2,1)S(1)}, u32[]{:S(2)}, u32[]{:S(2)}) %all-to-all-start) | async-done | bytes 393248 | tf_op jit(solution)/shard_map/all_to_all | solution.py:112
  60.1 2.9 %collective-permute-start.6 = (f32[64,3,128]{2,0,1:T(8,128)S(1)}, f32[64,3,128]{2,0,1:T(8,128)S(1)}, u32[]{:S(2)}, u32[]{:S(2)}) collective-permute-start(f32[64,3,128]{2,0,1:T(8,128)S(1)} %convert_reduce_fusion), channel_id=1, source_target_pairs={{0,6},{1,7},{2,0},{3,1},{4,2},{5,3},{6,4},{7,5},{8,14},{9,15},{10,... | collective-permute-start | bytes 294920 | tf_op jit(solution)/shard_map/ppermute | solution.py:115
  63.0 0.4 collective-permute-start.8
  63.4 1.9 %collective-permute-start.10 = (f32[64,3,128]{2,0,1:T(8,128)S(1)}, f32[64,3,128]{2,0,1:T(8,128)S(1)}, u32[]{:S(2)}, u32[]{:S(2)}) collective-permute-start(f32[64,3,128]{2,0,1:T(8,128)S(1)} %convert_reduce_fusion), channel_id=1, source_target_pairs={{0,2},{1,3},{2,4},{3,5},{4,6},{5,7},{6,0},{7,1},{8,10},{9,11},{10,... | collective-permute-start | bytes 294920 | tf_op jit(solution)/shard_map/ppermute | solution.py:115
  65.3 1.5 %collective-permute-done.5 = f32[64,3,128]{2,0,1:T(8,128)S(1)} collective-permute-done((f32[64,3,128]{2,0,1:T(8,128)S(1)}, f32[64,3,128]{2,0,1:T(8,128)S(1)}, u32[]{:S(2)}, u32[]{:S(2)}) %collective-permute-start.5) | collective-permute-done | bytes 98336 | tf_op jit(solution)/shard_map/ppermute | solution.py:115
  66.8 1.8 %collective-permute-done.6 = f32[64,3,128]{2,0,1:T(8,128)S(1)} collective-permute-done((f32[64,3,128]{2,0,1:T(8,128)S(1)}, f32[64,3,128]{2,0,1:T(8,128)S(1)}, u32[]{:S(2)}, u32[]{:S(2)}) %collective-permute-start.6) | collective-permute-done | bytes 98336 | tf_op jit(solution)/shard_map/ppermute | solution.py:115
  68.6 2.0 %collective-permute-start.7 = (f32[2,64,3,128]{3,1,2,0:T(8,128)S(1)}, f32[2,64,3,128]{3,1,2,0:T(8,128)S(1)}, u32[]{:S(2)}, u32[]{:S(2)}) collective-permute-start(f32[2,64,3,128]{3,1,2,0:T(8,128)S(1)} %pad_maximum_fusion.4), channel_id=1, source_target_pairs={{0,6},{1,7},{2,0},{3,1},{4,2},{5,3},{6,4},{7,5},{8,14},{9,15},{10,... | collective-permute-start | bytes 589832 | tf_op jit(solution)/shard_map/ppermute | solution.py:115
  70.6 3.8 %collective-permute-start.9 = (f32[64,3,128]{2,0,1:T(8,128)S(1)}, f32[64,3,128]{2,0,1:T(8,128)S(1)}, u32[]{:S(2)}, u32[]{:S(2)}) collective-permute-start(f32[64,3,128]{2,0,1:T(8,128)S(1)} %collective-permute-done.8), channel_id=1, source_target_pairs={{0,2},{1,3},{2,4},{3,5},{4,6},{5,7},{6,0},{7,1},{8,10},{9,11},{10,... | collective-permute-start | bytes 294920 | tf_op jit(solution)/shard_map/ppermute | solution.py:115
  74.4 7.0 %collective-permute-done.7 = f32[2,64,3,128]{3,1,2,0:T(8,128)S(1)} collective-permute-done((f32[2,64,3,128]{3,1,2,0:T(8,128)S(1)}, f32[2,64,3,128]{3,1,2,0:T(8,128)S(1)}, u32[]{:S(2)}, u32[]{:S(2)}) %collective-permute-start.7) | collective-permute-done | bytes 196640 | tf_op jit(solution)/shard_map/ppermute | solution.py:115
  81.5 0.7 gather_fusion.1
  82.4 2.0 %collective-permute-start.11 = (f32[6,64,128]{2,1,0:T(8,128)S(1)}, f32[6,64,128]{2,1,0:T(8,128)S(1)}, u32[]{:S(2)}, u32[]{:S(2)}) collective-permute-start(f32[6,64,128]{2,1,0:T(8,128)S(1)} %get-tuple-element.9), channel_id=1, source_target_pairs={{0,16},{8,24},{16,0},{24,8},{1,17},{9,25},{17,1},{25,9},{2,18},{10... | collective-permute-start | bytes 589832 | tf_op jit(solution)/shard_map/ppermute | solution.py:143
  84.4 2.0 %collective-permute-start.12 = (f32[6,64,128]{2,1,0:T(8,128)S(1)}, f32[6,64,128]{2,1,0:T(8,128)S(1)}, u32[]{:S(2)}, u32[]{:S(2)}) collective-permute-start(f32[6,64,128]{2,1,0:T(8,128)S(1)} %get-tuple-element.11), channel_id=1, source_target_pairs={{0,8},{8,16},{16,24},{24,0},{1,9},{9,17},{17,25},{25,1},{2,10},{10... | collective-permute-start | bytes 589832 | tf_op jit(solution)/shard_map/ppermute | solution.py:143
  86.4 5.4 %collective-permute-done.11 = f32[6,64,128]{2,1,0:T(8,128)S(1)} collective-permute-done((f32[6,64,128]{2,1,0:T(8,128)S(1)}, f32[6,64,128]{2,1,0:T(8,128)S(1)}, u32[]{:S(2)}, u32[]{:S(2)}) %collective-permute-start.11) | collective-permute-done | bytes 196640 | tf_op jit(solution)/shard_map/ppermute | solution.py:143
  91.8 0.8 collective-permute-done.12
  92.6 2.3 %collective-permute-done.13 = f32[6,64,128]{2,1,0:T(8,128)S(1)} collective-permute-done((f32[6,64,128]{2,1,0:T(8,128)S(1)}, f32[6,64,128]{2,1,0:T(8,128)S(1)}, u32[]{:S(2)}, u32[]{:S(2)}) %collective-permute-start.13) | collective-permute-done | bytes 196640 | tf_op jit(solution)/shard_map/ppermute | solution.py:143
  94.9 0.8 fusion.73
  (57 shorter events, 2.6 us)
Async XLA Ops:
  20.8 12.9 %copy-start = (s32[6,2]{0,1:T(2,128)S(1)}, s32[6,2]{0,1:T(2,128)}, u32[]{:S(2)}) copy-start(s32[6,2]{0,1:T(2,128)} %param.3) | copy-start | bytes 148
  22.2 19.5 %collective-permute-start.3 = (bf16[2,512,128]{2,1,0:T(8,128)(2,1)S(1)}, bf16[2,512,128]{2,1,0:T(8,128)(2,1)S(1)}, u32[]{:S(2)}, u32[]{:S(2)}) collective-permute-start(bf16[2,512,128]{2,1,0:T(8,128)(2,1)S(1)} %pad_maximum_fusion.3), channel_id=1, source_target_pairs={{0,1},{1,2},{2,3},{3,4},{4,5},{5,6},{6,7},{7,8},{8,9},{9,10},{10,1... | collective-permute-start | bytes 786440 | tf_op jit(solution)/shard_map/ppermute | solution.py:105
  26.1 18.5 %collective-permute-start.4 = (bf16[2,512,128]{2,1,0:T(8,128)(2,1)S(1)}, bf16[2,512,128]{2,1,0:T(8,128)(2,1)S(1)}, u32[]{:S(2)}, u32[]{:S(2)}) collective-permute-start(bf16[2,512,128]{2,1,0:T(8,128)(2,1)S(1)} %pad_maximum_fusion.3), channel_id=1, source_target_pairs={{2,0},{3,1},{4,2},{5,3},{6,4},{7,5},{8,6},{9,7},{10,8},{11,9},{12,... | collective-permute-start | bytes 786440 | tf_op jit(solution)/shard_map/ppermute | solution.py:105
  33.7 7.5 %collective-permute-start = (s32[6,2]{0,1:T(2,128)S(1)}, s32[6,2]{0,1:T(2,128)S(1)}, u32[]{:S(2)}, u32[]{:S(2)}) collective-permute-start(s32[6,2]{0,1:T(2,128)S(1)} %copy-done), channel_id=1, source_target_pairs={{0,8},{8,16},{16,24},{24,0},{1,9},{9,17},{17,25},{25,1},{2,10},{10... | collective-permute-start | bytes 152 | tf_op jit(solution)/shard_map/ppermute | solution.py:128
  33.7 7.4 %collective-permute-start.1 = (s32[6,2]{0,1:T(2,128)S(1)}, s32[6,2]{0,1:T(2,128)S(1)}, u32[]{:S(2)}, u32[]{:S(2)}) collective-permute-start(s32[6,2]{0,1:T(2,128)S(1)} %copy-done), channel_id=1, source_target_pairs={{0,16},{8,24},{16,0},{24,8},{1,17},{9,25},{17,1},{25,9},{2,18},{10... | collective-permute-start | bytes 152 | tf_op jit(solution)/shard_map/ppermute | solution.py:128
  36.3 4.8 %collective-permute-start.2 = (s32[6,2]{0,1:T(2,128)S(1)}, s32[6,2]{0,1:T(2,128)S(1)}, u32[]{:S(2)}, u32[]{:S(2)}) collective-permute-start(s32[6,2]{0,1:T(2,128)S(1)} %copy-done), channel_id=1, source_target_pairs={{0,24},{8,0},{16,8},{24,16},{1,25},{9,1},{17,9},{25,17},{2,26},{10... | collective-permute-start | bytes 152 | tf_op jit(solution)/shard_map/ppermute | solution.py:128
  46.5 13.4 %all-to-all-start = ((bf16[8,64,3,128]{3,1,2,0:T(8,128)(2,1)}), bf16[8,64,3,128]{3,1,2,0:T(8,128)(2,1)S(1)}, u32[]{:S(2)}, u32[]{:S(2)}) async-start(bf16[8,64,3,128]{3,1,2,0:T(8,128)(2,1)} %copy.7), calls=%async_computation | async-start | bytes 786432 | tf_op jit(solution)/shard_map/all_to_all | solution.py:112
  60.0 6.8 %collective-permute-start.5 = (f32[64,3,128]{2,0,1:T(8,128)S(1)}, f32[64,3,128]{2,0,1:T(8,128)S(1)}, u32[]{:S(2)}, u32[]{:S(2)}) collective-permute-start(f32[64,3,128]{2,0,1:T(8,128)S(1)} %convert_reduce_fusion), channel_id=1, source_target_pairs={{0,7},{1,0},{2,1},{3,2},{4,3},{5,4},{6,5},{7,6},{8,15},{9,8},{10,9... | collective-permute-start | bytes 294920 | tf_op jit(solution)/shard_map/ppermute | solution.py:115
  60.1 8.5 %collective-permute-start.6 = (f32[64,3,128]{2,0,1:T(8,128)S(1)}, f32[64,3,128]{2,0,1:T(8,128)S(1)}, u32[]{:S(2)}, u32[]{:S(2)}) collective-permute-start(f32[64,3,128]{2,0,1:T(8,128)S(1)} %convert_reduce_fusion), channel_id=1, source_target_pairs={{0,6},{1,7},{2,0},{3,1},{4,2},{5,3},{6,4},{7,5},{8,14},{9,15},{10,... | collective-permute-start | bytes 294920 | tf_op jit(solution)/shard_map/ppermute | solution.py:115
  63.0 7.5 %collective-permute-start.8 = (f32[64,3,128]{2,0,1:T(8,128)S(1)}, f32[64,3,128]{2,0,1:T(8,128)S(1)}, u32[]{:S(2)}, u32[]{:S(2)}) collective-permute-start(f32[64,3,128]{2,0,1:T(8,128)S(1)} %convert_reduce_fusion), channel_id=1, source_target_pairs={{0,1},{1,2},{2,3},{3,4},{4,5},{5,6},{6,7},{7,0},{8,9},{9,10},{10,1... | collective-permute-start | bytes 294920 | tf_op jit(solution)/shard_map/ppermute | solution.py:115
  63.4 18.1 %collective-permute-start.10 = (f32[64,3,128]{2,0,1:T(8,128)S(1)}, f32[64,3,128]{2,0,1:T(8,128)S(1)}, u32[]{:S(2)}, u32[]{:S(2)}) collective-permute-start(f32[64,3,128]{2,0,1:T(8,128)S(1)} %convert_reduce_fusion), channel_id=1, source_target_pairs={{0,2},{1,3},{2,4},{3,5},{4,6},{5,7},{6,0},{7,1},{8,10},{9,11},{10,... | collective-permute-start | bytes 294920 | tf_op jit(solution)/shard_map/ppermute | solution.py:115
  68.6 12.8 %collective-permute-start.7 = (f32[2,64,3,128]{3,1,2,0:T(8,128)S(1)}, f32[2,64,3,128]{3,1,2,0:T(8,128)S(1)}, u32[]{:S(2)}, u32[]{:S(2)}) collective-permute-start(f32[2,64,3,128]{3,1,2,0:T(8,128)S(1)} %pad_maximum_fusion.4), channel_id=1, source_target_pairs={{0,6},{1,7},{2,0},{3,1},{4,2},{5,3},{6,4},{7,5},{8,14},{9,15},{10,... | collective-permute-start | bytes 589832 | tf_op jit(solution)/shard_map/ppermute | solution.py:115
  70.6 10.9 %collective-permute-start.9 = (f32[64,3,128]{2,0,1:T(8,128)S(1)}, f32[64,3,128]{2,0,1:T(8,128)S(1)}, u32[]{:S(2)}, u32[]{:S(2)}) collective-permute-start(f32[64,3,128]{2,0,1:T(8,128)S(1)} %collective-permute-done.8), channel_id=1, source_target_pairs={{0,2},{1,3},{2,4},{3,5},{4,6},{5,7},{6,0},{7,1},{8,10},{9,11},{10,... | collective-permute-start | bytes 294920 | tf_op jit(solution)/shard_map/ppermute | solution.py:115
  82.4 9.4 %collective-permute-start.11 = (f32[6,64,128]{2,1,0:T(8,128)S(1)}, f32[6,64,128]{2,1,0:T(8,128)S(1)}, u32[]{:S(2)}, u32[]{:S(2)}) collective-permute-start(f32[6,64,128]{2,1,0:T(8,128)S(1)} %get-tuple-element.9), channel_id=1, source_target_pairs={{0,16},{8,24},{16,0},{24,8},{1,17},{9,25},{17,1},{25,9},{2,18},{10... | collective-permute-start | bytes 589832 | tf_op jit(solution)/shard_map/ppermute | solution.py:143
  84.4 8.2 %collective-permute-start.12 = (f32[6,64,128]{2,1,0:T(8,128)S(1)}, f32[6,64,128]{2,1,0:T(8,128)S(1)}, u32[]{:S(2)}, u32[]{:S(2)}) collective-permute-start(f32[6,64,128]{2,1,0:T(8,128)S(1)} %get-tuple-element.11), channel_id=1, source_target_pairs={{0,8},{8,16},{16,24},{24,0},{1,9},{9,17},{17,25},{25,1},{2,10},{10... | collective-permute-start | bytes 589832 | tf_op jit(solution)/shard_map/ppermute | solution.py:143
  86.4 8.5 %collective-permute-start.13 = (f32[6,64,128]{2,1,0:T(8,128)S(1)}, f32[6,64,128]{2,1,0:T(8,128)S(1)}, u32[]{:S(2)}, u32[]{:S(2)}) collective-permute-start(f32[6,64,128]{2,1,0:T(8,128)S(1)} %get-tuple-element.10), channel_id=1, source_target_pairs={{0,24},{8,0},{16,8},{24,16},{1,25},{9,1},{17,9},{25,17},{2,26},{10... | collective-permute-start | bytes 589832 | tf_op jit(solution)/shard_map/ppermute | solution.py:143

commit v15 on v14

--- a/solution.py
+++ b/solution.py
@@ -117,10 +117,9 @@
     gathered = {0: corr}
     for step in (2, -2, 1, -1):
         gathered[step % nz] = shift_z(corr, step)
-    ahead = shift_z(jnp.stack([gathered[1], gathered[2]]), 2)
-    behind = shift_z(gathered[nz - 1], -2)
-    gathered[3], gathered[4] = ahead[0], ahead[1]
-    gathered[nz - 3] = behind
+    gathered[4] = shift_z(gathered[2], 2)
+    gathered[3] = shift_z(gathered[2], 1)
+    gathered[nz - 3] = shift_z(gathered[nz - 2], -1)
     ring = jnp.stack([gathered[j] for j in range(nz)])
     me_x = lax.axis_index("cx")
     shifted = [pair_blocks]

time: 96.1 us -> 93.6 us (0.974)
  waiting for transfers between devices: 30.4 us -> 27.7 us
    ppermute x3, starting transfers between devices: 4.01 us -> 5.96 us  [body(): lax.ppermute(chunk, 'cx', [(k, (k + step) % nx) for k in range(nx)])]
    ppermute x3, waiting for transfers between devices: 8.48 us -> 6.87 us  [body(): lax.ppermute(chunk, 'cx', [(k, (k + step) % nx) for k in range(nx)])]
    ppermute x6 -> x7, starting transfers between devices: 11.1 us -> 9.48 us  [shift_z(): return lax.ppermute(value, 'cz', [(k, (k - step) % nz) for k in range(nz)])]
    ppermute x6 -> x7, waiting for transfers between devices: 10.3 us -> 9.23 us  [shift_z(): return lax.ppermute(value, 'cz', [(k, (k - step) % nz) for k in range(nz)])]
    another operation x3 -> x2, other arithmetic: 5.02 us -> 5.01 us
  transfers between devices with their start and end apart: 15 -> 16, of which waited for: 8 -> 9; matrix products, arithmetic and copies ran while one was open for 6% -> 6% of each run, Pallas kernels for 0% -> 0%
where the time goes in v15:
time: 93.6 us; the launch traced here: 93.3 us
  starting transfers between devices  34 us (36%)
  waiting for transfers between devices  27.7 us (30%)
  matrix products  19.4 us (21%)
  other arithmetic  8.1 us (9%)
  local copies, waits for them, and re-layouts  3.77 us (4%)
    ppermute x2, starting transfers between devices, body(): received[shift] = lax.ppermute(white, ('cx', 'cz'), perm)  11.4 us
    ppermute x7, starting transfers between devices, shift_z(): return lax.ppermute(value, 'cz', [(k, (k - step) % nz) for k in range(nz)])  9.48 us
    ppermute x7, waiting for transfers between devices, shift_z(): return lax.ppermute(value, 'cz', [(k, (k - step) % nz) for k in range(nz)])  9.23 us
    all_to_all x1, waiting for transfers between devices, body(): corr = lax.all_to_all(corr.astype(jnp.bfloat16), 'win', 0, 0)  8.78 us
    dot_general x1, matrix products, band_dft(): jnp.einsum('rb,bac->rac', basis1, xb, precision=prec, preferred_element_t...  8 us
    dot_general x1, matrix products, band_dft(): jnp.einsum('rxpa,rpac->rxc', m, z, precision=prec, preferred_element_type...  7.93 us
    ppermute x3, waiting for transfers between devices, body(): lax.ppermute(chunk, 'cx', [(k, (k + step) % nx) for k in range(nx)])  6.87 us
    ppermute x3, starting transfers between devices, body(): lax.ppermute(chunk, 'cx', [(k, (k + step) % nx) for k in range(nx)])  5.96 us
  transfers between devices with their start and end apart: 16, of which 9 were waited for; matrix products, arithmetic and copies ran while one was open for 6% of the time, Pallas kernels for 0%

profile of v15, /device:TPU:6, one launch (start us, length us, event | category | flops | bytes accessed | tf_op | source)
XLA Modules:
  0.0 93.3 jit_solution(11303865023323760820)
XLA Ops:
  0.2 1.5 %fusion.75 = (f32[63,2,5,1,120]{4,0,3,2,1:T(8,128)S(1)}, f32[63,2,5,1,120]{4,0,3,2,1:T(8,128)S(1)}, f32[63,2,5,1,120]{4,0,3,2,1:T(8,128)S(1)}, f32[63,2,5,1,120]{4,0,3,2,1:T(8,128)S(1)}) fusion(s32[63]{0:T(128)S(1)} %iota_negate_fusion, pred[2]{0:T(512)(128)(4,1)S(1)} %iota_compare_fusion.4), kind=kLoop, calls=%fused_computation.96 | loop fusion | flops 1285200 | bytes 1209854 | tf_op jit(solution)/shard_map/cos | solution.py:55
  1.6 8.0 %fusion = f32[63,2,120,128]{3,0,2,1:T(8,128)S(1)} fusion(f32[125,120,128]{2,1,0:T(8,128)} %bitcast.73, pred[2]{0:T(512)(128)(4,1)S(1)} %iota_compare_fusion.4), kind=kOutput, calls=%fused_computation.2 | convolution fusion | flops 1451693312 | bytes 15421442 | tf_op jit(solution)/shard_map/rb,bac->rac/dot_general | solution.py:45
  9.8 7.9 %fusion.20 = f32[63,20,128]{2,1,0:T(8,128)S(1)} fusion(f32[63,2,120,128]{3,0,2,1:T(8,128)S(1)} %fusion, f32[63,20,2,120]{3,0,2,1:T(8,128)S(1)} %bitcast.74), kind=kOutput, calls=%fused_computation.26 | convolution fusion | flops 232243200 | bytes 9596160 | tf_op jit(solution)/shard_map/rxpa,rpac->rxc/dot_general | solution.py:60
  19.4 1.3 %fusion.8 = f32[576,256]{1,0:T(8,128)S(1)} fusion(f32[630,256]{1,0:T(8,128)S(1)} %reshape.399, s32[576]{0:T(1024)S(1)} %broadcast_remainder_fusion, s32[576]{0:T(1024)S(1)} %get-tuple-element.28, s32[630]{0:T(1024)S(1)} %sub.65, s32[630]{0:T(1024)S(1)} %add.300, s32[576]{0:T(1024)S(1)} %get-tuple-element.27, pred[576]{0:T(1024)(128)(4,1)S(1)} %compare_and_fusion.1, ...), kind=kOutput, calls=%fused_computation.14 | convolution fusion | flops 1118033280 | bytes 1249362 | tf_op jit(solution)/shard_map/dot_general | solution.py:69
  20.8 1.4 %fusion.70 = (bf16[512,128]{1,0:T(8,128)(2,1)S(1)}, bf16[512,128]{1,0:T(8,128)(2,1)S(1)}) fusion(f32[576,256]{1,0:T(8,128)S(1)} %fusion.8, s32[512]{0:T(512)S(1)} %get-tuple-element.26, f32[512]{0:T(512)S(1)} %multiply_sine_fusion), kind=kOutput, calls=%fused_computation.85 | convolution fusion | flops 454778880 | bytes 1380352 | tf_op jit(solution)/shard_map/dot_general | solution.py:77
  22.2 3.8 %collective-permute-start.3 = (bf16[2,512,128]{2,1,0:T(8,128)(2,1)S(1)}, bf16[2,512,128]{2,1,0:T(8,128)(2,1)S(1)}, u32[]{:S(2)}, u32[]{:S(2)}) collective-permute-start(bf16[2,512,128]{2,1,0:T(8,128)(2,1)S(1)} %pad_maximum_fusion.3), channel_id=1, source_target_pairs={{0,1},{1,2},{2,3},{3,4},{4,5},{5,6},{6,7},{7,8},{8,9},{9,10},{10,1... | collective-permute-start | bytes 786440 | tf_op jit(solution)/shard_map/ppermute | solution.py:105
  26.1 7.6 %collective-permute-start.4 = (bf16[2,512,128]{2,1,0:T(8,128)(2,1)S(1)}, bf16[2,512,128]{2,1,0:T(8,128)(2,1)S(1)}, u32[]{:S(2)}, u32[]{:S(2)}) collective-permute-start(bf16[2,512,128]{2,1,0:T(8,128)(2,1)S(1)} %pad_maximum_fusion.3), channel_id=1, source_target_pairs={{2,0},{3,1},{4,2},{5,3},{6,4},{7,5},{8,6},{9,7},{10,8},{11,9},{12,... | collective-permute-start | bytes 786440 | tf_op jit(solution)/shard_map/ppermute | solution.py:105
  33.7 2.6 %collective-permute-start.1 = (s32[6,2]{0,1:T(2,128)S(1)}, s32[6,2]{0,1:T(2,128)S(1)}, u32[]{:S(2)}, u32[]{:S(2)}) collective-permute-start(s32[6,2]{0,1:T(2,128)S(1)} %copy-done), channel_id=1, source_target_pairs={{0,16},{8,24},{16,0},{24,8},{1,17},{9,25},{17,1},{25,9},{2,18},{10... | collective-permute-start | bytes 152 | tf_op jit(solution)/shard_map/ppermute | solution.py:127
  36.3 4.7 %cosine_convert_fusion = (bf16[512,1,512]{2,0,1:T(8,128)(2,1)S(1)}, bf16[512,1,512]{2,0,1:T(8,128)(2,1)S(1)}) fusion(s32[512]{0:T(512)S(1)} %get-tuple-element.25, s32[512]{0:T(512)S(1)} %get-tuple-element.26), kind=kLoop, calls=%fused_computation.37 | loop fusion | flops 3145728 | bytes 1052672 | tf_op jit(solution)/shard_map/convert.10
  41.2 0.6 gather_fusion
  41.7 2.8 %collective-permute-done.4 = bf16[2,512,128]{2,1,0:T(8,128)(2,1)S(1)} collective-permute-done((bf16[2,512,128]{2,1,0:T(8,128)(2,1)S(1)}, bf16[2,512,128]{2,1,0:T(8,128)(2,1)S(1)}, u32[]{:S(2)}, u32[]{:S(2)}) %collective-permute-start.4) | collective-permute-done | bytes 262176 | tf_op jit(solution)/shard_map/ppermute | solution.py:105
  44.7 0.3 fusion.43
  45.0 0.7 fusion.25
  45.8 0.8 copy.7
  46.5 4.5 %all-to-all-start = ((bf16[8,64,3,128]{3,1,2,0:T(8,128)(2,1)}), bf16[8,64,3,128]{3,1,2,0:T(8,128)(2,1)S(1)}, u32[]{:S(2)}, u32[]{:S(2)}) async-start(bf16[8,64,3,128]{3,1,2,0:T(8,128)(2,1)} %copy.7), calls=%async_computation | async-start | bytes 786432 | tf_op jit(solution)/shard_map/all_to_all | solution.py:112
  51.2 8.8 %all-to-all-done = bf16[8,64,3,128]{3,1,2,0:T(8,128)(2,1)S(1)} async-done(((bf16[8,64,3,128]{3,1,2,0:T(8,128)(2,1)}), bf16[8,64,3,128]{3,1,2,0:T(8,128)(2,1)S(1)}, u32[]{:S(2)}, u32[]{:S(2)}) %all-to-all-start) | async-done | bytes 393248 | tf_op jit(solution)/shard_map/all_to_all | solution.py:112
  60.1 2.9 %collective-permute-start.6 = (f32[64,3,128]{2,0,1:T(8,128)S(1)}, f32[64,3,128]{2,0,1:T(8,128)S(1)}, u32[]{:S(2)}, u32[]{:S(2)}) collective-permute-start(f32[64,3,128]{2,0,1:T(8,128)S(1)} %convert_reduce_fusion), channel_id=1, source_target_pairs={{0,6},{1,7},{2,0},{3,1},{4,2},{5,3},{6,4},{7,5},{8,14},{9,15},{10,... | collective-permute-start | bytes 294920 | tf_op jit(solution)/shard_map/ppermute | solution.py:115
  63.0 0.4 collective-permute-start.9
  63.4 1.9 %collective-permute-start.11 = (f32[64,3,128]{2,0,1:T(8,128)S(1)}, f32[64,3,128]{2,0,1:T(8,128)S(1)}, u32[]{:S(2)}, u32[]{:S(2)}) collective-permute-start(f32[64,3,128]{2,0,1:T(8,128)S(1)} %convert_reduce_fusion), channel_id=1, source_target_pairs={{0,1},{1,2},{2,3},{3,4},{4,5},{5,6},{6,7},{7,0},{8,9},{9,10},{10,1... | collective-permute-start | bytes 294920 | tf_op jit(solution)/shard_map/ppermute | solution.py:115
  65.3 3.3 %collective-permute-done.6 = f32[64,3,128]{2,0,1:T(8,128)S(1)} collective-permute-done((f32[64,3,128]{2,0,1:T(8,128)S(1)}, f32[64,3,128]{2,0,1:T(8,128)S(1)}, u32[]{:S(2)}, u32[]{:S(2)}) %collective-permute-start.6) | collective-permute-done | bytes 98336 | tf_op jit(solution)/shard_map/ppermute | solution.py:115
  68.6 2.8 %collective-permute-start.7 = (f32[64,3,128]{2,0,1:T(8,128)S(1)}, f32[64,3,128]{2,0,1:T(8,128)S(1)}, u32[]{:S(2)}, u32[]{:S(2)}) collective-permute-start(f32[64,3,128]{2,0,1:T(8,128)S(1)} %collective-permute-done.6), channel_id=1, source_target_pairs={{0,7},{1,0},{2,1},{3,2},{4,3},{5,4},{6,5},{7,6},{8,15},{9,8},{10,9... | collective-permute-start | bytes 294920 | tf_op jit(solution)/shard_map/ppermute | solution.py:115
  71.3 1.0 %collective-permute-start.8 = (f32[64,3,128]{2,0,1:T(8,128)S(1)}, f32[64,3,128]{2,0,1:T(8,128)S(1)}, u32[]{:S(2)}, u32[]{:S(2)}) collective-permute-start(f32[64,3,128]{2,0,1:T(8,128)S(1)} %collective-permute-done.6), channel_id=1, source_target_pairs={{0,6},{1,7},{2,0},{3,1},{4,2},{5,3},{6,4},{7,5},{8,14},{9,15},{10,... | collective-permute-start | bytes 294920 | tf_op jit(solution)/shard_map/ppermute | solution.py:115
  72.4 0.5 collective-permute-start.10
  72.9 0.6 collective-permute-done.7
  73.5 5.2 %collective-permute-done.8 = f32[64,3,128]{2,0,1:T(8,128)S(1)} collective-permute-done((f32[64,3,128]{2,0,1:T(8,128)S(1)}, f32[64,3,128]{2,0,1:T(8,128)S(1)}, u32[]{:S(2)}, u32[]{:S(2)}) %collective-permute-start.8) | collective-permute-done | bytes 98336 | tf_op jit(solution)/shard_map/ppermute | solution.py:115
  78.9 0.7 gather_fusion.1
  79.7 3.9 %collective-permute-start.12 = (f32[6,64,128]{2,1,0:T(8,128)S(1)}, f32[6,64,128]{2,1,0:T(8,128)S(1)}, u32[]{:S(2)}, u32[]{:S(2)}) collective-permute-start(f32[6,64,128]{2,1,0:T(8,128)S(1)} %get-tuple-element.9), channel_id=1, source_target_pairs={{0,16},{8,24},{16,0},{24,8},{1,17},{9,25},{17,1},{25,9},{2,18},{10... | collective-permute-start | bytes 589832 | tf_op jit(solution)/shard_map/ppermute | solution.py:142
  83.6 2.1 %collective-permute-start.13 = (f32[6,64,128]{2,1,0:T(8,128)S(1)}, f32[6,64,128]{2,1,0:T(8,128)S(1)}, u32[]{:S(2)}, u32[]{:S(2)}) collective-permute-start(f32[6,64,128]{2,1,0:T(8,128)S(1)} %get-tuple-element.11), channel_id=1, source_target_pairs={{0,8},{8,16},{16,24},{24,0},{1,9},{9,17},{17,25},{25,1},{2,10},{10... | collective-permute-start | bytes 589832 | tf_op jit(solution)/shard_map/ppermute | solution.py:142
  85.7 2.0 %collective-permute-done.12 = f32[6,64,128]{2,1,0:T(8,128)S(1)} collective-permute-done((f32[6,64,128]{2,1,0:T(8,128)S(1)}, f32[6,64,128]{2,1,0:T(8,128)S(1)}, u32[]{:S(2)}, u32[]{:S(2)}) %collective-permute-start.12) | collective-permute-done | bytes 196640 | tf_op jit(solution)/shard_map/ppermute | solution.py:142
  87.7 1.6 %collective-permute-done.13 = f32[6,64,128]{2,1,0:T(8,128)S(1)} collective-permute-done((f32[6,64,128]{2,1,0:T(8,128)S(1)}, f32[6,64,128]{2,1,0:T(8,128)S(1)}, u32[]{:S(2)}, u32[]{:S(2)}) %collective-permute-start.13) | collective-permute-done | bytes 196640 | tf_op jit(solution)/shard_map/ppermute | solution.py:142
  89.3 3.3 %collective-permute-done.14 = f32[6,64,128]{2,1,0:T(8,128)S(1)} collective-permute-done((f32[6,64,128]{2,1,0:T(8,128)S(1)}, f32[6,64,128]{2,1,0:T(8,128)S(1)}, u32[]{:S(2)}, u32[]{:S(2)}) %collective-permute-start.14) | collective-permute-done | bytes 196640 | tf_op jit(solution)/shard_map/ppermute | solution.py:142
  92.6 0.8 fusion.73
  (59 shorter events, 2.9 us)
Async XLA Ops:
  20.8 12.9 %copy-start = (s32[6,2]{0,1:T(2,128)S(1)}, s32[6,2]{0,1:T(2,128)}, u32[]{:S(2)}) copy-start(s32[6,2]{0,1:T(2,128)} %param.3) | copy-start | bytes 148
  22.2 19.5 %collective-permute-start.3 = (bf16[2,512,128]{2,1,0:T(8,128)(2,1)S(1)}, bf16[2,512,128]{2,1,0:T(8,128)(2,1)S(1)}, u32[]{:S(2)}, u32[]{:S(2)}) collective-permute-start(bf16[2,512,128]{2,1,0:T(8,128)(2,1)S(1)} %pad_maximum_fusion.3), channel_id=1, source_target_pairs={{0,1},{1,2},{2,3},{3,4},{4,5},{5,6},{6,7},{7,8},{8,9},{9,10},{10,1... | collective-permute-start | bytes 786440 | tf_op jit(solution)/shard_map/ppermute | solution.py:105
  26.1 18.5 %collective-permute-start.4 = (bf16[2,512,128]{2,1,0:T(8,128)(2,1)S(1)}, bf16[2,512,128]{2,1,0:T(8,128)(2,1)S(1)}, u32[]{:S(2)}, u32[]{:S(2)}) collective-permute-start(bf16[2,512,128]{2,1,0:T(8,128)(2,1)S(1)} %pad_maximum_fusion.3), channel_id=1, source_target_pairs={{2,0},{3,1},{4,2},{5,3},{6,4},{7,5},{8,6},{9,7},{10,8},{11,9},{12,... | collective-permute-start | bytes 786440 | tf_op jit(solution)/shard_map/ppermute | solution.py:105
  33.7 7.5 %collective-permute-start = (s32[6,2]{0,1:T(2,128)S(1)}, s32[6,2]{0,1:T(2,128)S(1)}, u32[]{:S(2)}, u32[]{:S(2)}) collective-permute-start(s32[6,2]{0,1:T(2,128)S(1)} %copy-done), channel_id=1, source_target_pairs={{0,8},{8,16},{16,24},{24,0},{1,9},{9,17},{17,25},{25,1},{2,10},{10... | collective-permute-start | bytes 152 | tf_op jit(solution)/shard_map/ppermute | solution.py:127
  33.7 7.4 %collective-permute-start.1 = (s32[6,2]{0,1:T(2,128)S(1)}, s32[6,2]{0,1:T(2,128)S(1)}, u32[]{:S(2)}, u32[]{:S(2)}) collective-permute-start(s32[6,2]{0,1:T(2,128)S(1)} %copy-done), channel_id=1, source_target_pairs={{0,16},{8,24},{16,0},{24,8},{1,17},{9,25},{17,1},{25,9},{2,18},{10... | collective-permute-start | bytes 152 | tf_op jit(solution)/shard_map/ppermute | solution.py:127
  36.3 4.8 %collective-permute-start.2 = (s32[6,2]{0,1:T(2,128)S(1)}, s32[6,2]{0,1:T(2,128)S(1)}, u32[]{:S(2)}, u32[]{:S(2)}) collective-permute-start(s32[6,2]{0,1:T(2,128)S(1)} %copy-done), channel_id=1, source_target_pairs={{0,24},{8,0},{16,8},{24,16},{1,25},{9,1},{17,9},{25,17},{2,26},{10... | collective-permute-start | bytes 152 | tf_op jit(solution)/shard_map/ppermute | solution.py:127
  46.5 13.4 %all-to-all-start = ((bf16[8,64,3,128]{3,1,2,0:T(8,128)(2,1)}), bf16[8,64,3,128]{3,1,2,0:T(8,128)(2,1)S(1)}, u32[]{:S(2)}, u32[]{:S(2)}) async-start(bf16[8,64,3,128]{3,1,2,0:T(8,128)(2,1)} %copy.7), calls=%async_computation | async-start | bytes 786432 | tf_op jit(solution)/shard_map/all_to_all | solution.py:112
  60.0 12.3 %collective-permute-start.5 = (f32[64,3,128]{2,0,1:T(8,128)S(1)}, f32[64,3,128]{2,0,1:T(8,128)S(1)}, u32[]{:S(2)}, u32[]{:S(2)}) collective-permute-start(f32[64,3,128]{2,0,1:T(8,128)S(1)} %convert_reduce_fusion), channel_id=1, source_target_pairs={{0,7},{1,0},{2,1},{3,2},{4,3},{5,4},{6,5},{7,6},{8,15},{9,8},{10,9... | collective-permute-start | bytes 294920 | tf_op jit(solution)/shard_map/ppermute | solution.py:115
  60.1 8.5 %collective-permute-start.6 = (f32[64,3,128]{2,0,1:T(8,128)S(1)}, f32[64,3,128]{2,0,1:T(8,128)S(1)}, u32[]{:S(2)}, u32[]{:S(2)}) collective-permute-start(f32[64,3,128]{2,0,1:T(8,128)S(1)} %convert_reduce_fusion), channel_id=1, source_target_pairs={{0,6},{1,7},{2,0},{3,1},{4,2},{5,3},{6,4},{7,5},{8,14},{9,15},{10,... | collective-permute-start | bytes 294920 | tf_op jit(solution)/shard_map/ppermute | solution.py:115
  63.0 9.4 %collective-permute-start.9 = (f32[64,3,128]{2,0,1:T(8,128)S(1)}, f32[64,3,128]{2,0,1:T(8,128)S(1)}, u32[]{:S(2)}, u32[]{:S(2)}) collective-permute-start(f32[64,3,128]{2,0,1:T(8,128)S(1)} %convert_reduce_fusion), channel_id=1, source_target_pairs={{0,2},{1,3},{2,4},{3,5},{4,6},{5,7},{6,0},{7,1},{8,10},{9,11},{10,... | collective-permute-start | bytes 294920 | tf_op jit(solution)/shard_map/ppermute | solution.py:115
  63.4 15.4 %collective-permute-start.11 = (f32[64,3,128]{2,0,1:T(8,128)S(1)}, f32[64,3,128]{2,0,1:T(8,128)S(1)}, u32[]{:S(2)}, u32[]{:S(2)}) collective-permute-start(f32[64,3,128]{2,0,1:T(8,128)S(1)} %convert_reduce_fusion), channel_id=1, source_target_pairs={{0,1},{1,2},{2,3},{3,4},{4,5},{5,6},{6,7},{7,0},{8,9},{9,10},{10,1... | collective-permute-start | bytes 294920 | tf_op jit(solution)/shard_map/ppermute | solution.py:115
  68.6 5.0 %collective-permute-start.7 = (f32[64,3,128]{2,0,1:T(8,128)S(1)}, f32[64,3,128]{2,0,1:T(8,128)S(1)}, u32[]{:S(2)}, u32[]{:S(2)}) collective-permute-start(f32[64,3,128]{2,0,1:T(8,128)S(1)} %collective-permute-done.6), channel_id=1, source_target_pairs={{0,7},{1,0},{2,1},{3,2},{4,3},{5,4},{6,5},{7,6},{8,15},{9,8},{10,9... | collective-permute-start | bytes 294920 | tf_op jit(solution)/shard_map/ppermute | solution.py:115
  71.3 7.5 %collective-permute-start.8 = (f32[64,3,128]{2,0,1:T(8,128)S(1)}, f32[64,3,128]{2,0,1:T(8,128)S(1)}, u32[]{:S(2)}, u32[]{:S(2)}) collective-permute-start(f32[64,3,128]{2,0,1:T(8,128)S(1)} %collective-permute-done.6), channel_id=1, source_target_pairs={{0,6},{1,7},{2,0},{3,1},{4,2},{5,3},{6,4},{7,5},{8,14},{9,15},{10,... | collective-permute-start | bytes 294920 | tf_op jit(solution)/shard_map/ppermute | solution.py:115
  72.4 6.4 %collective-permute-start.10 = (f32[64,3,128]{2,0,1:T(8,128)S(1)}, f32[64,3,128]{2,0,1:T(8,128)S(1)}, u32[]{:S(2)}, u32[]{:S(2)}) collective-permute-start(f32[64,3,128]{2,0,1:T(8,128)S(1)} %collective-permute-done.9), channel_id=1, source_target_pairs={{0,1},{1,2},{2,3},{3,4},{4,5},{5,6},{6,7},{7,0},{8,9},{9,10},{10,1... | collective-permute-start | bytes 294920 | tf_op jit(solution)/shard_map/ppermute | solution.py:115
  79.7 7.9 %collective-permute-start.12 = (f32[6,64,128]{2,1,0:T(8,128)S(1)}, f32[6,64,128]{2,1,0:T(8,128)S(1)}, u32[]{:S(2)}, u32[]{:S(2)}) collective-permute-start(f32[6,64,128]{2,1,0:T(8,128)S(1)} %get-tuple-element.9), channel_id=1, source_target_pairs={{0,16},{8,24},{16,0},{24,8},{1,17},{9,25},{17,1},{25,9},{2,18},{10... | collective-permute-start | bytes 589832 | tf_op jit(solution)/shard_map/ppermute | solution.py:142
  83.6 5.7 %collective-permute-start.13 = (f32[6,64,128]{2,1,0:T(8,128)S(1)}, f32[6,64,128]{2,1,0:T(8,128)S(1)}, u32[]{:S(2)}, u32[]{:S(2)}) collective-permute-start(f32[6,64,128]{2,1,0:T(8,128)S(1)} %get-tuple-element.11), channel_id=1, source_target_pairs={{0,8},{8,16},{16,24},{24,0},{1,9},{9,17},{17,25},{25,1},{2,10},{10... | collective-permute-start | bytes 589832 | tf_op jit(solution)/shard_map/ppermute | solution.py:142
  85.7 6.9 %collective-permute-start.14 = (f32[6,64,128]{2,1,0:T(8,128)S(1)}, f32[6,64,128]{2,1,0:T(8,128)S(1)}, u32[]{:S(2)}, u32[]{:S(2)}) collective-permute-start(f32[6,64,128]{2,1,0:T(8,128)S(1)} %get-tuple-element.10), channel_id=1, source_target_pairs={{0,24},{8,0},{16,8},{24,16},{1,25},{9,1},{17,9},{25,17},{2,26},{10... | collective-permute-start | bytes 589832 | tf_op jit(solution)/shard_map/ppermute | solution.py:142

commit v16 on v15

--- a/solution.py
+++ b/solution.py
@@ -19,9 +19,7 @@
     width = NB + 2 * HALF
     rows = lax.broadcasted_iota(jnp.int32, (NB, width), 0)
     cols = lax.broadcasted_iota(jnp.int32, (NB, width), 1)
-    smoother = jnp.where(
-        (cols >= rows) & (cols <= rows + 2 * HALF), 1.0 / (2 * HALF + 1), 0.0
-    ).astype(jnp.float32)
+    smoother = jnp.where((cols >= rows) & (cols <= rows + 2 * HALF), 1.0, 0.0).astype(jnp.float32)
     taper = jnp.sin(
         math.pi * (lax.broadcasted_iota(jnp.int32, (NB,), 0).astype(jnp.float32) + 0.5) / NB
     )
@@ -74,7 +72,7 @@
     width = NB + 2 * HALF
     real, imag = band_dft(trace, F_LO - HALF, width)
     power = real * real + imag * imag
-    level = jnp.dot(smoother, power, precision=lax.Precision.HIGHEST) + 1e-06
+    level = jnp.dot(smoother, power, precision=lax.Precision.HIGH) * (1.0 / (2 * HALF + 1)) + 1e-06
     factor = taper[:, None] * lax.rsqrt(level)
     white = jnp.stack([real[HALF : HALF + NB] * factor, imag[HALF : HALF + NB] * factor])
     return white.astype(jnp.bfloat16)

time: 93.6 us -> 93.3 us (level)
  waiting for transfers between devices: 27.7 us -> 28.8 us
    ppermute x7, waiting for transfers between devices: 9.23 us -> 10.3 us  [shift_z(): return lax.ppermute(value, 'cz', [(k, (k - step) % nz) for k in range(nz)])]
where the time goes in v16:
time: 93.3 us; the launch traced here: 93.1 us
  starting transfers between devices  33.3 us (36%)
  waiting for transfers between devices  28.8 us (31%)
  matrix products  18.8 us (20%)
  other arithmetic  8.1 us (9%)
  local copies, waits for them, and re-layouts  3.77 us (4%)
    ppermute x2, starting transfers between devices, body(): received[shift] = lax.ppermute(white, ('cx', 'cz'), perm)  11.4 us
    ppermute x7, waiting for transfers between devices, shift_z(): return lax.ppermute(value, 'cz', [(k, (k - step) % nz) for k in range(nz)])  10.3 us
    all_to_all x1, waiting for transfers between devices, body(): corr = lax.all_to_all(corr.astype(jnp.bfloat16), 'win', 0, 0)  8.78 us
    ppermute x7, starting transfers between devices, shift_z(): return lax.ppermute(value, 'cz', [(k, (k - step) % nz) for k in range(nz)])  8.61 us
    dot_general x1, matrix products, band_dft(): jnp.einsum('rb,bac->rac', basis1, xb, precision=prec, preferred_element_t...  8 us
    dot_general x1, matrix products, band_dft(): jnp.einsum('rxpa,rpac->rxc', m, z, precision=prec, preferred_element_type...  7.93 us
    ppermute x3, waiting for transfers between devices, body(): lax.ppermute(chunk, 'cx', [(k, (k + step) % nx) for k in range(nx)])  6.87 us
    ppermute x3, starting transfers between devices, body(): lax.ppermute(chunk, 'cx', [(k, (k + step) % nx) for k in range(nx)])  6.09 us
  transfers between devices with their start and end apart: 16, of which 9 were waited for; matrix products, arithmetic and copies ran while one was open for 6% of the time, Pallas kernels for 0%

profile of v16, /device:TPU:6, one launch (start us, length us, event | category | flops | bytes accessed | tf_op | source)
XLA Modules:
  0.0 93.1 jit_solution(13216631159461981761)
XLA Ops:
  0.2 1.5 %fusion.78 = (f32[63,2,5,1,120]{4,0,3,2,1:T(8,128)S(1)}, f32[63,2,5,1,120]{4,0,3,2,1:T(8,128)S(1)}, f32[63,2,5,1,120]{4,0,3,2,1:T(8,128)S(1)}, f32[63,2,5,1,120]{4,0,3,2,1:T(8,128)S(1)}) fusion(s32[63]{0:T(128)S(1)} %iota_negate_fusion, pred[2]{0:T(512)(128)(4,1)S(1)} %iota_compare_fusion.4), kind=kLoop, calls=%fused_computation.97 | loop fusion | flops 1285200 | bytes 1209854 | tf_op jit(solution)/shard_map/cos | solution.py:53
  1.6 8.0 %fusion = f32[63,2,120,128]{3,0,2,1:T(8,128)S(1)} fusion(f32[125,120,128]{2,1,0:T(8,128)} %bitcast.73, pred[2]{0:T(512)(128)(4,1)S(1)} %iota_compare_fusion.4), kind=kOutput, calls=%fused_computation.2 | convolution fusion | flops 1451693312 | bytes 15421442 | tf_op jit(solution)/shard_map/rb,bac->rac/dot_general | solution.py:43
  9.8 7.9 %fusion.20 = f32[63,20,128]{2,1,0:T(8,128)S(1)} fusion(f32[63,2,120,128]{3,0,2,1:T(8,128)S(1)} %fusion, f32[63,20,2,120]{3,0,2,1:T(8,128)S(1)} %bitcast.74), kind=kOutput, calls=%fused_computation.26 | convolution fusion | flops 232243200 | bytes 9596160 | tf_op jit(solution)/shard_map/rxpa,rpac->rxc/dot_general | solution.py:58
  19.4 1.3 %fusion.8 = f32[576,256]{1,0:T(8,128)S(1)} fusion(f32[630,256]{1,0:T(8,128)S(1)} %reshape.399, s32[576]{0:T(1024)S(1)} %broadcast_remainder_fusion, s32[576]{0:T(1024)S(1)} %get-tuple-element.28, s32[630]{0:T(1024)S(1)} %sub.65, s32[630]{0:T(1024)S(1)} %add.300, s32[576]{0:T(1024)S(1)} %get-tuple-element.27, pred[576]{0:T(1024)(128)(4,1)S(1)} %compare_and_fusion.1, ...), kind=kOutput, calls=%fused_computation.14 | convolution fusion | flops 1118033280 | bytes 1249362 | tf_op jit(solution)/shard_map/dot_general | solution.py:67
  20.8 0.8 fusion.73
  21.6 3.8 %collective-permute-start.3 = (bf16[2,512,128]{2,1,0:T(8,128)(2,1)S(1)}, bf16[2,512,128]{2,1,0:T(8,128)(2,1)S(1)}, u32[]{:S(2)}, u32[]{:S(2)}) collective-permute-start(bf16[2,512,128]{2,1,0:T(8,128)(2,1)S(1)} %pad_maximum_fusion.3), channel_id=1, source_target_pairs={{0,1},{1,2},{2,3},{3,4},{4,5},{5,6},{6,7},{7,8},{8,9},{9,10},{10,1... | collective-permute-start | bytes 786440 | tf_op jit(solution)/shard_map/ppermute | solution.py:103
  25.4 7.6 %collective-permute-start.4 = (bf16[2,512,128]{2,1,0:T(8,128)(2,1)S(1)}, bf16[2,512,128]{2,1,0:T(8,128)(2,1)S(1)}, u32[]{:S(2)}, u32[]{:S(2)}) collective-permute-start(bf16[2,512,128]{2,1,0:T(8,128)(2,1)S(1)} %pad_maximum_fusion.3), channel_id=1, source_target_pairs={{2,0},{3,1},{4,2},{5,3},{6,4},{7,5},{8,6},{9,7},{10,8},{11,9},{12,... | collective-permute-start | bytes 786440 | tf_op jit(solution)/shard_map/ppermute | solution.py:103
  33.1 2.6 %collective-permute-start.1 = (s32[6,2]{0,1:T(2,128)S(1)}, s32[6,2]{0,1:T(2,128)S(1)}, u32[]{:S(2)}, u32[]{:S(2)}) collective-permute-start(s32[6,2]{0,1:T(2,128)S(1)} %copy-done), channel_id=1, source_target_pairs={{0,16},{8,24},{16,0},{24,8},{1,17},{9,25},{17,1},{25,9},{2,18},{10... | collective-permute-start | bytes 152 | tf_op jit(solution)/shard_map/ppermute | solution.py:125
  35.7 4.7 %cosine_convert_fusion = (bf16[512,1,512]{2,0,1:T(8,128)(2,1)S(1)}, bf16[512,1,512]{2,0,1:T(8,128)(2,1)S(1)}) fusion(s32[512]{0:T(512)S(1)} %get-tuple-element.25, s32[512]{0:T(512)S(1)} %get-tuple-element.26), kind=kLoop, calls=%fused_computation.38 | loop fusion | flops 3145728 | bytes 1052672 | tf_op jit(solution)/shard_map/convert.10
  40.5 0.6 gather_fusion
  41.1 2.8 %collective-permute-done.4 = bf16[2,512,128]{2,1,0:T(8,128)(2,1)S(1)} collective-permute-done((bf16[2,512,128]{2,1,0:T(8,128)(2,1)S(1)}, bf16[2,512,128]{2,1,0:T(8,128)(2,1)S(1)}, u32[]{:S(2)}, u32[]{:S(2)}) %collective-permute-start.4) | collective-permute-done | bytes 262176 | tf_op jit(solution)/shard_map/ppermute | solution.py:103
  44.1 0.3 fusion.46
  44.4 0.7 fusion.25
  45.1 0.8 copy.7
  45.9 4.5 %all-to-all-start = ((bf16[8,64,3,128]{3,1,2,0:T(8,128)(2,1)}), bf16[8,64,3,128]{3,1,2,0:T(8,128)(2,1)S(1)}, u32[]{:S(2)}, u32[]{:S(2)}) async-start(bf16[8,64,3,128]{3,1,2,0:T(8,128)(2,1)} %copy.7), calls=%async_computation | async-start | bytes 786432 | tf_op jit(solution)/shard_map/all_to_all | solution.py:110
  50.6 8.8 %all-to-all-done = bf16[8,64,3,128]{3,1,2,0:T(8,128)(2,1)S(1)} async-done(((bf16[8,64,3,128]{3,1,2,0:T(8,128)(2,1)}), bf16[8,64,3,128]{3,1,2,0:T(8,128)(2,1)S(1)}, u32[]{:S(2)}, u32[]{:S(2)}) %all-to-all-start) | async-done | bytes 393248 | tf_op jit(solution)/shard_map/all_to_all | solution.py:110
  59.5 2.9 %collective-permute-start.6 = (f32[64,3,128]{2,0,1:T(8,128)S(1)}, f32[64,3,128]{2,0,1:T(8,128)S(1)}, u32[]{:S(2)}, u32[]{:S(2)}) collective-permute-start(f32[64,3,128]{2,0,1:T(8,128)S(1)} %convert_reduce_fusion), channel_id=1, source_target_pairs={{0,6},{1,7},{2,0},{3,1},{4,2},{5,3},{6,4},{7,5},{8,14},{9,15},{10,... | collective-permute-start | bytes 294920 | tf_op jit(solution)/shard_map/ppermute | solution.py:113
  62.4 0.4 collective-permute-start.9
  62.8 1.9 %collective-permute-start.11 = (f32[64,3,128]{2,0,1:T(8,128)S(1)}, f32[64,3,128]{2,0,1:T(8,128)S(1)}, u32[]{:S(2)}, u32[]{:S(2)}) collective-permute-start(f32[64,3,128]{2,0,1:T(8,128)S(1)} %convert_reduce_fusion), channel_id=1, source_target_pairs={{0,1},{1,2},{2,3},{3,4},{4,5},{5,6},{6,7},{7,0},{8,9},{9,10},{10,1... | collective-permute-start | bytes 294920 | tf_op jit(solution)/shard_map/ppermute | solution.py:113
  64.7 3.9 %collective-permute-done.6 = f32[64,3,128]{2,0,1:T(8,128)S(1)} collective-permute-done((f32[64,3,128]{2,0,1:T(8,128)S(1)}, f32[64,3,128]{2,0,1:T(8,128)S(1)}, u32[]{:S(2)}, u32[]{:S(2)}) %collective-permute-start.6) | collective-permute-done | bytes 98336 | tf_op jit(solution)/shard_map/ppermute | solution.py:113
  68.6 2.0 %collective-permute-start.7 = (f32[64,3,128]{2,0,1:T(8,128)S(1)}, f32[64,3,128]{2,0,1:T(8,128)S(1)}, u32[]{:S(2)}, u32[]{:S(2)}) collective-permute-start(f32[64,3,128]{2,0,1:T(8,128)S(1)} %collective-permute-done.6), channel_id=1, source_target_pairs={{0,7},{1,0},{2,1},{3,2},{4,3},{5,4},{6,5},{7,6},{8,15},{9,8},{10,9... | collective-permute-start | bytes 294920 | tf_op jit(solution)/shard_map/ppermute | solution.py:113
  70.6 1.2 %collective-permute-start.8 = (f32[64,3,128]{2,0,1:T(8,128)S(1)}, f32[64,3,128]{2,0,1:T(8,128)S(1)}, u32[]{:S(2)}, u32[]{:S(2)}) collective-permute-start(f32[64,3,128]{2,0,1:T(8,128)S(1)} %collective-permute-done.6), channel_id=1, source_target_pairs={{0,6},{1,7},{2,0},{3,1},{4,2},{5,3},{6,4},{7,5},{8,14},{9,15},{10,... | collective-permute-start | bytes 294920 | tf_op jit(solution)/shard_map/ppermute | solution.py:113
  71.8 0.2 collective-permute-done.9
  72.2 1.1 %collective-permute-done.7 = f32[64,3,128]{2,0,1:T(8,128)S(1)} collective-permute-done((f32[64,3,128]{2,0,1:T(8,128)S(1)}, f32[64,3,128]{2,0,1:T(8,128)S(1)}, u32[]{:S(2)}, u32[]{:S(2)}) %collective-permute-start.7) | collective-permute-done | bytes 98336 | tf_op jit(solution)/shard_map/ppermute | solution.py:113
  73.3 5.2 %collective-permute-done.8 = f32[64,3,128]{2,0,1:T(8,128)S(1)} collective-permute-done((f32[64,3,128]{2,0,1:T(8,128)S(1)}, f32[64,3,128]{2,0,1:T(8,128)S(1)}, u32[]{:S(2)}, u32[]{:S(2)}) %collective-permute-start.8) | collective-permute-done | bytes 98336 | tf_op jit(solution)/shard_map/ppermute | solution.py:113
  78.5 0.7 gather_fusion.1
  79.4 3.9 %collective-permute-start.12 = (f32[6,64,128]{2,1,0:T(8,128)S(1)}, f32[6,64,128]{2,1,0:T(8,128)S(1)}, u32[]{:S(2)}, u32[]{:S(2)}) collective-permute-start(f32[6,64,128]{2,1,0:T(8,128)S(1)} %get-tuple-element.9), channel_id=1, source_target_pairs={{0,16},{8,24},{16,0},{24,8},{1,17},{9,25},{17,1},{25,9},{2,18},{10... | collective-permute-start | bytes 589832 | tf_op jit(solution)/shard_map/ppermute | solution.py:140
  83.3 2.2 %collective-permute-start.13 = (f32[6,64,128]{2,1,0:T(8,128)S(1)}, f32[6,64,128]{2,1,0:T(8,128)S(1)}, u32[]{:S(2)}, u32[]{:S(2)}) collective-permute-start(f32[6,64,128]{2,1,0:T(8,128)S(1)} %get-tuple-element.11), channel_id=1, source_target_pairs={{0,8},{8,16},{16,24},{24,0},{1,9},{9,17},{17,25},{25,1},{2,10},{10... | collective-permute-start | bytes 589832 | tf_op jit(solution)/shard_map/ppermute | solution.py:140
  85.5 1.8 %collective-permute-done.12 = f32[6,64,128]{2,1,0:T(8,128)S(1)} collective-permute-done((f32[6,64,128]{2,1,0:T(8,128)S(1)}, f32[6,64,128]{2,1,0:T(8,128)S(1)}, u32[]{:S(2)}, u32[]{:S(2)}) %collective-permute-start.12) | collective-permute-done | bytes 196640 | tf_op jit(solution)/shard_map/ppermute | solution.py:140
  87.3 1.7 %collective-permute-done.13 = f32[6,64,128]{2,1,0:T(8,128)S(1)} collective-permute-done((f32[6,64,128]{2,1,0:T(8,128)S(1)}, f32[6,64,128]{2,1,0:T(8,128)S(1)}, u32[]{:S(2)}, u32[]{:S(2)}) %collective-permute-start.13) | collective-permute-done | bytes 196640 | tf_op jit(solution)/shard_map/ppermute | solution.py:140
  89.0 3.4 %collective-permute-done.14 = f32[6,64,128]{2,1,0:T(8,128)S(1)} collective-permute-done((f32[6,64,128]{2,1,0:T(8,128)S(1)}, f32[6,64,128]{2,1,0:T(8,128)S(1)}, u32[]{:S(2)}, u32[]{:S(2)}) %collective-permute-start.14) | collective-permute-done | bytes 196640 | tf_op jit(solution)/shard_map/ppermute | solution.py:140
  92.3 0.8 fusion.76
  (59 shorter events, 3.0 us)
Async XLA Ops:
  20.8 12.3 %copy-start = (s32[6,2]{0,1:T(2,128)S(1)}, s32[6,2]{0,1:T(2,128)}, u32[]{:S(2)}) copy-start(s32[6,2]{0,1:T(2,128)} %param.3) | copy-start | bytes 148
  21.6 19.5 %collective-permute-start.3 = (bf16[2,512,128]{2,1,0:T(8,128)(2,1)S(1)}, bf16[2,512,128]{2,1,0:T(8,128)(2,1)S(1)}, u32[]{:S(2)}, u32[]{:S(2)}) collective-permute-start(bf16[2,512,128]{2,1,0:T(8,128)(2,1)S(1)} %pad_maximum_fusion.3), channel_id=1, source_target_pairs={{0,1},{1,2},{2,3},{3,4},{4,5},{5,6},{6,7},{7,8},{8,9},{9,10},{10,1... | collective-permute-start | bytes 786440 | tf_op jit(solution)/shard_map/ppermute | solution.py:103
  25.4 18.5 %collective-permute-start.4 = (bf16[2,512,128]{2,1,0:T(8,128)(2,1)S(1)}, bf16[2,512,128]{2,1,0:T(8,128)(2,1)S(1)}, u32[]{:S(2)}, u32[]{:S(2)}) collective-permute-start(bf16[2,512,128]{2,1,0:T(8,128)(2,1)S(1)} %pad_maximum_fusion.3), channel_id=1, source_target_pairs={{2,0},{3,1},{4,2},{5,3},{6,4},{7,5},{8,6},{9,7},{10,8},{11,9},{12,... | collective-permute-start | bytes 786440 | tf_op jit(solution)/shard_map/ppermute | solution.py:103
  33.0 7.5 %collective-permute-start = (s32[6,2]{0,1:T(2,128)S(1)}, s32[6,2]{0,1:T(2,128)S(1)}, u32[]{:S(2)}, u32[]{:S(2)}) collective-permute-start(s32[6,2]{0,1:T(2,128)S(1)} %copy-done), channel_id=1, source_target_pairs={{0,8},{8,16},{16,24},{24,0},{1,9},{9,17},{17,25},{25,1},{2,10},{10... | collective-permute-start | bytes 152 | tf_op jit(solution)/shard_map/ppermute | solution.py:125
  33.1 7.4 %collective-permute-start.1 = (s32[6,2]{0,1:T(2,128)S(1)}, s32[6,2]{0,1:T(2,128)S(1)}, u32[]{:S(2)}, u32[]{:S(2)}) collective-permute-start(s32[6,2]{0,1:T(2,128)S(1)} %copy-done), channel_id=1, source_target_pairs={{0,16},{8,24},{16,0},{24,8},{1,17},{9,25},{17,1},{25,9},{2,18},{10... | collective-permute-start | bytes 152 | tf_op jit(solution)/shard_map/ppermute | solution.py:125
  35.7 4.8 %collective-permute-start.2 = (s32[6,2]{0,1:T(2,128)S(1)}, s32[6,2]{0,1:T(2,128)S(1)}, u32[]{:S(2)}, u32[]{:S(2)}) collective-permute-start(s32[6,2]{0,1:T(2,128)S(1)} %copy-done), channel_id=1, source_target_pairs={{0,24},{8,0},{16,8},{24,16},{1,25},{9,1},{17,9},{25,17},{2,26},{10... | collective-permute-start | bytes 152 | tf_op jit(solution)/shard_map/ppermute | solution.py:125
  45.9 13.4 %all-to-all-start = ((bf16[8,64,3,128]{3,1,2,0:T(8,128)(2,1)}), bf16[8,64,3,128]{3,1,2,0:T(8,128)(2,1)S(1)}, u32[]{:S(2)}, u32[]{:S(2)}) async-start(bf16[8,64,3,128]{3,1,2,0:T(8,128)(2,1)} %copy.7), calls=%async_computation | async-start | bytes 786432 | tf_op jit(solution)/shard_map/all_to_all | solution.py:110
  59.4 12.4 %collective-permute-start.5 = (f32[64,3,128]{2,0,1:T(8,128)S(1)}, f32[64,3,128]{2,0,1:T(8,128)S(1)}, u32[]{:S(2)}, u32[]{:S(2)}) collective-permute-start(f32[64,3,128]{2,0,1:T(8,128)S(1)} %convert_reduce_fusion), channel_id=1, source_target_pairs={{0,7},{1,0},{2,1},{3,2},{4,3},{5,4},{6,5},{7,6},{8,15},{9,8},{10,9... | collective-permute-start | bytes 294920 | tf_op jit(solution)/shard_map/ppermute | solution.py:113
  59.5 9.1 %collective-permute-start.6 = (f32[64,3,128]{2,0,1:T(8,128)S(1)}, f32[64,3,128]{2,0,1:T(8,128)S(1)}, u32[]{:S(2)}, u32[]{:S(2)}) collective-permute-start(f32[64,3,128]{2,0,1:T(8,128)S(1)} %convert_reduce_fusion), channel_id=1, source_target_pairs={{0,6},{1,7},{2,0},{3,1},{4,2},{5,3},{6,4},{7,5},{8,14},{9,15},{10,... | collective-permute-start | bytes 294920 | tf_op jit(solution)/shard_map/ppermute | solution.py:113
  62.4 9.6 %collective-permute-start.9 = (f32[64,3,128]{2,0,1:T(8,128)S(1)}, f32[64,3,128]{2,0,1:T(8,128)S(1)}, u32[]{:S(2)}, u32[]{:S(2)}) collective-permute-start(f32[64,3,128]{2,0,1:T(8,128)S(1)} %convert_reduce_fusion), channel_id=1, source_target_pairs={{0,2},{1,3},{2,4},{3,5},{4,6},{5,7},{6,0},{7,1},{8,10},{9,11},{10,... | collective-permute-start | bytes 294920 | tf_op jit(solution)/shard_map/ppermute | solution.py:113
  62.8 15.7 %collective-permute-start.11 = (f32[64,3,128]{2,0,1:T(8,128)S(1)}, f32[64,3,128]{2,0,1:T(8,128)S(1)}, u32[]{:S(2)}, u32[]{:S(2)}) collective-permute-start(f32[64,3,128]{2,0,1:T(8,128)S(1)} %convert_reduce_fusion), channel_id=1, source_target_pairs={{0,1},{1,2},{2,3},{3,4},{4,5},{5,6},{6,7},{7,0},{8,9},{9,10},{10,1... | collective-permute-start | bytes 294920 | tf_op jit(solution)/shard_map/ppermute | solution.py:113
  68.6 4.6 %collective-permute-start.7 = (f32[64,3,128]{2,0,1:T(8,128)S(1)}, f32[64,3,128]{2,0,1:T(8,128)S(1)}, u32[]{:S(2)}, u32[]{:S(2)}) collective-permute-start(f32[64,3,128]{2,0,1:T(8,128)S(1)} %collective-permute-done.6), channel_id=1, source_target_pairs={{0,7},{1,0},{2,1},{3,2},{4,3},{5,4},{6,5},{7,6},{8,15},{9,8},{10,9... | collective-permute-start | bytes 294920 | tf_op jit(solution)/shard_map/ppermute | solution.py:113
  70.6 7.8 %collective-permute-start.8 = (f32[64,3,128]{2,0,1:T(8,128)S(1)}, f32[64,3,128]{2,0,1:T(8,128)S(1)}, u32[]{:S(2)}, u32[]{:S(2)}) collective-permute-start(f32[64,3,128]{2,0,1:T(8,128)S(1)} %collective-permute-done.6), channel_id=1, source_target_pairs={{0,6},{1,7},{2,0},{3,1},{4,2},{5,3},{6,4},{7,5},{8,14},{9,15},{10,... | collective-permute-start | bytes 294920 | tf_op jit(solution)/shard_map/ppermute | solution.py:113
  72.0 6.4 %collective-permute-start.10 = (f32[64,3,128]{2,0,1:T(8,128)S(1)}, f32[64,3,128]{2,0,1:T(8,128)S(1)}, u32[]{:S(2)}, u32[]{:S(2)}) collective-permute-start(f32[64,3,128]{2,0,1:T(8,128)S(1)} %collective-permute-done.9), channel_id=1, source_target_pairs={{0,1},{1,2},{2,3},{3,4},{4,5},{5,6},{6,7},{7,0},{8,9},{9,10},{10,1... | collective-permute-start | bytes 294920 | tf_op jit(solution)/shard_map/ppermute | solution.py:113
  79.4 7.9 %collective-permute-start.12 = (f32[6,64,128]{2,1,0:T(8,128)S(1)}, f32[6,64,128]{2,1,0:T(8,128)S(1)}, u32[]{:S(2)}, u32[]{:S(2)}) collective-permute-start(f32[6,64,128]{2,1,0:T(8,128)S(1)} %get-tuple-element.9), channel_id=1, source_target_pairs={{0,16},{8,24},{16,0},{24,8},{1,17},{9,25},{17,1},{25,9},{2,18},{10... | collective-permute-start | bytes 589832 | tf_op jit(solution)/shard_map/ppermute | solution.py:140
  83.3 5.7 %collective-permute-start.13 = (f32[6,64,128]{2,1,0:T(8,128)S(1)}, f32[6,64,128]{2,1,0:T(8,128)S(1)}, u32[]{:S(2)}, u32[]{:S(2)}) collective-permute-start(f32[6,64,128]{2,1,0:T(8,128)S(1)} %get-tuple-element.11), channel_id=1, source_target_pairs={{0,8},{8,16},{16,24},{24,0},{1,9},{9,17},{17,25},{25,1},{2,10},{10... | collective-permute-start | bytes 589832 | tf_op jit(solution)/shard_map/ppermute | solution.py:140
  85.5 6.9 %collective-permute-start.14 = (f32[6,64,128]{2,1,0:T(8,128)S(1)}, f32[6,64,128]{2,1,0:T(8,128)S(1)}, u32[]{:S(2)}, u32[]{:S(2)}) collective-permute-start(f32[6,64,128]{2,1,0:T(8,128)S(1)} %get-tuple-element.10), channel_id=1, source_target_pairs={{0,24},{8,0},{16,8},{24,16},{1,25},{9,1},{17,9},{25,17},{2,26},{10... | collective-permute-start | bytes 589832 | tf_op jit(solution)/shard_map/ppermute | solution.py:140
